TPU v7x, 128 devices: a whole 4x4x4 slice. The times are simulated.
128 devices in a mesh: req: 8 (over x, core), seq: 16 (over z, y).
Axes of the slice: x: 4, y: 4, z: 4, core: 2. Of those that a mesh axis runs over, the one named last changes fastest.
Arguments:
- hidden: bfloat16 [8, 2048, 2048], P('req', 'seq'), may hold values from -6 to 6
- lengths: int32 [8], replicated, may hold values from 1 to 2048, 10240 in all
- slot_request: int32 [8], replicated, may hold values from 0 to 7, each once
- norm_gain: bfloat16 [2048], replicated, may hold values from 0.099609375 to 1.8984375
- in_weight: bfloat16 [2, 2048, 4096], P(None, 'req', 'seq'), may hold values from -0.125 to 0.125
- conv_weight: bfloat16 [4, 4096], P(None, 'seq'), may hold values from -3 to 3
- conv_bias: bfloat16 [4096], P('seq'), may hold values from -0.5 to 0.5
- xproj_weight: bfloat16 [4096, 160], P('seq'), may hold values from -0.09375 to 0.09375
- dt_weight: bfloat16 [128, 4096], P(None, 'seq'), may hold values from -0.5 to 0.5
- dt_bias: bfloat16 [4096], P('seq'), may hold values from -6.91 to -2.25
- a_log: float32 [16, 4096], replicated, may hold values from -2.3 to 1.39
- skip_gain: float32 [4096], replicated, may hold values from 0.5 to 1.5
- out_weight: bfloat16 [4096, 2048], P('seq', 'req'), may hold values from -0.09375 to 0.09375
Outputs:
- mixed: bfloat16 [8, 2048, 2048], P('req', 'seq')
- final_state: float32 [8, 16, 4096], P('req', None, 'seq')
Inputs may be any that keep to these rules, and one draw needn't show every extreme that they name: `lengths`: each slot's length is at least 1, the longest is exactly 2048, and they sum to 10240. `slot_request`: A permutation of the requests.
All inputs are finite; a program needn't handle non-finite values.
Results may differ from a plain program's by a relative error of at most 0.015.
Values may be sent and summed in bfloat16 or wider, within the bound.
No kernel may reach another device: no remote copies, remote signals or barrier semaphores. Data moves between devices by JAX's collectives and lax.ppermute only.
A program may use at most 128 MiB of HBM per device.

v0:
```python
import jax
import jax.numpy as jnp
from jax import lax
from jax.sharding import PartitionSpec as P

STATE = 16
RANK = 128


def shifted(block, axis, distance):
    devices = range(lax.axis_size(axis))
    route = [(i - distance, i) for i in devices if i - distance in devices]
    return lax.ppermute(block, axis, route)


def spread(array, axis, root):
    mine = lax.axis_index(axis) == root
    return lax.psum(jnp.where(mine, array, jnp.zeros_like(array)), axis)


def to_blocks(array):
    pieces, length, columns = array.shape
    return jnp.moveaxis(array.reshape(pieces, 16, length // 16, columns), 1, 0)


def from_blocks(array):
    count, pieces, group, columns = array.shape
    return jnp.moveaxis(array, 0, 1).reshape(pieces, count * group, columns)


def piece_scan(rates, values, entry, readout, decay):
    pieces, length, columns = rates.shape
    group = length // 16
    positions = jnp.arange(length, dtype=jnp.int32)
    lower = (positions[None, :] <= positions[:, None]).astype(jnp.float32)
    running = jnp.einsum("rs,psw->prw", lower, rates, precision=lax.Precision.HIGHEST)

    def advance(state, items):
        rate, value, into, outof = items
        outputs = []
        for place in range(group):
            factor = jnp.exp(rate[:, place][:, None, :] * decay[None])
            state = (
                factor * state
                + (rate[:, place] * value[:, place])[:, None, :] * into[:, place][:, :, None]
            )
            outputs.append(jnp.sum(outof[:, place][:, :, None] * state, axis=1))
        return (state, jnp.stack(outputs, axis=1))

    start = jnp.zeros((pieces, decay.shape[0], columns), jnp.float32)
    end_local, local_out = lax.scan(
        advance, start, (to_blocks(rates), to_blocks(values), to_blocks(entry), to_blocks(readout))
    )
    total_decay = jnp.exp(running[:, length - 1][:, None, :] * decay[None])
    return (end_local, from_blocks(local_out), total_decay, running)


def carried_part(running, readout, decay, carry_in):

    def correct(items):
        total, outof = items
        kept = jnp.exp(total[:, :, None, :] * decay[None, None]) * carry_in[:, None]
        return jnp.sum(outof[:, :, :, None] * kept, axis=2)

    return from_blocks(lax.map(correct, (to_blocks(running), to_blocks(readout))))


def per_device(
    hidden,
    lengths,
    slot_request,
    norm_gain,
    in_weight,
    conv_weight,
    conv_bias,
    xproj_weight,
    dt_weight,
    dt_bias,
    a_log,
    skip_gain,
    out_weight,
):
    seq_count = lax.axis_size("seq")
    seq_index = lax.axis_index("seq")
    req_index = lax.axis_index("req")
    rows = hidden.shape[1]
    span = rows * seq_count
    width = in_weight.shape[2]
    taps_count = conv_weight.shape[0]
    state_count = a_log.shape[0]
    total_inner = a_log.shape[1]
    tokens = hidden[0].astype(jnp.float32)
    scale = lax.rsqrt(jnp.mean(tokens * tokens, axis=-1, keepdims=True) + 1e-05)
    normed = (tokens * scale * norm_gain.astype(jnp.float32)).astype(jnp.bfloat16)
    w_in = lax.all_gather(in_weight, "req", axis=1, tiled=True)
    w_flat = jnp.concatenate((w_in[0], w_in[1]), axis=1)
    both = jnp.dot(
        lax.all_gather(normed, "seq", axis=0, tiled=True),
        w_flat,
        preferred_element_type=jnp.float32,
    )
    xin = both[:, :width]
    zgate = both[:, width:].astype(jnp.bfloat16)
    padded = jnp.pad(xin, ((taps_count - 1, 0), (0, 0)))
    taps = conv_weight.astype(jnp.float32)
    convolved = conv_bias.astype(jnp.float32) + jnp.zeros_like(xin)
    for tap in range(taps_count):
        convolved = convolved + taps[tap] * padded[tap : tap + span, :]
    inner = jax.nn.silu(convolved).astype(jnp.bfloat16)
    partial_proj = jnp.dot(inner, xproj_weight, preferred_element_type=jnp.float32)
    length_here = lax.dynamic_index_in_dim(lengths, req_index, 0, keepdims=False)
    summed = lax.psum(partial_proj, "seq")
    live_all = (jnp.arange(span, dtype=jnp.int32) < length_here).astype(jnp.float32)
    rate_low = summed[:, :RANK].astype(jnp.bfloat16)
    delta_ch = (
        jax.nn.softplus(
            jnp.dot(rate_low, dt_weight, preferred_element_type=jnp.float32)
            + dt_bias.astype(jnp.float32)
        )
        * live_all[:, None]
    )
    w_out = lax.all_gather(out_weight, "req", axis=1, tiled=True)
    inner_tok = lax.all_to_all(inner, "seq", split_axis=0, concat_axis=1, tiled=True)
    delta_tok = lax.all_to_all(
        delta_ch.astype(jnp.bfloat16), "seq", split_axis=0, concat_axis=1, tiled=True
    ).astype(delta_ch.dtype)
    own_proj = lax.dynamic_slice_in_dim(summed, seq_index * rows, rows, 0)
    decay = -jnp.exp(a_log)
    inner_f = inner_tok.astype(jnp.float32)
    entry = own_proj[None, :, RANK : RANK + STATE]
    readout = own_proj[None, :, RANK + STATE :]
    end_local, local_out, total_decay, running = piece_scan(
        delta_tok[None], inner_f[None], entry, readout, decay
    )
    zeros_state = jnp.zeros((state_count, total_inner), jnp.float32)

    def relay(turn, incoming):
        return shifted(total_decay[0] * incoming + end_local[0], "seq", 1)

    carry_in = lax.fori_loop(0, seq_count - 1, relay, zeros_state)
    carried = carried_part(running, readout, decay, carry_in[None])
    scanned = ((local_out + carried)[0] + skip_gain * inner_f).astype(jnp.bfloat16)
    last = spread(
        (total_decay[0] * carry_in + end_local[0]).astype(jnp.bfloat16), "seq", seq_count - 1
    ).astype(jnp.float32)
    mine = lax.dynamic_slice_in_dim(last, seq_index * width, width, 1)
    scanned_ch = lax.all_to_all(scanned, "seq", split_axis=1, concat_axis=0, tiled=True)
    gated_ch = (scanned_ch.astype(jnp.float32) * jax.nn.silu(zgate.astype(jnp.float32))).astype(
        jnp.bfloat16
    )
    branch = lax.psum_scatter(
        jnp.dot(gated_ch, w_out, preferred_element_type=jnp.float32).astype(jnp.bfloat16),
        "seq",
        scatter_dimension=0,
        tiled=True,
    ).astype(jnp.float32)
    slot_all = lax.all_gather(mine[None], "req", axis=0, tiled=True)
    picked = (slot_request == req_index).astype(jnp.float32)
    final_state = jnp.sum(picked[:, None, None] * slot_all, axis=0, keepdims=True)
    mixed = (tokens + branch).astype(jnp.bfloat16)[None]
    return (mixed, final_state)


def solution(mesh):
    in_specs = (
        P("req", "seq", None),
        P(),
        P(),
        P(),
        P(None, "req", "seq"),
        P(None, "seq"),
        P("seq"),
        P("seq", None),
        P(None, "seq"),
        P("seq"),
        P(),
        P(),
        P("seq", "req"),
    )
    out_specs = (P("req", "seq", None), P("req", None, "seq"))
    return jax.shard_map(
        per_device, mesh=mesh, in_specs=in_specs, out_specs=out_specs, check_vma=False
    )
```

profile of v0, /device:TPU:1, one launch (start us, length us, event | category | flops | bytes accessed | tf_op | source)
XLA Modules:
  0.0 717.0 jit_solution(14593859675135900258)
XLA Ops:
  12.1 26.5 %all-gather.7.cloned.1.call-done = bf16[2,2048,256]{2,1,0:T(8,128)(2,1)} async-done(((bf16[2,256,256]{2,1,0:T(8,128)(2,1)}), bf16[2,2048,256]{2,1,0:T(8,128)(2,1)}) %all-gather.7.cloned.1.call-update) | async-done | bytes 2097168 | tf_op jit(solution)/shard_map/all_gather | solution.py:95
  40.3 71.8 %all-gather.5.cloned.1.call-done = bf16[2048,2048]{1,0:T(8,128)(2,1)} async-done(((bf16[128,2048]{1,0:T(8,128)(2,1)}), bf16[2048,2048]{1,0:T(8,128)(2,1)}) %all-gather.5.cloned.1.call-update) | async-done | bytes 8388624 | tf_op jit(solution)/shard_map/all_gather | solution.py:98
  112.1 6.9 fusion.33
  126.1 5.2 all-to-all-start.1
  132.5 87.7 %all-reduce.4.cloned.1.call-done = f32[2048,160]{0,1:T(8,128)} async-done(((f32[2048,160]{0,1:T(8,128)}), f32[2048,160]{0,1:T(8,128)}) %all-reduce.4.cloned.1.call-update) | async-done | bytes 1310736 | tf_op jit(solution)/shard_map/psum | solution.py:112
  224.3 4.5 all-to-all-start
  237.1 6.5 all-to-all-done
  253.4 65.7 %while.35 = (s32[]{:T(128)}, f32[1,16,4096]{2,1,0:T(8,128)S(1)}, f32[16,1,8,4096]{3,2,1,0:T(8,128)}, f32[16,1,8,4096]{3,2,1,0:T(8,128)}, f32[16,4096]{1,0:T(8,12...) while((s32[]{:T(128)}, f32[1,16,4096]{2,1,0:T(8,128)S(1)}, ...), condition=%wide.region_11.12_spmd.clone, body=%wide.region_2.11_spmd.clone.sunk | while | flops 4849667 | bytes 4347896 | solution.py:51
  319.2 134.4 %while.33 = (s32[]{:T(128)}, f32[16,4096]{1,0:T(8,128)S(1)}, f32[1,16,4096]{2,1,0:T(8,128)S(1)}, f32[1,16,4096]{2,1,0:T(8,128)S(1)}, s32[]{:T(128)}) while((s32[]{:T(128)}, f32[16,4096]{1,0:T(8,128)S(1)}, f32[1,16,4096]{2,1,0:T(8,128)S(1)}, f32[1,16,4096]{2,1,0:T(8,128)S(1)}, s32[]{:T(128)}) %tuple.124), condition=%wide.region_13.14_spmd, body=%wide.region_12.13_spmd.sunk | while | flops 131074 | bytes 2097253 | solution.py:140
  335.6 4.4 collective-permute-done
  343.9 5.5 collective-permute-done
  353.3 5.5 collective-permute-done
  358.9 4.1 collective-permute-start
  363.0 4.6 collective-permute-done
  367.7 4.1 collective-permute-start
  375.6 4.1 collective-permute-start
  383.1 9.5 %collective-permute-start = (f32[16,4096]{1,0:T(8,128)S(1)}, f32[16,4096]{1,0:T(8,128)S(1)}, u32[]{:S(2)}, u32[]{:S(2)}) collective-permute-start(f32[16,4096]{1,0:T(8,128)S(1)} %bitcast_add_fusion.3), channel_id=1, source_target_pairs={{0,1},{1,2},{2,3},{3,4},{4,5},{5,6},{6,7},{7,8},{8,9},{9,10},{10,1... | collective-permute-start | bytes 786440 | tf_op jit(solution)/shard_map/while/body/eval_jaxpr/ppermute | solution.py:13
  392.6 5.1 collective-permute-done
  397.7 5.6 collective-permute-start
  403.3 3.9 collective-permute-done
  407.3 5.0 collective-permute-start
  415.7 6.2 collective-permute-start
  425.2 6.2 collective-permute-start
  434.8 6.2 collective-permute-start
  444.4 5.9 collective-permute-start
  455.1 35.8 %while.34 = (s32[]{:T(128)}, f32[16,1,8,4096]{3,2,1,0:T(8,128)}, f32[16,1,8,16]{3,2,1,0:T(8,128)S(1)}, f32[16,1,8,4096]{3,2,1,0:T(8,128)}, f32[16,4096]{1,0:T(8,128)S(1)}, /*index=5*/f32[16,4096]{1,0:T(8,128)S(1)}, s32[]{:T(128)}) while((s32[]{:T(128)}, f32[16,1,8,4096]{3,2,1,0:T(8,128)}, f32[16,1,8,16]{3,2,1,0:T(8,128)S(1)}, ...), condition=%wide.region_16.17_spmd, body=%wide.region_14.16_spmd.sunk | while | flops 2064386 | bytes 1312853 | solution.py:65
  496.4 16.5 %all-to-all-start.2 = ((bf16[128,16,256]{2,0,1:T(8,128)(2,1)}), bf16[128,16,256]{2,0,1:T(8,128)(2,1)S(1)}, u32[]{:S(2)}, u32[]{:S(2)}) async-start(bf16[128,16,256]{2,0,1:T(8,128)(2,1)} %fusion.30), calls=%async_computation.2 | async-start | bytes 2097152 | tf_op jit(solution)/shard_map/all_to_all | solution.py:147
  514.1 11.1 %all-to-all-done.2 = bf16[128,16,256]{2,0,1:T(8,128)(2,1)S(1)} async-done(((bf16[128,16,256]{2,0,1:T(8,128)(2,1)}), bf16[128,16,256]{2,0,1:T(8,128)(2,1)S(1)}, u32[]{:S(2)}, u32[]{:S(2)}) %all-to-all-start.2) | async-done | bytes 1048608 | tf_op jit(solution)/shard_map/all_to_all | solution.py:147
  527.5 6.8 convolution_convert_fusion
  534.9 84.1 %all-reduce.6.cloned.1.call-done = bf16[16,4096]{1,0:T(8,128)(2,1)} async-done(((bf16[16,4096]{1,0:T(8,128)(2,1)}), bf16[16,4096]{1,0:T(8,128)(2,1)}) %all-reduce.6.cloned.1.call-update) | async-done | bytes 131088 | tf_op jit(solution)/shard_map/psum | solution.py:18
  619.8 15.4 %all-gather = f32[128,256]{1,0:T(8,128)S(1)} all-gather(f32[16,256]{1,0:T(8,128)S(1)} %dynamic-slice_convert_fusion), channel_id=2, replica_groups=mesh['req'=8,'seq'=16] {'req'}, dimensions={0}, use_global_device_ids=true | all-gather | bytes 147456 | tf_op jit(solution)/shard_map/all_gather | solution.py:157
  635.8 72.3 %reduce-scatter.2.cloned.1.call-done = bf16[128,2048]{1,0:T(8,128)(2,1)} async-done(((bf16[2048,2048]{1,0:T(8,128)(2,1)}), bf16[128,2048]{1,0:T(8,128)(2,1)}) %reduce-scatter.2.cloned.1.call-update) | async-done | bytes 524304 | tf_op jit(solution)/shard_map/reduce_scatter | solution.py:151
  (356 shorter events, 199.7 us)
Async XLA Ops:
  7.2 116.0 %copy-start = (bf16[256,160]{0,1:T(8,128)(2,1)S(1)}, bf16[256,160]{0,1:T(8,128)(2,1)}, u32[]{:S(2)}) copy-start(bf16[256,160]{0,1:T(8,128)(2,1)} %param.26) | copy-start | bytes 245764
  7.2 31.4 %all-gather.7.cloned.1.call-start = ((), (), s32[]{:S(2)}) async-start(), calls=%async_computation.5 | async-start | bytes 2359296 | tf_op jit(solution)/shard_map/all_gather | solution.py:95
  7.9 104.1 %all-gather.5.cloned.1.call-start = ((), (), s32[]{:S(2)}) async-start(), calls=%async_computation.4 | async-start | bytes 8912896 | tf_op jit(solution)/shard_map/all_gather | solution.py:98
  12.0 208.3 %all-reduce.4.cloned.1.call-start = ((), (), s32[]{:S(2)}) async-start(), calls=%async_computation.6 | async-start | bytes 2621440 | tf_op jit(solution)/shard_map/psum | solution.py:112
  126.0 94.2 %copy-start.11 = (bf16[128,256]{1,0:T(8,128)(2,1)S(1)}, bf16[128,256]{1,0:T(8,128)(2,1)}, u32[]{:S(2)}) copy-start(bf16[128,256]{1,0:T(8,128)(2,1)} %param.27) | copy-start | bytes 196612
  126.1 98.3 %all-to-all-start.1 = ((bf16[16,128,256]{2,1,0:T(8,128)(2,1)}), bf16[16,128,256]{2,1,0:T(8,128)(2,1)S(1)}, u32[]{:S(2)}, u32[]{:S(2)}) async-start(bf16[16,128,256]{2,1,0:T(8,128)(2,1)} %bitcast.17), calls=%async_computation.1 | async-start | bytes 2097152 | tf_op jit(solution)/shard_map/all_to_all | solution.py:123
  223.0 6.4 copy-start.9
  224.3 19.3 %all-to-all-start = ((bf16[16,128,256]{1,2,0:T(8,128)(2,1)}), bf16[16,128,256]{1,2,0:T(8,128)(2,1)S(1)}, u32[]{:S(2)}, u32[]{:S(2)}) async-start(bf16[16,128,256]{1,2,0:T(8,128)(2,1)} %copy.43), calls=%async_computation | async-start | bytes 2097152 | tf_op jit(solution)/shard_map/all_to_all | solution.py:124
  228.8 298.7 %all-gather.9.cloned.1.call-start = ((), (), s32[]{:S(2)}) async-start(), calls=%async_computation.7 | async-start | bytes 1179648 | tf_op jit(solution)/shard_map/all_gather | solution.py:122
  245.4 5.4 copy-start.6
  319.2 5.4 collective-permute-start
  324.6 7.1 collective-permute-start
  331.8 8.2 %collective-permute-start = (f32[16,4096]{1,0:T(8,128)S(1)}, f32[16,4096]{1,0:T(8,128)S(1)}, u32[]{:S(2)}, u32[]{:S(2)}) collective-permute-start(f32[16,4096]{1,0:T(8,128)S(1)} %bitcast_add_fusion.3), channel_id=1, source_target_pairs={{0,1},{1,2},{2,3},{3,4},{4,5},{5,6},{6,7},{7,8},{8,9},{9,10},{10,1... | collective-permute-start | bytes 786440 | tf_op jit(solution)/shard_map/while/body/eval_jaxpr/ppermute | solution.py:13
  340.1 9.4 %collective-permute-start = (f32[16,4096]{1,0:T(8,128)S(1)}, f32[16,4096]{1,0:T(8,128)S(1)}, u32[]{:S(2)}, u32[]{:S(2)}) collective-permute-start(f32[16,4096]{1,0:T(8,128)S(1)} %bitcast_add_fusion.3), channel_id=1, source_target_pairs={{0,1},{1,2},{2,3},{3,4},{4,5},{5,6},{6,7},{7,8},{8,9},{9,10},{10,1... | collective-permute-start | bytes 786440 | tf_op jit(solution)/shard_map/while/body/eval_jaxpr/ppermute | solution.py:13
  349.5 9.3 %collective-permute-start = (f32[16,4096]{1,0:T(8,128)S(1)}, f32[16,4096]{1,0:T(8,128)S(1)}, u32[]{:S(2)}, u32[]{:S(2)}) collective-permute-start(f32[16,4096]{1,0:T(8,128)S(1)} %bitcast_add_fusion.3), channel_id=1, source_target_pairs={{0,1},{1,2},{2,3},{3,4},{4,5},{5,6},{6,7},{7,8},{8,9},{9,10},{10,1... | collective-permute-start | bytes 786440 | tf_op jit(solution)/shard_map/while/body/eval_jaxpr/ppermute | solution.py:13
  358.9 8.8 %collective-permute-start = (f32[16,4096]{1,0:T(8,128)S(1)}, f32[16,4096]{1,0:T(8,128)S(1)}, u32[]{:S(2)}, u32[]{:S(2)}) collective-permute-start(f32[16,4096]{1,0:T(8,128)S(1)} %bitcast_add_fusion.3), channel_id=1, source_target_pairs={{0,1},{1,2},{2,3},{3,4},{4,5},{5,6},{6,7},{7,8},{8,9},{9,10},{10,1... | collective-permute-start | bytes 786440 | tf_op jit(solution)/shard_map/while/body/eval_jaxpr/ppermute | solution.py:13
  367.7 7.9 %collective-permute-start = (f32[16,4096]{1,0:T(8,128)S(1)}, f32[16,4096]{1,0:T(8,128)S(1)}, u32[]{:S(2)}, u32[]{:S(2)}) collective-permute-start(f32[16,4096]{1,0:T(8,128)S(1)} %bitcast_add_fusion.3), channel_id=1, source_target_pairs={{0,1},{1,2},{2,3},{3,4},{4,5},{5,6},{6,7},{7,8},{8,9},{9,10},{10,1... | collective-permute-start | bytes 786440 | tf_op jit(solution)/shard_map/while/body/eval_jaxpr/ppermute | solution.py:13
  375.6 7.4 %collective-permute-start = (f32[16,4096]{1,0:T(8,128)S(1)}, f32[16,4096]{1,0:T(8,128)S(1)}, u32[]{:S(2)}, u32[]{:S(2)}) collective-permute-start(f32[16,4096]{1,0:T(8,128)S(1)} %bitcast_add_fusion.3), channel_id=1, source_target_pairs={{0,1},{1,2},{2,3},{3,4},{4,5},{5,6},{6,7},{7,8},{8,9},{9,10},{10,1... | collective-permute-start | bytes 786440 | tf_op jit(solution)/shard_map/while/body/eval_jaxpr/ppermute | solution.py:13
  383.1 14.6 %collective-permute-start = (f32[16,4096]{1,0:T(8,128)S(1)}, f32[16,4096]{1,0:T(8,128)S(1)}, u32[]{:S(2)}, u32[]{:S(2)}) collective-permute-start(f32[16,4096]{1,0:T(8,128)S(1)} %bitcast_add_fusion.3), channel_id=1, source_target_pairs={{0,1},{1,2},{2,3},{3,4},{4,5},{5,6},{6,7},{7,8},{8,9},{9,10},{10,1... | collective-permute-start | bytes 786440 | tf_op jit(solution)/shard_map/while/body/eval_jaxpr/ppermute | solution.py:13
  397.7 9.5 %collective-permute-start = (f32[16,4096]{1,0:T(8,128)S(1)}, f32[16,4096]{1,0:T(8,128)S(1)}, u32[]{:S(2)}, u32[]{:S(2)}) collective-permute-start(f32[16,4096]{1,0:T(8,128)S(1)} %bitcast_add_fusion.3), channel_id=1, source_target_pairs={{0,1},{1,2},{2,3},{3,4},{4,5},{5,6},{6,7},{7,8},{8,9},{9,10},{10,1... | collective-permute-start | bytes 786440 | tf_op jit(solution)/shard_map/while/body/eval_jaxpr/ppermute | solution.py:13
  407.3 8.3 %collective-permute-start = (f32[16,4096]{1,0:T(8,128)S(1)}, f32[16,4096]{1,0:T(8,128)S(1)}, u32[]{:S(2)}, u32[]{:S(2)}) collective-permute-start(f32[16,4096]{1,0:T(8,128)S(1)} %bitcast_add_fusion.3), channel_id=1, source_target_pairs={{0,1},{1,2},{2,3},{3,4},{4,5},{5,6},{6,7},{7,8},{8,9},{9,10},{10,1... | collective-permute-start | bytes 786440 | tf_op jit(solution)/shard_map/while/body/eval_jaxpr/ppermute | solution.py:13
  415.7 9.5 %collective-permute-start = (f32[16,4096]{1,0:T(8,128)S(1)}, f32[16,4096]{1,0:T(8,128)S(1)}, u32[]{:S(2)}, u32[]{:S(2)}) collective-permute-start(f32[16,4096]{1,0:T(8,128)S(1)} %bitcast_add_fusion.3), channel_id=1, source_target_pairs={{0,1},{1,2},{2,3},{3,4},{4,5},{5,6},{6,7},{7,8},{8,9},{9,10},{10,1... | collective-permute-start | bytes 786440 | tf_op jit(solution)/shard_map/while/body/eval_jaxpr/ppermute | solution.py:13
  425.2 9.5 %collective-permute-start = (f32[16,4096]{1,0:T(8,128)S(1)}, f32[16,4096]{1,0:T(8,128)S(1)}, u32[]{:S(2)}, u32[]{:S(2)}) collective-permute-start(f32[16,4096]{1,0:T(8,128)S(1)} %bitcast_add_fusion.3), channel_id=1, source_target_pairs={{0,1},{1,2},{2,3},{3,4},{4,5},{5,6},{6,7},{7,8},{8,9},{9,10},{10,1... | collective-permute-start | bytes 786440 | tf_op jit(solution)/shard_map/while/body/eval_jaxpr/ppermute | solution.py:13
  434.8 9.5 %collective-permute-start = (f32[16,4096]{1,0:T(8,128)S(1)}, f32[16,4096]{1,0:T(8,128)S(1)}, u32[]{:S(2)}, u32[]{:S(2)}) collective-permute-start(f32[16,4096]{1,0:T(8,128)S(1)} %bitcast_add_fusion.3), channel_id=1, source_target_pairs={{0,1},{1,2},{2,3},{3,4},{4,5},{5,6},{6,7},{7,8},{8,9},{9,10},{10,1... | collective-permute-start | bytes 786440 | tf_op jit(solution)/shard_map/while/body/eval_jaxpr/ppermute | solution.py:13
  444.4 9.2 %collective-permute-start = (f32[16,4096]{1,0:T(8,128)S(1)}, f32[16,4096]{1,0:T(8,128)S(1)}, u32[]{:S(2)}, u32[]{:S(2)}) collective-permute-start(f32[16,4096]{1,0:T(8,128)S(1)} %bitcast_add_fusion.3), channel_id=1, source_target_pairs={{0,1},{1,2},{2,3},{3,4},{4,5},{5,6},{6,7},{7,8},{8,9},{9,10},{10,1... | collective-permute-start | bytes 786440 | tf_op jit(solution)/shard_map/while/body/eval_jaxpr/ppermute | solution.py:13
  496.4 16.6 %copy-start.5 = (f32[16,4096]{1,0:T(8,128)S(1)}, f32[16,4096]{1,0:T(8,128)}, u32[]{:S(2)}) copy-start(f32[16,4096]{1,0:T(8,128)} %param.29) | copy-start | bytes 786436
  496.4 16.6 %copy-start.7 = (f32[1,1,4096]{2,1,0:T(1,128)S(1)}, f32[1,1,4096]{2,1,0:T(1,128)}, u32[]{:S(2)}) copy-start(f32[1,1,4096]{2,1,0:T(1,128)} %copy-done.6) | copy-start | bytes 49156
  496.4 28.7 %all-to-all-start.2 = ((bf16[128,16,256]{2,0,1:T(8,128)(2,1)}), bf16[128,16,256]{2,0,1:T(8,128)(2,1)S(1)}, u32[]{:S(2)}, u32[]{:S(2)}) async-start(bf16[128,16,256]{2,0,1:T(8,128)(2,1)} %fusion.30), calls=%async_computation.2 | async-start | bytes 2097152 | tf_op jit(solution)/shard_map/all_to_all | solution.py:147
  513.0 106.1 %all-reduce.6.cloned.1.call-start = ((), (), s32[]{:S(2)}) async-start(), calls=%async_computation.9 | async-start | bytes 262144 | tf_op jit(solution)/shard_map/psum | solution.py:18
  513.8 194.4 %reduce-scatter.2.cloned.1.call-start = ((), (), s32[]{:S(2)}) async-start(), calls=%async_computation.8 | async-start | bytes 8912896 | tf_op jit(solution)/shard_map/reduce_scatter | solution.py:151
  534.3 173.9 %copy-start.2 = (bf16[1,128,2048]{2,1,0:T(8,128)(2,1)S(1)}, bf16[1,128,2048]{2,1,0:T(8,128)(2,1)}, u32[]{:S(2)}) copy-start(bf16[1,128,2048]{2,1,0:T(8,128)(2,1)} %param.19) | copy-start | bytes 1572868
  534.3 175.9 %copy-start.1 = (bf16[256,160]{0,1:T(8,128)(2,1)S(1)}, bf16[256,160]{0,1:T(8,128)(2,1)}, u32[]{:S(2)}) copy-start(bf16[256,160]{0,1:T(8,128)(2,1)} %param.26) | copy-start | bytes 245764
  (8 other events, 24.8 us)
Sparse Core Ops, SparseCore 0:
  9.7 28.8 all-gather.6
  41.3 70.7 all-gather.4
  126.2 94.0 all-reduce.3
  231.0 27.1 all-gather.8
  517.2 101.7 all-reduce.5
  622.3 85.8 reduce-scatter.1
where the time goes:
time: 720 us; the launch traced here: 717 us
  waiting for transfers between devices  420 us (58%)
  starting transfers between devices  101 us (14%)
  local copies, waits for them, and re-layouts  89.9 us (12%)
  other arithmetic  54.7 us (8%)
  matrix products  19.6 us (3%)
  blocking collectives  15.4 us (2%)
  between operations  14.4 us (2%)
    psum x1, waiting for transfers between devices, per_device(): summed = lax.psum(partial_proj, 'seq')  87.7 us
    psum x1, waiting for transfers between devices, spread(): return lax.psum(jnp.where(mine, array, jnp.zeros_like(array)), axis)  84.1 us
    ppermute x15, starting transfers between devices, shifted(): return lax.ppermute(block, axis, route)  74.6 us
    reduce_scatter x1, waiting for transfers between devices, per_device(): lax.psum_scatter(jnp.dot(gated_ch, w_out, preferred_element_type=jnp.floa...  72.3 us
    all_gather x1, waiting for transfers between devices, per_device(): lax.all_gather(normed, 'seq', axis=0, tiled=True)  71.8 us
    ppermute x15, waiting for transfers between devices, shifted(): return lax.ppermute(block, axis, route)  59 us
    squeeze x32, local copies, waits for them, and re-layouts, piece_scan(): lax.scan(advance, start, (to_blocks(rates), to_blocks(values), to_blocks(...  26.9 us
    all_gather x1, waiting for transfers between devices, per_device(): w_in = lax.all_gather(in_weight, 'req', axis=1, tiled=True)  26.5 us
  transfers between devices with their start and end apart: 24, of which 22 were waited for; matrix products, arithmetic and copies ran while one was open for 20% of the time, Pallas kernels for 0%

commit v1 on v0

--- a/solution.py
+++ b/solution.py
@@ -7,15 +7,14 @@
 RANK = 128
 
 
-def shifted(block, axis, distance):
-    devices = range(lax.axis_size(axis))
-    route = [(i - distance, i) for i in devices if i - distance in devices]
-    return lax.ppermute(block, axis, route)
-
-
-def spread(array, axis, root):
-    mine = lax.axis_index(axis) == root
-    return lax.psum(jnp.where(mine, array, jnp.zeros_like(array)), axis)
+def gather_a2a(block, axis, dim):
+    count = lax.axis_size(axis)
+    copies = jnp.broadcast_to(block[None], (count,) + block.shape)
+    stacked = lax.all_to_all(copies, axis, split_axis=0, concat_axis=0, tiled=True)
+    moved = jnp.moveaxis(stacked, 0, dim)
+    shape = list(block.shape)
+    shape[dim] = shape[dim] * count
+    return moved.reshape(shape)
 
 
 def to_blocks(array):
@@ -88,11 +87,10 @@
     width = in_weight.shape[2]
     taps_count = conv_weight.shape[0]
     state_count = a_log.shape[0]
-    total_inner = a_log.shape[1]
     tokens = hidden[0].astype(jnp.float32)
     scale = lax.rsqrt(jnp.mean(tokens * tokens, axis=-1, keepdims=True) + 1e-05)
     normed = (tokens * scale * norm_gain.astype(jnp.float32)).astype(jnp.bfloat16)
-    w_in = lax.all_gather(in_weight, "req", axis=1, tiled=True)
+    w_in = gather_a2a(in_weight, "req", 1)
     w_flat = jnp.concatenate((w_in[0], w_in[1]), axis=1)
     both = jnp.dot(
         lax.all_gather(normed, "seq", axis=0, tiled=True),
@@ -107,43 +105,43 @@
     for tap in range(taps_count):
         convolved = convolved + taps[tap] * padded[tap : tap + span, :]
     inner = jax.nn.silu(convolved).astype(jnp.bfloat16)
-    partial_proj = jnp.dot(inner, xproj_weight, preferred_element_type=jnp.float32)
+    inner_tok = lax.all_to_all(inner, "seq", split_axis=0, concat_axis=1, tiled=True)
+    xproj_full = gather_a2a(xproj_weight, "seq", 0)
+    dt_full = gather_a2a(dt_weight, "seq", 1)
+    dt_bias_full = gather_a2a(dt_bias, "seq", 0)
+    proj = jnp.dot(inner_tok, xproj_full, preferred_element_type=jnp.float32)
     length_here = lax.dynamic_index_in_dim(lengths, req_index, 0, keepdims=False)
-    summed = lax.psum(partial_proj, "seq")
-    live_all = (jnp.arange(span, dtype=jnp.int32) < length_here).astype(jnp.float32)
-    rate_low = summed[:, :RANK].astype(jnp.bfloat16)
-    delta_ch = (
+    positions = seq_index * rows + jnp.arange(rows, dtype=jnp.int32)
+    live = (positions < length_here).astype(jnp.float32)
+    rate_low = proj[:, :RANK].astype(jnp.bfloat16)
+    delta_tok = (
         jax.nn.softplus(
-            jnp.dot(rate_low, dt_weight, preferred_element_type=jnp.float32)
-            + dt_bias.astype(jnp.float32)
+            jnp.dot(rate_low, dt_full, preferred_element_type=jnp.float32)
+            + dt_bias_full.astype(jnp.float32)
         )
-        * live_all[:, None]
+        * live[:, None]
     )
-    w_out = lax.all_gather(out_weight, "req", axis=1, tiled=True)
-    inner_tok = lax.all_to_all(inner, "seq", split_axis=0, concat_axis=1, tiled=True)
-    delta_tok = lax.all_to_all(
-        delta_ch.astype(jnp.bfloat16), "seq", split_axis=0, concat_axis=1, tiled=True
-    ).astype(delta_ch.dtype)
-    own_proj = lax.dynamic_slice_in_dim(summed, seq_index * rows, rows, 0)
+    w_out = gather_a2a(out_weight, "req", 1)
     decay = -jnp.exp(a_log)
     inner_f = inner_tok.astype(jnp.float32)
-    entry = own_proj[None, :, RANK : RANK + STATE]
-    readout = own_proj[None, :, RANK + STATE :]
+    entry = proj[None, :, RANK : RANK + STATE]
+    readout = proj[None, :, RANK + STATE :]
     end_local, local_out, total_decay, running = piece_scan(
         delta_tok[None], inner_f[None], entry, readout, decay
     )
-    zeros_state = jnp.zeros((state_count, total_inner), jnp.float32)
-
-    def relay(turn, incoming):
-        return shifted(total_decay[0] * incoming + end_local[0], "seq", 1)
-
-    carry_in = lax.fori_loop(0, seq_count - 1, relay, zeros_state)
+    pair = jnp.stack((total_decay[0], end_local[0])).reshape(2, state_count, seq_count, width)
+    pair_ch = lax.all_to_all(pair, "seq", split_axis=2, concat_axis=2, tiled=True)
+    carry = jnp.zeros((state_count, width), jnp.float32)
+    carries = []
+    for block in range(seq_count):
+        carries.append(carry)
+        carry = pair_ch[0, :, block] * carry + pair_ch[1, :, block]
+    carry_ch = jnp.stack(carries, axis=1)
+    carry_in = lax.all_to_all(carry_ch, "seq", split_axis=1, concat_axis=1, tiled=True).reshape(
+        state_count, seq_count * width
+    )
     carried = carried_part(running, readout, decay, carry_in[None])
     scanned = ((local_out + carried)[0] + skip_gain * inner_f).astype(jnp.bfloat16)
-    last = spread(
-        (total_decay[0] * carry_in + end_local[0]).astype(jnp.bfloat16), "seq", seq_count - 1
-    ).astype(jnp.float32)
-    mine = lax.dynamic_slice_in_dim(last, seq_index * width, width, 1)
     scanned_ch = lax.all_to_all(scanned, "seq", split_axis=1, concat_axis=0, tiled=True)
     gated_ch = (scanned_ch.astype(jnp.float32) * jax.nn.silu(zgate.astype(jnp.float32))).astype(
         jnp.bfloat16
@@ -154,7 +152,7 @@
         scatter_dimension=0,
         tiled=True,
     ).astype(jnp.float32)
-    slot_all = lax.all_gather(mine[None], "req", axis=0, tiled=True)
+    slot_all = gather_a2a(carry[None], "req", 0)
     picked = (slot_request == req_index).astype(jnp.float32)
     final_state = jnp.sum(picked[:, None, None] * slot_all, axis=0, keepdims=True)
     mixed = (tokens + branch).astype(jnp.bfloat16)[None]

time: 720 us -> 441 us (0.61)
  waiting for transfers between devices: 420 us -> 209 us
  starting transfers between devices: 101 us -> 53.5 us
  blocking collectives: 15.4 us -> 0 us
    psum x2 -> x0, waiting for transfers between devices: 172 us -> none  [the longest x1 87.7 us: per_device(): summed = lax.psum(partial_proj, 'seq')]
    ppermute x15 -> x0, starting transfers between devices: 74.6 us -> none  [shifted(): return lax.ppermute(block, axis, route)]
    all_to_all x1 -> x8, waiting for transfers between devices: 6.51 us -> 76 us  [the longest x6 60.1 us: gather_a2a(): lax.all_to_all(copies, axis, split_axis=0, concat_axis=0, tiled=True)]
    ppermute x15 -> x0, waiting for transfers between devices: 59 us -> none  [shifted(): return lax.ppermute(block, axis, route)]
    all_to_all x1 -> x8, starting transfers between devices: 4.46 us -> 44.2 us  [the longest x6 37 us: gather_a2a(): lax.all_to_all(copies, axis, split_axis=0, concat_axis=0, tiled=True)]
    all_gather x1, waiting for transfers between devices: 71.8 us -> 35.1 us  [per_device(): lax.all_gather(normed, 'seq', axis=0, tiled=True)]
    all_gather x2 -> x0, waiting for transfers between devices: 26.6 us -> none  [the longest x1 26.5 us: per_device(): w_in = lax.all_gather(in_weight, 'req', axis=1, tiled=True)]
    all_to_all x1, waiting for transfers between devices: 0.01 us -> 15.7 us  [per_device(): lax.all_to_all(inner, 'seq', split_axis=0, concat_axis=1, tiled=True)]
  transfers between devices with their start and end apart: 24 -> 12, of which waited for: 22 -> 11; matrix products, arithmetic and copies ran while one was open for 20% -> 5% of each run, Pallas kernels for 0% -> 0%
where the time goes in v1:
time: 441 us; the launch traced here: 439 us
  waiting for transfers between devices  209 us (47%)
  local copies, waits for them, and re-layouts  83.7 us (19%)
  other arithmetic  59.4 us (13%)
  starting transfers between devices  53.5 us (12%)
  matrix products  17.2 us (4%)
  between operations  14.4 us (3%)
    reduce_scatter x1, waiting for transfers between devices, per_device(): lax.psum_scatter(jnp.dot(gated_ch, w_out, preferred_element_type=jnp.floa...  70 us
    all_to_all x6, waiting for transfers between devices, gather_a2a(): lax.all_to_all(copies, axis, split_axis=0, concat_axis=0, tiled=True)  60.1 us
    all_to_all x6, starting transfers between devices, gather_a2a(): lax.all_to_all(copies, axis, split_axis=0, concat_axis=0, tiled=True)  37 us
    all_gather x1, waiting for transfers between devices, per_device(): lax.all_gather(normed, 'seq', axis=0, tiled=True)  35.1 us
    dynamic_update_slice x32, local copies, waits for them, and re-layouts, piece_scan(): lax.scan(advance, start, (to_blocks(rates), to_blocks(values), to_blocks(...  21.3 us
    reduce_sum x48, other arithmetic, advance(): outputs.append(jnp.sum(outof[:, place][:, :, None] * state, axis=1))  19.8 us
    squeeze x32, local copies, waits for them, and re-layouts, piece_scan(): lax.scan(advance, start, (to_blocks(rates), to_blocks(values), to_blocks(...  15.9 us
    all_to_all x1, waiting for transfers between devices, per_device(): lax.all_to_all(inner, 'seq', split_axis=0, concat_axis=1, tiled=True)  15.7 us
  transfers between devices with their start and end apart: 12, of which 11 were waited for; matrix products, arithmetic and copies ran while one was open for 5% of the time, Pallas kernels for 0%

profile of v1, /device:TPU:1, one launch (start us, length us, event | category | flops | bytes accessed | tf_op | source)
XLA Modules:
  0.0 438.7 jit_solution(5524272800325330019)
XLA Ops:
  12.9 5.9 %all-to-all-start = ((bf16[8,2,256,256]{3,2,1,0:T(8,128)(2,1)}), bf16[8,2,256,256]{3,2,1,0:T(8,128)(2,1)S(1)}, u32[]{:S(2)}, u32[]{:S(2)}) async-start(bf16[8,2,256,256]{3,2,1,0:T(8,128)(2,1)} %broadcast_in_dim.25), calls=%async_computation | async-start | bytes 4194304 | tf_op jit(solution)/shard_map/all_to_all | solution.py:13
  20.6 24.3 %all-to-all-done = bf16[8,2,256,256]{3,2,1,0:T(8,128)(2,1)S(1)} async-done(((bf16[8,2,256,256]{3,2,1,0:T(8,128)(2,1)}), bf16[8,2,256,256]{3,2,1,0:T(8,128)(2,1)S(1)}, u32[]{:S(2)}, u32[]{:S(2)}) %all-to-all-start) | async-done | bytes 2097184 | tf_op jit(solution)/shard_map/all_to_all | solution.py:13
  45.0 7.8 %all-to-all-start.4 = ((bf16[16,2,128]{2,1,0:T(2,128)(2,1)}), bf16[16,2,128]{2,1,0:T(2,128)(2,1)S(1)}, u32[]{:S(2)}, u32[]{:S(2)}) async-start(bf16[16,2,128]{2,1,0:T(2,128)(2,1)} %reshape.2341), calls=%async_computation.4 | async-start | bytes 16384 | tf_op jit(solution)/shard_map/all_to_all | solution.py:13
  54.2 5.0 %all-to-all-done.4 = bf16[16,2,128]{2,1,0:T(2,128)(2,1)S(1)} async-done(((bf16[16,2,128]{2,1,0:T(2,128)(2,1)}), bf16[16,2,128]{2,1,0:T(2,128)(2,1)S(1)}, u32[]{:S(2)}, u32[]{:S(2)}) %all-to-all-start.4) | async-done | bytes 8224 | tf_op jit(solution)/shard_map/all_to_all | solution.py:13
  60.5 3.7 all-to-all-start.2
  64.2 35.1 %all-gather.2.cloned.1.call-done = bf16[2048,2048]{1,0:T(8,128)(2,1)} async-done(((bf16[128,2048]{1,0:T(8,128)(2,1)}), bf16[2048,2048]{1,0:T(8,128)(2,1)}) %all-gather.2.cloned.1.call-update) | async-done | bytes 8388624 | tf_op jit(solution)/shard_map/all_gather | solution.py:96
  99.3 7.2 %fusion.29 = f32[2048,512]{1,0:T(8,128)S(1)} fusion(bf16[2048,2048]{1,0:T(8,128)(2,1)} %all-gather.2.cloned.1.call-done, bf16[2048,256]{1,0:T(8,128)(2,1)} %bitcast.737, bf16[2048,256]{1,0:T(8,128)(2,1)S(1)} %bitcast.736), kind=kOutput, calls=%fused_computation.84 | convolution fusion | flops 4299161600 | bytes 14680064 | tf_op jit(solution)/shard_map/dot_general | solution.py:95
  108.4 2.3 multiply_convert_fusion
  110.8 5.2 %all-to-all-start.1 = ((bf16[16,128,256]{2,1,0:T(8,128)(2,1)}), bf16[16,128,256]{2,1,0:T(8,128)(2,1)S(1)}, u32[]{:S(2)}, u32[]{:S(2)}) async-start(bf16[16,128,256]{2,1,0:T(8,128)(2,1)} %bitcast.691), calls=%async_computation.1 | async-start | bytes 2097152 | tf_op jit(solution)/shard_map/all_to_all | solution.py:108
  116.1 15.7 %all-to-all-done.1 = bf16[16,128,256]{2,1,0:T(8,128)(2,1)S(1)} async-done(((bf16[16,128,256]{2,1,0:T(8,128)(2,1)}), bf16[16,128,256]{2,1,0:T(8,128)(2,1)S(1)}, u32[]{:S(2)}, u32[]{:S(2)}) %all-to-all-start.1) | async-done | bytes 1048608 | tf_op jit(solution)/shard_map/all_to_all | solution.py:108
  133.1 4.5 %all-to-all-start.3 = ((bf16[16,128,256]{1,2,0:T(8,128)(2,1)}), bf16[16,128,256]{1,2,0:T(8,128)(2,1)}, u32[]{:S(2)}, u32[]{:S(2)}) async-start(bf16[16,128,256]{1,2,0:T(8,128)(2,1)} %broadcast_in_dim.27), calls=%async_computation.3 | async-start | bytes 2097152 | tf_op jit(solution)/shard_map/all_to_all | solution.py:13
  139.4 12.7 %all-to-all-done.3 = bf16[16,128,256]{1,2,0:T(8,128)(2,1)} async-done(((bf16[16,128,256]{1,2,0:T(8,128)(2,1)}), bf16[16,128,256]{1,2,0:T(8,128)(2,1)}, u32[]{:S(2)}, u32[]{:S(2)}) %all-to-all-start.3) | async-done | bytes 1048608 | tf_op jit(solution)/shard_map/all_to_all | solution.py:13
  152.2 2.7 fusion.28
  158.0 2.6 copy.158
  160.6 2.9 reshape.2325
  165.1 55.2 %while.24 = (s32[]{:T(128)}, f32[1,16,4096]{2,1,0:T(8,128)S(1)}, f32[16,1,8,4096]{3,2,1,0:T(8,128)}, f32[16,1,8,4096]{3,2,1,0:T(8,128)}, f32[16,4096]{1,0:T(8,12...) while((s32[]{:T(128)}, f32[1,16,4096]{2,1,0:T(8,128)S(1)}, ...), condition=%wide.region_10.11_spmd.clone, body=%wide.region_1.10_spmd.clone.sunk | while | flops 4849667 | bytes 4347896 | solution.py:50
  221.6 3.7 all-to-all-start.5
  225.9 8.5 %all-to-all-done.5 = f32[2,16,16,256]{3,1,0,2:T(8,128)S(1)} async-done(((f32[2,16,16,256]{3,1,0,2:T(8,128)}), f32[2,16,16,256]{3,1,0,2:T(8,128)S(1)}, u32[]{:S(2)}, u32[]{:S(2)}) %all-to-all-start.5) | async-done | bytes 524320 | tf_op jit(solution)/shard_map/all_to_all | solution.py:133
  243.5 3.5 all-to-all-start.6
  247.1 7.5 %all-to-all-done.6 = f32[16,16,256]{2,0,1:T(8,128)S(1)} async-done(((f32[16,16,256]{2,0,1:T(8,128)}), f32[16,16,256]{2,0,1:T(8,128)S(1)}, u32[]{:S(2)}, u32[]{:S(2)}) %all-to-all-start.6) | async-done | bytes 262176 | tf_op jit(solution)/shard_map/all_to_all | solution.py:140
  256.3 38.5 %while.23 = (s32[]{:T(128)}, f32[16,1,8,4096]{3,2,1,0:T(8,128)}, f32[16,1,8,16]{3,2,1,0:T(8,128)S(1)}, f32[16,1,8,4096]{3,2,1,0:T(8,128)}, f32[16,4096]{1,0:T(8,128)S(1)}, /*index=5*/f32[16,16,256]{2,1,0:T(8,128)S(1)}, s32[]{:T(128)}) while((s32[]{:T(128)}, f32[16,1,8,4096]{3,2,1,0:T(8,128)}, f32[16,1,8,16]{3,2,1,0:T(8,128)S(1)}, ...), condition=%wide.region_13.14_spmd, body=%wide.region_11.13_spmd.sunk | while | flops 2064386 | bytes 1837141 | solution.py:64
  294.8 2.5 add.814
  298.0 2.3 fusion.33
  300.3 4.0 all-to-all-start.7
  304.4 12.0 %all-to-all-done.7 = bf16[128,16,256]{2,0,1:T(8,128)(2,1)S(1)} async-done(((bf16[128,16,256]{2,0,1:T(8,128)(2,1)}), bf16[128,16,256]{2,0,1:T(8,128)(2,1)S(1)}, u32[]{:S(2)}, u32[]{:S(2)}) %all-to-all-start.7) | async-done | bytes 1048608 | tf_op jit(solution)/shard_map/all_to_all | solution.py:145
  317.5 10.9 %all-to-all-start.8 = ((bf16[8,256,256]{1,2,0:T(8,128)(2,1)}), bf16[8,256,256]{1,2,0:T(8,128)(2,1)S(1)}, u32[]{:S(2)}, u32[]{:S(2)}) async-start(bf16[8,256,256]{1,2,0:T(8,128)(2,1)} %broadcast_in_dim.29), calls=%async_computation.8 | async-start | bytes 2097152 | tf_op jit(solution)/shard_map/all_to_all | solution.py:13
  328.4 2.3 fusion.36
  330.7 12.7 %all-to-all-done.8 = bf16[8,256,256]{1,2,0:T(8,128)(2,1)S(1)} async-done(((bf16[8,256,256]{1,2,0:T(8,128)(2,1)}), bf16[8,256,256]{1,2,0:T(8,128)(2,1)S(1)}, u32[]{:S(2)}, u32[]{:S(2)}) %all-to-all-start.8) | async-done | bytes 1048608 | tf_op jit(solution)/shard_map/all_to_all | solution.py:13
  343.3 5.6 %convolution_convert_fusion = bf16[2048,2048]{1,0:T(8,128)(2,1)} fusion(bf16[2048,256]{1,0:T(8,128)(2,1)S(1)} %fusion.36, bf16[256,2048]{0,1:T(8,128)(2,1)S(1)} %bitcast.692), kind=kOutput, calls=%fused_computation.73 | convolution fusion | flops 2151677952 | bytes 10485760 | tf_op jit(solution)/shard_map/dot_general | solution.py:150
  349.7 4.2 all-to-all-start.9
  353.9 5.3 %all-to-all-done.9 = f32[8,1,16,256]{3,2,1,0:T(8,128)S(1)} async-done(((f32[8,1,16,256]{3,2,1,0:T(8,128)}), f32[8,1,16,256]{3,2,1,0:T(8,128)S(1)}, u32[]{:S(2)}, u32[]{:S(2)}) %all-to-all-start.9) | async-done | bytes 131104 | tf_op jit(solution)/shard_map/all_to_all | solution.py:13
  359.9 70.0 %reduce-scatter.2.cloned.1.call-done = bf16[128,2048]{1,0:T(8,128)(2,1)} async-done(((bf16[2048,2048]{1,0:T(8,128)(2,1)}), bf16[128,2048]{1,0:T(8,128)(2,1)}) %reduce-scatter.2.cloned.1.call-update) | async-done | bytes 524304 | tf_op jit(solution)/shard_map/reduce_scatter | solution.py:149
  (354 shorter events, 130.1 us)
Async XLA Ops:
  7.2 4.1 copy-start.5
  7.2 92.1 %all-gather.2.cloned.1.call-start = ((), (), s32[]{:S(2)}) async-start(), calls=%async_computation.11 | async-start | bytes 8912896 | tf_op jit(solution)/shard_map/all_gather | solution.py:96
  12.9 5.9 %copy-start.13 = (bf16[256]{0:T(256)(128)(2,1)S(1)}, bf16[256]{0:T(256)(128)(2,1)}, u32[]{:S(2)}) copy-start(bf16[256]{0:T(256)(128)(2,1)} %param.23) | copy-start | bytes 1540
  12.9 5.9 %copy-start.12 = (bf16[256]{0:T(256)(128)(2,1)S(1)}, bf16[256]{0:T(256)(128)(2,1)}, u32[]{:S(2)}) copy-start(bf16[256]{0:T(256)(128)(2,1)} %param.26) | copy-start | bytes 1540
  12.9 7.8 %copy-start.11 = (bf16[4,256]{1,0:T(4,128)(2,1)S(1)}, bf16[4,256]{1,0:T(4,128)(2,1)}, u32[]{:S(2)}) copy-start(bf16[4,256]{1,0:T(4,128)(2,1)} %param.22) | copy-start | bytes 6148
  12.9 32.1 %all-to-all-start = ((bf16[8,2,256,256]{3,2,1,0:T(8,128)(2,1)}), bf16[8,2,256,256]{3,2,1,0:T(8,128)(2,1)S(1)}, u32[]{:S(2)}, u32[]{:S(2)}) async-start(bf16[8,2,256,256]{3,2,1,0:T(8,128)(2,1)} %broadcast_in_dim.25), calls=%async_computation | async-start | bytes 4194304 | tf_op jit(solution)/shard_map/all_to_all | solution.py:13
  45.0 14.3 %all-to-all-start.4 = ((bf16[16,2,128]{2,1,0:T(2,128)(2,1)}), bf16[16,2,128]{2,1,0:T(2,128)(2,1)S(1)}, u32[]{:S(2)}, u32[]{:S(2)}) async-start(bf16[16,2,128]{2,1,0:T(2,128)(2,1)} %reshape.2341), calls=%async_computation.4 | async-start | bytes 16384 | tf_op jit(solution)/shard_map/all_to_all | solution.py:13
  52.8 6.5 %copy-start.8 = (bf16[256,160]{0,1:T(8,128)(2,1)S(1)}, bf16[256,160]{0,1:T(8,128)(2,1)}, u32[]{:S(2)}) copy-start(bf16[256,160]{0,1:T(8,128)(2,1)} %param.24) | copy-start | bytes 245764
  54.2 45.1 %copy-start.4 = (bf16[1,8,256,256]{3,2,0,1:T(8,128)(2,1)S(1)}, bf16[1,8,256,256]{3,2,0,1:T(8,128)(2,1)}, u32[]{:S(2)}) copy-start(bf16[1,8,256,256]{3,2,0,1:T(8,128)(2,1)} %get-tuple-element.265) | copy-start | bytes 3145732
  60.5 50.3 %all-to-all-start.2 = ((bf16[16,256,160]{1,2,0:T(8,128)(2,1)}), bf16[16,256,160]{1,2,0:T(8,128)(2,1)S(1)}, u32[]{:S(2)}, u32[]{:S(2)}) async-start(bf16[16,256,160]{1,2,0:T(8,128)(2,1)} %broadcast_in_dim.26), calls=%async_computation.2 | async-start | bytes 2621440 | tf_op jit(solution)/shard_map/all_to_all | solution.py:13
  106.5 1.9 copy-start.3
  108.4 7.6 %copy-start.9 = (bf16[128,256]{1,0:T(8,128)(2,1)S(1)}, bf16[128,256]{1,0:T(8,128)(2,1)}, u32[]{:S(2)}) copy-start(bf16[128,256]{1,0:T(8,128)(2,1)} %param.25) | copy-start | bytes 196612
  110.8 21.1 %all-to-all-start.1 = ((bf16[16,128,256]{2,1,0:T(8,128)(2,1)}), bf16[16,128,256]{2,1,0:T(8,128)(2,1)S(1)}, u32[]{:S(2)}, u32[]{:S(2)}) async-start(bf16[16,128,256]{2,1,0:T(8,128)(2,1)} %bitcast.691), calls=%async_computation.1 | async-start | bytes 2097152 | tf_op jit(solution)/shard_map/all_to_all | solution.py:108
  116.0 21.6 %copy-start.14 = (s32[8]{0:T(128)S(1)}, s32[8]{0:T(128)}, u32[]{:S(2)}) copy-start(s32[8]{0:T(128)} %param.18) | copy-start | bytes 100
  133.1 19.1 %all-to-all-start.3 = ((bf16[16,128,256]{1,2,0:T(8,128)(2,1)}), bf16[16,128,256]{1,2,0:T(8,128)(2,1)}, u32[]{:S(2)}, u32[]{:S(2)}) async-start(bf16[16,128,256]{1,2,0:T(8,128)(2,1)} %broadcast_in_dim.27), calls=%async_computation.3 | async-start | bytes 2097152 | tf_op jit(solution)/shard_map/all_to_all | solution.py:13
  154.9 1.4 copy-start.2
  156.3 1.3 copy-start.1
  160.6 2.9 copy-start.6
  220.5 26.6 %copy-start.10 = (f32[4096]{0:T(1024)S(1)}, f32[4096]{0:T(1024)}, u32[]{:S(2)}) copy-start(f32[4096]{0:T(1024)} %param.28) | copy-start | bytes 49156
  221.6 12.8 %all-to-all-start.5 = ((f32[2,16,16,256]{3,1,0,2:T(8,128)}), f32[2,16,16,256]{3,1,0,2:T(8,128)S(1)}, u32[]{:S(2)}, u32[]{:S(2)}) async-start(f32[2,16,16,256]{3,1,0,2:T(8,128)} %copy.165), calls=%async_computation.5 | async-start | bytes 1048576 | tf_op jit(solution)/shard_map/all_to_all | solution.py:133
  243.5 11.0 %all-to-all-start.6 = ((f32[16,16,256]{2,0,1:T(8,128)}), f32[16,16,256]{2,0,1:T(8,128)S(1)}, u32[]{:S(2)}, u32[]{:S(2)}) async-start(f32[16,16,256]{2,0,1:T(8,128)} %constant_dynamic-update-slice_fusion), calls=%async_computation.6 | async-start | bytes 524288 | tf_op jit(solution)/shard_map/all_to_all | solution.py:140
  300.3 4.0 copy-start.7
  300.3 16.1 %all-to-all-start.7 = ((bf16[128,16,256]{2,0,1:T(8,128)(2,1)}), bf16[128,16,256]{2,0,1:T(8,128)(2,1)S(1)}, u32[]{:S(2)}, u32[]{:S(2)}) async-start(bf16[128,16,256]{2,0,1:T(8,128)(2,1)} %fusion.33), calls=%async_computation.7 | async-start | bytes 2097152 | tf_op jit(solution)/shard_map/all_to_all | solution.py:145
  317.5 25.8 %all-to-all-start.8 = ((bf16[8,256,256]{1,2,0:T(8,128)(2,1)}), bf16[8,256,256]{1,2,0:T(8,128)(2,1)S(1)}, u32[]{:S(2)}, u32[]{:S(2)}) async-start(bf16[8,256,256]{1,2,0:T(8,128)(2,1)} %broadcast_in_dim.29), calls=%async_computation.8 | async-start | bytes 2097152 | tf_op jit(solution)/shard_map/all_to_all | solution.py:13
  328.4 101.6 %reduce-scatter.2.cloned.1.call-start = ((), (), s32[]{:S(2)}) async-start(), calls=%async_computation.12 | async-start | bytes 8912896 | tf_op jit(solution)/shard_map/reduce_scatter | solution.py:149
  349.0 4.9 %copy-start.15 = (s32[8]{0:T(128)S(1)}, s32[8]{0:T(128)}, u32[]{:S(2)}) copy-start(s32[8]{0:T(128)} %param.19) | copy-start | bytes 100
  349.0 80.9 %copy-start = (bf16[1,128,2048]{2,1,0:T(8,128)(2,1)S(1)}, bf16[1,128,2048]{2,1,0:T(8,128)(2,1)}, u32[]{:S(2)}) copy-start(bf16[1,128,2048]{2,1,0:T(8,128)(2,1)} %param.17) | copy-start | bytes 1572868
  349.7 9.6 %all-to-all-start.9 = ((f32[8,1,16,256]{3,2,1,0:T(8,128)}), f32[8,1,16,256]{3,2,1,0:T(8,128)S(1)}, u32[]{:S(2)}, u32[]{:S(2)}) async-start(f32[8,1,16,256]{3,2,1,0:T(8,128)} %broadcast_in_dim.31), calls=%async_computation.10 | async-start | bytes 262144 | tf_op jit(solution)/shard_map/all_to_all | solution.py:13
Sparse Core Ops, SparseCore 0:
  11.4 87.8 all-gather.1
  349.1 80.7 reduce-scatter.1

commit v2 on v1

--- a/solution.py
+++ b/solution.py
@@ -1,6 +1,10 @@
+import functools
+
 import jax
 import jax.numpy as jnp
 from jax import lax
+from jax.experimental import pallas as pl
+from jax.experimental.pallas import tpu as pltpu
 from jax.sharding import PartitionSpec as P
 
 STATE = 16
@@ -17,51 +21,75 @@
     return moved.reshape(shape)
 
 
-def to_blocks(array):
-    pieces, length, columns = array.shape
-    return jnp.moveaxis(array.reshape(pieces, 16, length // 16, columns), 1, 0)
-
-
-def from_blocks(array):
-    count, pieces, group, columns = array.shape
-    return jnp.moveaxis(array, 0, 1).reshape(pieces, count * group, columns)
-
-
-def piece_scan(rates, values, entry, readout, decay):
-    pieces, length, columns = rates.shape
-    group = length // 16
-    positions = jnp.arange(length, dtype=jnp.int32)
-    lower = (positions[None, :] <= positions[:, None]).astype(jnp.float32)
-    running = jnp.einsum("rs,psw->prw", lower, rates, precision=lax.Precision.HIGHEST)
-
-    def advance(state, items):
-        rate, value, into, outof = items
-        outputs = []
-        for place in range(group):
-            factor = jnp.exp(rate[:, place][:, None, :] * decay[None])
-            state = (
-                factor * state
-                + (rate[:, place] * value[:, place])[:, None, :] * into[:, place][:, :, None]
-            )
-            outputs.append(jnp.sum(outof[:, place][:, :, None] * state, axis=1))
-        return (state, jnp.stack(outputs, axis=1))
-
-    start = jnp.zeros((pieces, decay.shape[0], columns), jnp.float32)
-    end_local, local_out = lax.scan(
-        advance, start, (to_blocks(rates), to_blocks(values), to_blocks(entry), to_blocks(readout))
-    )
-    total_decay = jnp.exp(running[:, length - 1][:, None, :] * decay[None])
-    return (end_local, from_blocks(local_out), total_decay, running)
-
-
-def carried_part(running, readout, decay, carry_in):
-
-    def correct(items):
-        total, outof = items
-        kept = jnp.exp(total[:, :, None, :] * decay[None, None]) * carry_in[:, None]
-        return jnp.sum(outof[:, :, :, None] * kept, axis=2)
-
-    return from_blocks(lax.map(correct, (to_blocks(running), to_blocks(readout))))
+LANES = 128
+SUB = 8
+
+
+def scan_body(emit, into_ref, outof_ref, rate_ref, value_ref, decay_ref, start_ref, skip_ref, *outs):
+    steps = rate_ref.shape[0]
+    states = decay_ref.shape[0]
+    decay = [decay_ref[n] for n in range(states)]
+    if emit:
+        out_ref, = outs
+        skip = skip_ref[...]
+    else:
+        end_ref, total_ref = outs
+
+    def step(t, carry):
+        held, acc = carry
+        rate = rate_ref[t]
+        value = value_ref[t]
+        push = rate * value
+        row = t * states
+        new = []
+        result = skip * value if emit else None
+        for n in range(states):
+            s = jnp.exp(rate * decay[n]) * held[n] + push * into_ref[row + n]
+            if emit:
+                result = result + outof_ref[row + n] * s
+            new.append(s)
+        if emit:
+            out_ref[t] = result
+        else:
+            acc = acc + rate
+        return (tuple(new), acc)
+
+    held0 = tuple(start_ref[n] for n in range(states))
+    acc0 = jnp.zeros((SUB, LANES), jnp.float32)
+    held, acc = lax.fori_loop(0, steps, step, (held0, acc0))
+    if not emit:
+        for n in range(states):
+            end_ref[n] = held[n]
+            total_ref[n] = jnp.exp(acc * decay[n])
+
+
+def run_scan(emit, into, outof, rate, value, decay, start, skip):
+    steps, rows, lanes = rate.shape
+    states = decay.shape[0]
+    chunks = rows // SUB
+    smem = pl.BlockSpec(memory_space=pltpu.MemorySpace.SMEM)
+    seq_spec = pl.BlockSpec((steps, SUB, lanes), lambda i: (0, i, 0))
+    st_spec = pl.BlockSpec((states, SUB, lanes), lambda i: (0, i, 0))
+    skip_spec = pl.BlockSpec((SUB, lanes), lambda i: (i, 0))
+    if emit:
+        out_shape = jax.ShapeDtypeStruct((steps, rows, lanes), jnp.float32)
+        out_specs = seq_spec
+    else:
+        out_shape = (jax.ShapeDtypeStruct((states, rows, lanes), jnp.float32),) * 2
+        out_specs = (st_spec, st_spec)
+    flops = steps * rows * lanes * states * 6
+    return pl.pallas_call(
+        functools.partial(scan_body, emit),
+        grid=(chunks,),
+        in_specs=[smem, smem, seq_spec, seq_spec, st_spec, st_spec, skip_spec],
+        out_specs=out_specs,
+        out_shape=out_shape,
+        cost_estimate=pl.CostEstimate(
+            flops=flops,
+            transcendentals=steps * rows * lanes * states,
+            bytes_accessed=(3 if emit else 2) * steps * rows * lanes * 4,
+        ),
+    )(into, outof, rate, value, decay, start, skip)
 
 
 def per_device(
@@ -87,6 +115,7 @@
     width = in_weight.shape[2]
     taps_count = conv_weight.shape[0]
     state_count = a_log.shape[0]
+    total_inner = a_log.shape[1]
     tokens = hidden[0].astype(jnp.float32)
     scale = lax.rsqrt(jnp.mean(tokens * tokens, axis=-1, keepdims=True) + 1e-05)
     normed = (tokens * scale * norm_gain.astype(jnp.float32)).astype(jnp.bfloat16)
@@ -123,13 +152,22 @@
     )
     w_out = gather_a2a(out_weight, "req", 1)
     decay = -jnp.exp(a_log)
+    lanes = 128
+    groups = total_inner // lanes
     inner_f = inner_tok.astype(jnp.float32)
-    entry = proj[None, :, RANK : RANK + STATE]
-    readout = proj[None, :, RANK + STATE :]
-    end_local, local_out, total_decay, running = piece_scan(
-        delta_tok[None], inner_f[None], entry, readout, decay
-    )
-    pair = jnp.stack((total_decay[0], end_local[0])).reshape(2, state_count, seq_count, width)
+    into = proj[:, RANK : RANK + STATE].reshape(-1)
+    outof = proj[:, RANK + STATE :].reshape(-1)
+    rate_l = delta_tok.reshape(rows, groups, lanes)
+    value_l = inner_f.reshape(rows, groups, lanes)
+    decay_l = decay.reshape(state_count, groups, lanes)
+    skip_l = skip_gain.reshape(groups, lanes)
+    end_l, total_l = run_scan(
+        False, into, outof, rate_l, value_l, decay_l,
+        jnp.zeros((state_count, groups, lanes), jnp.float32), skip_l,
+    )
+    pair = jnp.stack(
+        (total_l.reshape(state_count, total_inner), end_l.reshape(state_count, total_inner))
+    ).reshape(2, state_count, seq_count, width)
     pair_ch = lax.all_to_all(pair, "seq", split_axis=2, concat_axis=2, tiled=True)
     carry = jnp.zeros((state_count, width), jnp.float32)
     carries = []
@@ -137,11 +175,12 @@
         carries.append(carry)
         carry = pair_ch[0, :, block] * carry + pair_ch[1, :, block]
     carry_ch = jnp.stack(carries, axis=1)
-    carry_in = lax.all_to_all(carry_ch, "seq", split_axis=1, concat_axis=1, tiled=True).reshape(
-        state_count, seq_count * width
-    )
-    carried = carried_part(running, readout, decay, carry_in[None])
-    scanned = ((local_out + carried)[0] + skip_gain * inner_f).astype(jnp.bfloat16)
+    carry_in = lax.all_to_all(carry_ch, "seq", split_axis=1, concat_axis=1, tiled=True)
+    out_l = run_scan(
+        True, into, outof, rate_l, value_l, decay_l,
+        carry_in.reshape(state_count, groups, lanes), skip_l,
+    )
+    scanned = out_l.reshape(rows, total_inner).astype(jnp.bfloat16)
     scanned_ch = lax.all_to_all(scanned, "seq", split_axis=1, concat_axis=0, tiled=True)
     gated_ch = (scanned_ch.astype(jnp.float32) * jax.nn.silu(zgate.astype(jnp.float32))).astype(
         jnp.bfloat16

time: 441 us -> 366 us (0.83)
  local copies, waits for them, and re-layouts: 83.7 us -> 23.4 us
  other arithmetic: 59.4 us -> 16.7 us
  Pallas kernels: 0 us -> 32.4 us
  blocking collectives: 0 us -> 10.1 us
  waiting for transfers between devices: 209 us -> 203 us
  starting transfers between devices: 53.5 us -> 48.9 us
    pallas_call x0 -> x2, Pallas kernels: none -> 32.4 us  [run_scan(): pl.pallas_call(functools.partial(scan_body, emit), grid=(chunks,), in_spe...]
    reduce_sum x64 -> x0, other arithmetic: 29.9 us -> none  [the longest x48 19.8 us: advance(): outputs.append(jnp.sum(outof[:, place][:, :, None] * state, axis=1))]
    dynamic_update_slice x32 -> x0, local copies, waits for them, and re-layouts: 21.3 us -> none  [piece_scan(): lax.scan(advance, start, (to_blocks(rates), to_blocks(values), to_blocks(...]
    squeeze x32 -> x0, local copies, waits for them, and re-layouts: 15.9 us -> none  [piece_scan(): lax.scan(advance, start, (to_blocks(rates), to_blocks(values), to_blocks(...]
    mul x65 -> x0, local copies, waits for them, and re-layouts: 15 us -> none  [the longest x16 14.6 us: correct(): kept = jnp.exp(total[:, :, None, :] * decay[None, None]) * carry_in[:, None]]
    all_to_all x0 -> x1, blocking collectives: none -> 10.1 us  [per_device(): lax.all_to_all(carry_ch, 'seq', split_axis=1, concat_axis=1, tiled=True)]
    all_to_all x1 -> x0, waiting for transfers between devices: 7.48 us -> none  [per_device(): lax.all_to_all(carry_ch, 'seq', split_axis=1, concat_axis=1, tiled=True)]
    unnamed x14, other arithmetic: 7.88 us -> 1.11 us
  transfers between devices with their start and end apart: 12 -> 11, of which waited for: 11 -> 10; matrix products, arithmetic and copies ran while one was open for 5% -> 6% of each run, Pallas kernels for 0% -> 0%
where the time goes in v2:
time: 366 us; the launch traced here: 364 us
  waiting for transfers between devices  203 us (55%)
  starting transfers between devices  48.9 us (13%)
  Pallas kernels  32.4 us (9%)
  local copies, waits for them, and re-layouts  23.4 us (6%)
  other arithmetic  16.7 us (5%)
  matrix products  14.8 us (4%)
  between operations  14.4 us (4%)
  blocking collectives  10.1 us (3%)
    reduce_scatter x1, waiting for transfers between devices, per_device(): lax.psum_scatter(jnp.dot(gated_ch, w_out, preferred_element_type=jnp.floa...  69.9 us
    all_to_all x6, waiting for transfers between devices, gather_a2a(): lax.all_to_all(copies, axis, split_axis=0, concat_axis=0, tiled=True)  59.1 us
    all_to_all x6, starting transfers between devices, gather_a2a(): lax.all_to_all(copies, axis, split_axis=0, concat_axis=0, tiled=True)  35.2 us
    all_gather x1, waiting for transfers between devices, per_device(): lax.all_gather(normed, 'seq', axis=0, tiled=True)  35.1 us
    pallas_call x2, Pallas kernels, run_scan(): pl.pallas_call(functools.partial(scan_body, emit), grid=(chunks,), in_spe...  32.4 us
    all_to_all x1, waiting for transfers between devices, per_device(): lax.all_to_all(inner, 'seq', split_axis=0, concat_axis=1, tiled=True)  15.7 us
    all_to_all x1, waiting for transfers between devices, per_device(): lax.all_to_all(scanned, 'seq', split_axis=1, concat_axis=0, tiled=True)  13.4 us
    all_to_all x1, blocking collectives, per_device(): lax.all_to_all(carry_ch, 'seq', split_axis=1, concat_axis=1, tiled=True)  10.1 us
  transfers between devices with their start and end apart: 11, of which 10 were waited for; matrix products, arithmetic and copies ran while one was open for 6% of the time, Pallas kernels for 0%

profile of v2, /device:TPU:1, one launch (start us, length us, event | category | flops | bytes accessed | tf_op | source)
XLA Modules:
  0.0 363.8 jit_solution(9038402511912606423)
XLA Ops:
  9.2 2.0 fusion.15
  11.2 1.6 broadcast_in_dim.18
  12.8 5.9 %all-to-all-start = ((bf16[8,2,256,256]{3,2,1,0:T(8,128)(2,1)}), bf16[8,2,256,256]{3,2,1,0:T(8,128)(2,1)S(1)}, u32[]{:S(2)}, u32[]{:S(2)}) async-start(bf16[8,2,256,256]{3,2,1,0:T(8,128)(2,1)} %broadcast_in_dim.18), calls=%async_computation | async-start | bytes 4194304 | tf_op jit(solution)/shard_map/all_to_all | solution.py:17
  20.6 24.3 %all-to-all-done = bf16[8,2,256,256]{3,2,1,0:T(8,128)(2,1)S(1)} async-done(((bf16[8,2,256,256]{3,2,1,0:T(8,128)(2,1)}), bf16[8,2,256,256]{3,2,1,0:T(8,128)(2,1)S(1)}, u32[]{:S(2)}, u32[]{:S(2)}) %all-to-all-start) | async-done | bytes 2097184 | tf_op jit(solution)/shard_map/all_to_all | solution.py:17
  44.9 7.8 %all-to-all-start.4 = ((bf16[16,2,128]{2,1,0:T(2,128)(2,1)}), bf16[16,2,128]{2,1,0:T(2,128)(2,1)S(1)}, u32[]{:S(2)}, u32[]{:S(2)}) async-start(bf16[16,2,128]{2,1,0:T(2,128)(2,1)} %reshape.1431), calls=%async_computation.4 | async-start | bytes 16384 | tf_op jit(solution)/shard_map/all_to_all | solution.py:17
  53.9 5.3 %all-to-all-done.4 = bf16[16,2,128]{2,1,0:T(2,128)(2,1)S(1)} async-done(((bf16[16,2,128]{2,1,0:T(2,128)(2,1)}), bf16[16,2,128]{2,1,0:T(2,128)(2,1)S(1)}, u32[]{:S(2)}, u32[]{:S(2)}) %all-to-all-start.4) | async-done | bytes 8224 | tf_op jit(solution)/shard_map/all_to_all | solution.py:17
  60.4 3.7 %all-to-all-start.2 = ((bf16[16,256,160]{1,2,0:T(8,128)(2,1)}), bf16[16,256,160]{1,2,0:T(8,128)(2,1)S(1)}, u32[]{:S(2)}, u32[]{:S(2)}) async-start(bf16[16,256,160]{1,2,0:T(8,128)(2,1)} %broadcast_in_dim.19), calls=%async_computation.2 | async-start | bytes 2621440 | tf_op jit(solution)/shard_map/all_to_all | solution.py:17
  64.2 35.1 %all-gather.2.cloned.1.call-done = bf16[2048,2048]{1,0:T(8,128)(2,1)} async-done(((bf16[128,2048]{1,0:T(8,128)(2,1)}), bf16[2048,2048]{1,0:T(8,128)(2,1)}) %all-gather.2.cloned.1.call-update) | async-done | bytes 8388624 | tf_op jit(solution)/shard_map/all_gather | solution.py:125
  99.3 7.2 %fusion.6 = f32[2048,512]{1,0:T(8,128)S(1)} fusion(bf16[2048,2048]{1,0:T(8,128)(2,1)} %all-gather.2.cloned.1.call-done, bf16[2048,256]{1,0:T(8,128)(2,1)} %bitcast.430, bf16[2048,256]{1,0:T(8,128)(2,1)S(1)} %bitcast.429), kind=kOutput, calls=%fused_computation.12 | convolution fusion | flops 4299161600 | bytes 14680064 | tf_op jit(solution)/shard_map/dot_general | solution.py:124
  106.7 1.7 copy-done.1
  108.4 2.4 multiply_convert_fusion
  110.8 5.2 %all-to-all-start.1 = ((bf16[16,128,256]{2,1,0:T(8,128)(2,1)}), bf16[16,128,256]{2,1,0:T(8,128)(2,1)S(1)}, u32[]{:S(2)}, u32[]{:S(2)}) async-start(bf16[16,128,256]{2,1,0:T(8,128)(2,1)} %bitcast.9), calls=%async_computation.1 | async-start | bytes 2097152 | tf_op jit(solution)/shard_map/all_to_all | solution.py:137
  116.2 15.7 %all-to-all-done.1 = bf16[16,128,256]{2,1,0:T(8,128)(2,1)S(1)} async-done(((bf16[16,128,256]{2,1,0:T(8,128)(2,1)}), bf16[16,128,256]{2,1,0:T(8,128)(2,1)S(1)}, u32[]{:S(2)}, u32[]{:S(2)}) %all-to-all-start.1) | async-done | bytes 1048608 | tf_op jit(solution)/shard_map/all_to_all | solution.py:137
  133.2 4.2 %all-to-all-start.3 = ((bf16[16,128,256]{1,2,0:T(8,128)(2,1)}), bf16[16,128,256]{1,2,0:T(8,128)(2,1)S(1)}, u32[]{:S(2)}, u32[]{:S(2)}) async-start(bf16[16,128,256]{1,2,0:T(8,128)(2,1)} %broadcast_in_dim.20), calls=%async_computation.3 | async-start | bytes 2097152 | tf_op jit(solution)/shard_map/all_to_all | solution.py:17
  141.0 11.4 %all-to-all-done.3 = bf16[16,128,256]{1,2,0:T(8,128)(2,1)S(1)} async-done(((bf16[16,128,256]{1,2,0:T(8,128)(2,1)}), bf16[16,128,256]{1,2,0:T(8,128)(2,1)S(1)}, u32[]{:S(2)}, u32[]{:S(2)}) %all-to-all-start.3) | async-done | bytes 1048608 | tf_op jit(solution)/shard_map/all_to_all | solution.py:17
  153.9 1.7 copy.130
  160.9 14.5 %shard_map.140 = (f32[16,32,128]{2,1,0:T(8,128)}, f32[16,32,128]{2,1,0:T(8,128)}) custom-call(f32[2048]{0:T(1024)} %reshape.1405.into_ref, f32[2048]{0:T(1024)} %reshape.1406.outof_ref, f32[128,32,128]{2,1,0:T(8,128)} %bitcast.426, f32[128,32,128]{2,1,0:T(8,128)} %reshape.1416.value_ref, f32[16,32,128]{2,1,0:T(8,128)} %bitcast.431, ...), custom_call_target="tpu_custom_call" | custom-call | flops 50331648 | bytes 4194304 | tf_op jit(solution)/shard_map/pallas_call | solution.py:81
  178.6 4.8 %all-to-all-start.5 = ((f32[2,16,16,256]{3,1,0,2:T(8,128)}), f32[2,16,16,256]{3,1,0,2:T(8,128)S(1)}, u32[]{:S(2)}, u32[]{:S(2)}) async-start(f32[2,16,16,256]{3,1,0,2:T(8,128)} %pad_maximum_fusion), calls=%async_computation.5 | async-start | bytes 1048576 | tf_op jit(solution)/shard_map/all_to_all | solution.py:171
  183.4 9.5 %all-to-all-done.5 = f32[2,16,16,256]{3,1,0,2:T(8,128)S(1)} async-done(((f32[2,16,16,256]{3,1,0,2:T(8,128)}), f32[2,16,16,256]{3,1,0,2:T(8,128)S(1)}, u32[]{:S(2)}, u32[]{:S(2)}) %all-to-all-start.5) | async-done | bytes 524320 | tf_op jit(solution)/shard_map/all_to_all | solution.py:171
  193.3 10.1 %all_to_all.67 = f32[16,16,256]{2,0,1:T(8,128)S(1)} all-to-all(f32[16,16,256]{2,0,1:T(8,128)S(1)} %constant_dynamic-update-slice_fusion), channel_id=1, replica_groups=mesh['req'=8,'seq'=16] {'seq'}, dimensions={1} | all-to-all | bytes 524288 | tf_op jit(solution)/shard_map/all_to_all | solution.py:178
  204.3 17.9 %shard_map.141 = f32[128,32,128]{2,1,0:T(8,128)} custom-call(f32[2048]{0:T(1024)} %reshape.1405.into_ref, f32[2048]{0:T(1024)} %reshape.1406.outof_ref, f32[128,32,128]{2,1,0:T(8,128)} %bitcast.427, f32[128,32,128]{2,1,0:T(8,128)} %reshape.1416.value_ref, f32[16,32,128]{2,1,0:T(8,128)} %bitcast.432, f32[16,32,128]{2,1,0:T(8,128)} %reshape.1411.start_ref, ...), custom_call_target="tpu_custom_call" | custom-call | flops 50331648 | bytes 6291456 | tf_op jit(solution)/shard_map/pallas_call | solution.py:81
  222.2 1.8 convert_element_type.95
  225.8 3.7 %all-to-all-start.7 = ((bf16[128,16,256]{2,0,1:T(8,128)(2,1)}), bf16[128,16,256]{2,0,1:T(8,128)(2,1)S(1)}, u32[]{:S(2)}, u32[]{:S(2)}) async-start(bf16[128,16,256]{2,0,1:T(8,128)(2,1)} %copy.96), calls=%async_computation.7 | async-start | bytes 2097152 | tf_op jit(solution)/shard_map/all_to_all | solution.py:184
  229.6 13.4 %all-to-all-done.7 = bf16[128,16,256]{2,0,1:T(8,128)(2,1)S(1)} async-done(((bf16[128,16,256]{2,0,1:T(8,128)(2,1)}), bf16[128,16,256]{2,0,1:T(8,128)(2,1)S(1)}, u32[]{:S(2)}, u32[]{:S(2)}) %all-to-all-start.7) | async-done | bytes 1048608 | tf_op jit(solution)/shard_map/all_to_all | solution.py:184
  244.1 9.4 %all-to-all-start.8 = ((bf16[8,256,256]{1,2,0:T(8,128)(2,1)}), bf16[8,256,256]{1,2,0:T(8,128)(2,1)S(1)}, u32[]{:S(2)}, u32[]{:S(2)}) async-start(bf16[8,256,256]{1,2,0:T(8,128)(2,1)} %broadcast_in_dim.23), calls=%async_computation.8 | async-start | bytes 2097152 | tf_op jit(solution)/shard_map/all_to_all | solution.py:17
  253.5 2.3 fusion.12
  255.8 12.7 %all-to-all-done.8 = bf16[8,256,256]{1,2,0:T(8,128)(2,1)S(1)} async-done(((bf16[8,256,256]{1,2,0:T(8,128)(2,1)}), bf16[8,256,256]{1,2,0:T(8,128)(2,1)S(1)}, u32[]{:S(2)}, u32[]{:S(2)}) %all-to-all-start.8) | async-done | bytes 1048608 | tf_op jit(solution)/shard_map/all_to_all | solution.py:17
  268.4 5.7 %convolution_convert_fusion = bf16[2048,2048]{1,0:T(8,128)(2,1)} fusion(bf16[2048,256]{1,0:T(8,128)(2,1)S(1)} %fusion.12, bf16[256,2048]{0,1:T(8,128)(2,1)S(1)} %bitcast.425), kind=kOutput, calls=%fused_computation | convolution fusion | flops 2151677952 | bytes 10485760 | tf_op jit(solution)/shard_map/dot_general | solution.py:189
  274.8 4.2 %all-to-all-start.9 = ((f32[8,1,16,256]{3,2,1,0:T(8,128)}), f32[8,1,16,256]{3,2,1,0:T(8,128)S(1)}, u32[]{:S(2)}, u32[]{:S(2)}) async-start(f32[8,1,16,256]{3,2,1,0:T(8,128)} %broadcast_in_dim.25), calls=%async_computation.10 | async-start | bytes 262144 | tf_op jit(solution)/shard_map/all_to_all | solution.py:17
  279.0 5.3 %all-to-all-done.9 = f32[8,1,16,256]{3,2,1,0:T(8,128)S(1)} async-done(((f32[8,1,16,256]{3,2,1,0:T(8,128)}), f32[8,1,16,256]{3,2,1,0:T(8,128)S(1)}, u32[]{:S(2)}, u32[]{:S(2)}) %all-to-all-start.9) | async-done | bytes 131104 | tf_op jit(solution)/shard_map/all_to_all | solution.py:17
  285.0 69.9 %reduce-scatter.2.cloned.1.call-done = bf16[128,2048]{1,0:T(8,128)(2,1)} async-done(((bf16[2048,2048]{1,0:T(8,128)(2,1)}), bf16[128,2048]{1,0:T(8,128)(2,1)}) %reduce-scatter.2.cloned.1.call-update) | async-done | bytes 524304 | tf_op jit(solution)/shard_map/reduce_scatter | solution.py:188
  355.0 2.0 fusion.18
  (88 shorter events, 26.7 us)
Async XLA Ops:
  7.2 4.1 %copy-start.2 = (bf16[2,256,256]{2,1,0:T(8,128)(2,1)S(1)}, bf16[2,256,256]{2,1,0:T(8,128)(2,1)}, u32[]{:S(2)}) copy-start(bf16[2,256,256]{2,1,0:T(8,128)(2,1)} %param.17) | copy-start | bytes 786436
  7.2 92.1 %all-gather.2.cloned.1.call-start = ((), (), s32[]{:S(2)}) async-start(), calls=%async_computation.11 | async-start | bytes 8912896 | tf_op jit(solution)/shard_map/all_gather | solution.py:125
  12.8 5.9 %copy-start.8 = (bf16[256]{0:T(256)(128)(2,1)S(1)}, bf16[256]{0:T(256)(128)(2,1)}, u32[]{:S(2)}) copy-start(bf16[256]{0:T(256)(128)(2,1)} %param.19) | copy-start | bytes 1540
  12.8 5.9 %copy-start.7 = (bf16[256]{0:T(256)(128)(2,1)S(1)}, bf16[256]{0:T(256)(128)(2,1)}, u32[]{:S(2)}) copy-start(bf16[256]{0:T(256)(128)(2,1)} %param.22) | copy-start | bytes 1540
  12.8 7.8 %copy-start.6 = (bf16[4,256]{1,0:T(4,128)(2,1)S(1)}, bf16[4,256]{1,0:T(4,128)(2,1)}, u32[]{:S(2)}) copy-start(bf16[4,256]{1,0:T(4,128)(2,1)} %param.18) | copy-start | bytes 6148
  12.8 32.1 %all-to-all-start = ((bf16[8,2,256,256]{3,2,1,0:T(8,128)(2,1)}), bf16[8,2,256,256]{3,2,1,0:T(8,128)(2,1)S(1)}, u32[]{:S(2)}, u32[]{:S(2)}) async-start(bf16[8,2,256,256]{3,2,1,0:T(8,128)(2,1)} %broadcast_in_dim.18), calls=%async_computation | async-start | bytes 4194304 | tf_op jit(solution)/shard_map/all_to_all | solution.py:17
  44.9 14.3 %all-to-all-start.4 = ((bf16[16,2,128]{2,1,0:T(2,128)(2,1)}), bf16[16,2,128]{2,1,0:T(2,128)(2,1)S(1)}, u32[]{:S(2)}, u32[]{:S(2)}) async-start(bf16[16,2,128]{2,1,0:T(2,128)(2,1)} %reshape.1431), calls=%async_computation.4 | async-start | bytes 16384 | tf_op jit(solution)/shard_map/all_to_all | solution.py:17
  52.7 6.5 %copy-start.4 = (bf16[256,160]{0,1:T(8,128)(2,1)S(1)}, bf16[256,160]{0,1:T(8,128)(2,1)}, u32[]{:S(2)}) copy-start(bf16[256,160]{0,1:T(8,128)(2,1)} %param.20) | copy-start | bytes 245764
  60.4 50.4 %all-to-all-start.2 = ((bf16[16,256,160]{1,2,0:T(8,128)(2,1)}), bf16[16,256,160]{1,2,0:T(8,128)(2,1)S(1)}, u32[]{:S(2)}, u32[]{:S(2)}) async-start(bf16[16,256,160]{1,2,0:T(8,128)(2,1)} %broadcast_in_dim.19), calls=%async_computation.2 | async-start | bytes 2621440 | tf_op jit(solution)/shard_map/all_to_all | solution.py:17
  106.5 2.0 copy-start.1
  108.4 7.6 %copy-start.5 = (bf16[128,256]{1,0:T(8,128)(2,1)S(1)}, bf16[128,256]{1,0:T(8,128)(2,1)}, u32[]{:S(2)}) copy-start(bf16[128,256]{1,0:T(8,128)(2,1)} %param.21) | copy-start | bytes 196612
  110.8 21.1 %all-to-all-start.1 = ((bf16[16,128,256]{2,1,0:T(8,128)(2,1)}), bf16[16,128,256]{2,1,0:T(8,128)(2,1)S(1)}, u32[]{:S(2)}, u32[]{:S(2)}) async-start(bf16[16,128,256]{2,1,0:T(8,128)(2,1)} %bitcast.9), calls=%async_computation.1 | async-start | bytes 2097152 | tf_op jit(solution)/shard_map/all_to_all | solution.py:137
  116.2 23.0 %copy-start.9 = (s32[8]{0:T(128)S(1)}, s32[8]{0:T(128)}, u32[]{:S(2)}) copy-start(s32[8]{0:T(128)} %param.14) | copy-start | bytes 100
  133.2 19.3 %all-to-all-start.3 = ((bf16[16,128,256]{1,2,0:T(8,128)(2,1)}), bf16[16,128,256]{1,2,0:T(8,128)(2,1)S(1)}, u32[]{:S(2)}, u32[]{:S(2)}) async-start(bf16[16,128,256]{1,2,0:T(8,128)(2,1)} %broadcast_in_dim.20), calls=%async_computation.3 | async-start | bytes 2097152 | tf_op jit(solution)/shard_map/all_to_all | solution.py:17
  178.6 14.3 %all-to-all-start.5 = ((f32[2,16,16,256]{3,1,0,2:T(8,128)}), f32[2,16,16,256]{3,1,0,2:T(8,128)S(1)}, u32[]{:S(2)}, u32[]{:S(2)}) async-start(f32[2,16,16,256]{3,1,0,2:T(8,128)} %pad_maximum_fusion), calls=%async_computation.5 | async-start | bytes 1048576 | tf_op jit(solution)/shard_map/all_to_all | solution.py:171
  224.4 5.1 %copy-start.3 = (bf16[256,256]{1,0:T(8,128)(2,1)S(1)}, bf16[256,256]{1,0:T(8,128)(2,1)}, u32[]{:S(2)}) copy-start(bf16[256,256]{1,0:T(8,128)(2,1)} %param.25) | copy-start | bytes 393220
  225.8 17.2 %all-to-all-start.7 = ((bf16[128,16,256]{2,0,1:T(8,128)(2,1)}), bf16[128,16,256]{2,0,1:T(8,128)(2,1)S(1)}, u32[]{:S(2)}, u32[]{:S(2)}) async-start(bf16[128,16,256]{2,0,1:T(8,128)(2,1)} %copy.96), calls=%async_computation.7 | async-start | bytes 2097152 | tf_op jit(solution)/shard_map/all_to_all | solution.py:184
  244.1 24.3 %all-to-all-start.8 = ((bf16[8,256,256]{1,2,0:T(8,128)(2,1)}), bf16[8,256,256]{1,2,0:T(8,128)(2,1)S(1)}, u32[]{:S(2)}, u32[]{:S(2)}) async-start(bf16[8,256,256]{1,2,0:T(8,128)(2,1)} %broadcast_in_dim.23), calls=%async_computation.8 | async-start | bytes 2097152 | tf_op jit(solution)/shard_map/all_to_all | solution.py:17
  253.5 101.5 %reduce-scatter.2.cloned.1.call-start = ((), (), s32[]{:S(2)}) async-start(), calls=%async_computation.12 | async-start | bytes 8912896 | tf_op jit(solution)/shard_map/reduce_scatter | solution.py:188
  274.1 4.9 %copy-start.10 = (s32[8]{0:T(128)S(1)}, s32[8]{0:T(128)}, u32[]{:S(2)}) copy-start(s32[8]{0:T(128)} %param.15) | copy-start | bytes 100
  274.1 80.9 %copy-start = (bf16[1,128,2048]{2,1,0:T(8,128)(2,1)S(1)}, bf16[1,128,2048]{2,1,0:T(8,128)(2,1)}, u32[]{:S(2)}) copy-start(bf16[1,128,2048]{2,1,0:T(8,128)(2,1)} %param.13) | copy-start | bytes 1572868
  274.8 9.6 %all-to-all-start.9 = ((f32[8,1,16,256]{3,2,1,0:T(8,128)}), f32[8,1,16,256]{3,2,1,0:T(8,128)S(1)}, u32[]{:S(2)}, u32[]{:S(2)}) async-start(f32[8,1,16,256]{3,2,1,0:T(8,128)} %broadcast_in_dim.25), calls=%async_computation.10 | async-start | bytes 262144 | tf_op jit(solution)/shard_map/all_to_all | solution.py:17
Sparse Core Ops, SparseCore 0:
  11.4 87.8 all-gather.1
  274.2 80.6 reduce-scatter.1

commit v3 on v2

--- a/solution.py
+++ b/solution.py
@@ -5,7 +5,7 @@
 from jax import lax
 from jax.experimental import pallas as pl
 from jax.experimental.pallas import tpu as pltpu
-from jax.sharding import PartitionSpec as P
+from jax.sharding import Mesh, PartitionSpec as P
 
 STATE = 16
 RANK = 128
@@ -107,8 +107,11 @@
     skip_gain,
     out_weight,
 ):
-    seq_count = lax.axis_size("seq")
-    seq_index = lax.axis_index("seq")
+    seq = ("sz", "sy")
+    rows_n = lax.axis_size("sz")
+    cols_n = lax.axis_size("sy")
+    seq_count = rows_n * cols_n
+    seq_index = lax.axis_index(seq)
     req_index = lax.axis_index("req")
     rows = hidden.shape[1]
     span = rows * seq_count
@@ -116,28 +119,37 @@
     taps_count = conv_weight.shape[0]
     state_count = a_log.shape[0]
     total_inner = a_log.shape[1]
+    model = hidden.shape[2]
+    w_in = gather_a2a(in_weight, "req", 1)
+    w_out = gather_a2a(out_weight, "req", 1)
+    xproj_full = gather_a2a(xproj_weight, seq, 0)
+    dt_full = gather_a2a(dt_weight, seq, 1)
+    dt_bias_full = gather_a2a(dt_bias, seq, 0)
+    w_col = lax.all_gather(w_out, "sz", axis=0, tiled=False)
+    w_in, w_col, xproj_full, dt_full, dt_bias_full = lax.optimization_barrier(
+        (w_in, w_col, xproj_full, dt_full, dt_bias_full)
+    )
     tokens = hidden[0].astype(jnp.float32)
     scale = lax.rsqrt(jnp.mean(tokens * tokens, axis=-1, keepdims=True) + 1e-05)
     normed = (tokens * scale * norm_gain.astype(jnp.float32)).astype(jnp.bfloat16)
-    w_in = gather_a2a(in_weight, "req", 1)
     w_flat = jnp.concatenate((w_in[0], w_in[1]), axis=1)
     both = jnp.dot(
-        lax.all_gather(normed, "seq", axis=0, tiled=True),
+        lax.all_gather(normed, seq, axis=0, tiled=True),
         w_flat,
         preferred_element_type=jnp.float32,
     )
     xin = both[:, :width]
     zgate = both[:, width:].astype(jnp.bfloat16)
+    z_grid = lax.all_to_all(
+        zgate.reshape(rows_n, span // rows_n, width), "sz", split_axis=0, concat_axis=0, tiled=True
+    )
     padded = jnp.pad(xin, ((taps_count - 1, 0), (0, 0)))
     taps = conv_weight.astype(jnp.float32)
     convolved = conv_bias.astype(jnp.float32) + jnp.zeros_like(xin)
     for tap in range(taps_count):
         convolved = convolved + taps[tap] * padded[tap : tap + span, :]
     inner = jax.nn.silu(convolved).astype(jnp.bfloat16)
-    inner_tok = lax.all_to_all(inner, "seq", split_axis=0, concat_axis=1, tiled=True)
-    xproj_full = gather_a2a(xproj_weight, "seq", 0)
-    dt_full = gather_a2a(dt_weight, "seq", 1)
-    dt_bias_full = gather_a2a(dt_bias, "seq", 0)
+    inner_tok = lax.all_to_all(inner, seq, split_axis=0, concat_axis=1, tiled=True)
     proj = jnp.dot(inner_tok, xproj_full, preferred_element_type=jnp.float32)
     length_here = lax.dynamic_index_in_dim(lengths, req_index, 0, keepdims=False)
     positions = seq_index * rows + jnp.arange(rows, dtype=jnp.int32)
@@ -150,7 +162,6 @@
         )
         * live[:, None]
     )
-    w_out = gather_a2a(out_weight, "req", 1)
     decay = -jnp.exp(a_log)
     lanes = 128
     groups = total_inner // lanes
@@ -168,28 +179,30 @@
     pair = jnp.stack(
         (total_l.reshape(state_count, total_inner), end_l.reshape(state_count, total_inner))
     ).reshape(2, state_count, seq_count, width)
-    pair_ch = lax.all_to_all(pair, "seq", split_axis=2, concat_axis=2, tiled=True)
+    pair_ch = lax.all_to_all(pair, seq, split_axis=2, concat_axis=2, tiled=True)
     carry = jnp.zeros((state_count, width), jnp.float32)
     carries = []
     for block in range(seq_count):
         carries.append(carry)
         carry = pair_ch[0, :, block] * carry + pair_ch[1, :, block]
     carry_ch = jnp.stack(carries, axis=1)
-    carry_in = lax.all_to_all(carry_ch, "seq", split_axis=1, concat_axis=1, tiled=True)
+    carry_in = lax.all_to_all(carry_ch, seq, split_axis=1, concat_axis=1, tiled=True)
     out_l = run_scan(
         True, into, outof, rate_l, value_l, decay_l,
         carry_in.reshape(state_count, groups, lanes), skip_l,
     )
-    scanned = out_l.reshape(rows, total_inner).astype(jnp.bfloat16)
-    scanned_ch = lax.all_to_all(scanned, "seq", split_axis=1, concat_axis=0, tiled=True)
-    gated_ch = (scanned_ch.astype(jnp.float32) * jax.nn.silu(zgate.astype(jnp.float32))).astype(
-        jnp.bfloat16
-    )
+    scanned = out_l.reshape(rows, rows_n, cols_n, width).astype(jnp.bfloat16)
+    scanned_grid = lax.all_to_all(scanned, "sy", split_axis=2, concat_axis=0, tiled=True)
+    z_here = z_grid.reshape(rows_n, cols_n, rows, width).transpose(1, 2, 0, 3)
+    gated = (
+        scanned_grid.reshape(cols_n, rows, rows_n, width).astype(jnp.float32)
+        * jax.nn.silu(z_here.astype(jnp.float32))
+    ).astype(jnp.bfloat16)
+    partial = jnp.einsum(
+        "ktac,acd->ktd", gated, w_col, preferred_element_type=jnp.float32
+    ).astype(jnp.bfloat16)
     branch = lax.psum_scatter(
-        jnp.dot(gated_ch, w_out, preferred_element_type=jnp.float32).astype(jnp.bfloat16),
-        "seq",
-        scatter_dimension=0,
-        tiled=True,
+        partial.reshape(cols_n * rows, model), "sy", scatter_dimension=0, tiled=True
     ).astype(jnp.float32)
     slot_all = gather_a2a(carry[None], "req", 0)
     picked = (slot_request == req_index).astype(jnp.float32)
@@ -199,22 +212,28 @@
 
 
 def solution(mesh):
+    seq_n = mesh.shape["seq"]
+    rows_n = 1
+    while rows_n * rows_n < seq_n:
+        rows_n *= 2
+    grid = Mesh(mesh.devices.reshape(mesh.shape["req"], rows_n, seq_n // rows_n), ("req", "sz", "sy"))
+    seq = ("sz", "sy")
     in_specs = (
-        P("req", "seq", None),
-        P(),
-        P(),
-        P(),
-        P(None, "req", "seq"),
-        P(None, "seq"),
-        P("seq"),
-        P("seq", None),
-        P(None, "seq"),
-        P("seq"),
-        P(),
-        P(),
-        P("seq", "req"),
-    )
-    out_specs = (P("req", "seq", None), P("req", None, "seq"))
+        P("req", seq, None),
+        P(),
+        P(),
+        P(),
+        P(None, "req", seq),
+        P(None, seq),
+        P(seq),
+        P(seq, None),
+        P(None, seq),
+        P(seq),
+        P(),
+        P(),
+        P(seq, "req"),
+    )
+    out_specs = (P("req", seq, None), P("req", None, seq))
     return jax.shard_map(
-        per_device, mesh=mesh, in_specs=in_specs, out_specs=out_specs, check_vma=False
-    )
+        per_device, mesh=grid, in_specs=in_specs, out_specs=out_specs, check_vma=False
+    )

time: 366 us -> 360 us (0.984)
  waiting for transfers between devices: 203 us -> 139 us
  blocking collectives: 10.1 us -> 72.7 us
  starting transfers between devices: 48.9 us -> 36.3 us
  local copies, waits for them, and re-layouts: 23.4 us -> 29.8 us
    all_to_all x1 -> x4, blocking collectives: 10.1 us -> 72.7 us  [the longest x3 59 us: gather_a2a(): lax.all_to_all(copies, axis, split_axis=0, concat_axis=0, tiled=True)]
    reduce_scatter x1, waiting for transfers between devices: 69.9 us -> 17.7 us  [per_device(): lax.psum_scatter(partial.reshape(cols_n * rows, model), 'sy', scatter_dim...]
    all_to_all x6 -> x3, starting transfers between devices: 35.2 us -> 19.6 us  [gather_a2a(): lax.all_to_all(copies, axis, split_axis=0, concat_axis=0, tiled=True)]
    all_to_all x3 -> x4, waiting for transfers between devices: 38.7 us -> 27.8 us  [the longest x1 13.8 us: per_device(): lax.all_to_all(inner, seq, split_axis=0, concat_axis=1, tiled=True)]
    all_to_all x6 -> x3, waiting for transfers between devices: 59.1 us -> 50.5 us  [gather_a2a(): lax.all_to_all(copies, axis, split_axis=0, concat_axis=0, tiled=True)]
    all_gather x1 -> x2, waiting for transfers between devices: 35.1 us -> 42.8 us  [the longest x1 42.8 us: per_device(): lax.all_gather(normed, seq, axis=0, tiled=True)]
    unnamed x14, other arithmetic: 1.11 us -> 7.91 us
    all_to_all x3 -> x4, starting transfers between devices: 13.7 us -> 16.6 us  [the longest x1 5.14 us: per_device(): lax.all_to_all(inner, seq, split_axis=0, concat_axis=1, tiled=True)]
  transfers between devices with their start and end apart: 11 -> 10, of which waited for: 10 -> 8; matrix products, arithmetic and copies ran while one was open for 6% -> 6% of each run, Pallas kernels for 0% -> 5%
where the time goes in v3:
time: 360 us; the launch traced here: 359 us
  waiting for transfers between devices  139 us (39%)
  blocking collectives  72.7 us (20%)
  starting transfers between devices  36.3 us (10%)
  Pallas kernels  32.4 us (9%)
  local copies, waits for them, and re-layouts  29.8 us (8%)
  other arithmetic  18.8 us (5%)
  matrix products  16.1 us (4%)
  between operations  14.1 us (4%)
    all_to_all x3, blocking collectives, gather_a2a(): lax.all_to_all(copies, axis, split_axis=0, concat_axis=0, tiled=True)  59 us
    all_to_all x3, waiting for transfers between devices, gather_a2a(): lax.all_to_all(copies, axis, split_axis=0, concat_axis=0, tiled=True)  50.5 us
    all_gather x1, waiting for transfers between devices, per_device(): lax.all_gather(normed, seq, axis=0, tiled=True)  42.8 us
    pallas_call x2, Pallas kernels, run_scan(): pl.pallas_call(functools.partial(scan_body, emit), grid=(chunks,), in_spe...  32.4 us
    all_to_all x3, starting transfers between devices, gather_a2a(): lax.all_to_all(copies, axis, split_axis=0, concat_axis=0, tiled=True)  19.6 us
    reduce_scatter x1, waiting for transfers between devices, per_device(): lax.psum_scatter(partial.reshape(cols_n * rows, model), 'sy', scatter_dim...  17.7 us
    all_to_all x1, waiting for transfers between devices, per_device(): lax.all_to_all(inner, seq, split_axis=0, concat_axis=1, tiled=True)  13.8 us
    all_to_all x1, blocking collectives, per_device(): lax.all_to_all(scanned, 'sy', split_axis=2, concat_axis=0, tiled=True)  13.7 us
  transfers between devices with their start and end apart: 10, of which 8 were waited for; matrix products, arithmetic and copies ran while one was open for 6% of the time, Pallas kernels for 5%

profile of v3, /device:TPU:1, one launch (start us, length us, event | category | flops | bytes accessed | tf_op | source)
XLA Modules:
  0.0 359.1 jit_solution(2575466108746650654)
XLA Ops:
  8.2 20.5 %all_to_all.74 = bf16[8,256,256]{2,1,0:T(8,128)(2,1)S(1)} all-to-all(bf16[8,256,256]{2,1,0:T(8,128)(2,1)S(1)} %broadcast_in_dim.19), channel_id=1, replica_groups=mesh['req'=8,'sz'=4,'sy'=4] {'req'}, dimensions={0} | all-to-all | bytes 2097152 | tf_op jit(solution)/shard_map/all_to_all | solution.py:17
  33.3 14.0 %all_to_all.75 = bf16[16,2,128]{2,1,0:T(2,128)(2,1)S(1)} all-to-all(bf16[16,2,128]{2,1,0:T(2,128)(2,1)S(1)} %reshape.1440), channel_id=1, replica_groups=mesh['req'=8,'sz'=4,'sy'=4] {'sz','sy'}, dimensions={0} | all-to-all | bytes 16384 | tf_op jit(solution)/shard_map/all_to_all | solution.py:17
  47.4 24.4 %all_to_all.76 = bf16[16,256,160]{1,2,0:T(8,128)(2,1)} all-to-all(bf16[16,256,160]{1,2,0:T(8,128)(2,1)S(1)} %broadcast_in_dim.20), channel_id=1, replica_groups=mesh['req'=8,'sz'=4,'sy'=4] {'sz','sy'}, dimensions={0} | all-to-all | bytes 2621440 | tf_op jit(solution)/shard_map/all_to_all | solution.py:17
  73.4 6.2 %all-to-all-start = ((bf16[8,2,256,256]{3,2,1,0:T(8,128)(2,1)}), bf16[8,2,256,256]{3,2,1,0:T(8,128)(2,1)S(1)}, u32[]{:S(2)}, u32[]{:S(2)}) async-start(bf16[8,2,256,256]{3,2,1,0:T(8,128)(2,1)} %broadcast_in_dim.18), calls=%async_computation | async-start | bytes 4194304 | tf_op jit(solution)/shard_map/all_to_all | solution.py:17
  79.7 26.1 %all-to-all-done = bf16[8,2,256,256]{3,2,1,0:T(8,128)(2,1)S(1)} async-done(((bf16[8,2,256,256]{3,2,1,0:T(8,128)(2,1)}), bf16[8,2,256,256]{3,2,1,0:T(8,128)(2,1)S(1)}, u32[]{:S(2)}, u32[]{:S(2)}) %all-to-all-start) | async-done | bytes 2097184 | tf_op jit(solution)/shard_map/all_to_all | solution.py:17
  107.0 4.3 %all-to-all-start.3 = ((bf16[16,128,256]{1,2,0:T(8,128)(2,1)}), bf16[16,128,256]{1,2,0:T(8,128)(2,1)}, u32[]{:S(2)}, u32[]{:S(2)}) async-start(bf16[16,128,256]{1,2,0:T(8,128)(2,1)} %broadcast_in_dim.21), calls=%async_computation.3 | async-start | bytes 2097152 | tf_op jit(solution)/shard_map/all_to_all | solution.py:17
  114.4 19.2 %all-to-all-done.3 = bf16[16,128,256]{1,2,0:T(8,128)(2,1)} async-done(((bf16[16,128,256]{1,2,0:T(8,128)(2,1)}), bf16[16,128,256]{1,2,0:T(8,128)(2,1)}, u32[]{:S(2)}, u32[]{:S(2)}) %all-to-all-start.3) | async-done | bytes 1048608 | tf_op jit(solution)/shard_map/all_to_all | solution.py:17
  133.6 1.7 slice_bitcast_fusion.1
  135.3 42.8 %all-gather.3.cloned.1.call-done = bf16[2048,2048]{1,0:T(8,128)(2,1)} async-done(((bf16[128,2048]{1,0:T(8,128)(2,1)}), bf16[2048,2048]{1,0:T(8,128)(2,1)}) %all-gather.3.cloned.1.call-update) | async-done | bytes 8388624 | tf_op jit(solution)/shard_map/all_gather | solution.py:137
  178.1 6.9 %fusion.6 = f32[2048,512]{1,0:T(8,128)S(1)} fusion(bf16[2048,2048]{1,0:T(8,128)(2,1)} %all-gather.3.cloned.1.call-done, bf16[2048,256]{1,0:T(8,128)(2,1)S(1)} %get-tuple-element.31, bf16[2048,256]{1,0:T(8,128)(2,1)S(1)} %get-tuple-element.30), kind=kOutput, calls=%fused_computation.8 | convolution fusion | flops 4299161600 | bytes 14680064 | tf_op jit(solution)/shard_map/dot_general | solution.py:136
  185.2 1.7 copy-done.2
  186.9 2.3 multiply_convert_fusion
  189.3 5.1 %all-to-all-start.5 = ((bf16[16,128,256]{2,1,0:T(8,128)(2,1)}), bf16[16,128,256]{2,1,0:T(8,128)(2,1)S(1)}, u32[]{:S(2)}, u32[]{:S(2)}) async-start(bf16[16,128,256]{2,1,0:T(8,128)(2,1)} %bitcast.14), calls=%async_computation.5 | async-start | bytes 2097152 | tf_op jit(solution)/shard_map/all_to_all | solution.py:152
  196.5 13.8 %all-to-all-done.5 = bf16[16,128,256]{2,1,0:T(8,128)(2,1)S(1)} async-done(((bf16[16,128,256]{2,1,0:T(8,128)(2,1)}), bf16[16,128,256]{2,1,0:T(8,128)(2,1)S(1)}, u32[]{:S(2)}, u32[]{:S(2)}) %all-to-all-start.5) | async-done | bytes 1048608 | tf_op jit(solution)/shard_map/all_to_all | solution.py:152
  211.5 2.7 fusion.5
  214.2 1.7 copy.182
  217.5 1.9 copy.148.value_ref
  220.1 14.6 %shard_map.140 = (f32[16,32,128]{2,1,0:T(8,128)}, f32[16,32,128]{2,1,0:T(8,128)}) custom-call(f32[2048]{0:T(1024)} %reshape.1411.into_ref, f32[2048]{0:T(1024)} %reshape.1412.outof_ref, f32[128,32,128]{2,1,0:T(8,128)} %bitcast.473, f32[128,32,128]{2,1,0:T(8,128)} %copy.148.value_ref, f32[16,32,128]{2,1,0:T(8,128)} %bitcast.477, ...), custom_call_target="tpu_custom_call" | custom-call | flops 50331648 | bytes 4194304 | tf_op jit(solution)/shard_map/pallas_call | solution.py:81
  237.9 4.2 %all-to-all-start.6 = ((f32[2,16,16,256]{3,1,0,2:T(8,128)}), f32[2,16,16,256]{3,1,0,2:T(8,128)S(1)}, u32[]{:S(2)}, u32[]{:S(2)}) async-start(f32[2,16,16,256]{3,1,0,2:T(8,128)} %pad_maximum_fusion), calls=%async_computation.6 | async-start | bytes 1048576 | tf_op jit(solution)/shard_map/all_to_all | solution.py:182
  242.7 9.1 %all-to-all-done.6 = f32[2,16,16,256]{3,1,0,2:T(8,128)S(1)} async-done(((f32[2,16,16,256]{3,1,0,2:T(8,128)}), f32[2,16,16,256]{3,1,0,2:T(8,128)S(1)}, u32[]{:S(2)}, u32[]{:S(2)}) %all-to-all-start.6) | async-done | bytes 524320 | tf_op jit(solution)/shard_map/all_to_all | solution.py:182
  260.9 3.5 all-to-all-start.7
  264.4 2.7 slice.370
  267.1 4.9 %all-to-all-done.7 = f32[16,16,256]{2,0,1:T(8,128)S(1)} async-done(((f32[16,16,256]{2,0,1:T(8,128)}), f32[16,16,256]{2,0,1:T(8,128)S(1)}, u32[]{:S(2)}, u32[]{:S(2)}) %all-to-all-start.7) | async-done | bytes 262176 | tf_op jit(solution)/shard_map/all_to_all | solution.py:189
  272.0 3.7 %all-to-all-start.9 = ((bf16[4,512,256]{2,1,0:T(8,128)(2,1)}), bf16[4,512,256]{2,1,0:T(8,128)(2,1)S(1)}, u32[]{:S(2)}, u32[]{:S(2)}) async-start(bf16[4,512,256]{2,1,0:T(8,128)(2,1)} %bitcast.53), calls=%async_computation.9 | async-start | bytes 2097152 | tf_op jit(solution)/shard_map/all_to_all | solution.py:143
  276.6 17.9 %shard_map.141 = f32[128,32,128]{2,1,0:T(8,128)} custom-call(f32[2048]{0:T(1024)} %reshape.1411.into_ref, f32[2048]{0:T(1024)} %reshape.1412.outof_ref, f32[128,32,128]{2,1,0:T(8,128)} %bitcast.474, f32[128,32,128]{2,1,0:T(8,128)} %copy.148.value_ref, f32[16,32,128]{2,1,0:T(8,128)} %bitcast.478, f32[16,32,128]{2,1,0:T(8,128)} %reshape.1416.start_ref, ...), custom_call_target="tpu_custom_call" | custom-call | flops 50331648 | bytes 6291456 | tf_op jit(solution)/shard_map/pallas_call | solution.py:81
  294.5 1.8 convert_element_type.95
  297.4 13.7 %all_to_all.77 = bf16[128,4,4,256]{3,0,1,2:T(8,128)(2,1)S(1)} all-to-all(bf16[128,4,4,256]{3,0,1,2:T(8,128)(2,1)S(1)} %copy.144), channel_id=1, replica_groups=mesh['req'=8,'sz'=4,'sy'=4] {'sy'}, dimensions={2} | all-to-all | bytes 2097152 | tf_op jit(solution)/shard_map/all_to_all | solution.py:195
  311.1 6.1 %bitcast_convert_fusion = bf16[4,128,2048]{2,1,0:T(8,128)(2,1)} fusion(bf16[4,256,2048]{2,1,0:T(8,128)(2,1)} %all-gather.5.cloned.1.call-done, bf16[4,4,128,256]{3,2,1,0:T(8,128)(2,1)S(1)} %bitcast.476, bf16[128,4,4,256]{3,0,1,2:T(8,128)(2,1)S(1)} %all_to_all.77), kind=kOutput, calls=%fused_computation.4 | convolution fusion | flops 2152726528 | bytes 8388608 | tf_op jit(solution)/shard_map/ktac,acd->ktd/dot_general | solution.py:201
  317.9 9.1 %all-to-all-start.10 = ((f32[8,1,16,256]{3,2,1,0:T(8,128)}), f32[8,1,16,256]{3,2,1,0:T(8,128)S(1)}, u32[]{:S(2)}, u32[]{:S(2)}) async-start(f32[8,1,16,256]{3,2,1,0:T(8,128)} %broadcast_in_dim.25), calls=%async_computation.11 | async-start | bytes 262144 | tf_op jit(solution)/shard_map/all_to_all | solution.py:17
  327.0 5.2 %all-to-all-done.10 = f32[8,1,16,256]{3,2,1,0:T(8,128)S(1)} async-done(((f32[8,1,16,256]{3,2,1,0:T(8,128)}), f32[8,1,16,256]{3,2,1,0:T(8,128)S(1)}, u32[]{:S(2)}, u32[]{:S(2)}) %all-to-all-start.10) | async-done | bytes 131104 | tf_op jit(solution)/shard_map/all_to_all | solution.py:17
  332.9 17.7 %reduce-scatter.2.cloned.1.call-done = bf16[128,2048]{1,0:T(8,128)(2,1)} async-done(((bf16[512,2048]{1,0:T(8,128)(2,1)}), bf16[128,2048]{1,0:T(8,128)(2,1)}) %reduce-scatter.2.cloned.1.call-update) | async-done | bytes 524304 | tf_op jit(solution)/shard_map/reduce_scatter | solution.py:204
  350.6 2.0 fusion.26
  (98 shorter events, 33.4 us)
Async XLA Ops:
  7.2 126.4 %all-gather.5.cloned.1.call-start = ((), (), s32[]{:S(2)}) async-start(), calls=%async_computation.13 | async-start | bytes 5242880 | tf_op jit(solution)/shard_map/all_gather | solution.py:128
  29.2 1.6 copy-start.8
  29.2 1.6 copy-start
  30.7 1.3 copy-start.9
  30.7 16.6 %copy-start.5 = (bf16[256,160]{0,1:T(8,128)(2,1)S(1)}, bf16[256,160]{0,1:T(8,128)(2,1)}, u32[]{:S(2)}) copy-start(bf16[256,160]{0,1:T(8,128)(2,1)} %param.20) | copy-start | bytes 245764
  30.7 147.3 %all-gather.3.cloned.1.call-start = ((), (), s32[]{:S(2)}) async-start(), calls=%async_computation.12 | async-start | bytes 8912896 | tf_op jit(solution)/shard_map/all_gather | solution.py:137
  32.0 39.8 %copy-start.3 = (bf16[2,256,256]{2,1,0:T(8,128)(2,1)S(1)}, bf16[2,256,256]{2,1,0:T(8,128)(2,1)}, u32[]{:S(2)}) copy-start(bf16[2,256,256]{2,1,0:T(8,128)(2,1)} %param.17) | copy-start | bytes 786436
  73.4 6.2 %copy-start.6 = (bf16[128,256]{1,0:T(8,128)(2,1)S(1)}, bf16[128,256]{1,0:T(8,128)(2,1)}, u32[]{:S(2)}) copy-start(bf16[128,256]{1,0:T(8,128)(2,1)} %param.21) | copy-start | bytes 196612
  73.4 32.4 %all-to-all-start = ((bf16[8,2,256,256]{3,2,1,0:T(8,128)(2,1)}), bf16[8,2,256,256]{3,2,1,0:T(8,128)(2,1)S(1)}, u32[]{:S(2)}, u32[]{:S(2)}) async-start(bf16[8,2,256,256]{3,2,1,0:T(8,128)(2,1)} %broadcast_in_dim.18), calls=%async_computation | async-start | bytes 4194304 | tf_op jit(solution)/shard_map/all_to_all | solution.py:17
  79.6 31.8 %copy-start.10 = (bf16[256]{0:T(256)(128)(2,1)S(1)}, bf16[256]{0:T(256)(128)(2,1)}, u32[]{:S(2)}) copy-start(bf16[256]{0:T(256)(128)(2,1)} %param.19) | copy-start | bytes 1540
  79.6 31.8 %copy-start.7 = (bf16[4,256]{1,0:T(4,128)(2,1)S(1)}, bf16[4,256]{1,0:T(4,128)(2,1)}, u32[]{:S(2)}) copy-start(bf16[4,256]{1,0:T(4,128)(2,1)} %param.18) | copy-start | bytes 6148
  107.0 26.6 %all-to-all-start.3 = ((bf16[16,128,256]{1,2,0:T(8,128)(2,1)}), bf16[16,128,256]{1,2,0:T(8,128)(2,1)}, u32[]{:S(2)}, u32[]{:S(2)}) async-start(bf16[16,128,256]{1,2,0:T(8,128)(2,1)} %broadcast_in_dim.21), calls=%async_computation.3 | async-start | bytes 2097152 | tf_op jit(solution)/shard_map/all_to_all | solution.py:17
  185.0 2.0 copy-start.2
  186.9 7.5 %copy-start.4 = (f32[16,4096]{1,0:T(8,128)S(1)}, f32[16,4096]{1,0:T(8,128)}, u32[]{:S(2)}) copy-start(f32[16,4096]{1,0:T(8,128)} %param.23) | copy-start | bytes 786436
  189.3 6.0 %copy-start.11 = (s32[8]{0:T(128)S(1)}, s32[8]{0:T(128)}, u32[]{:S(2)}) copy-start(s32[8]{0:T(128)} %param.14) | copy-start | bytes 100
  189.3 21.0 %all-to-all-start.5 = ((bf16[16,128,256]{2,1,0:T(8,128)(2,1)}), bf16[16,128,256]{2,1,0:T(8,128)(2,1)S(1)}, u32[]{:S(2)}, u32[]{:S(2)}) async-start(bf16[16,128,256]{2,1,0:T(8,128)(2,1)} %bitcast.14), calls=%async_computation.5 | async-start | bytes 2097152 | tf_op jit(solution)/shard_map/all_to_all | solution.py:152
  237.9 13.9 %all-to-all-start.6 = ((f32[2,16,16,256]{3,1,0,2:T(8,128)}), f32[2,16,16,256]{3,1,0,2:T(8,128)S(1)}, u32[]{:S(2)}, u32[]{:S(2)}) async-start(f32[2,16,16,256]{3,1,0,2:T(8,128)} %pad_maximum_fusion), calls=%async_computation.6 | async-start | bytes 1048576 | tf_op jit(solution)/shard_map/all_to_all | solution.py:182
  260.9 11.1 %all-to-all-start.7 = ((f32[16,16,256]{2,0,1:T(8,128)}), f32[16,16,256]{2,0,1:T(8,128)S(1)}, u32[]{:S(2)}, u32[]{:S(2)}) async-start(f32[16,16,256]{2,0,1:T(8,128)} %constant_dynamic-update-slice_fusion), calls=%async_computation.7 | async-start | bytes 524288 | tf_op jit(solution)/shard_map/all_to_all | solution.py:189
  272.0 25.4 %all-to-all-start.9 = ((bf16[4,512,256]{2,1,0:T(8,128)(2,1)}), bf16[4,512,256]{2,1,0:T(8,128)(2,1)S(1)}, u32[]{:S(2)}, u32[]{:S(2)}) async-start(bf16[4,512,256]{2,1,0:T(8,128)(2,1)} %bitcast.53), calls=%async_computation.9 | async-start | bytes 2097152 | tf_op jit(solution)/shard_map/all_to_all | solution.py:143
  275.7 74.9 %reduce-scatter.2.cloned.1.call-start = ((), (), s32[]{:S(2)}) async-start(), calls=%async_computation.14 | async-start | bytes 2621440 | tf_op jit(solution)/shard_map/reduce_scatter | solution.py:204
  317.2 9.8 %copy-start.12 = (s32[8]{0:T(128)S(1)}, s32[8]{0:T(128)}, u32[]{:S(2)}) copy-start(s32[8]{0:T(128)} %param.15) | copy-start | bytes 100
  317.2 33.4 %copy-start.1 = (bf16[1,128,2048]{2,1,0:T(8,128)(2,1)S(1)}, bf16[1,128,2048]{2,1,0:T(8,128)(2,1)}, u32[]{:S(2)}) copy-start(bf16[1,128,2048]{2,1,0:T(8,128)(2,1)} %param.13) | copy-start | bytes 1572868
  317.9 14.3 %all-to-all-start.10 = ((f32[8,1,16,256]{3,2,1,0:T(8,128)}), f32[8,1,16,256]{3,2,1,0:T(8,128)S(1)}, u32[]{:S(2)}, u32[]{:S(2)}) async-start(f32[8,1,16,256]{3,2,1,0:T(8,128)} %broadcast_in_dim.25), calls=%async_computation.11 | async-start | bytes 262144 | tf_op jit(solution)/shard_map/all_to_all | solution.py:17
Sparse Core Ops, SparseCore 0:
  30.9 63.2 all-gather.4
  96.9 81.1 all-gather.2
  317.3 33.2 reduce-scatter.1

commit v4 on v3

--- a/solution.py
+++ b/solution.py
@@ -121,22 +121,22 @@
     total_inner = a_log.shape[1]
     model = hidden.shape[2]
     w_in = gather_a2a(in_weight, "req", 1)
-    w_out = gather_a2a(out_weight, "req", 1)
-    xproj_full = gather_a2a(xproj_weight, seq, 0)
-    dt_full = gather_a2a(dt_weight, seq, 1)
-    dt_bias_full = gather_a2a(dt_bias, seq, 0)
-    w_col = lax.all_gather(w_out, "sz", axis=0, tiled=False)
-    w_in, w_col, xproj_full, dt_full, dt_bias_full = lax.optimization_barrier(
-        (w_in, w_col, xproj_full, dt_full, dt_bias_full)
-    )
     tokens = hidden[0].astype(jnp.float32)
     scale = lax.rsqrt(jnp.mean(tokens * tokens, axis=-1, keepdims=True) + 1e-05)
     normed = (tokens * scale * norm_gain.astype(jnp.float32)).astype(jnp.bfloat16)
+    half = model // 2
+    normed_a = lax.all_gather(normed[:, :half], seq, axis=0, tiled=True)
+    normed_b = gather_a2a(normed[:, half:], seq, 0)
+    xproj_w, dt_w, dt_b, w_late, _, _ = lax.optimization_barrier(
+        (xproj_weight, dt_weight, dt_bias, out_weight, normed_a, normed_b)
+    )
+    xproj_full = gather_a2a(xproj_w, seq, 0)
+    dt_full = gather_a2a(dt_w, seq, 1)
+    dt_bias_full = gather_a2a(dt_b, seq, 0)
+    w_col = lax.all_gather(gather_a2a(w_late, "req", 1), "sz", axis=0, tiled=False)
     w_flat = jnp.concatenate((w_in[0], w_in[1]), axis=1)
-    both = jnp.dot(
-        lax.all_gather(normed, seq, axis=0, tiled=True),
-        w_flat,
-        preferred_element_type=jnp.float32,
+    both = jnp.dot(normed_a, w_flat[:half], preferred_element_type=jnp.float32) + jnp.dot(
+        normed_b, w_flat[half:], preferred_element_type=jnp.float32
     )
     xin = both[:, :width]
     zgate = both[:, width:].astype(jnp.bfloat16)

time: 360 us -> 370 us (1.028)
  starting transfers between devices: 36.3 us -> 49.1 us
  waiting for transfers between devices: 139 us -> 130 us
  matrix products: 16.1 us -> 23.1 us
  blocking collectives: 72.7 us -> 66.9 us
    all_to_all x3 -> x6, waiting for transfers between devices: 50.5 us -> 99.8 us  [gather_a2a(): lax.all_to_all(copies, axis, split_axis=0, concat_axis=0, tiled=True)]
    all_gather x2, waiting for transfers between devices: 42.8 us -> 0.01 us  [the longest x1 0.01 us: per_device(): normed_a = lax.all_gather(normed[:, :half], seq, axis=0, tiled=True)]
    all_to_all x3 -> x1, blocking collectives: 59 us -> 31.8 us  [gather_a2a(): lax.all_to_all(copies, axis, split_axis=0, concat_axis=0, tiled=True)]
    all_to_all x0 -> x1, blocking collectives: none -> 22 us  [per_device(): lax.all_to_all(inner, seq, split_axis=0, concat_axis=1, tiled=True)]
    all_to_all x3 -> x6, starting transfers between devices: 19.6 us -> 34.1 us  [gather_a2a(): lax.all_to_all(copies, axis, split_axis=0, concat_axis=0, tiled=True)]
    all_to_all x1 -> x0, waiting for transfers between devices: 13.8 us -> none  [per_device(): lax.all_to_all(inner, seq, split_axis=0, concat_axis=1, tiled=True)]
    dot_general x1 -> x2, matrix products: 6.86 us -> 12.5 us  [the longest x1 6.71 us: per_device(): jnp.dot(normed_a, w_flat[:half], preferred_element_type=jnp.float32)]
    all_to_all x1 -> x0, starting transfers between devices: 5.14 us -> none  [per_device(): lax.all_to_all(inner, seq, split_axis=0, concat_axis=1, tiled=True)]
  transfers between devices with their start and end apart: 10 -> 12, of which waited for: 8 -> 8; matrix products, arithmetic and copies ran while one was open for 6% -> 15% of each run, Pallas kernels for 5% -> 9%
where the time goes in v4:
time: 370 us; the launch traced here: 369 us
  waiting for transfers between devices  130 us (35%)
  blocking collectives  66.9 us (18%)
  starting transfers between devices  49.1 us (13%)
  Pallas kernels  32.5 us (9%)
  local copies, waits for them, and re-layouts  31.3 us (8%)
  matrix products  23.1 us (6%)
  other arithmetic  21.6 us (6%)
  between operations  14.1 us (4%)
    all_to_all x6, waiting for transfers between devices, gather_a2a(): lax.all_to_all(copies, axis, split_axis=0, concat_axis=0, tiled=True)  99.8 us
    all_to_all x6, starting transfers between devices, gather_a2a(): lax.all_to_all(copies, axis, split_axis=0, concat_axis=0, tiled=True)  34.1 us
    pallas_call x2, Pallas kernels, run_scan(): pl.pallas_call(functools.partial(scan_body, emit), grid=(chunks,), in_spe...  32.5 us
    all_to_all x1, blocking collectives, gather_a2a(): lax.all_to_all(copies, axis, split_axis=0, concat_axis=0, tiled=True)  31.8 us
    all_to_all x1, blocking collectives, per_device(): lax.all_to_all(inner, seq, split_axis=0, concat_axis=1, tiled=True)  22 us
    reduce_scatter x1, waiting for transfers between devices, per_device(): lax.psum_scatter(partial.reshape(cols_n * rows, model), 'sy', scatter_dim...  16.8 us
    all_to_all x1, blocking collectives, per_device(): lax.all_to_all(scanned, 'sy', split_axis=2, concat_axis=0, tiled=True)  13.2 us
    unnamed x14, other arithmetic  9.56 us
  transfers between devices with their start and end apart: 12, of which 8 were waited for; matrix products, arithmetic and copies ran while one was open for 15% of the time, Pallas kernels for 9%

profile of v4, /device:TPU:1, one launch (start us, length us, event | category | flops | bytes accessed | tf_op | source)
XLA Modules:
  0.0 368.5 jit_solution(6975682017489827082)
XLA Ops:
  11.4 31.8 %all_to_all.76 = bf16[8,2,256,256]{3,2,1,0:T(8,128)(2,1)S(1)} all-to-all(bf16[8,2,256,256]{3,2,1,0:T(8,128)(2,1)S(1)} %broadcast_in_dim.20), channel_id=1, replica_groups=mesh['req'=8,'sz'=4,'sy'=4] {'req'}, dimensions={0} | all-to-all | bytes 4194304 | tf_op jit(solution)/shard_map/all_to_all | solution.py:17
  43.2 2.6 broadcast_in_dim.21
  45.7 8.0 %all-to-all-start.1 = ((bf16[16,128,1024]{2,1,0:T(8,128)(2,1)}), bf16[16,128,1024]{2,1,0:T(8,128)(2,1)}, u32[]{:S(2)}, u32[]{:S(2)}) async-start(bf16[16,128,1024]{2,1,0:T(8,128)(2,1)} %broadcast_in_dim.21), calls=%async_computation.1 | async-start | bytes 8388608 | tf_op jit(solution)/shard_map/all_to_all | solution.py:17
  54.9 69.8 %all-to-all-done.1 = bf16[16,128,1024]{2,1,0:T(8,128)(2,1)} async-done(((bf16[16,128,1024]{2,1,0:T(8,128)(2,1)}), bf16[16,128,1024]{2,1,0:T(8,128)(2,1)}, u32[]{:S(2)}, u32[]{:S(2)}) %all-to-all-start.1) | async-done | bytes 4194336 | tf_op jit(solution)/shard_map/all_to_all | solution.py:17
  126.5 3.5 all-to-all-start.5
  130.0 6.7 %fusion.20 = f32[2048,512]{1,0:T(8,128)} fusion(bf16[2048,1024]{1,0:T(8,128)(2,1)} %all-gather.3.cloned.1.call-done, bf16[2048,256]{1,0:T(8,128)(2,1)} %bitcast.470, bf16[2048,256]{1,0:T(8,128)(2,1)S(1)} %bitcast.468), kind=kOutput, calls=%fused_computation.32 | convolution fusion | flops 2149580800 | bytes 10485760 | tf_op jit(solution)/shard_map/dot_general | solution.py:138
  137.8 5.3 %all-to-all-start.10 = ((bf16[8,256,256]{2,1,0:T(8,128)(2,1)}), bf16[8,256,256]{2,1,0:T(8,128)(2,1)S(1)}, u32[]{:S(2)}, u32[]{:S(2)}) async-start(bf16[8,256,256]{2,1,0:T(8,128)(2,1)} %broadcast_in_dim.26), calls=%async_computation.10 | async-start | bytes 2097152 | tf_op jit(solution)/shard_map/all_to_all | solution.py:17
  143.2 5.8 %convolution_add_fusion.1 = f32[2048,512]{1,0:T(8,128)S(1)} fusion(f32[2048,512]{1,0:T(8,128)} %fusion.20, bf16[2048,1024]{1,0:T(8,128)(2,1)} %bitcast.6, bf16[2048,256]{1,0:T(8,128)(2,1)S(1)} %bitcast.469, bf16[2048,256]{1,0:T(8,128)(2,1)S(1)} %bitcast.471), kind=kOutput, calls=%fused_computation.5 | convolution fusion | flops 2150629376 | bytes 14680064 | tf_op jit(solution)/shard_map/dot_general | solution.py:138
  149.2 1.8 copy-done.2
  152.3 5.8 %all-to-all-done.10 = bf16[8,256,256]{2,1,0:T(8,128)(2,1)S(1)} async-done(((bf16[8,256,256]{2,1,0:T(8,128)(2,1)}), bf16[8,256,256]{2,1,0:T(8,128)(2,1)S(1)}, u32[]{:S(2)}, u32[]{:S(2)}) %all-to-all-start.10) | async-done | bytes 1048608 | tf_op jit(solution)/shard_map/all_to_all | solution.py:17
  158.2 22.0 %all_to_all.77 = bf16[16,128,256]{2,1,0:T(8,128)(2,1)S(1)} all-to-all(bf16[16,128,256]{2,1,0:T(8,128)(2,1)S(1)} %bitcast.462), channel_id=1, replica_groups=mesh['req'=8,'sz'=4,'sy'=4] {'sz','sy'}, dimensions={0} | all-to-all | bytes 2097152 | tf_op jit(solution)/shard_map/all_to_all | solution.py:152
  181.4 3.7 %all-to-all-start.3 = ((bf16[16,256,160]{1,2,0:T(8,128)(2,1)}), bf16[16,256,160]{1,2,0:T(8,128)(2,1)S(1)}, u32[]{:S(2)}, u32[]{:S(2)}) async-start(bf16[16,256,160]{1,2,0:T(8,128)(2,1)} %broadcast_in_dim.22), calls=%async_computation.3 | async-start | bytes 2621440 | tf_op jit(solution)/shard_map/all_to_all | solution.py:17
  185.2 17.6 %all-to-all-done.3 = bf16[16,256,160]{1,2,0:T(8,128)(2,1)S(1)} async-done(((bf16[16,256,160]{1,2,0:T(8,128)(2,1)}), bf16[16,256,160]{1,2,0:T(8,128)(2,1)S(1)}, u32[]{:S(2)}, u32[]{:S(2)}) %all-to-all-start.3) | async-done | bytes 1310752 | tf_op jit(solution)/shard_map/all_to_all | solution.py:17
  204.1 5.0 %all-to-all-start.4 = ((bf16[16,128,256]{1,2,0:T(8,128)(2,1)}), bf16[16,128,256]{1,2,0:T(8,128)(2,1)}, u32[]{:S(2)}, u32[]{:S(2)}) async-start(bf16[16,128,256]{1,2,0:T(8,128)(2,1)} %broadcast_in_dim.23), calls=%async_computation.4 | async-start | bytes 2097152 | tf_op jit(solution)/shard_map/all_to_all | solution.py:17
  218.9 1.8 convolution_bitcast_fusion
  223.7 2.7 fusion.5
  226.4 1.7 copy.173
  228.8 14.6 %shard_map.140 = (f32[16,32,128]{2,1,0:T(8,128)}, f32[16,32,128]{2,1,0:T(8,128)}) custom-call(f32[2048]{0:T(1024)} %reshape.1416.into_ref, f32[2048]{0:T(1024)} %reshape.1417.outof_ref, f32[128,32,128]{2,1,0:T(8,128)} %bitcast.464, f32[128,32,128]{2,1,0:T(8,128)} %reshape.1428.value_ref, f32[16,32,128]{2,1,0:T(8,128)} %bitcast.472, ...), custom_call_target="tpu_custom_call" | custom-call | flops 50331648 | bytes 4194304 | tf_op jit(solution)/shard_map/pallas_call | solution.py:81
  246.6 5.3 %all-to-all-start.6 = ((f32[2,16,16,256]{3,1,0,2:T(8,128)}), f32[2,16,16,256]{3,1,0,2:T(8,128)S(1)}, u32[]{:S(2)}, u32[]{:S(2)}) async-start(f32[2,16,16,256]{3,1,0,2:T(8,128)} %pad_maximum_fusion.2), calls=%async_computation.6 | async-start | bytes 1048576 | tf_op jit(solution)/shard_map/all_to_all | solution.py:182
  252.5 8.4 %all-to-all-done.6 = f32[2,16,16,256]{3,1,0,2:T(8,128)S(1)} async-done(((f32[2,16,16,256]{3,1,0,2:T(8,128)}), f32[2,16,16,256]{3,1,0,2:T(8,128)S(1)}, u32[]{:S(2)}, u32[]{:S(2)}) %all-to-all-start.6) | async-done | bytes 524320 | tf_op jit(solution)/shard_map/all_to_all | solution.py:182
  270.1 5.9 %all-to-all-start.7 = ((f32[16,16,256]{2,0,1:T(8,128)}), f32[16,16,256]{2,0,1:T(8,128)S(1)}, u32[]{:S(2)}, u32[]{:S(2)}) async-start(f32[16,16,256]{2,0,1:T(8,128)} %constant_dynamic-update-slice_fusion), calls=%async_computation.7 | async-start | bytes 524288 | tf_op jit(solution)/shard_map/all_to_all | solution.py:189
  275.9 2.7 slice.400
  278.6 4.9 %all-to-all-done.7 = f32[16,16,256]{2,0,1:T(8,128)S(1)} async-done(((f32[16,16,256]{2,0,1:T(8,128)}), f32[16,16,256]{2,0,1:T(8,128)S(1)}, u32[]{:S(2)}, u32[]{:S(2)}) %all-to-all-start.7) | async-done | bytes 262176 | tf_op jit(solution)/shard_map/all_to_all | solution.py:189
  283.6 3.5 all-to-all-start.9
  288.0 17.9 %shard_map.141 = f32[128,32,128]{2,1,0:T(8,128)} custom-call(f32[2048]{0:T(1024)} %reshape.1416.into_ref, f32[2048]{0:T(1024)} %reshape.1417.outof_ref, f32[128,32,128]{2,1,0:T(8,128)} %bitcast.465, f32[128,32,128]{2,1,0:T(8,128)} %reshape.1428.value_ref, f32[16,32,128]{2,1,0:T(8,128)} %bitcast.473, f32[16,32,128]{2,1,0:T(8,128)} %reshape.1422.start_ref, ...), custom_call_target="tpu_custom_call" | custom-call | flops 50331648 | bytes 6291456 | tf_op jit(solution)/shard_map/pallas_call | solution.py:81
  305.9 1.8 convert_element_type.103
  308.8 13.2 %all_to_all.78 = bf16[128,4,4,256]{3,0,1,2:T(8,128)(2,1)S(1)} all-to-all(bf16[128,4,4,256]{3,0,1,2:T(8,128)(2,1)S(1)} %copy.136), channel_id=1, replica_groups=mesh['req'=8,'sz'=4,'sy'=4] {'sy'}, dimensions={2} | all-to-all | bytes 2097152 | tf_op jit(solution)/shard_map/all_to_all | solution.py:195
  322.0 6.1 %bitcast_convert_fusion = bf16[4,128,2048]{2,1,0:T(8,128)(2,1)} fusion(bf16[4,256,2048]{2,1,0:T(8,128)(2,1)} %all-gather.5.cloned.1.call-done, bf16[4,4,128,256]{3,2,1,0:T(8,128)(2,1)S(1)} %bitcast.467, bf16[128,4,4,256]{3,0,1,2:T(8,128)(2,1)S(1)} %all_to_all.78), kind=kOutput, calls=%fused_computation.4 | convolution fusion | flops 2152726528 | bytes 8388608 | tf_op jit(solution)/shard_map/ktac,acd->ktd/dot_general | solution.py:201
  328.8 8.6 %all-to-all-start.11 = ((f32[8,1,16,256]{3,2,1,0:T(8,128)}), f32[8,1,16,256]{3,2,1,0:T(8,128)S(1)}, u32[]{:S(2)}, u32[]{:S(2)}) async-start(f32[8,1,16,256]{3,2,1,0:T(8,128)} %broadcast_in_dim.28), calls=%async_computation.12 | async-start | bytes 262144 | tf_op jit(solution)/shard_map/all_to_all | solution.py:17
  337.4 5.3 %all-to-all-done.11 = f32[8,1,16,256]{3,2,1,0:T(8,128)S(1)} async-done(((f32[8,1,16,256]{3,2,1,0:T(8,128)}), f32[8,1,16,256]{3,2,1,0:T(8,128)S(1)}, u32[]{:S(2)}, u32[]{:S(2)}) %all-to-all-start.11) | async-done | bytes 131104 | tf_op jit(solution)/shard_map/all_to_all | solution.py:17
  343.3 16.8 %reduce-scatter.2.cloned.1.call-done = bf16[128,2048]{1,0:T(8,128)(2,1)} async-done(((bf16[512,2048]{1,0:T(8,128)(2,1)}), bf16[128,2048]{1,0:T(8,128)(2,1)}) %reduce-scatter.2.cloned.1.call-update) | async-done | bytes 524304 | tf_op jit(solution)/shard_map/reduce_scatter | solution.py:204
  360.0 2.0 fusion.27
  (101 shorter events, 42.2 us)
Async XLA Ops:
  7.2 4.0 %copy-start.4 = (bf16[2,256,256]{2,1,0:T(8,128)(2,1)S(1)}, bf16[2,256,256]{2,1,0:T(8,128)(2,1)}, u32[]{:S(2)}) copy-start(bf16[2,256,256]{2,1,0:T(8,128)(2,1)} %param.17) | copy-start | bytes 786436
  7.2 117.5 %all-gather.3.cloned.1.call-start = ((), (), s32[]{:S(2)}) async-start(), calls=%async_computation.13 | async-start | bytes 4456448 | tf_op jit(solution)/shard_map/all_gather | solution.py:128
  45.7 8.0 %copy-start.10 = (bf16[256]{0:T(256)(128)(2,1)S(1)}, bf16[256]{0:T(256)(128)(2,1)}, u32[]{:S(2)}) copy-start(bf16[256]{0:T(256)(128)(2,1)} %param.19) | copy-start | bytes 1540
  45.7 8.0 %copy-start.8 = (bf16[4,256]{1,0:T(4,128)(2,1)S(1)}, bf16[4,256]{1,0:T(4,128)(2,1)}, u32[]{:S(2)}) copy-start(bf16[4,256]{1,0:T(4,128)(2,1)} %param.18) | copy-start | bytes 6148
  45.7 79.0 %all-to-all-start.1 = ((bf16[16,128,1024]{2,1,0:T(8,128)(2,1)}), bf16[16,128,1024]{2,1,0:T(8,128)(2,1)}, u32[]{:S(2)}, u32[]{:S(2)}) async-start(bf16[16,128,1024]{2,1,0:T(8,128)(2,1)} %broadcast_in_dim.21), calls=%async_computation.1 | async-start | bytes 8388608 | tf_op jit(solution)/shard_map/all_to_all | solution.py:17
  53.7 71.0 %copy-start.9 = (bf16[256]{0:T(256)(128)(2,1)S(1)}, bf16[256]{0:T(256)(128)(2,1)}, u32[]{:S(2)}) copy-start(bf16[256]{0:T(256)(128)(2,1)} %param.22) | copy-start | bytes 1540
  126.5 10.2 %all-to-all-start.5 = ((bf16[16,2,128]{2,1,0:T(2,128)(2,1)}), bf16[16,2,128]{2,1,0:T(2,128)(2,1)S(1)}, u32[]{:S(2)}, u32[]{:S(2)}) async-start(bf16[16,2,128]{2,1,0:T(2,128)(2,1)} %reshape.1447), calls=%async_computation.5 | async-start | bytes 16384 | tf_op jit(solution)/shard_map/all_to_all | solution.py:17
  130.0 6.7 %copy-start.5 = (bf16[256,256]{1,0:T(8,128)(2,1)S(1)}, bf16[256,256]{1,0:T(8,128)(2,1)}, u32[]{:S(2)}) copy-start(bf16[256,256]{1,0:T(8,128)(2,1)} %param.25) | copy-start | bytes 393220
  136.7 6.4 %copy-start.3 = (bf16[1,8,256,256]{3,2,0,1:T(8,128)(2,1)S(1)}, bf16[1,8,256,256]{3,2,0,1:T(8,128)(2,1)}, u32[]{:S(2)}) copy-start(bf16[1,8,256,256]{3,2,0,1:T(8,128)(2,1)} %get-tuple-element.29) | copy-start | bytes 3145732
  137.8 20.3 %all-to-all-start.10 = ((bf16[8,256,256]{2,1,0:T(8,128)(2,1)}), bf16[8,256,256]{2,1,0:T(8,128)(2,1)S(1)}, u32[]{:S(2)}, u32[]{:S(2)}) async-start(bf16[8,256,256]{2,1,0:T(8,128)(2,1)} %broadcast_in_dim.26), calls=%async_computation.10 | async-start | bytes 2097152 | tf_op jit(solution)/shard_map/all_to_all | solution.py:17
  149.0 2.0 copy-start.2
  151.0 29.2 %copy-start.6 = (bf16[256,160]{0,1:T(8,128)(2,1)S(1)}, bf16[256,160]{0,1:T(8,128)(2,1)}, u32[]{:S(2)}) copy-start(bf16[256,160]{0,1:T(8,128)(2,1)} %param.20) | copy-start | bytes 245764
  180.1 4.9 %copy-start.7 = (bf16[128,256]{1,0:T(8,128)(2,1)S(1)}, bf16[128,256]{1,0:T(8,128)(2,1)}, u32[]{:S(2)}) copy-start(bf16[128,256]{1,0:T(8,128)(2,1)} %param.21) | copy-start | bytes 196612
  181.4 21.4 %all-to-all-start.3 = ((bf16[16,256,160]{1,2,0:T(8,128)(2,1)}), bf16[16,256,160]{1,2,0:T(8,128)(2,1)S(1)}, u32[]{:S(2)}, u32[]{:S(2)}) async-start(bf16[16,256,160]{1,2,0:T(8,128)(2,1)} %broadcast_in_dim.22), calls=%async_computation.3 | async-start | bytes 2621440 | tf_op jit(solution)/shard_map/all_to_all | solution.py:17
  185.2 27.6 %copy-start.11 = (s32[8]{0:T(128)S(1)}, s32[8]{0:T(128)}, u32[]{:S(2)}) copy-start(s32[8]{0:T(128)} %param.14) | copy-start | bytes 100
  202.8 10.0 %copy-start = (bf16[16,256,160]{1,2,0:T(8,128)(2,1)}, bf16[16,256,160]{1,2,0:T(8,128)(2,1)S(1)}, u32[]{:S(2)}) copy-start(bf16[16,256,160]{1,2,0:T(8,128)(2,1)S(1)} %all-to-all-done.3) | copy-start | bytes 3932164
  204.1 19.6 %all-to-all-start.4 = ((bf16[16,128,256]{1,2,0:T(8,128)(2,1)}), bf16[16,128,256]{1,2,0:T(8,128)(2,1)}, u32[]{:S(2)}, u32[]{:S(2)}) async-start(bf16[16,128,256]{1,2,0:T(8,128)(2,1)} %broadcast_in_dim.23), calls=%async_computation.4 | async-start | bytes 2097152 | tf_op jit(solution)/shard_map/all_to_all | solution.py:17
  209.1 112.9 %all-gather.5.cloned.1.call-start = ((), (), s32[]{:S(2)}) async-start(), calls=%async_computation.14 | async-start | bytes 5242880 | tf_op jit(solution)/shard_map/all_gather | solution.py:136
  246.6 14.3 %all-to-all-start.6 = ((f32[2,16,16,256]{3,1,0,2:T(8,128)}), f32[2,16,16,256]{3,1,0,2:T(8,128)S(1)}, u32[]{:S(2)}, u32[]{:S(2)}) async-start(f32[2,16,16,256]{3,1,0,2:T(8,128)} %pad_maximum_fusion.2), calls=%async_computation.6 | async-start | bytes 1048576 | tf_op jit(solution)/shard_map/all_to_all | solution.py:182
  270.1 13.5 %all-to-all-start.7 = ((f32[16,16,256]{2,0,1:T(8,128)}), f32[16,16,256]{2,0,1:T(8,128)S(1)}, u32[]{:S(2)}, u32[]{:S(2)}) async-start(f32[16,16,256]{2,0,1:T(8,128)} %constant_dynamic-update-slice_fusion), calls=%async_computation.7 | async-start | bytes 524288 | tf_op jit(solution)/shard_map/all_to_all | solution.py:189
  283.6 25.2 %all-to-all-start.9 = ((bf16[4,512,256]{2,1,0:T(8,128)(2,1)}), bf16[4,512,256]{2,1,0:T(8,128)(2,1)S(1)}, u32[]{:S(2)}, u32[]{:S(2)}) async-start(bf16[4,512,256]{2,1,0:T(8,128)(2,1)} %bitcast.50), calls=%async_computation.9 | async-start | bytes 2097152 | tf_op jit(solution)/shard_map/all_to_all | solution.py:143
  287.1 73.0 %reduce-scatter.2.cloned.1.call-start = ((), (), s32[]{:S(2)}) async-start(), calls=%async_computation.15 | async-start | bytes 2621440 | tf_op jit(solution)/shard_map/reduce_scatter | solution.py:204
  328.1 9.3 %copy-start.12 = (s32[8]{0:T(128)S(1)}, s32[8]{0:T(128)}, u32[]{:S(2)}) copy-start(s32[8]{0:T(128)} %param.15) | copy-start | bytes 100
  328.1 32.0 %copy-start.1 = (bf16[1,128,2048]{2,1,0:T(8,128)(2,1)S(1)}, bf16[1,128,2048]{2,1,0:T(8,128)(2,1)}, u32[]{:S(2)}) copy-start(bf16[1,128,2048]{2,1,0:T(8,128)(2,1)} %param.13) | copy-start | bytes 1572868
  328.8 13.8 %all-to-all-start.11 = ((f32[8,1,16,256]{3,2,1,0:T(8,128)}), f32[8,1,16,256]{3,2,1,0:T(8,128)S(1)}, u32[]{:S(2)}, u32[]{:S(2)}) async-start(f32[8,1,16,256]{3,2,1,0:T(8,128)} %broadcast_in_dim.28), calls=%async_computation.12 | async-start | bytes 262144 | tf_op jit(solution)/shard_map/all_to_all | solution.py:17
Sparse Core Ops, SparseCore 0:
  11.3 78.1 all-gather.2
  216.2 55.7 all-gather.4
  328.2 31.7 reduce-scatter.1

commit v5 on v4

--- a/solution.py
+++ b/solution.py
@@ -120,24 +120,22 @@
     state_count = a_log.shape[0]
     total_inner = a_log.shape[1]
     model = hidden.shape[2]
-    w_in = gather_a2a(in_weight, "req", 1)
     tokens = hidden[0].astype(jnp.float32)
     scale = lax.rsqrt(jnp.mean(tokens * tokens, axis=-1, keepdims=True) + 1e-05)
     normed = (tokens * scale * norm_gain.astype(jnp.float32)).astype(jnp.bfloat16)
-    half = model // 2
-    normed_a = lax.all_gather(normed[:, :half], seq, axis=0, tiled=True)
-    normed_b = gather_a2a(normed[:, half:], seq, 0)
-    xproj_w, dt_w, dt_b, w_late, _, _ = lax.optimization_barrier(
-        (xproj_weight, dt_weight, dt_bias, out_weight, normed_a, normed_b)
-    )
+    normed_all = lax.all_gather(normed, seq, axis=0, tiled=True)
+    w_in = gather_a2a(in_weight, "req", 1)
+    xproj_w, dt_w, dt_b, _ = lax.optimization_barrier((xproj_weight, dt_weight, dt_bias, normed))
     xproj_full = gather_a2a(xproj_w, seq, 0)
     dt_full = gather_a2a(dt_w, seq, 1)
     dt_bias_full = gather_a2a(dt_b, seq, 0)
+    w_in, xproj_full, dt_full, dt_bias_full = lax.optimization_barrier(
+        (w_in, xproj_full, dt_full, dt_bias_full)
+    )
+    w_late, _ = lax.optimization_barrier((out_weight, normed_all))
     w_col = lax.all_gather(gather_a2a(w_late, "req", 1), "sz", axis=0, tiled=False)
     w_flat = jnp.concatenate((w_in[0], w_in[1]), axis=1)
-    both = jnp.dot(normed_a, w_flat[:half], preferred_element_type=jnp.float32) + jnp.dot(
-        normed_b, w_flat[half:], preferred_element_type=jnp.float32
-    )
+    both = jnp.dot(normed_all, w_flat, preferred_element_type=jnp.float32)
     xin = both[:, :width]
     zgate = both[:, width:].astype(jnp.bfloat16)
     z_grid = lax.all_to_all(

time: 370 us -> 308 us (0.83)
  waiting for transfers between devices: 130 us -> 92.2 us
  blocking collectives: 66.9 us -> 55 us
  starting transfers between devices: 49.1 us -> 40.8 us
  matrix products: 23.1 us -> 16.5 us
    all_to_all x6 -> x4, waiting for transfers between devices: 99.8 us -> 51.8 us  [gather_a2a(): lax.all_to_all(copies, axis, split_axis=0, concat_axis=0, tiled=True)]
    all_to_all x1 -> x0, blocking collectives: 22 us -> none  [per_device(): lax.all_to_all(inner, seq, split_axis=0, concat_axis=1, tiled=True)]
    all_to_all x6 -> x4, starting transfers between devices: 34.1 us -> 22.9 us  [gather_a2a(): lax.all_to_all(copies, axis, split_axis=0, concat_axis=0, tiled=True)]
    all_to_all x0 -> x1, waiting for transfers between devices: none -> 9.3 us  [per_device(): lax.all_to_all(inner, seq, split_axis=0, concat_axis=1, tiled=True)]
    all_to_all x1 -> x2, blocking collectives: 31.8 us -> 40.4 us  [gather_a2a(): lax.all_to_all(copies, axis, split_axis=0, concat_axis=0, tiled=True)]
    dot_general x2 -> x1, matrix products: 12.5 us -> 7.17 us  [per_device(): both = jnp.dot(normed_all, w_flat, preferred_element_type=jnp.float32)]
    broadcast_in_dim x8 -> x7, local copies, waits for them, and re-layouts: 7.55 us -> 5.19 us  [gather_a2a(): copies = jnp.broadcast_to(block[None], (count,) + block.shape)]
  transfers between devices with their start and end apart: 12 -> 11, of which waited for: 8 -> 8; matrix products, arithmetic and copies ran while one was open for 15% -> 19% of each run, Pallas kernels for 9% -> 11%
where the time goes in v5:
time: 308 us; the launch traced here: 306 us
  waiting for transfers between devices  92.2 us (30%)
  blocking collectives  55 us (18%)
  starting transfers between devices  40.8 us (13%)
  local copies, waits for them, and re-layouts  32.7 us (11%)
  Pallas kernels  32.5 us (11%)
  other arithmetic  22.5 us (7%)
  matrix products  16.5 us (5%)
  between operations  14.1 us (5%)
    all_to_all x4, waiting for transfers between devices, gather_a2a(): lax.all_to_all(copies, axis, split_axis=0, concat_axis=0, tiled=True)  51.8 us
    all_to_all x2, blocking collectives, gather_a2a(): lax.all_to_all(copies, axis, split_axis=0, concat_axis=0, tiled=True)  40.4 us
    pallas_call x2, Pallas kernels, run_scan(): pl.pallas_call(functools.partial(scan_body, emit), grid=(chunks,), in_spe...  32.5 us
    all_to_all x4, starting transfers between devices, gather_a2a(): lax.all_to_all(copies, axis, split_axis=0, concat_axis=0, tiled=True)  22.9 us
    reduce_scatter x1, waiting for transfers between devices, per_device(): lax.psum_scatter(partial.reshape(cols_n * rows, model), 'sy', scatter_dim...  17 us
    all_to_all x1, blocking collectives, per_device(): lax.all_to_all(scanned, 'sy', split_axis=2, concat_axis=0, tiled=True)  14.6 us
    all_to_all x1, waiting for transfers between devices, per_device(): lax.all_to_all(inner, seq, split_axis=0, concat_axis=1, tiled=True)  9.3 us
    all_to_all x1, waiting for transfers between devices, per_device(): pair_ch = lax.all_to_all(pair, seq, split_axis=2, concat_axis=2, tiled=True)  9.16 us
  transfers between devices with their start and end apart: 11, of which 8 were waited for; matrix products, arithmetic and copies ran while one was open for 19% of the time, Pallas kernels for 11%

profile of v5, /device:TPU:1, one launch (start us, length us, event | category | flops | bytes accessed | tf_op | source)
XLA Modules:
  0.0 306.2 jit_solution(9026082878669585154)
XLA Ops:
  9.2 2.0 fusion.21
  12.5 14.8 %all_to_all.74 = bf16[16,2,128]{2,1,0:T(2,128)(2,1)S(1)} all-to-all(bf16[16,2,128]{2,1,0:T(2,128)(2,1)S(1)} %reshape.1440), channel_id=1, replica_groups=mesh['req'=8,'sz'=4,'sy'=4] {'sz','sy'}, dimensions={0} | all-to-all | bytes 16384 | tf_op jit(solution)/shard_map/all_to_all | solution.py:17
  27.4 25.6 %all_to_all.75 = bf16[16,256,160]{1,2,0:T(8,128)(2,1)} all-to-all(bf16[16,256,160]{1,2,0:T(8,128)(2,1)S(1)} %broadcast_in_dim.19), channel_id=1, replica_groups=mesh['req'=8,'sz'=4,'sy'=4] {'sz','sy'}, dimensions={0} | all-to-all | bytes 2621440 | tf_op jit(solution)/shard_map/all_to_all | solution.py:17
  54.6 5.8 %all-to-all-start = ((bf16[8,2,256,256]{3,2,1,0:T(8,128)(2,1)}), bf16[8,2,256,256]{3,2,1,0:T(8,128)(2,1)S(1)}, u32[]{:S(2)}, u32[]{:S(2)}) async-start(bf16[8,2,256,256]{3,2,1,0:T(8,128)(2,1)} %broadcast_in_dim.18), calls=%async_computation | async-start | bytes 4194304 | tf_op jit(solution)/shard_map/all_to_all | solution.py:17
  60.6 26.1 %all-to-all-done = bf16[8,2,256,256]{3,2,1,0:T(8,128)(2,1)S(1)} async-done(((bf16[8,2,256,256]{3,2,1,0:T(8,128)(2,1)}), bf16[8,2,256,256]{3,2,1,0:T(8,128)(2,1)S(1)}, u32[]{:S(2)}, u32[]{:S(2)}) %all-to-all-start) | async-done | bytes 2097184 | tf_op jit(solution)/shard_map/all_to_all | solution.py:17
  87.9 4.4 %all-to-all-start.2 = ((bf16[16,128,256]{1,2,0:T(8,128)(2,1)}), bf16[16,128,256]{1,2,0:T(8,128)(2,1)}, u32[]{:S(2)}, u32[]{:S(2)}) async-start(bf16[16,128,256]{1,2,0:T(8,128)(2,1)} %broadcast_in_dim.20), calls=%async_computation.2 | async-start | bytes 2097152 | tf_op jit(solution)/shard_map/all_to_all | solution.py:17
  95.4 17.1 %all-to-all-done.2 = bf16[16,128,256]{1,2,0:T(8,128)(2,1)} async-done(((bf16[16,128,256]{1,2,0:T(8,128)(2,1)}), bf16[16,128,256]{1,2,0:T(8,128)(2,1)}, u32[]{:S(2)}, u32[]{:S(2)}) %all-to-all-start.2) | async-done | bytes 1048608 | tf_op jit(solution)/shard_map/all_to_all | solution.py:17
  112.5 2.7 slice_bitcast_fusion.1
  116.2 5.6 %all-to-all-start.9 = ((bf16[8,256,256]{2,1,0:T(8,128)(2,1)}), bf16[8,256,256]{2,1,0:T(8,128)(2,1)S(1)}, u32[]{:S(2)}, u32[]{:S(2)}) async-start(bf16[8,256,256]{2,1,0:T(8,128)(2,1)} %broadcast_in_dim.23), calls=%async_computation.9 | async-start | bytes 2097152 | tf_op jit(solution)/shard_map/all_to_all | solution.py:17
  121.8 7.2 %fusion.6 = f32[2048,512]{1,0:T(8,128)S(1)} fusion(bf16[2048,2048]{1,0:T(8,128)(2,1)} %all-gather.3.cloned.1.call-done, bf16[2048,256]{1,0:T(8,128)(2,1)} %get-tuple-element.37, bf16[2048,256]{1,0:T(8,128)(2,1)S(1)} %get-tuple-element.36), kind=kOutput, calls=%fused_computation.8 | convolution fusion | flops 4299161600 | bytes 14680064 | tf_op jit(solution)/shard_map/dot_general | solution.py:138
  131.0 2.4 multiply_convert_fusion
  133.4 3.4 %all-to-all-done.9 = bf16[8,256,256]{2,1,0:T(8,128)(2,1)S(1)} async-done(((bf16[8,256,256]{2,1,0:T(8,128)(2,1)}), bf16[8,256,256]{2,1,0:T(8,128)(2,1)S(1)}, u32[]{:S(2)}, u32[]{:S(2)}) %all-to-all-start.9) | async-done | bytes 1048608 | tf_op jit(solution)/shard_map/all_to_all | solution.py:17
  136.8 3.7 %all-to-all-start.4 = ((bf16[16,128,256]{2,1,0:T(8,128)(2,1)}), bf16[16,128,256]{2,1,0:T(8,128)(2,1)S(1)}, u32[]{:S(2)}, u32[]{:S(2)}) async-start(bf16[16,128,256]{2,1,0:T(8,128)(2,1)} %bitcast.12), calls=%async_computation.4 | async-start | bytes 2097152 | tf_op jit(solution)/shard_map/all_to_all | solution.py:150
  144.9 2.3 copy.145
  147.1 9.3 %all-to-all-done.4 = bf16[16,128,256]{2,1,0:T(8,128)(2,1)S(1)} async-done(((bf16[16,128,256]{2,1,0:T(8,128)(2,1)}), bf16[16,128,256]{2,1,0:T(8,128)(2,1)S(1)}, u32[]{:S(2)}, u32[]{:S(2)}) %all-to-all-start.4) | async-done | bytes 1048608 | tf_op jit(solution)/shard_map/all_to_all | solution.py:150
  157.6 2.8 fusion.5
  163.7 1.8 copy.148.value_ref
  166.2 14.5 %shard_map.140 = (f32[16,32,128]{2,1,0:T(8,128)}, f32[16,32,128]{2,1,0:T(8,128)}) custom-call(f32[2048]{0:T(1024)} %reshape.1411.into_ref, f32[2048]{0:T(1024)} %reshape.1412.outof_ref, f32[128,32,128]{2,1,0:T(8,128)} %bitcast.473, f32[128,32,128]{2,1,0:T(8,128)} %copy.148.value_ref, f32[16,32,128]{2,1,0:T(8,128)} %bitcast.477, ...), custom_call_target="tpu_custom_call" | custom-call | flops 50331648 | bytes 4194304 | tf_op jit(solution)/shard_map/pallas_call | solution.py:81
  184.0 4.2 %all-to-all-start.5 = ((f32[2,16,16,256]{3,1,0,2:T(8,128)}), f32[2,16,16,256]{3,1,0,2:T(8,128)S(1)}, u32[]{:S(2)}, u32[]{:S(2)}) async-start(f32[2,16,16,256]{3,1,0,2:T(8,128)} %pad_maximum_fusion), calls=%async_computation.5 | async-start | bytes 1048576 | tf_op jit(solution)/shard_map/all_to_all | solution.py:180
  188.8 9.2 %all-to-all-done.5 = f32[2,16,16,256]{3,1,0,2:T(8,128)S(1)} async-done(((f32[2,16,16,256]{3,1,0,2:T(8,128)}), f32[2,16,16,256]{3,1,0,2:T(8,128)S(1)}, u32[]{:S(2)}, u32[]{:S(2)}) %all-to-all-start.5) | async-done | bytes 524320 | tf_op jit(solution)/shard_map/all_to_all | solution.py:180
  207.1 6.2 %all-to-all-start.6 = ((f32[16,16,256]{2,0,1:T(8,128)}), f32[16,16,256]{2,0,1:T(8,128)S(1)}, u32[]{:S(2)}, u32[]{:S(2)}) async-start(f32[16,16,256]{2,0,1:T(8,128)} %constant_dynamic-update-slice_fusion), calls=%async_computation.6 | async-start | bytes 524288 | tf_op jit(solution)/shard_map/all_to_all | solution.py:187
  213.2 2.7 slice.370
  215.9 4.9 %all-to-all-done.6 = f32[16,16,256]{2,0,1:T(8,128)S(1)} async-done(((f32[16,16,256]{2,0,1:T(8,128)}), f32[16,16,256]{2,0,1:T(8,128)S(1)}, u32[]{:S(2)}, u32[]{:S(2)}) %all-to-all-start.6) | async-done | bytes 262176 | tf_op jit(solution)/shard_map/all_to_all | solution.py:187
  220.8 3.5 %all-to-all-start.8 = ((bf16[4,512,256]{2,1,0:T(8,128)(2,1)}), bf16[4,512,256]{2,1,0:T(8,128)(2,1)S(1)}, u32[]{:S(2)}, u32[]{:S(2)}) async-start(bf16[4,512,256]{2,1,0:T(8,128)(2,1)} %bitcast.51), calls=%async_computation.8 | async-start | bytes 2097152 | tf_op jit(solution)/shard_map/all_to_all | solution.py:141
  225.4 17.9 %shard_map.141 = f32[128,32,128]{2,1,0:T(8,128)} custom-call(f32[2048]{0:T(1024)} %reshape.1411.into_ref, f32[2048]{0:T(1024)} %reshape.1412.outof_ref, f32[128,32,128]{2,1,0:T(8,128)} %bitcast.474, f32[128,32,128]{2,1,0:T(8,128)} %copy.148.value_ref, f32[16,32,128]{2,1,0:T(8,128)} %bitcast.478, f32[16,32,128]{2,1,0:T(8,128)} %reshape.1416.start_ref, ...), custom_call_target="tpu_custom_call" | custom-call | flops 50331648 | bytes 6291456 | tf_op jit(solution)/shard_map/pallas_call | solution.py:81
  243.4 1.8 convert_element_type.95
  246.2 14.6 %all_to_all.76 = bf16[128,4,4,256]{3,0,1,2:T(8,128)(2,1)S(1)} all-to-all(bf16[128,4,4,256]{3,0,1,2:T(8,128)(2,1)S(1)} %copy.142), channel_id=1, replica_groups=mesh['req'=8,'sz'=4,'sy'=4] {'sy'}, dimensions={2} | all-to-all | bytes 2097152 | tf_op jit(solution)/shard_map/all_to_all | solution.py:193
  260.8 6.1 %bitcast_convert_fusion = bf16[4,128,2048]{2,1,0:T(8,128)(2,1)} fusion(bf16[4,256,2048]{2,1,0:T(8,128)(2,1)} %all-gather.5.cloned.1.call-done, bf16[4,4,128,256]{3,2,1,0:T(8,128)(2,1)S(1)} %bitcast.476, bf16[128,4,4,256]{3,0,1,2:T(8,128)(2,1)S(1)} %all_to_all.76), kind=kOutput, calls=%fused_computation.4 | convolution fusion | flops 2152726528 | bytes 8388608 | tf_op jit(solution)/shard_map/ktac,acd->ktd/dot_general | solution.py:199
  267.6 7.1 %all-to-all-start.10 = ((f32[8,1,16,256]{3,2,1,0:T(8,128)}), f32[8,1,16,256]{3,2,1,0:T(8,128)S(1)}, u32[]{:S(2)}, u32[]{:S(2)}) async-start(f32[8,1,16,256]{3,2,1,0:T(8,128)} %broadcast_in_dim.25), calls=%async_computation.11 | async-start | bytes 262144 | tf_op jit(solution)/shard_map/all_to_all | solution.py:17
  274.8 5.3 %all-to-all-done.10 = f32[8,1,16,256]{3,2,1,0:T(8,128)S(1)} async-done(((f32[8,1,16,256]{3,2,1,0:T(8,128)}), f32[8,1,16,256]{3,2,1,0:T(8,128)S(1)}, u32[]{:S(2)}, u32[]{:S(2)}) %all-to-all-start.10) | async-done | bytes 131104 | tf_op jit(solution)/shard_map/all_to_all | solution.py:17
  280.7 17.0 %reduce-scatter.2.cloned.1.call-done = bf16[128,2048]{1,0:T(8,128)(2,1)} async-done(((bf16[512,2048]{1,0:T(8,128)(2,1)}), bf16[128,2048]{1,0:T(8,128)(2,1)}) %reduce-scatter.2.cloned.1.call-update) | async-done | bytes 524304 | tf_op jit(solution)/shard_map/reduce_scatter | solution.py:202
  297.7 2.0 fusion.26
  (95 shorter events, 38.5 us)
Async XLA Ops:
  7.2 20.1 %copy-start.4 = (bf16[256,160]{0,1:T(8,128)(2,1)S(1)}, bf16[256,160]{0,1:T(8,128)(2,1)}, u32[]{:S(2)}) copy-start(bf16[256,160]{0,1:T(8,128)(2,1)} %param.20) | copy-start | bytes 245764
  7.2 4.0 %copy-start.7 = (bf16[256]{0:T(256)(128)(2,1)S(1)}, bf16[256]{0:T(256)(128)(2,1)}, u32[]{:S(2)}) copy-start(bf16[256]{0:T(256)(128)(2,1)} %param.22) | copy-start | bytes 1540
  7.2 108.0 %all-gather.3.cloned.1.call-start = ((), (), s32[]{:S(2)}) async-start(), calls=%async_computation.12 | async-start | bytes 8912896 | tf_op jit(solution)/shard_map/all_gather | solution.py:126
  11.2 41.8 %copy-start.2 = (bf16[2,256,256]{2,1,0:T(8,128)(2,1)S(1)}, bf16[2,256,256]{2,1,0:T(8,128)(2,1)}, u32[]{:S(2)}) copy-start(bf16[2,256,256]{2,1,0:T(8,128)(2,1)} %param.17) | copy-start | bytes 786436
  54.6 5.9 %copy-start.5 = (bf16[128,256]{1,0:T(8,128)(2,1)S(1)}, bf16[128,256]{1,0:T(8,128)(2,1)}, u32[]{:S(2)}) copy-start(bf16[128,256]{1,0:T(8,128)(2,1)} %param.21) | copy-start | bytes 196612
  54.6 32.0 %all-to-all-start = ((bf16[8,2,256,256]{3,2,1,0:T(8,128)(2,1)}), bf16[8,2,256,256]{3,2,1,0:T(8,128)(2,1)S(1)}, u32[]{:S(2)}, u32[]{:S(2)}) async-start(bf16[8,2,256,256]{3,2,1,0:T(8,128)(2,1)} %broadcast_in_dim.18), calls=%async_computation | async-start | bytes 4194304 | tf_op jit(solution)/shard_map/all_to_all | solution.py:17
  60.5 31.8 %copy-start.8 = (bf16[256]{0:T(256)(128)(2,1)S(1)}, bf16[256]{0:T(256)(128)(2,1)}, u32[]{:S(2)}) copy-start(bf16[256]{0:T(256)(128)(2,1)} %param.19) | copy-start | bytes 1540
  60.5 31.8 %copy-start.6 = (bf16[4,256]{1,0:T(4,128)(2,1)S(1)}, bf16[4,256]{1,0:T(4,128)(2,1)}, u32[]{:S(2)}) copy-start(bf16[4,256]{1,0:T(4,128)(2,1)} %param.18) | copy-start | bytes 6148
  87.9 24.6 %all-to-all-start.2 = ((bf16[16,128,256]{1,2,0:T(8,128)(2,1)}), bf16[16,128,256]{1,2,0:T(8,128)(2,1)}, u32[]{:S(2)}, u32[]{:S(2)}) async-start(bf16[16,128,256]{1,2,0:T(8,128)(2,1)} %broadcast_in_dim.20), calls=%async_computation.2 | async-start | bytes 2097152 | tf_op jit(solution)/shard_map/all_to_all | solution.py:17
  112.5 2.7 copy-start.3
  116.2 20.5 %all-to-all-start.9 = ((bf16[8,256,256]{2,1,0:T(8,128)(2,1)}), bf16[8,256,256]{2,1,0:T(8,128)(2,1)S(1)}, u32[]{:S(2)}, u32[]{:S(2)}) async-start(bf16[8,256,256]{2,1,0:T(8,128)(2,1)} %broadcast_in_dim.23), calls=%async_computation.9 | async-start | bytes 2097152 | tf_op jit(solution)/shard_map/all_to_all | solution.py:17
  129.0 2.0 copy-start.1
  133.4 8.9 %copy-start.9 = (s32[8]{0:T(128)S(1)}, s32[8]{0:T(128)}, u32[]{:S(2)}) copy-start(s32[8]{0:T(128)} %param.14) | copy-start | bytes 100
  136.8 19.7 %all-to-all-start.4 = ((bf16[16,128,256]{2,1,0:T(8,128)(2,1)}), bf16[16,128,256]{2,1,0:T(8,128)(2,1)S(1)}, u32[]{:S(2)}, u32[]{:S(2)}) async-start(bf16[16,128,256]{2,1,0:T(8,128)(2,1)} %bitcast.12), calls=%async_computation.4 | async-start | bytes 2097152 | tf_op jit(solution)/shard_map/all_to_all | solution.py:150
  140.4 120.4 %all-gather.5.cloned.1.call-start = ((), (), s32[]{:S(2)}) async-start(), calls=%async_computation.13 | async-start | bytes 5242880 | tf_op jit(solution)/shard_map/all_gather | solution.py:136
  184.0 14.0 %all-to-all-start.5 = ((f32[2,16,16,256]{3,1,0,2:T(8,128)}), f32[2,16,16,256]{3,1,0,2:T(8,128)S(1)}, u32[]{:S(2)}, u32[]{:S(2)}) async-start(f32[2,16,16,256]{3,1,0,2:T(8,128)} %pad_maximum_fusion), calls=%async_computation.5 | async-start | bytes 1048576 | tf_op jit(solution)/shard_map/all_to_all | solution.py:180
  207.1 13.7 %all-to-all-start.6 = ((f32[16,16,256]{2,0,1:T(8,128)}), f32[16,16,256]{2,0,1:T(8,128)S(1)}, u32[]{:S(2)}, u32[]{:S(2)}) async-start(f32[16,16,256]{2,0,1:T(8,128)} %constant_dynamic-update-slice_fusion), calls=%async_computation.6 | async-start | bytes 524288 | tf_op jit(solution)/shard_map/all_to_all | solution.py:187
  220.8 25.4 %all-to-all-start.8 = ((bf16[4,512,256]{2,1,0:T(8,128)(2,1)}), bf16[4,512,256]{2,1,0:T(8,128)(2,1)S(1)}, u32[]{:S(2)}, u32[]{:S(2)}) async-start(bf16[4,512,256]{2,1,0:T(8,128)(2,1)} %bitcast.51), calls=%async_computation.8 | async-start | bytes 2097152 | tf_op jit(solution)/shard_map/all_to_all | solution.py:141
  224.3 73.4 %reduce-scatter.2.cloned.1.call-start = ((), (), s32[]{:S(2)}) async-start(), calls=%async_computation.14 | async-start | bytes 2621440 | tf_op jit(solution)/shard_map/reduce_scatter | solution.py:202
  266.9 7.8 %copy-start.10 = (s32[8]{0:T(128)S(1)}, s32[8]{0:T(128)}, u32[]{:S(2)}) copy-start(s32[8]{0:T(128)} %param.15) | copy-start | bytes 100
  266.9 30.8 %copy-start = (bf16[1,128,2048]{2,1,0:T(8,128)(2,1)S(1)}, bf16[1,128,2048]{2,1,0:T(8,128)(2,1)}, u32[]{:S(2)}) copy-start(bf16[1,128,2048]{2,1,0:T(8,128)(2,1)} %param.13) | copy-start | bytes 1572868
  267.6 12.4 %all-to-all-start.10 = ((f32[8,1,16,256]{3,2,1,0:T(8,128)}), f32[8,1,16,256]{3,2,1,0:T(8,128)S(1)}, u32[]{:S(2)}, u32[]{:S(2)}) async-start(f32[8,1,16,256]{3,2,1,0:T(8,128)} %broadcast_in_dim.25), calls=%async_computation.11 | async-start | bytes 262144 | tf_op jit(solution)/shard_map/all_to_all | solution.py:17
Sparse Core Ops, SparseCore 0:
  11.3 86.9 all-gather.2
  147.3 53.7 all-gather.4
  267.1 30.6 reduce-scatter.1

commit v6 on v5

--- a/solution.py
+++ b/solution.py
@@ -56,11 +56,11 @@
 
     held0 = tuple(start_ref[n] for n in range(states))
     acc0 = jnp.zeros((SUB, LANES), jnp.float32)
-    held, acc = lax.fori_loop(0, steps, step, (held0, acc0))
+    held, acc = lax.fori_loop(0, steps, step, (held0, acc0), unroll=2)
     if not emit:
         for n in range(states):
             end_ref[n] = held[n]
-            total_ref[n] = jnp.exp(acc * decay[n])
+        total_ref[0] = acc
 
 
 def run_scan(emit, into, outof, rate, value, decay, start, skip):
@@ -75,8 +75,11 @@
         out_shape = jax.ShapeDtypeStruct((steps, rows, lanes), jnp.float32)
         out_specs = seq_spec
     else:
-        out_shape = (jax.ShapeDtypeStruct((states, rows, lanes), jnp.float32),) * 2
-        out_specs = (st_spec, st_spec)
+        out_shape = (
+            jax.ShapeDtypeStruct((states, rows, lanes), jnp.float32),
+            jax.ShapeDtypeStruct((1, rows, lanes), jnp.float32),
+        )
+        out_specs = (st_spec, pl.BlockSpec((1, SUB, lanes), lambda i: (0, i, 0)))
     flops = steps * rows * lanes * states * 6
     return pl.pallas_call(
         functools.partial(scan_body, emit),
@@ -174,15 +177,17 @@
         False, into, outof, rate_l, value_l, decay_l,
         jnp.zeros((state_count, groups, lanes), jnp.float32), skip_l,
     )
-    pair = jnp.stack(
-        (total_l.reshape(state_count, total_inner), end_l.reshape(state_count, total_inner))
-    ).reshape(2, state_count, seq_count, width)
-    pair_ch = lax.all_to_all(pair, seq, split_axis=2, concat_axis=2, tiled=True)
+    pair = jnp.concatenate(
+        (end_l.reshape(state_count, total_inner), total_l.reshape(1, total_inner))
+    ).reshape(state_count + 1, seq_count, width)
+    pair_ch = lax.all_to_all(pair, seq, split_axis=1, concat_axis=1, tiled=True)
+    decay_ch = lax.dynamic_slice_in_dim(decay, seq_index * width, width, 1)
+    falls = jnp.exp(pair_ch[state_count][None] * decay_ch[:, None, :])
     carry = jnp.zeros((state_count, width), jnp.float32)
     carries = []
     for block in range(seq_count):
         carries.append(carry)
-        carry = pair_ch[0, :, block] * carry + pair_ch[1, :, block]
+        carry = falls[:, block] * carry + pair_ch[:state_count, block]
     carry_ch = jnp.stack(carries, axis=1)
     carry_in = lax.all_to_all(carry_ch, seq, split_axis=1, concat_axis=1, tiled=True)
     out_l = run_scan(

time: 308 us -> 300 us (0.974)
  Pallas kernels: 32.5 us -> 27.1 us
    pallas_call x2, Pallas kernels: 32.5 us -> 27.1 us  [run_scan(): pl.pallas_call(functools.partial(scan_body, emit), grid=(chunks,), in_spe...]
    unnamed x14 -> x10, other arithmetic: 8.88 us -> 6.06 us
    unnamed x29 -> x33, local copies, waits for them, and re-layouts: 5.54 us -> 7.27 us
  transfers between devices with their start and end apart: 11 -> 11, of which waited for: 8 -> 8; matrix products, arithmetic and copies ran while one was open for 19% -> 19% of each run, Pallas kernels for 11% -> 9%
where the time goes in v6:
time: 300 us; the launch traced here: 299 us
  waiting for transfers between devices  89.8 us (30%)
  blocking collectives  55.7 us (19%)
  starting transfers between devices  39.5 us (13%)
  local copies, waits for them, and re-layouts  33.9 us (11%)
  Pallas kernels  27.1 us (9%)
  other arithmetic  22.1 us (7%)
  matrix products  16.6 us (6%)
  between operations  14.1 us (5%)
    all_to_all x4, waiting for transfers between devices, gather_a2a(): lax.all_to_all(copies, axis, split_axis=0, concat_axis=0, tiled=True)  52 us
    all_to_all x2, blocking collectives, gather_a2a(): lax.all_to_all(copies, axis, split_axis=0, concat_axis=0, tiled=True)  40.4 us
    pallas_call x2, Pallas kernels, run_scan(): pl.pallas_call(functools.partial(scan_body, emit), grid=(chunks,), in_spe...  27.1 us
    all_to_all x4, starting transfers between devices, gather_a2a(): lax.all_to_all(copies, axis, split_axis=0, concat_axis=0, tiled=True)  22.2 us
    reduce_scatter x1, waiting for transfers between devices, per_device(): lax.psum_scatter(partial.reshape(cols_n * rows, model), 'sy', scatter_dim...  17 us
    all_to_all x1, blocking collectives, per_device(): lax.all_to_all(scanned, 'sy', split_axis=2, concat_axis=0, tiled=True)  15.3 us
    all_to_all x1, waiting for transfers between devices, per_device(): lax.all_to_all(inner, seq, split_axis=0, concat_axis=1, tiled=True)  8.59 us
    unnamed x33, local copies, waits for them, and re-layouts  7.27 us
  transfers between devices with their start and end apart: 11, of which 8 were waited for; matrix products, arithmetic and copies ran while one was open for 19% of the time, Pallas kernels for 9%

profile of v6, /device:TPU:1, one launch (start us, length us, event | category | flops | bytes accessed | tf_op | source)
XLA Modules:
  0.0 298.7 jit_solution(5577399602720565602)
XLA Ops:
  9.2 2.0 fusion.21
  12.5 14.8 %all_to_all.74 = bf16[16,2,128]{2,1,0:T(2,128)(2,1)S(1)} all-to-all(bf16[16,2,128]{2,1,0:T(2,128)(2,1)S(1)} %reshape.300), channel_id=1, replica_groups=mesh['req'=8,'sz'=4,'sy'=4] {'sz','sy'}, dimensions={0} | all-to-all | bytes 16384 | tf_op jit(solution)/shard_map/all_to_all | solution.py:17
  27.4 25.6 %all_to_all.75 = bf16[16,256,160]{1,2,0:T(8,128)(2,1)} all-to-all(bf16[16,256,160]{1,2,0:T(8,128)(2,1)S(1)} %broadcast_in_dim.19), channel_id=1, replica_groups=mesh['req'=8,'sz'=4,'sy'=4] {'sz','sy'}, dimensions={0} | all-to-all | bytes 2621440 | tf_op jit(solution)/shard_map/all_to_all | solution.py:17
  54.5 5.9 %all-to-all-start = ((bf16[8,2,256,256]{3,2,1,0:T(8,128)(2,1)}), bf16[8,2,256,256]{3,2,1,0:T(8,128)(2,1)S(1)}, u32[]{:S(2)}, u32[]{:S(2)}) async-start(bf16[8,2,256,256]{3,2,1,0:T(8,128)(2,1)} %broadcast_in_dim.18), calls=%async_computation | async-start | bytes 4194304 | tf_op jit(solution)/shard_map/all_to_all | solution.py:17
  60.5 26.1 %all-to-all-done = bf16[8,2,256,256]{3,2,1,0:T(8,128)(2,1)S(1)} async-done(((bf16[8,2,256,256]{3,2,1,0:T(8,128)(2,1)}), bf16[8,2,256,256]{3,2,1,0:T(8,128)(2,1)S(1)}, u32[]{:S(2)}, u32[]{:S(2)}) %all-to-all-start) | async-done | bytes 2097184 | tf_op jit(solution)/shard_map/all_to_all | solution.py:17
  87.8 4.4 %all-to-all-start.2 = ((bf16[16,128,256]{1,2,0:T(8,128)(2,1)}), bf16[16,128,256]{1,2,0:T(8,128)(2,1)}, u32[]{:S(2)}, u32[]{:S(2)}) async-start(bf16[16,128,256]{1,2,0:T(8,128)(2,1)} %broadcast_in_dim.20), calls=%async_computation.2 | async-start | bytes 2097152 | tf_op jit(solution)/shard_map/all_to_all | solution.py:17
  95.3 17.2 %all-to-all-done.2 = bf16[16,128,256]{1,2,0:T(8,128)(2,1)} async-done(((bf16[16,128,256]{1,2,0:T(8,128)(2,1)}), bf16[16,128,256]{1,2,0:T(8,128)(2,1)}, u32[]{:S(2)}, u32[]{:S(2)}) %all-to-all-start.2) | async-done | bytes 1048608 | tf_op jit(solution)/shard_map/all_to_all | solution.py:17
  112.5 2.7 slice_bitcast_fusion.1
  116.3 5.5 %all-to-all-start.9 = ((bf16[8,256,256]{2,1,0:T(8,128)(2,1)}), bf16[8,256,256]{2,1,0:T(8,128)(2,1)S(1)}, u32[]{:S(2)}, u32[]{:S(2)}) async-start(bf16[8,256,256]{2,1,0:T(8,128)(2,1)} %broadcast_in_dim.23), calls=%async_computation.9 | async-start | bytes 2097152 | tf_op jit(solution)/shard_map/all_to_all | solution.py:17
  121.8 7.2 %fusion.6 = f32[2048,512]{1,0:T(8,128)S(1)} fusion(bf16[2048,2048]{1,0:T(8,128)(2,1)} %all-gather.3.cloned.1.call-done, bf16[2048,256]{1,0:T(8,128)(2,1)} %get-tuple-element.34, bf16[2048,256]{1,0:T(8,128)(2,1)S(1)} %get-tuple-element.33), kind=kOutput, calls=%fused_computation.8 | convolution fusion | flops 4299161600 | bytes 14680064 | tf_op jit(solution)/shard_map/dot_general | solution.py:141
  131.0 2.3 multiply_convert_fusion
  133.3 3.5 %all-to-all-done.9 = bf16[8,256,256]{2,1,0:T(8,128)(2,1)S(1)} async-done(((bf16[8,256,256]{2,1,0:T(8,128)(2,1)}), bf16[8,256,256]{2,1,0:T(8,128)(2,1)S(1)}, u32[]{:S(2)}, u32[]{:S(2)}) %all-to-all-start.9) | async-done | bytes 1048608 | tf_op jit(solution)/shard_map/all_to_all | solution.py:17
  136.8 3.7 %all-to-all-start.4 = ((bf16[16,128,256]{2,1,0:T(8,128)(2,1)}), bf16[16,128,256]{2,1,0:T(8,128)(2,1)S(1)}, u32[]{:S(2)}, u32[]{:S(2)}) async-start(bf16[16,128,256]{2,1,0:T(8,128)(2,1)} %bitcast.12), calls=%async_computation.4 | async-start | bytes 2097152 | tf_op jit(solution)/shard_map/all_to_all | solution.py:153
  145.5 2.3 copy.86
  147.8 8.6 %all-to-all-done.4 = bf16[16,128,256]{2,1,0:T(8,128)(2,1)S(1)} async-done(((bf16[16,128,256]{2,1,0:T(8,128)(2,1)}), bf16[16,128,256]{2,1,0:T(8,128)(2,1)S(1)}, u32[]{:S(2)}, u32[]{:S(2)}) %all-to-all-start.4) | async-done | bytes 1048608 | tf_op jit(solution)/shard_map/all_to_all | solution.py:153
  157.6 2.8 fusion.5
  163.7 1.8 copy.88.value_ref
  166.2 11.7 %shard_map.140 = (f32[16,32,128]{2,1,0:T(8,128)}, f32[1,32,128]{2,1,0:T(8,128)}) custom-call(f32[2048]{0:T(1024)} %reshape.271.into_ref, f32[2048]{0:T(1024)} %reshape.272.outof_ref, f32[128,32,128]{2,1,0:T(8,128)} %bitcast.173, f32[128,32,128]{2,1,0:T(8,128)} %copy.88.value_ref, f32[16,32,128]{2,1,0:T(8,128)} %bitcast.177, ...), custom_call_target="tpu_custom_call" | custom-call | flops 50331648 | bytes 4194304 | tf_op jit(solution)/shard_map/pallas_call | solution.py:84
  180.6 4.0 %all-to-all-start.5 = ((f32[17,16,256]{2,0,1:T(8,128)}), f32[17,16,256]{2,0,1:T(8,128)S(1)}, u32[]{:S(2)}, u32[]{:S(2)}) async-start(f32[17,16,256]{2,0,1:T(8,128)} %pad_maximum_fusion), calls=%async_computation.5 | async-start | bytes 786432 | tf_op jit(solution)/shard_map/all_to_all | solution.py:183
  185.9 7.1 %all-to-all-done.5 = f32[17,16,256]{2,0,1:T(8,128)S(1)} async-done(((f32[17,16,256]{2,0,1:T(8,128)}), f32[17,16,256]{2,0,1:T(8,128)S(1)}, u32[]{:S(2)}, u32[]{:S(2)}) %all-to-all-start.5) | async-done | bytes 278560 | tf_op jit(solution)/shard_map/all_to_all | solution.py:183
  202.3 5.8 %all-to-all-start.6 = ((f32[16,16,256]{2,0,1:T(8,128)}), f32[16,16,256]{2,0,1:T(8,128)S(1)}, u32[]{:S(2)}, u32[]{:S(2)}) async-start(f32[16,16,256]{2,0,1:T(8,128)} %constant_dynamic-update-slice_fusion), calls=%async_computation.6 | async-start | bytes 524288 | tf_op jit(solution)/shard_map/all_to_all | solution.py:192
  208.1 2.7 slice.371
  210.8 5.0 %all-to-all-done.6 = f32[16,16,256]{2,0,1:T(8,128)S(1)} async-done(((f32[16,16,256]{2,0,1:T(8,128)}), f32[16,16,256]{2,0,1:T(8,128)S(1)}, u32[]{:S(2)}, u32[]{:S(2)}) %all-to-all-start.6) | async-done | bytes 262176 | tf_op jit(solution)/shard_map/all_to_all | solution.py:192
  215.7 3.5 %all-to-all-start.8 = ((bf16[4,512,256]{2,1,0:T(8,128)(2,1)}), bf16[4,512,256]{2,1,0:T(8,128)(2,1)S(1)}, u32[]{:S(2)}, u32[]{:S(2)}) async-start(bf16[4,512,256]{2,1,0:T(8,128)(2,1)} %bitcast.23), calls=%async_computation.8 | async-start | bytes 2097152 | tf_op jit(solution)/shard_map/all_to_all | solution.py:144
  220.4 15.5 %shard_map.141 = f32[128,32,128]{2,1,0:T(8,128)} custom-call(f32[2048]{0:T(1024)} %reshape.271.into_ref, f32[2048]{0:T(1024)} %reshape.272.outof_ref, f32[128,32,128]{2,1,0:T(8,128)} %bitcast.174, f32[128,32,128]{2,1,0:T(8,128)} %copy.88.value_ref, f32[16,32,128]{2,1,0:T(8,128)} %bitcast.178, f32[16,32,128]{2,1,0:T(8,128)} %reshape.276.start_ref, ...), custom_call_target="tpu_custom_call" | custom-call | flops 50331648 | bytes 6291456 | tf_op jit(solution)/shard_map/pallas_call | solution.py:84
  235.9 1.8 convert_element_type.95
  238.7 15.3 %all_to_all.76 = bf16[128,4,4,256]{3,0,1,2:T(8,128)(2,1)S(1)} all-to-all(bf16[128,4,4,256]{3,0,1,2:T(8,128)(2,1)S(1)} %copy.83), channel_id=1, replica_groups=mesh['req'=8,'sz'=4,'sy'=4] {'sy'}, dimensions={2} | all-to-all | bytes 2097152 | tf_op jit(solution)/shard_map/all_to_all | solution.py:198
  254.0 6.1 %bitcast_convert_fusion = bf16[4,128,2048]{2,1,0:T(8,128)(2,1)} fusion(bf16[4,256,2048]{2,1,0:T(8,128)(2,1)} %all-gather.5.cloned.1.call-done, bf16[4,4,128,256]{3,2,1,0:T(8,128)(2,1)S(1)} %bitcast.176, bf16[128,4,4,256]{3,0,1,2:T(8,128)(2,1)S(1)} %all_to_all.76), kind=kOutput, calls=%fused_computation.4 | convolution fusion | flops 2152726528 | bytes 8388608 | tf_op jit(solution)/shard_map/ktac,acd->ktd/dot_general | solution.py:204
  260.8 6.5 %all-to-all-start.10 = ((f32[8,1,16,256]{3,2,1,0:T(8,128)}), f32[8,1,16,256]{3,2,1,0:T(8,128)S(1)}, u32[]{:S(2)}, u32[]{:S(2)}) async-start(f32[8,1,16,256]{3,2,1,0:T(8,128)} %broadcast_in_dim.25), calls=%async_computation.11 | async-start | bytes 262144 | tf_op jit(solution)/shard_map/all_to_all | solution.py:17
  267.3 5.3 %all-to-all-done.10 = f32[8,1,16,256]{3,2,1,0:T(8,128)S(1)} async-done(((f32[8,1,16,256]{3,2,1,0:T(8,128)}), f32[8,1,16,256]{3,2,1,0:T(8,128)S(1)}, u32[]{:S(2)}, u32[]{:S(2)}) %all-to-all-start.10) | async-done | bytes 131104 | tf_op jit(solution)/shard_map/all_to_all | solution.py:17
  273.2 17.0 %reduce-scatter.2.cloned.1.call-done = bf16[128,2048]{1,0:T(8,128)(2,1)} async-done(((bf16[512,2048]{1,0:T(8,128)(2,1)}), bf16[128,2048]{1,0:T(8,128)(2,1)}) %reduce-scatter.2.cloned.1.call-update) | async-done | bytes 524304 | tf_op jit(solution)/shard_map/reduce_scatter | solution.py:207
  290.2 2.0 fusion.26
  (97 shorter events, 39.2 us)
Async XLA Ops:
  7.2 20.1 %copy-start.4 = (bf16[256,160]{0,1:T(8,128)(2,1)S(1)}, bf16[256,160]{0,1:T(8,128)(2,1)}, u32[]{:S(2)}) copy-start(bf16[256,160]{0,1:T(8,128)(2,1)} %param.20) | copy-start | bytes 245764
  7.2 4.0 %copy-start.7 = (bf16[256]{0:T(256)(128)(2,1)S(1)}, bf16[256]{0:T(256)(128)(2,1)}, u32[]{:S(2)}) copy-start(bf16[256]{0:T(256)(128)(2,1)} %param.22) | copy-start | bytes 1540
  7.2 108.0 %all-gather.3.cloned.1.call-start = ((), (), s32[]{:S(2)}) async-start(), calls=%async_computation.12 | async-start | bytes 8912896 | tf_op jit(solution)/shard_map/all_gather | solution.py:129
  11.2 41.8 %copy-start.2 = (bf16[2,256,256]{2,1,0:T(8,128)(2,1)S(1)}, bf16[2,256,256]{2,1,0:T(8,128)(2,1)}, u32[]{:S(2)}) copy-start(bf16[2,256,256]{2,1,0:T(8,128)(2,1)} %param.17) | copy-start | bytes 786436
  54.5 5.9 %copy-start.5 = (bf16[128,256]{1,0:T(8,128)(2,1)S(1)}, bf16[128,256]{1,0:T(8,128)(2,1)}, u32[]{:S(2)}) copy-start(bf16[128,256]{1,0:T(8,128)(2,1)} %param.21) | copy-start | bytes 196612
  54.5 32.1 %all-to-all-start = ((bf16[8,2,256,256]{3,2,1,0:T(8,128)(2,1)}), bf16[8,2,256,256]{3,2,1,0:T(8,128)(2,1)S(1)}, u32[]{:S(2)}, u32[]{:S(2)}) async-start(bf16[8,2,256,256]{3,2,1,0:T(8,128)(2,1)} %broadcast_in_dim.18), calls=%async_computation | async-start | bytes 4194304 | tf_op jit(solution)/shard_map/all_to_all | solution.py:17
  60.4 31.8 %copy-start.8 = (bf16[256]{0:T(256)(128)(2,1)S(1)}, bf16[256]{0:T(256)(128)(2,1)}, u32[]{:S(2)}) copy-start(bf16[256]{0:T(256)(128)(2,1)} %param.19) | copy-start | bytes 1540
  60.4 31.8 %copy-start.6 = (bf16[4,256]{1,0:T(4,128)(2,1)S(1)}, bf16[4,256]{1,0:T(4,128)(2,1)}, u32[]{:S(2)}) copy-start(bf16[4,256]{1,0:T(4,128)(2,1)} %param.18) | copy-start | bytes 6148
  87.8 24.7 %all-to-all-start.2 = ((bf16[16,128,256]{1,2,0:T(8,128)(2,1)}), bf16[16,128,256]{1,2,0:T(8,128)(2,1)}, u32[]{:S(2)}, u32[]{:S(2)}) async-start(bf16[16,128,256]{1,2,0:T(8,128)(2,1)} %broadcast_in_dim.20), calls=%async_computation.2 | async-start | bytes 2097152 | tf_op jit(solution)/shard_map/all_to_all | solution.py:17
  112.5 2.7 copy-start.3
  116.3 20.5 %all-to-all-start.9 = ((bf16[8,256,256]{2,1,0:T(8,128)(2,1)}), bf16[8,256,256]{2,1,0:T(8,128)(2,1)S(1)}, u32[]{:S(2)}, u32[]{:S(2)}) async-start(bf16[8,256,256]{2,1,0:T(8,128)(2,1)} %broadcast_in_dim.23), calls=%async_computation.9 | async-start | bytes 2097152 | tf_op jit(solution)/shard_map/all_to_all | solution.py:17
  129.0 2.0 copy-start.1
  133.3 9.6 %copy-start.9 = (s32[8]{0:T(128)S(1)}, s32[8]{0:T(128)}, u32[]{:S(2)}) copy-start(s32[8]{0:T(128)} %param.14) | copy-start | bytes 100
  136.8 19.7 %all-to-all-start.4 = ((bf16[16,128,256]{2,1,0:T(8,128)(2,1)}), bf16[16,128,256]{2,1,0:T(8,128)(2,1)S(1)}, u32[]{:S(2)}, u32[]{:S(2)}) async-start(bf16[16,128,256]{2,1,0:T(8,128)(2,1)} %bitcast.12), calls=%async_computation.4 | async-start | bytes 2097152 | tf_op jit(solution)/shard_map/all_to_all | solution.py:153
  140.4 113.6 %all-gather.5.cloned.1.call-start = ((), (), s32[]{:S(2)}) async-start(), calls=%async_computation.13 | async-start | bytes 5242880 | tf_op jit(solution)/shard_map/all_gather | solution.py:139
  180.6 12.5 %all-to-all-start.5 = ((f32[17,16,256]{2,0,1:T(8,128)}), f32[17,16,256]{2,0,1:T(8,128)S(1)}, u32[]{:S(2)}, u32[]{:S(2)}) async-start(f32[17,16,256]{2,0,1:T(8,128)} %pad_maximum_fusion), calls=%async_computation.5 | async-start | bytes 786432 | tf_op jit(solution)/shard_map/all_to_all | solution.py:183
  202.3 13.5 %all-to-all-start.6 = ((f32[16,16,256]{2,0,1:T(8,128)}), f32[16,16,256]{2,0,1:T(8,128)S(1)}, u32[]{:S(2)}, u32[]{:S(2)}) async-start(f32[16,16,256]{2,0,1:T(8,128)} %constant_dynamic-update-slice_fusion), calls=%async_computation.6 | async-start | bytes 524288 | tf_op jit(solution)/shard_map/all_to_all | solution.py:192
  215.7 23.0 %all-to-all-start.8 = ((bf16[4,512,256]{2,1,0:T(8,128)(2,1)}), bf16[4,512,256]{2,1,0:T(8,128)(2,1)S(1)}, u32[]{:S(2)}, u32[]{:S(2)}) async-start(bf16[4,512,256]{2,1,0:T(8,128)(2,1)} %bitcast.23), calls=%async_computation.8 | async-start | bytes 2097152 | tf_op jit(solution)/shard_map/all_to_all | solution.py:144
  219.3 71.0 %reduce-scatter.2.cloned.1.call-start = ((), (), s32[]{:S(2)}) async-start(), calls=%async_computation.14 | async-start | bytes 2621440 | tf_op jit(solution)/shard_map/reduce_scatter | solution.py:207
  260.1 7.2 %copy-start.10 = (s32[8]{0:T(128)S(1)}, s32[8]{0:T(128)}, u32[]{:S(2)}) copy-start(s32[8]{0:T(128)} %param.15) | copy-start | bytes 100
  260.1 30.1 %copy-start = (bf16[1,128,2048]{2,1,0:T(8,128)(2,1)S(1)}, bf16[1,128,2048]{2,1,0:T(8,128)(2,1)}, u32[]{:S(2)}) copy-start(bf16[1,128,2048]{2,1,0:T(8,128)(2,1)} %param.13) | copy-start | bytes 1572868
  260.8 11.7 %all-to-all-start.10 = ((f32[8,1,16,256]{3,2,1,0:T(8,128)}), f32[8,1,16,256]{3,2,1,0:T(8,128)S(1)}, u32[]{:S(2)}, u32[]{:S(2)}) async-start(f32[8,1,16,256]{3,2,1,0:T(8,128)} %broadcast_in_dim.25), calls=%async_computation.11 | async-start | bytes 262144 | tf_op jit(solution)/shard_map/all_to_all | solution.py:17
Sparse Core Ops, SparseCore 0:
  11.3 87.4 all-gather.2
  147.9 52.3 all-gather.4
  260.2 29.9 reduce-scatter.1

commit v7 on v6

--- a/solution.py
+++ b/solution.py
@@ -93,6 +93,33 @@
             bytes_accessed=(3 if emit else 2) * steps * rows * lanes * 4,
         ),
     )(into, outof, rate, value, decay, start, skip)
+
+
+def combine_body(pair_ref, decay_ref, carries_ref, final_ref):
+    blocks = pair_ref.shape[0]
+    states = decay_ref.shape[0]
+    decay = decay_ref[...]
+    carry = jnp.zeros(decay.shape, jnp.float32)
+    for block in range(blocks):
+        carries_ref[block] = carry
+        rows = pair_ref[block]
+        carry = jnp.exp(rows[states : states + 1] * decay) * carry + rows[:states]
+    final_ref[...] = carry
+
+
+def run_combine(pair, decay):
+    blocks = pair.shape[0]
+    states, width = decay.shape
+    vmem = pl.BlockSpec(memory_space=pltpu.MemorySpace.VMEM)
+    return pl.pallas_call(
+        combine_body,
+        in_specs=[vmem, vmem],
+        out_specs=(vmem, vmem),
+        out_shape=(
+            jax.ShapeDtypeStruct((blocks, states, width), jnp.float32),
+            jax.ShapeDtypeStruct((states, width), jnp.float32),
+        ),
+    )(pair, decay)
 
 
 def per_device(
@@ -129,9 +156,12 @@
     normed_all = lax.all_gather(normed, seq, axis=0, tiled=True)
     w_in = gather_a2a(in_weight, "req", 1)
     xproj_w, dt_w, dt_b, _ = lax.optimization_barrier((xproj_weight, dt_weight, dt_bias, normed))
-    xproj_full = gather_a2a(xproj_w, seq, 0)
-    dt_full = gather_a2a(dt_w, seq, 1)
-    dt_bias_full = gather_a2a(dt_b, seq, 0)
+    proj_cols = xproj_w.shape[1]
+    small = jnp.concatenate((xproj_w, dt_w.T, dt_b[:, None]), axis=1)
+    small_full = gather_a2a(small, seq, 0)
+    xproj_full = small_full[:, :proj_cols]
+    dt_full = small_full[:, proj_cols : proj_cols + RANK].T
+    dt_bias_full = small_full[:, proj_cols + RANK]
     w_in, xproj_full, dt_full, dt_bias_full = lax.optimization_barrier(
         (w_in, xproj_full, dt_full, dt_bias_full)
     )
@@ -180,16 +210,13 @@
     pair = jnp.concatenate(
         (end_l.reshape(state_count, total_inner), total_l.reshape(1, total_inner))
     ).reshape(state_count + 1, seq_count, width)
-    pair_ch = lax.all_to_all(pair, seq, split_axis=1, concat_axis=1, tiled=True)
+    pair_ch = lax.all_to_all(
+        jnp.swapaxes(pair, 0, 1), seq, split_axis=0, concat_axis=0, tiled=True
+    )
     decay_ch = lax.dynamic_slice_in_dim(decay, seq_index * width, width, 1)
-    falls = jnp.exp(pair_ch[state_count][None] * decay_ch[:, None, :])
-    carry = jnp.zeros((state_count, width), jnp.float32)
-    carries = []
-    for block in range(seq_count):
-        carries.append(carry)
-        carry = falls[:, block] * carry + pair_ch[:state_count, block]
-    carry_ch = jnp.stack(carries, axis=1)
-    carry_in = lax.all_to_all(carry_ch, seq, split_axis=1, concat_axis=1, tiled=True)
+    carry_ch, carry = run_combine(pair_ch, decay_ch)
+    carry_in = lax.all_to_all(carry_ch, seq, split_axis=0, concat_axis=0, tiled=True)
+    carry_in = jnp.swapaxes(carry_in, 0, 1).reshape(state_count, total_inner)
     out_l = run_scan(
         True, into, outof, rate_l, value_l, decay_l,
         carry_in.reshape(state_count, groups, lanes), skip_l,

time: 300 us -> 307 us (1.023)
  waiting for transfers between devices: 89.8 us -> 140 us
  blocking collectives: 55.7 us -> 13.8 us
  other arithmetic: 22.1 us -> 13.7 us
  starting transfers between devices: 39.5 us -> 45.1 us
    all_to_all x4, waiting for transfers between devices: 52 us -> 97.1 us  [gather_a2a(): lax.all_to_all(copies, axis, split_axis=0, concat_axis=0, tiled=True)]
    all_to_all x2 -> x0, blocking collectives: 40.4 us -> none  [gather_a2a(): lax.all_to_all(copies, axis, split_axis=0, concat_axis=0, tiled=True)]
    unnamed x10 -> x0, other arithmetic: 6.06 us -> none
    all_to_all x1, waiting for transfers between devices: 8.59 us -> 14.5 us  [per_device(): lax.all_to_all(inner, seq, split_axis=0, concat_axis=1, tiled=True)]
    all_to_all x4, starting transfers between devices: 22.2 us -> 27 us  [gather_a2a(): lax.all_to_all(copies, axis, split_axis=0, concat_axis=0, tiled=True)]
    unnamed x33 -> x40, local copies, waits for them, and re-layouts: 7.27 us -> 8.1 us
  transfers between devices with their start and end apart: 11 -> 11, of which waited for: 8 -> 8; matrix products, arithmetic and copies ran while one was open for 19% -> 14% of each run, Pallas kernels for 9% -> 9%
where the time goes in v7:
time: 307 us; the launch traced here: 306 us
  waiting for transfers between devices  140 us (46%)
  starting transfers between devices  45.1 us (15%)
  local copies, waits for them, and re-layouts  35.8 us (12%)
  Pallas kernels  28.9 us (9%)
  matrix products  14.9 us (5%)
  between operations  14.1 us (5%)
  blocking collectives  13.8 us (4%)
  other arithmetic  13.7 us (4%)
    all_to_all x4, waiting for transfers between devices, gather_a2a(): lax.all_to_all(copies, axis, split_axis=0, concat_axis=0, tiled=True)  97.1 us
    pallas_call x2, Pallas kernels, run_scan(): pl.pallas_call(functools.partial(scan_body, emit), grid=(chunks,), in_spe...  27.1 us
    all_to_all x4, starting transfers between devices, gather_a2a(): lax.all_to_all(copies, axis, split_axis=0, concat_axis=0, tiled=True)  27 us
    reduce_scatter x1, waiting for transfers between devices, per_device(): lax.psum_scatter(partial.reshape(cols_n * rows, model), 'sy', scatter_dim...  16.1 us
    all_to_all x1, waiting for transfers between devices, per_device(): lax.all_to_all(inner, seq, split_axis=0, concat_axis=1, tiled=True)  14.5 us
    all_to_all x1, blocking collectives, per_device(): lax.all_to_all(scanned, 'sy', split_axis=2, concat_axis=0, tiled=True)  13.8 us
    unnamed x40, local copies, waits for them, and re-layouts  8.1 us
    all_to_all x1, waiting for transfers between devices, per_device(): lax.all_to_all(jnp.swapaxes(pair, 0, 1), seq, split_axis=0, concat_axis=0...  7.1 us
  transfers between devices with their start and end apart: 11, of which 8 were waited for; matrix products, arithmetic and copies ran while one was open for 14% of the time, Pallas kernels for 9%

profile of v7, /device:TPU:1, one launch (start us, length us, event | category | flops | bytes accessed | tf_op | source)
XLA Modules:
  0.0 305.9 jit_solution(12516659821085253828)
XLA Ops:
  9.2 2.0 fusion.21
  12.8 5.9 %all-to-all-start = ((bf16[8,2,256,256]{3,2,1,0:T(8,128)(2,1)}), bf16[8,2,256,256]{3,2,1,0:T(8,128)(2,1)S(1)}, u32[]{:S(2)}, u32[]{:S(2)}) async-start(bf16[8,2,256,256]{3,2,1,0:T(8,128)(2,1)} %broadcast_in_dim.16), calls=%async_computation | async-start | bytes 4194304 | tf_op jit(solution)/shard_map/all_to_all | solution.py:17
  18.8 26.2 %all-to-all-done = bf16[8,2,256,256]{3,2,1,0:T(8,128)(2,1)S(1)} async-done(((bf16[8,2,256,256]{3,2,1,0:T(8,128)(2,1)}), bf16[8,2,256,256]{3,2,1,0:T(8,128)(2,1)S(1)}, u32[]{:S(2)}, u32[]{:S(2)}) %all-to-all-start) | async-done | bytes 2097184 | tf_op jit(solution)/shard_map/all_to_all | solution.py:17
  45.0 1.8 broadcast_in_dim.18
  47.1 7.8 %all-to-all-start.1 = ((bf16[16,256,289]{1,2,0:T(8,128)(2,1)}), bf16[16,256,289]{1,2,0:T(8,128)(2,1)S(1)}, u32[]{:S(2)}, u32[]{:S(2)}) async-start(bf16[16,256,289]{1,2,0:T(8,128)(2,1)} %broadcast_in_dim.18), calls=%async_computation.1 | async-start | bytes 4849664 | tf_op jit(solution)/shard_map/all_to_all | solution.py:17
  54.9 3.2 %copy.34 = bf16[8,2,256,256]{3,2,0,1:T(8,128)(2,1)} copy(bf16[8,2,256,256]{3,2,1,0:T(8,128)(2,1)} %copy-done.1) | data formatting | bytes 4194304 | tf_op jit(solution)/shard_map/all_to_all | solution.py:17
  58.1 51.7 %all-to-all-done.1 = bf16[16,256,289]{1,2,0:T(8,128)(2,1)S(1)} async-done(((bf16[16,256,289]{1,2,0:T(8,128)(2,1)}), bf16[16,256,289]{1,2,0:T(8,128)(2,1)S(1)}, u32[]{:S(2)}, u32[]{:S(2)}) %all-to-all-start.1) | async-done | bytes 2367520 | tf_op jit(solution)/shard_map/all_to_all | solution.py:17
  113.9 5.4 %all-to-all-start.7 = ((bf16[8,256,256]{2,1,0:T(8,128)(2,1)}), bf16[8,256,256]{2,1,0:T(8,128)(2,1)S(1)}, u32[]{:S(2)}, u32[]{:S(2)}) async-start(bf16[8,256,256]{2,1,0:T(8,128)(2,1)} %broadcast_in_dim.20), calls=%async_computation.7 | async-start | bytes 2097152 | tf_op jit(solution)/shard_map/all_to_all | solution.py:17
  120.4 13.9 %all-to-all-done.7 = bf16[8,256,256]{2,1,0:T(8,128)(2,1)S(1)} async-done(((bf16[8,256,256]{2,1,0:T(8,128)(2,1)}), bf16[8,256,256]{2,1,0:T(8,128)(2,1)S(1)}, u32[]{:S(2)}, u32[]{:S(2)}) %all-to-all-start.7) | async-done | bytes 1048608 | tf_op jit(solution)/shard_map/all_to_all | solution.py:17
  135.6 2.4 copy.45
  138.2 6.9 %fusion.6 = f32[2048,512]{1,0:T(8,128)S(1)} fusion(bf16[2048,2048]{1,0:T(8,128)(2,1)} %all-gather.3.cloned.1.call-done, bf16[2048,256]{1,0:T(8,128)(2,1)S(1)} %get-tuple-element.27, bf16[2048,256]{1,0:T(8,128)(2,1)S(1)} %get-tuple-element.26), kind=kOutput, calls=%fused_computation.9 | convolution fusion | flops 4299161600 | bytes 14680064 | tf_op jit(solution)/shard_map/dot_general | solution.py:171
  147.1 2.3 multiply_convert_fusion
  149.4 5.0 %all-to-all-start.2 = ((bf16[16,128,256]{2,1,0:T(8,128)(2,1)}), bf16[16,128,256]{2,1,0:T(8,128)(2,1)S(1)}, u32[]{:S(2)}, u32[]{:S(2)}) async-start(bf16[16,128,256]{2,1,0:T(8,128)(2,1)} %bitcast.12), calls=%async_computation.2 | async-start | bytes 2097152 | tf_op jit(solution)/shard_map/all_to_all | solution.py:183
  157.2 14.5 %all-to-all-done.2 = bf16[16,128,256]{2,1,0:T(8,128)(2,1)S(1)} async-done(((bf16[16,128,256]{2,1,0:T(8,128)(2,1)}), bf16[16,128,256]{2,1,0:T(8,128)(2,1)S(1)}, u32[]{:S(2)}, u32[]{:S(2)}) %all-to-all-start.2) | async-done | bytes 1048608 | tf_op jit(solution)/shard_map/all_to_all | solution.py:183
  175.1 1.7 copy.49
  178.4 1.9 copy.47.value_ref
  181.0 11.6 %shard_map.140 = (f32[16,32,128]{2,1,0:T(8,128)}, f32[1,32,128]{2,1,0:T(8,128)}) custom-call(f32[2048]{0:T(1024)} %reshape.87.into_ref, f32[2048]{0:T(1024)} %reshape.88.outof_ref, f32[128,32,128]{2,1,0:T(8,128)} %bitcast.111, f32[128,32,128]{2,1,0:T(8,128)} %copy.47.value_ref, f32[16,32,128]{2,1,0:T(8,128)} %bitcast.116, ...), custom_call_target="tpu_custom_call" | custom-call | flops 50331648 | bytes 4194304 | tf_op jit(solution)/shard_map/pallas_call | solution.py:84
  195.4 5.9 %all-to-all-start.3 = ((f32[16,17,256]{2,1,0:T(8,128)}), f32[16,17,256]{2,1,0:T(8,128)S(1)}, u32[]{:S(2)}, u32[]{:S(2)}) async-start(f32[16,17,256]{2,1,0:T(8,128)} %maximum_bitcast_fusion), calls=%async_computation.3 | async-start | bytes 786432 | tf_op jit(solution)/shard_map/all_to_all | solution.py:213
  202.6 7.1 %all-to-all-done.3.pair_ref = f32[16,17,256]{2,1,0:T(8,128)S(1)} async-done(((f32[16,17,256]{2,1,0:T(8,128)}), f32[16,17,256]{2,1,0:T(8,128)S(1)}, u32[]{:S(2)}, u32[]{:S(2)}) %all-to-all-start.3) | async-done | bytes 278560 | tf_op jit(solution)/shard_map/all_to_all | solution.py:213
  210.5 1.7 shard_map.141
  212.2 3.5 %all-to-all-start.4 = ((f32[16,16,256]{2,1,0:T(8,128)}), f32[16,16,256]{2,1,0:T(8,128)S(1)}, u32[]{:S(2)}, u32[]{:S(2)}) async-start(f32[16,16,256]{2,1,0:T(8,128)} %get-tuple-element.23), calls=%async_computation.4 | async-start | bytes 524288 | tf_op jit(solution)/shard_map/all_to_all | solution.py:218
  215.8 2.7 slice.99
  218.4 4.9 %all-to-all-done.4 = f32[16,16,256]{2,1,0:T(8,128)S(1)} async-done(((f32[16,16,256]{2,1,0:T(8,128)}), f32[16,16,256]{2,1,0:T(8,128)S(1)}, u32[]{:S(2)}, u32[]{:S(2)}) %all-to-all-start.4) | async-done | bytes 262176 | tf_op jit(solution)/shard_map/all_to_all | solution.py:218
  223.3 3.5 %all-to-all-start.6 = ((bf16[4,512,256]{2,1,0:T(8,128)(2,1)}), bf16[4,512,256]{2,1,0:T(8,128)(2,1)S(1)}, u32[]{:S(2)}, u32[]{:S(2)}) async-start(bf16[4,512,256]{2,1,0:T(8,128)(2,1)} %bitcast.25), calls=%async_computation.6 | async-start | bytes 2097152 | tf_op jit(solution)/shard_map/all_to_all | solution.py:174
  227.8 15.5 %shard_map.142 = f32[128,32,128]{2,1,0:T(8,128)} custom-call(f32[2048]{0:T(1024)} %reshape.87.into_ref, f32[2048]{0:T(1024)} %reshape.88.outof_ref, f32[128,32,128]{2,1,0:T(8,128)} %bitcast.112, f32[128,32,128]{2,1,0:T(8,128)} %copy.47.value_ref, f32[16,32,128]{2,1,0:T(8,128)} %bitcast.117, f32[16,32,128]{2,1,0:T(8,128)} %reshape_reshape.3.start_ref, ...), custom_call_target="tpu_custom_call" | custom-call | flops 50331648 | bytes 6291456 | tf_op jit(solution)/shard_map/pallas_call | solution.py:84
  243.3 1.8 convert_element_type.95
  246.1 13.8 %all_to_all.63 = bf16[128,4,4,256]{3,0,1,2:T(8,128)(2,1)S(1)} all-to-all(bf16[128,4,4,256]{3,0,1,2:T(8,128)(2,1)S(1)} %copy.42), channel_id=1, replica_groups=mesh['req'=8,'sz'=4,'sy'=4] {'sy'}, dimensions={2} | all-to-all | bytes 2097152 | tf_op jit(solution)/shard_map/all_to_all | solution.py:225
  260.0 6.1 %bitcast_convert_fusion = bf16[4,128,2048]{2,1,0:T(8,128)(2,1)} fusion(bf16[4,256,2048]{2,1,0:T(8,128)(2,1)} %all-gather.5.cloned.1.call-done, bf16[4,4,128,256]{3,2,1,0:T(8,128)(2,1)S(1)} %bitcast.114, bf16[128,4,4,256]{3,0,1,2:T(8,128)(2,1)S(1)} %all_to_all.63), kind=kOutput, calls=%fused_computation.4 | convolution fusion | flops 2152726528 | bytes 8388608 | tf_op jit(solution)/shard_map/ktac,acd->ktd/dot_general | solution.py:231
  267.4 7.9 %all-to-all-start.8 = ((f32[8,1,16,256]{3,2,1,0:T(8,128)}), f32[8,1,16,256]{3,2,1,0:T(8,128)S(1)}, u32[]{:S(2)}, u32[]{:S(2)}) async-start(f32[8,1,16,256]{3,2,1,0:T(8,128)} %broadcast_in_dim.22), calls=%async_computation.9 | async-start | bytes 262144 | tf_op jit(solution)/shard_map/all_to_all | solution.py:17
  275.3 5.3 %all-to-all-done.8 = f32[8,1,16,256]{3,2,1,0:T(8,128)S(1)} async-done(((f32[8,1,16,256]{3,2,1,0:T(8,128)}), f32[8,1,16,256]{3,2,1,0:T(8,128)S(1)}, u32[]{:S(2)}, u32[]{:S(2)}) %all-to-all-start.8) | async-done | bytes 131104 | tf_op jit(solution)/shard_map/all_to_all | solution.py:17
  281.3 16.1 %reduce-scatter.2.cloned.1.call-done = bf16[128,2048]{1,0:T(8,128)(2,1)} async-done(((bf16[512,2048]{1,0:T(8,128)(2,1)}), bf16[128,2048]{1,0:T(8,128)(2,1)}) %reduce-scatter.2.cloned.1.call-update) | async-done | bytes 524304 | tf_op jit(solution)/shard_map/reduce_scatter | solution.py:234
  297.5 2.0 fusion.26
  (88 shorter events, 29.8 us)
Async XLA Ops:
  7.2 4.1 %copy-start.7 = (bf16[2,256,256]{2,1,0:T(8,128)(2,1)S(1)}, bf16[2,256,256]{2,1,0:T(8,128)(2,1)}, u32[]{:S(2)}) copy-start(bf16[2,256,256]{2,1,0:T(8,128)(2,1)} %param.17) | copy-start | bytes 786436
  7.2 105.6 %all-gather.3.cloned.1.call-start = ((), (), s32[]{:S(2)}) async-start(), calls=%async_computation.10 | async-start | bytes 8912896 | tf_op jit(solution)/shard_map/all_gather | solution.py:156
  12.8 5.9 %copy-start.14 = (bf16[256]{0:T(256)(128)(2,1)S(1)}, bf16[256]{0:T(256)(128)(2,1)}, u32[]{:S(2)}) copy-start(bf16[256]{0:T(256)(128)(2,1)} %param.22) | copy-start | bytes 1540
  12.8 5.9 %copy-start.10 = (bf16[256,160]{0,1:T(8,128)(2,1)S(1)}, bf16[256,160]{0,1:T(8,128)(2,1)}, u32[]{:S(2)}) copy-start(bf16[256,160]{0,1:T(8,128)(2,1)} %param.20) | copy-start | bytes 245764
  12.8 5.9 %copy-start.11 = (bf16[128,256]{1,0:T(8,128)(2,1)S(1)}, bf16[128,256]{1,0:T(8,128)(2,1)}, u32[]{:S(2)}) copy-start(bf16[128,256]{1,0:T(8,128)(2,1)} %param.21) | copy-start | bytes 196612
  12.8 32.1 %all-to-all-start = ((bf16[8,2,256,256]{3,2,1,0:T(8,128)(2,1)}), bf16[8,2,256,256]{3,2,1,0:T(8,128)(2,1)S(1)}, u32[]{:S(2)}, u32[]{:S(2)}) async-start(bf16[8,2,256,256]{3,2,1,0:T(8,128)(2,1)} %broadcast_in_dim.16), calls=%async_computation | async-start | bytes 4194304 | tf_op jit(solution)/shard_map/all_to_all | solution.py:17
  45.0 2.1 copy-start.1
  46.7 8.1 %copy-start.15 = (bf16[256]{0:T(256)(128)(2,1)S(1)}, bf16[256]{0:T(256)(128)(2,1)}, u32[]{:S(2)}) copy-start(bf16[256]{0:T(256)(128)(2,1)} %param.19) | copy-start | bytes 1540
  46.7 8.2 %copy-start.13 = (bf16[4,256]{1,0:T(4,128)(2,1)S(1)}, bf16[4,256]{1,0:T(4,128)(2,1)}, u32[]{:S(2)}) copy-start(bf16[4,256]{1,0:T(4,128)(2,1)} %param.18) | copy-start | bytes 6148
  47.1 62.7 %all-to-all-start.1 = ((bf16[16,256,289]{1,2,0:T(8,128)(2,1)}), bf16[16,256,289]{1,2,0:T(8,128)(2,1)S(1)}, u32[]{:S(2)}, u32[]{:S(2)}) async-start(bf16[16,256,289]{1,2,0:T(8,128)(2,1)} %broadcast_in_dim.18), calls=%async_computation.1 | async-start | bytes 4849664 | tf_op jit(solution)/shard_map/all_to_all | solution.py:17
  111.6 1.3 copy-start.9
  113.9 20.4 %all-to-all-start.7 = ((bf16[8,256,256]{2,1,0:T(8,128)(2,1)}), bf16[8,256,256]{2,1,0:T(8,128)(2,1)S(1)}, u32[]{:S(2)}, u32[]{:S(2)}) async-start(bf16[8,256,256]{2,1,0:T(8,128)(2,1)} %broadcast_in_dim.20), calls=%async_computation.7 | async-start | bytes 2097152 | tf_op jit(solution)/shard_map/all_to_all | solution.py:17
  119.3 140.7 %all-gather.5.cloned.1.call-start = ((), (), s32[]{:S(2)}) async-start(), calls=%async_computation.11 | async-start | bytes 5242880 | tf_op jit(solution)/shard_map/all_gather | solution.py:169
  135.6 2.5 copy-start
  145.1 2.0 copy-start.4
  147.1 7.3 %copy-start.8 = (f32[16,4096]{1,0:T(8,128)S(1)}, f32[16,4096]{1,0:T(8,128)}, u32[]{:S(2)}) copy-start(f32[16,4096]{1,0:T(8,128)} %param.23) | copy-start | bytes 786436
  149.4 6.5 %copy-start.16 = (s32[8]{0:T(128)S(1)}, s32[8]{0:T(128)}, u32[]{:S(2)}) copy-start(s32[8]{0:T(128)} %param.14) | copy-start | bytes 100
  149.4 22.3 %all-to-all-start.2 = ((bf16[16,128,256]{2,1,0:T(8,128)(2,1)}), bf16[16,128,256]{2,1,0:T(8,128)(2,1)S(1)}, u32[]{:S(2)}, u32[]{:S(2)}) async-start(bf16[16,128,256]{2,1,0:T(8,128)(2,1)} %bitcast.12), calls=%async_computation.2 | async-start | bytes 2097152 | tf_op jit(solution)/shard_map/all_to_all | solution.py:183
  154.4 17.9 %copy-start.2 = (bf16[4096,160]{0,1:T(8,128)(2,1)S(1)}, bf16[4096,160]{0,1:T(8,128)(2,1)}, u32[]{:S(2)}) copy-start(bf16[4096,160]{0,1:T(8,128)(2,1)} %slice.71) | copy-start | bytes 3932164
  172.3 1.2 copy-start.6
  195.4 14.4 %all-to-all-start.3 = ((f32[16,17,256]{2,1,0:T(8,128)}), f32[16,17,256]{2,1,0:T(8,128)S(1)}, u32[]{:S(2)}, u32[]{:S(2)}) async-start(f32[16,17,256]{2,1,0:T(8,128)} %maximum_bitcast_fusion), calls=%async_computation.3 | async-start | bytes 786432 | tf_op jit(solution)/shard_map/all_to_all | solution.py:213
  209.7 0.7 copy-start.5
  212.2 11.1 %all-to-all-start.4 = ((f32[16,16,256]{2,1,0:T(8,128)}), f32[16,16,256]{2,1,0:T(8,128)S(1)}, u32[]{:S(2)}, u32[]{:S(2)}) async-start(f32[16,16,256]{2,1,0:T(8,128)} %get-tuple-element.23), calls=%async_computation.4 | async-start | bytes 524288 | tf_op jit(solution)/shard_map/all_to_all | solution.py:218
  223.3 22.8 %all-to-all-start.6 = ((bf16[4,512,256]{2,1,0:T(8,128)(2,1)}), bf16[4,512,256]{2,1,0:T(8,128)(2,1)S(1)}, u32[]{:S(2)}, u32[]{:S(2)}) async-start(bf16[4,512,256]{2,1,0:T(8,128)(2,1)} %bitcast.25), calls=%async_computation.6 | async-start | bytes 2097152 | tf_op jit(solution)/shard_map/all_to_all | solution.py:174
  226.8 70.6 %reduce-scatter.2.cloned.1.call-start = ((), (), s32[]{:S(2)}) async-start(), calls=%async_computation.12 | async-start | bytes 2621440 | tf_op jit(solution)/shard_map/reduce_scatter | solution.py:234
  266.0 0.7 copy-start.12
  266.0 9.3 %copy-start.17 = (s32[8]{0:T(128)S(1)}, s32[8]{0:T(128)}, u32[]{:S(2)}) copy-start(s32[8]{0:T(128)} %param.15) | copy-start | bytes 100
  266.0 31.4 %copy-start.3 = (bf16[1,128,2048]{2,1,0:T(8,128)(2,1)S(1)}, bf16[1,128,2048]{2,1,0:T(8,128)(2,1)}, u32[]{:S(2)}) copy-start(bf16[1,128,2048]{2,1,0:T(8,128)(2,1)} %param.13) | copy-start | bytes 1572868
  267.4 13.2 %all-to-all-start.8 = ((f32[8,1,16,256]{3,2,1,0:T(8,128)}), f32[8,1,16,256]{3,2,1,0:T(8,128)S(1)}, u32[]{:S(2)}, u32[]{:S(2)}) async-start(f32[8,1,16,256]{3,2,1,0:T(8,128)} %broadcast_in_dim.22), calls=%async_computation.9 | async-start | bytes 262144 | tf_op jit(solution)/shard_map/all_to_all | solution.py:17
Sparse Core Ops, SparseCore 0:
  11.4 99.7 all-gather.2
  138.2 57.4 all-gather.4
  266.2 31.2 reduce-scatter.1

commit v8 on v7

--- a/solution.py
+++ b/solution.py
@@ -154,21 +154,27 @@
     scale = lax.rsqrt(jnp.mean(tokens * tokens, axis=-1, keepdims=True) + 1e-05)
     normed = (tokens * scale * norm_gain.astype(jnp.float32)).astype(jnp.bfloat16)
     normed_all = lax.all_gather(normed, seq, axis=0, tiled=True)
-    w_in = gather_a2a(in_weight, "req", 1)
+    pieces = jnp.concatenate((in_weight, out_weight.T[None]), axis=0)
+    pieces_all = gather_a2a(pieces, "req", 1)
+    w_in = pieces_all[:2]
+    w_out_t = pieces_all[2]
     xproj_w, dt_w, dt_b, _ = lax.optimization_barrier((xproj_weight, dt_weight, dt_bias, normed))
     proj_cols = xproj_w.shape[1]
-    small = jnp.concatenate((xproj_w, dt_w.T, dt_b[:, None]), axis=1)
-    small_full = gather_a2a(small, seq, 0)
-    xproj_full = small_full[:, :proj_cols]
-    dt_full = small_full[:, proj_cols : proj_cols + RANK].T
-    dt_bias_full = small_full[:, proj_cols + RANK]
+    small = jnp.concatenate((xproj_w.T, dt_w, dt_b[None]), axis=0)
+    copies = jnp.broadcast_to(small[None], (seq_count,) + small.shape)
+    small_all = lax.all_to_all(copies, seq, split_axis=0, concat_axis=0, tiled=True)
+    xproj_full = jnp.swapaxes(small_all[:, :proj_cols], 1, 2).reshape(total_inner, proj_cols)
+    dt_full = jnp.swapaxes(small_all[:, proj_cols : proj_cols + RANK], 0, 1).reshape(
+        RANK, total_inner
+    )
+    dt_bias_full = small_all[:, proj_cols + RANK].reshape(total_inner)
     w_in, xproj_full, dt_full, dt_bias_full = lax.optimization_barrier(
         (w_in, xproj_full, dt_full, dt_bias_full)
     )
-    w_late, _ = lax.optimization_barrier((out_weight, normed_all))
-    w_col = lax.all_gather(gather_a2a(w_late, "req", 1), "sz", axis=0, tiled=False)
     w_flat = jnp.concatenate((w_in[0], w_in[1]), axis=1)
     both = jnp.dot(normed_all, w_flat, preferred_element_type=jnp.float32)
+    w_late, _ = lax.optimization_barrier((w_out_t, normed_all))
+    w_col = lax.all_gather(w_late.T, "sz", axis=0, tiled=False)
     xin = both[:, :width]
     zgate = both[:, width:].astype(jnp.bfloat16)
     z_grid = lax.all_to_all(

time: 307 us -> 287 us (0.935)
  waiting for transfers between devices: 140 us -> 125 us
  blocking collectives: 13.8 us -> 0 us
  local copies, waits for them, and re-layouts: 35.8 us -> 46.1 us
    all_to_all x4 -> x2, waiting for transfers between devices: 97.1 us -> 34.6 us  [gather_a2a(): lax.all_to_all(copies, axis, split_axis=0, concat_axis=0, tiled=True)]
    all_to_all x0 -> x2, waiting for transfers between devices: none -> 47.8 us  [the longest x1 42.4 us: per_device(): lax.all_to_all(copies, seq, split_axis=0, concat_axis=0, tiled=True)]
    all_to_all x1 -> x0, blocking collectives: 13.8 us -> none  [per_device(): lax.all_to_all(scanned, 'sy', split_axis=2, concat_axis=0, tiled=True)]
    all_to_all x4 -> x2, starting transfers between devices: 27 us -> 13.3 us  [gather_a2a(): lax.all_to_all(copies, axis, split_axis=0, concat_axis=0, tiled=True)]
    all_to_all x0 -> x2, starting transfers between devices: none -> 12.2 us  [the longest x1 8.72 us: per_device(): lax.all_to_all(copies, seq, split_axis=0, concat_axis=0, tiled=True)]
    all_gather x0 -> x1, local copies, waits for them, and re-layouts: none -> 6.56 us  [per_device(): w_col = lax.all_gather(w_late.T, 'sz', axis=0, tiled=False)]
    slice x2 -> x4, local copies, waits for them, and re-layouts: 1.21 us -> 7.24 us  [the longest x1 2.34 us: per_device(): small_all[:, proj_cols:proj_cols + RANK]]
    unnamed x40 -> x39, local copies, waits for them, and re-layouts: 8.1 us -> 9.56 us
  transfers between devices with their start and end apart: 11 -> 11, of which waited for: 8 -> 8; matrix products, arithmetic and copies ran while one was open for 14% -> 21% of each run, Pallas kernels for 9% -> 10%
where the time goes in v8:
time: 287 us; the launch traced here: 285 us
  waiting for transfers between devices  125 us (44%)
  local copies, waits for them, and re-layouts  46.1 us (16%)
  starting transfers between devices  42.9 us (15%)
  Pallas kernels  28.9 us (10%)
  matrix products  15 us (5%)
  between operations  14.1 us (5%)
  other arithmetic  13.8 us (5%)
    all_to_all x1, waiting for transfers between devices, per_device(): lax.all_to_all(copies, seq, split_axis=0, concat_axis=0, tiled=True)  42.4 us
    all_to_all x2, waiting for transfers between devices, gather_a2a(): lax.all_to_all(copies, axis, split_axis=0, concat_axis=0, tiled=True)  34.6 us
    pallas_call x2, Pallas kernels, run_scan(): pl.pallas_call(functools.partial(scan_body, emit), grid=(chunks,), in_spe...  27.1 us
    reduce_scatter x1, waiting for transfers between devices, per_device(): lax.psum_scatter(partial.reshape(cols_n * rows, model), 'sy', scatter_dim...  15.6 us
    all_to_all x1, waiting for transfers between devices, per_device(): lax.all_to_all(inner, seq, split_axis=0, concat_axis=1, tiled=True)  13.7 us
    all_to_all x2, starting transfers between devices, gather_a2a(): lax.all_to_all(copies, axis, split_axis=0, concat_axis=0, tiled=True)  13.3 us
    unnamed x39, local copies, waits for them, and re-layouts  9.56 us
    all_to_all x1, starting transfers between devices, per_device(): lax.all_to_all(copies, seq, split_axis=0, concat_axis=0, tiled=True)  8.72 us
  transfers between devices with their start and end apart: 11, of which 8 were waited for; matrix products, arithmetic and copies ran while one was open for 21% of the time, Pallas kernels for 10%

profile of v8, /device:TPU:1, one launch (start us, length us, event | category | flops | bytes accessed | tf_op | source)
XLA Modules:
  0.0 285.4 jit_solution(11867485280089442744)
XLA Ops:
  9.2 2.0 fusion.17
  13.0 8.7 %all-to-all-start.1 = ((bf16[16,289,256]{2,1,0:T(8,128)(2,1)}), bf16[16,289,256]{2,1,0:T(8,128)(2,1)S(1)}, u32[]{:S(2)}, u32[]{:S(2)}) async-start(bf16[16,289,256]{2,1,0:T(8,128)(2,1)} %broadcast_in_dim.19), calls=%async_computation.1 | async-start | bytes 4849664 | tf_op jit(solution)/shard_map/all_to_all | solution.py:165
  22.0 42.4 %all-to-all-done.1 = bf16[16,289,256]{2,1,0:T(8,128)(2,1)S(1)} async-done(((bf16[16,289,256]{2,1,0:T(8,128)(2,1)}), bf16[16,289,256]{2,1,0:T(8,128)(2,1)S(1)}, u32[]{:S(2)}, u32[]{:S(2)}) %all-to-all-start.1) | async-done | bytes 2367520 | tf_op jit(solution)/shard_map/all_to_all | solution.py:165
  64.4 2.2 broadcast_in_dim.17
  66.8 6.1 %all-to-all-start = ((bf16[8,3,256,256]{2,3,1,0:T(8,128)(2,1)}), bf16[8,3,256,256]{2,3,1,0:T(8,128)(2,1)S(1)}, u32[]{:S(2)}, u32[]{:S(2)}) async-start(bf16[8,3,256,256]{2,3,1,0:T(8,128)(2,1)} %broadcast_in_dim.17), calls=%async_computation | async-start | bytes 6291456 | tf_op jit(solution)/shard_map/all_to_all | solution.py:17
  76.4 2.3 slice.86
  78.8 2.3 copy.58
  81.1 29.2 %all-to-all-done = bf16[8,3,256,256]{2,3,1,0:T(8,128)(2,1)S(1)} async-done(((bf16[8,3,256,256]{2,3,1,0:T(8,128)(2,1)}), bf16[8,3,256,256]{2,3,1,0:T(8,128)(2,1)S(1)}, u32[]{:S(2)}, u32[]{:S(2)}) %all-to-all-start) | async-done | bytes 3145760 | tf_op jit(solution)/shard_map/all_to_all | solution.py:17
  110.3 2.8 copy.44
  113.1 2.3 slice.97
  117.3 6.9 %fusion.2 = f32[2048,512]{1,0:T(8,128)S(1)} fusion(bf16[2048,2048]{1,0:T(8,128)(2,1)} %all-gather.4.cloned.1.call-done, bf16[2048,256]{1,0:T(8,128)(2,1)S(1)} %get-tuple-element.27, bf16[2048,256]{1,0:T(8,128)(2,1)S(1)} %get-tuple-element.26), kind=kOutput, calls=%fused_computation.6 | convolution fusion | flops 4299161600 | bytes 14680064 | tf_op jit(solution)/shard_map/dot_general | solution.py:175
  126.2 2.4 multiply_convert_fusion
  128.6 3.8 %all-to-all-start.2 = ((bf16[16,128,256]{2,1,0:T(8,128)(2,1)}), bf16[16,128,256]{2,1,0:T(8,128)(2,1)S(1)}, u32[]{:S(2)}, u32[]{:S(2)}) async-start(bf16[16,128,256]{2,1,0:T(8,128)(2,1)} %bitcast.16), calls=%async_computation.2 | async-start | bytes 2097152 | tf_op jit(solution)/shard_map/all_to_all | solution.py:189
  135.1 13.7 %all-to-all-done.2 = bf16[16,128,256]{2,1,0:T(8,128)(2,1)S(1)} async-done(((bf16[16,128,256]{2,1,0:T(8,128)(2,1)}), bf16[16,128,256]{2,1,0:T(8,128)(2,1)S(1)}, u32[]{:S(2)}, u32[]{:S(2)}) %all-to-all-start.2) | async-done | bytes 1048608 | tf_op jit(solution)/shard_map/all_to_all | solution.py:189
  154.8 1.9 copy.57.value_ref
  157.4 11.6 %shard_map.140 = (f32[16,32,128]{2,1,0:T(8,128)}, f32[1,32,128]{2,1,0:T(8,128)}) custom-call(f32[2048]{0:T(1024)} %reshape.90.into_ref, f32[2048]{0:T(1024)} %reshape.91.outof_ref, f32[128,32,128]{2,1,0:T(8,128)} %bitcast.110, f32[128,32,128]{2,1,0:T(8,128)} %copy.57.value_ref, f32[16,32,128]{2,1,0:T(8,128)} %bitcast.116, ...), custom_call_target="tpu_custom_call" | custom-call | flops 50331648 | bytes 4194304 | tf_op jit(solution)/shard_map/pallas_call | solution.py:84
  171.7 6.3 %all-to-all-start.3 = ((f32[16,17,256]{2,1,0:T(8,128)}), f32[16,17,256]{2,1,0:T(8,128)S(1)}, u32[]{:S(2)}, u32[]{:S(2)}) async-start(f32[16,17,256]{2,1,0:T(8,128)} %maximum_bitcast_fusion), calls=%async_computation.3 | async-start | bytes 786432 | tf_op jit(solution)/shard_map/all_to_all | solution.py:219
  179.4 7.9 %all-to-all-done.3.pair_ref = f32[16,17,256]{2,1,0:T(8,128)S(1)} async-done(((f32[16,17,256]{2,1,0:T(8,128)}), f32[16,17,256]{2,1,0:T(8,128)S(1)}, u32[]{:S(2)}, u32[]{:S(2)}) %all-to-all-start.3) | async-done | bytes 278560 | tf_op jit(solution)/shard_map/all_to_all | solution.py:219
  189.8 3.5 %all-to-all-start.4 = ((f32[16,16,256]{2,1,0:T(8,128)}), f32[16,16,256]{2,1,0:T(8,128)S(1)}, u32[]{:S(2)}, u32[]{:S(2)}) async-start(f32[16,16,256]{2,1,0:T(8,128)} %get-tuple-element.23), calls=%async_computation.4 | async-start | bytes 524288 | tf_op jit(solution)/shard_map/all_to_all | solution.py:224
  193.4 2.7 slice.114
  196.0 5.0 %all-to-all-done.4 = f32[16,16,256]{2,1,0:T(8,128)S(1)} async-done(((f32[16,16,256]{2,1,0:T(8,128)}), f32[16,16,256]{2,1,0:T(8,128)S(1)}, u32[]{:S(2)}, u32[]{:S(2)}) %all-to-all-start.4) | async-done | bytes 262176 | tf_op jit(solution)/shard_map/all_to_all | solution.py:224
  201.0 3.7 %all-to-all-start.6 = ((bf16[4,512,256]{2,1,0:T(8,128)(2,1)}), bf16[4,512,256]{2,1,0:T(8,128)(2,1)S(1)}, u32[]{:S(2)}, u32[]{:S(2)}) async-start(bf16[4,512,256]{2,1,0:T(8,128)(2,1)} %bitcast.29), calls=%async_computation.6 | async-start | bytes 2097152 | tf_op jit(solution)/shard_map/all_to_all | solution.py:180
  205.6 15.5 %shard_map.142 = f32[128,32,128]{2,1,0:T(8,128)} custom-call(f32[2048]{0:T(1024)} %reshape.90.into_ref, f32[2048]{0:T(1024)} %reshape.91.outof_ref, f32[128,32,128]{2,1,0:T(8,128)} %bitcast.111, f32[128,32,128]{2,1,0:T(8,128)} %copy.57.value_ref, f32[16,32,128]{2,1,0:T(8,128)} %bitcast.117, f32[16,32,128]{2,1,0:T(8,128)} %reshape_reshape.3.start_ref, ...), custom_call_target="tpu_custom_call" | custom-call | flops 50331648 | bytes 6291456 | tf_op jit(solution)/shard_map/pallas_call | solution.py:84
  221.1 1.8 convert_element_type.95
  225.0 3.5 %all-to-all-start.5 = ((bf16[128,4,4,256]{3,0,1,2:T(8,128)(2,1)}), bf16[128,4,4,256]{3,0,1,2:T(8,128)(2,1)S(1)}, u32[]{:S(2)}, u32[]{:S(2)}) async-start(bf16[128,4,4,256]{3,0,1,2:T(8,128)(2,1)} %copy.53), calls=%async_computation.5 | async-start | bytes 2097152 | tf_op jit(solution)/shard_map/all_to_all | solution.py:231
  228.6 6.6 %copy.55 = bf16[1024,2048]{1,0:T(8,128)(2,1)} copy(bf16[1024,2048]{0,1:T(8,128)(2,1)} %all-gather.6.cloned.1.call-done) | data formatting | bytes 8388608 | tf_op jit(solution)/shard_map/all_gather | solution.py:177
  235.1 5.5 %all-to-all-done.5 = bf16[128,4,4,256]{3,0,1,2:T(8,128)(2,1)S(1)} async-done(((bf16[128,4,4,256]{3,0,1,2:T(8,128)(2,1)}), bf16[128,4,4,256]{3,0,1,2:T(8,128)(2,1)S(1)}, u32[]{:S(2)}, u32[]{:S(2)}) %all-to-all-start.5) | async-done | bytes 1048608 | tf_op jit(solution)/shard_map/all_to_all | solution.py:231
  240.6 6.1 %bitcast_convert_fusion = bf16[4,128,2048]{2,1,0:T(8,128)(2,1)} fusion(bf16[4,256,2048,1]{2,1,3,0:T(8,128)(2,1)} %bitcast.108, bf16[4,4,128,256]{3,2,1,0:T(8,128)(2,1)S(1)} %bitcast.114, bf16[128,4,4,256]{3,0,1,2:T(8,128)(2,1)S(1)} %all-to-all-done.5), kind=kOutput, calls=%fused_computation.2 | convolution fusion | flops 2152726528 | bytes 8388608 | tf_op jit(solution)/shard_map/ktac,acd->ktd/dot_general | solution.py:237
  248.1 7.2 %all-to-all-start.7 = ((f32[8,1,16,256]{3,2,1,0:T(8,128)}), f32[8,1,16,256]{3,2,1,0:T(8,128)S(1)}, u32[]{:S(2)}, u32[]{:S(2)}) async-start(f32[8,1,16,256]{3,2,1,0:T(8,128)} %broadcast_in_dim.44), calls=%async_computation.8 | async-start | bytes 262144 | tf_op jit(solution)/shard_map/all_to_all | solution.py:17
  255.3 5.3 %all-to-all-done.7 = f32[8,1,16,256]{3,2,1,0:T(8,128)S(1)} async-done(((f32[8,1,16,256]{3,2,1,0:T(8,128)}), f32[8,1,16,256]{3,2,1,0:T(8,128)S(1)}, u32[]{:S(2)}, u32[]{:S(2)}) %all-to-all-start.7) | async-done | bytes 131104 | tf_op jit(solution)/shard_map/all_to_all | solution.py:17
  261.3 15.6 %reduce-scatter.2.cloned.1.call-done = bf16[128,2048]{1,0:T(8,128)(2,1)} async-done(((bf16[512,2048]{1,0:T(8,128)(2,1)}), bf16[128,2048]{1,0:T(8,128)(2,1)}) %reduce-scatter.2.cloned.1.call-update) | async-done | bytes 524304 | tf_op jit(solution)/shard_map/reduce_scatter | solution.py:240
  276.9 2.0 fusion.22
  (88 shorter events, 32.6 us)
Async XLA Ops:
  7.2 4.1 %copy-start.13 = (bf16[256]{0:T(256)(128)(2,1)S(1)}, bf16[256]{0:T(256)(128)(2,1)}, u32[]{:S(2)}) copy-start(bf16[256]{0:T(256)(128)(2,1)} %param.22) | copy-start | bytes 1540
  7.2 4.1 %copy-start.10 = (bf16[128,256]{1,0:T(8,128)(2,1)S(1)}, bf16[128,256]{1,0:T(8,128)(2,1)}, u32[]{:S(2)}) copy-start(bf16[128,256]{1,0:T(8,128)(2,1)} %param.21) | copy-start | bytes 196612
  7.2 4.1 %copy-start.9 = (bf16[256,160]{0,1:T(8,128)(2,1)S(1)}, bf16[256,160]{0,1:T(8,128)(2,1)}, u32[]{:S(2)}) copy-start(bf16[256,160]{0,1:T(8,128)(2,1)} %param.20) | copy-start | bytes 245764
  7.2 110.0 %all-gather.4.cloned.1.call-start = ((), (), s32[]{:S(2)}) async-start(), calls=%async_computation.9 | async-start | bytes 8912896 | tf_op jit(solution)/shard_map/all_gather | solution.py:156
  13.0 8.7 %copy-start.8 = (bf16[256,256]{1,0:T(8,128)(2,1)S(1)}, bf16[256,256]{1,0:T(8,128)(2,1)}, u32[]{:S(2)}) copy-start(bf16[256,256]{1,0:T(8,128)(2,1)} %param.25) | copy-start | bytes 393220
  13.0 8.8 %copy-start.6 = (bf16[2,256,256]{2,1,0:T(8,128)(2,1)S(1)}, bf16[2,256,256]{2,1,0:T(8,128)(2,1)}, u32[]{:S(2)}) copy-start(bf16[2,256,256]{2,1,0:T(8,128)(2,1)} %param.17) | copy-start | bytes 786436
  13.0 51.4 %all-to-all-start.1 = ((bf16[16,289,256]{2,1,0:T(8,128)(2,1)}), bf16[16,289,256]{2,1,0:T(8,128)(2,1)S(1)}, u32[]{:S(2)}, u32[]{:S(2)}) async-start(bf16[16,289,256]{2,1,0:T(8,128)(2,1)} %broadcast_in_dim.19), calls=%async_computation.1 | async-start | bytes 4849664 | tf_op jit(solution)/shard_map/all_to_all | solution.py:165
  64.4 2.4 copy-start
  66.6 6.3 %copy-start.14 = (bf16[256]{0:T(256)(128)(2,1)S(1)}, bf16[256]{0:T(256)(128)(2,1)}, u32[]{:S(2)}) copy-start(bf16[256]{0:T(256)(128)(2,1)} %param.19) | copy-start | bytes 1540
  66.6 6.3 %copy-start.12 = (bf16[4,256]{1,0:T(4,128)(2,1)S(1)}, bf16[4,256]{1,0:T(4,128)(2,1)}, u32[]{:S(2)}) copy-start(bf16[4,256]{1,0:T(4,128)(2,1)} %param.18) | copy-start | bytes 6148
  66.8 43.5 %all-to-all-start = ((bf16[8,3,256,256]{2,3,1,0:T(8,128)(2,1)}), bf16[8,3,256,256]{2,3,1,0:T(8,128)(2,1)S(1)}, u32[]{:S(2)}, u32[]{:S(2)}) async-start(bf16[8,3,256,256]{2,3,1,0:T(8,128)(2,1)} %broadcast_in_dim.17), calls=%async_computation | async-start | bytes 6291456 | tf_op jit(solution)/shard_map/all_to_all | solution.py:17
  72.9 155.7 %all-gather.6.cloned.1.call-start = ((), (), s32[]{:S(2)}) async-start(), calls=%async_computation.11 | async-start | bytes 5242880 | tf_op jit(solution)/shard_map/all_gather | solution.py:177
  124.2 2.0 copy-start.3
  126.2 6.2 %copy-start.7 = (f32[16,4096]{1,0:T(8,128)S(1)}, f32[16,4096]{1,0:T(8,128)}, u32[]{:S(2)}) copy-start(f32[16,4096]{1,0:T(8,128)} %param.23) | copy-start | bytes 786436
  128.6 5.3 %copy-start.15 = (s32[8]{0:T(128)S(1)}, s32[8]{0:T(128)}, u32[]{:S(2)}) copy-start(s32[8]{0:T(128)} %param.14) | copy-start | bytes 100
  128.6 20.3 %all-to-all-start.2 = ((bf16[16,128,256]{2,1,0:T(8,128)(2,1)}), bf16[16,128,256]{2,1,0:T(8,128)(2,1)S(1)}, u32[]{:S(2)}, u32[]{:S(2)}) async-start(bf16[16,128,256]{2,1,0:T(8,128)(2,1)} %bitcast.16), calls=%async_computation.2 | async-start | bytes 2097152 | tf_op jit(solution)/shard_map/all_to_all | solution.py:189
  132.4 17.1 %copy-start.1 = (bf16[16,20,8,256]{3,2,0,1:T(8,128)(2,1)S(1)}, bf16[16,20,8,256]{3,2,0,1:T(8,128)(2,1)}, u32[]{:S(2)}) copy-start(bf16[16,20,8,256]{3,2,0,1:T(8,128)(2,1)} %copy.59) | copy-start | bytes 3932164
  149.5 2.1 copy-start.5
  171.7 15.6 %all-to-all-start.3 = ((f32[16,17,256]{2,1,0:T(8,128)}), f32[16,17,256]{2,1,0:T(8,128)S(1)}, u32[]{:S(2)}, u32[]{:S(2)}) async-start(f32[16,17,256]{2,1,0:T(8,128)} %maximum_bitcast_fusion), calls=%async_computation.3 | async-start | bytes 786432 | tf_op jit(solution)/shard_map/all_to_all | solution.py:219
  187.3 0.7 copy-start.4
  189.8 11.2 %all-to-all-start.4 = ((f32[16,16,256]{2,1,0:T(8,128)}), f32[16,16,256]{2,1,0:T(8,128)S(1)}, u32[]{:S(2)}, u32[]{:S(2)}) async-start(f32[16,16,256]{2,1,0:T(8,128)} %get-tuple-element.23), calls=%async_computation.4 | async-start | bytes 524288 | tf_op jit(solution)/shard_map/all_to_all | solution.py:224
  201.0 24.0 %all-to-all-start.6 = ((bf16[4,512,256]{2,1,0:T(8,128)(2,1)}), bf16[4,512,256]{2,1,0:T(8,128)(2,1)S(1)}, u32[]{:S(2)}, u32[]{:S(2)}) async-start(bf16[4,512,256]{2,1,0:T(8,128)(2,1)} %bitcast.29), calls=%async_computation.6 | async-start | bytes 2097152 | tf_op jit(solution)/shard_map/all_to_all | solution.py:180
  225.0 15.6 %all-to-all-start.5 = ((bf16[128,4,4,256]{3,0,1,2:T(8,128)(2,1)}), bf16[128,4,4,256]{3,0,1,2:T(8,128)(2,1)S(1)}, u32[]{:S(2)}, u32[]{:S(2)}) async-start(bf16[128,4,4,256]{3,0,1,2:T(8,128)(2,1)} %copy.53), calls=%async_computation.5 | async-start | bytes 2097152 | tf_op jit(solution)/shard_map/all_to_all | solution.py:231
  228.5 48.4 %reduce-scatter.2.cloned.1.call-start = ((), (), s32[]{:S(2)}) async-start(), calls=%async_computation.10 | async-start | bytes 2621440 | tf_op jit(solution)/shard_map/reduce_scatter | solution.py:240
  246.7 0.7 copy-start.11
  246.7 8.6 %copy-start.16 = (s32[8]{0:T(128)S(1)}, s32[8]{0:T(128)}, u32[]{:S(2)}) copy-start(s32[8]{0:T(128)} %param.15) | copy-start | bytes 100
  246.7 30.2 %copy-start.2 = (bf16[1,128,2048]{2,1,0:T(8,128)(2,1)S(1)}, bf16[1,128,2048]{2,1,0:T(8,128)(2,1)}, u32[]{:S(2)}) copy-start(bf16[1,128,2048]{2,1,0:T(8,128)(2,1)} %param.13) | copy-start | bytes 1572868
  248.1 12.5 %all-to-all-start.7 = ((f32[8,1,16,256]{3,2,1,0:T(8,128)}), f32[8,1,16,256]{3,2,1,0:T(8,128)S(1)}, u32[]{:S(2)}, u32[]{:S(2)}) async-start(f32[8,1,16,256]{3,2,1,0:T(8,128)} %broadcast_in_dim.44), calls=%async_computation.8 | async-start | bytes 262144 | tf_op jit(solution)/shard_map/all_to_all | solution.py:17
Sparse Core Ops, SparseCore 0:
  11.4 95.6 all-gather.3
  117.3 54.9 all-gather.5
  246.9 29.9 reduce-scatter.1

commit v9 on v8

--- a/solution.py
+++ b/solution.py
@@ -56,7 +56,7 @@
 
     held0 = tuple(start_ref[n] for n in range(states))
     acc0 = jnp.zeros((SUB, LANES), jnp.float32)
-    held, acc = lax.fori_loop(0, steps, step, (held0, acc0), unroll=2)
+    held, acc = lax.fori_loop(0, steps, step, (held0, acc0), unroll=4)
     if not emit:
         for n in range(states):
             end_ref[n] = held[n]
@@ -154,10 +154,10 @@
     scale = lax.rsqrt(jnp.mean(tokens * tokens, axis=-1, keepdims=True) + 1e-05)
     normed = (tokens * scale * norm_gain.astype(jnp.float32)).astype(jnp.bfloat16)
     normed_all = lax.all_gather(normed, seq, axis=0, tiled=True)
-    pieces = jnp.concatenate((in_weight, out_weight.T[None]), axis=0)
-    pieces_all = gather_a2a(pieces, "req", 1)
-    w_in = pieces_all[:2]
-    w_out_t = pieces_all[2]
+    pieces = jnp.concatenate((in_weight[0], in_weight[1], out_weight.T), axis=1)
+    pieces_all = gather_a2a(pieces, "req", 0)
+    w_flat = pieces_all[:, : 2 * width]
+    w_out_t = pieces_all[:, 2 * width :]
     xproj_w, dt_w, dt_b, _ = lax.optimization_barrier((xproj_weight, dt_weight, dt_bias, normed))
     proj_cols = xproj_w.shape[1]
     small = jnp.concatenate((xproj_w.T, dt_w, dt_b[None]), axis=0)
@@ -168,10 +168,9 @@
         RANK, total_inner
     )
     dt_bias_full = small_all[:, proj_cols + RANK].reshape(total_inner)
-    w_in, xproj_full, dt_full, dt_bias_full = lax.optimization_barrier(
-        (w_in, xproj_full, dt_full, dt_bias_full)
-    )
-    w_flat = jnp.concatenate((w_in[0], w_in[1]), axis=1)
+    w_flat, xproj_full, dt_full, dt_bias_full = lax.optimization_barrier(
+        (w_flat, xproj_full, dt_full, dt_bias_full)
+    )
     both = jnp.dot(normed_all, w_flat, preferred_element_type=jnp.float32)
     w_late, _ = lax.optimization_barrier((w_out_t, normed_all))
     w_col = lax.all_gather(w_late.T, "sz", axis=0, tiled=False)

time: 287 us -> 292 us (1.017)
  waiting for transfers between devices: 125 us -> 135 us
    all_gather x1, waiting for transfers between devices: 0.02 us -> 38.5 us  [per_device(): normed_all = lax.all_gather(normed, seq, axis=0, tiled=True)]
    all_to_all x1, waiting for transfers between devices: 42.4 us -> 5.36 us  [per_device(): lax.all_to_all(copies, seq, split_axis=0, concat_axis=0, tiled=True)]
    all_to_all x2, waiting for transfers between devices: 34.6 us -> 42.6 us  [gather_a2a(): lax.all_to_all(copies, axis, split_axis=0, concat_axis=0, tiled=True)]
    unnamed x39 -> x41, local copies, waits for them, and re-layouts: 9.56 us -> 9.57 us
  transfers between devices with their start and end apart: 11 -> 11, of which waited for: 8 -> 9; matrix products, arithmetic and copies ran while one was open for 21% -> 20% of each run, Pallas kernels for 10% -> 9%
where the time goes in v9:
time: 292 us; the launch traced here: 291 us
  waiting for transfers between devices  135 us (46%)
  local copies, waits for them, and re-layouts  43.9 us (15%)
  starting transfers between devices  42 us (14%)
  Pallas kernels  27.1 us (9%)
  matrix products  15 us (5%)
  between operations  14.1 us (5%)
  other arithmetic  13.8 us (5%)
    all_to_all x2, waiting for transfers between devices, gather_a2a(): lax.all_to_all(copies, axis, split_axis=0, concat_axis=0, tiled=True)  42.6 us
    all_gather x1, waiting for transfers between devices, per_device(): normed_all = lax.all_gather(normed, seq, axis=0, tiled=True)  38.5 us
    pallas_call x2, Pallas kernels, run_scan(): pl.pallas_call(functools.partial(scan_body, emit), grid=(chunks,), in_spe...  25.4 us
    reduce_scatter x1, waiting for transfers between devices, per_device(): lax.psum_scatter(partial.reshape(cols_n * rows, model), 'sy', scatter_dim...  16.5 us
    all_to_all x1, waiting for transfers between devices, per_device(): lax.all_to_all(inner, seq, split_axis=0, concat_axis=1, tiled=True)  14.5 us
    all_to_all x2, starting transfers between devices, gather_a2a(): lax.all_to_all(copies, axis, split_axis=0, concat_axis=0, tiled=True)  13.7 us
    unnamed x41, local copies, waits for them, and re-layouts  9.57 us
    all_to_all x1, starting transfers between devices, per_device(): lax.all_to_all(copies, seq, split_axis=0, concat_axis=0, tiled=True)  7.94 us
  transfers between devices with their start and end apart: 11, of which 9 were waited for; matrix products, arithmetic and copies ran while one was open for 20% of the time, Pallas kernels for 9%

profile of v9, /device:TPU:1, one launch (start us, length us, event | category | flops | bytes accessed | tf_op | source)
XLA Modules:
  0.0 290.6 jit_solution(1152432822711586878)
XLA Ops:
  9.2 2.0 fusion.13
  11.5 1.8 broadcast_in_dim.14
  13.4 5.9 %all-to-all-start = ((bf16[8,256,768]{1,2,0:T(8,128)(2,1)}), bf16[8,256,768]{1,2,0:T(8,128)(2,1)S(1)}, u32[]{:S(2)}, u32[]{:S(2)}) async-start(bf16[8,256,768]{1,2,0:T(8,128)(2,1)} %broadcast_in_dim.14), calls=%async_computation | async-start | bytes 6291456 | tf_op jit(solution)/shard_map/all_to_all | solution.py:17
  19.4 37.4 %all-to-all-done = bf16[8,256,768]{1,2,0:T(8,128)(2,1)S(1)} async-done(((bf16[8,256,768]{1,2,0:T(8,128)(2,1)}), bf16[8,256,768]{1,2,0:T(8,128)(2,1)S(1)}, u32[]{:S(2)}, u32[]{:S(2)}) %all-to-all-start) | async-done | bytes 3145760 | tf_op jit(solution)/shard_map/all_to_all | solution.py:17
  58.3 7.9 %all-to-all-start.1 = ((bf16[16,289,256]{2,1,0:T(8,128)(2,1)}), bf16[16,289,256]{2,1,0:T(8,128)(2,1)}, u32[]{:S(2)}, u32[]{:S(2)}) async-start(bf16[16,289,256]{2,1,0:T(8,128)(2,1)} %broadcast_in_dim.16), calls=%async_computation.1 | async-start | bytes 4849664 | tf_op jit(solution)/shard_map/all_to_all | solution.py:165
  66.4 2.8 copy.44
  69.2 2.3 slice.92
  71.5 38.5 %all-gather.4.cloned.1.call-done = bf16[2048,2048]{1,0:T(8,128)(2,1)} async-done(((bf16[128,2048]{1,0:T(8,128)(2,1)}), bf16[2048,2048]{1,0:T(8,128)(2,1)}) %all-gather.4.cloned.1.call-update) | async-done | bytes 8388624 | tf_op jit(solution)/shard_map/all_gather | solution.py:156
  110.0 5.4 %all-to-all-done.1 = bf16[16,289,256]{2,1,0:T(8,128)(2,1)} async-done(((bf16[16,289,256]{2,1,0:T(8,128)(2,1)}), bf16[16,289,256]{2,1,0:T(8,128)(2,1)}, u32[]{:S(2)}, u32[]{:S(2)}) %all-to-all-start.1) | async-done | bytes 2367520 | tf_op jit(solution)/shard_map/all_to_all | solution.py:165
  118.0 2.5 slice.81
  120.5 2.3 copy.60
  123.8 7.0 %fusion.25 = f32[2048,512]{1,0:T(8,128)S(1)} fusion(bf16[2048,2048]{1,0:T(8,128)(2,1)} %all-gather.4.cloned.1.call-done, bf16[2048,512]{1,0:T(8,128)(2,1)S(1)} %slice.79), kind=kOutput, calls=%fused_computation.47 | convolution fusion | flops 4294967296 | bytes 14680064 | tf_op jit(solution)/shard_map/dot_general | solution.py:174
  132.7 2.4 multiply_convert_fusion
  135.1 3.8 %all-to-all-start.2 = ((bf16[16,128,256]{2,1,0:T(8,128)(2,1)}), bf16[16,128,256]{2,1,0:T(8,128)(2,1)S(1)}, u32[]{:S(2)}, u32[]{:S(2)}) async-start(bf16[16,128,256]{2,1,0:T(8,128)(2,1)} %bitcast.14), calls=%async_computation.2 | async-start | bytes 2097152 | tf_op jit(solution)/shard_map/all_to_all | solution.py:188
  141.7 14.5 %all-to-all-done.2 = bf16[16,128,256]{2,1,0:T(8,128)(2,1)S(1)} async-done(((bf16[16,128,256]{2,1,0:T(8,128)(2,1)}), bf16[16,128,256]{2,1,0:T(8,128)(2,1)S(1)}, u32[]{:S(2)}, u32[]{:S(2)}) %all-to-all-start.2) | async-done | bytes 1048608 | tf_op jit(solution)/shard_map/all_to_all | solution.py:188
  162.2 1.9 copy.57.value_ref
  164.8 10.8 %shard_map.140 = (f32[16,32,128]{2,1,0:T(8,128)}, f32[1,32,128]{2,1,0:T(8,128)}) custom-call(f32[2048]{0:T(1024)} %reshape.90.into_ref, f32[2048]{0:T(1024)} %reshape.91.outof_ref, f32[128,32,128]{2,1,0:T(8,128)} %bitcast.104, f32[128,32,128]{2,1,0:T(8,128)} %copy.57.value_ref, f32[16,32,128]{2,1,0:T(8,128)} %bitcast.112, ...), custom_call_target="tpu_custom_call" | custom-call | flops 50331648 | bytes 4194304 | tf_op jit(solution)/shard_map/pallas_call | solution.py:84
  178.3 5.7 %all-to-all-start.3 = ((f32[16,17,256]{2,1,0:T(8,128)}), f32[16,17,256]{2,1,0:T(8,128)S(1)}, u32[]{:S(2)}, u32[]{:S(2)}) async-start(f32[16,17,256]{2,1,0:T(8,128)} %maximum_bitcast_fusion), calls=%async_computation.3 | async-start | bytes 786432 | tf_op jit(solution)/shard_map/all_to_all | solution.py:218
  185.3 7.5 %all-to-all-done.3.pair_ref = f32[16,17,256]{2,1,0:T(8,128)S(1)} async-done(((f32[16,17,256]{2,1,0:T(8,128)}), f32[16,17,256]{2,1,0:T(8,128)S(1)}, u32[]{:S(2)}, u32[]{:S(2)}) %all-to-all-start.3) | async-done | bytes 278560 | tf_op jit(solution)/shard_map/all_to_all | solution.py:218
  195.2 3.5 %all-to-all-start.4 = ((f32[16,16,256]{2,1,0:T(8,128)}), f32[16,16,256]{2,1,0:T(8,128)S(1)}, u32[]{:S(2)}, u32[]{:S(2)}) async-start(f32[16,16,256]{2,1,0:T(8,128)} %get-tuple-element.23), calls=%async_computation.4 | async-start | bytes 524288 | tf_op jit(solution)/shard_map/all_to_all | solution.py:223
  198.8 2.7 slice.107
  201.5 4.8 %all-to-all-done.4 = f32[16,16,256]{2,1,0:T(8,128)S(1)} async-done(((f32[16,16,256]{2,1,0:T(8,128)}), f32[16,16,256]{2,1,0:T(8,128)S(1)}, u32[]{:S(2)}, u32[]{:S(2)}) %all-to-all-start.4) | async-done | bytes 262176 | tf_op jit(solution)/shard_map/all_to_all | solution.py:223
  206.3 3.7 %all-to-all-start.6 = ((bf16[4,512,256]{2,1,0:T(8,128)(2,1)}), bf16[4,512,256]{2,1,0:T(8,128)(2,1)S(1)}, u32[]{:S(2)}, u32[]{:S(2)}) async-start(bf16[4,512,256]{2,1,0:T(8,128)(2,1)} %bitcast.27), calls=%async_computation.6 | async-start | bytes 2097152 | tf_op jit(solution)/shard_map/all_to_all | solution.py:179
  210.9 14.6 %shard_map.142 = f32[128,32,128]{2,1,0:T(8,128)} custom-call(f32[2048]{0:T(1024)} %reshape.90.into_ref, f32[2048]{0:T(1024)} %reshape.91.outof_ref, f32[128,32,128]{2,1,0:T(8,128)} %bitcast.105, f32[128,32,128]{2,1,0:T(8,128)} %copy.57.value_ref, f32[16,32,128]{2,1,0:T(8,128)} %bitcast.113, f32[16,32,128]{2,1,0:T(8,128)} %reshape_reshape.3.start_ref, ...), custom_call_target="tpu_custom_call" | custom-call | flops 50331648 | bytes 6291456 | tf_op jit(solution)/shard_map/pallas_call | solution.py:84
  229.4 3.5 %all-to-all-start.5 = ((bf16[128,4,4,256]{3,0,1,2:T(8,128)(2,1)}), bf16[128,4,4,256]{3,0,1,2:T(8,128)(2,1)S(1)}, u32[]{:S(2)}, u32[]{:S(2)}) async-start(bf16[128,4,4,256]{3,0,1,2:T(8,128)(2,1)} %copy.53), calls=%async_computation.5 | async-start | bytes 2097152 | tf_op jit(solution)/shard_map/all_to_all | solution.py:230
  233.0 6.6 %copy.55 = bf16[1024,2048]{1,0:T(8,128)(2,1)} copy(bf16[1024,2048]{0,1:T(8,128)(2,1)} %all-gather.6.cloned.1.call-done) | data formatting | bytes 8388608 | tf_op jit(solution)/shard_map/all_gather | solution.py:176
  239.5 4.8 %all-to-all-done.5 = bf16[128,4,4,256]{3,0,1,2:T(8,128)(2,1)S(1)} async-done(((bf16[128,4,4,256]{3,0,1,2:T(8,128)(2,1)}), bf16[128,4,4,256]{3,0,1,2:T(8,128)(2,1)S(1)}, u32[]{:S(2)}, u32[]{:S(2)}) %all-to-all-start.5) | async-done | bytes 1048608 | tf_op jit(solution)/shard_map/all_to_all | solution.py:230
  244.4 6.1 %bitcast_convert_fusion = bf16[4,128,2048]{2,1,0:T(8,128)(2,1)} fusion(bf16[4,256,2048,1]{2,1,3,0:T(8,128)(2,1)} %bitcast.102, bf16[4,4,128,256]{3,2,1,0:T(8,128)(2,1)S(1)} %bitcast.108, bf16[128,4,4,256]{3,0,1,2:T(8,128)(2,1)S(1)} %all-to-all-done.5), kind=kOutput, calls=%fused_computation.2 | convolution fusion | flops 2152726528 | bytes 8388608 | tf_op jit(solution)/shard_map/ktac,acd->ktd/dot_general | solution.py:236
  251.8 7.8 %all-to-all-start.7 = ((f32[8,1,16,256]{3,2,1,0:T(8,128)}), f32[8,1,16,256]{3,2,1,0:T(8,128)S(1)}, u32[]{:S(2)}, u32[]{:S(2)}) async-start(f32[8,1,16,256]{3,2,1,0:T(8,128)} %broadcast_in_dim.19), calls=%async_computation.8 | async-start | bytes 262144 | tf_op jit(solution)/shard_map/all_to_all | solution.py:17
  259.7 5.3 %all-to-all-done.7 = f32[8,1,16,256]{3,2,1,0:T(8,128)S(1)} async-done(((f32[8,1,16,256]{3,2,1,0:T(8,128)}), f32[8,1,16,256]{3,2,1,0:T(8,128)S(1)}, u32[]{:S(2)}, u32[]{:S(2)}) %all-to-all-start.7) | async-done | bytes 131104 | tf_op jit(solution)/shard_map/all_to_all | solution.py:17
  265.6 16.5 %reduce-scatter.2.cloned.1.call-done = bf16[128,2048]{1,0:T(8,128)(2,1)} async-done(((bf16[512,2048]{1,0:T(8,128)(2,1)}), bf16[128,2048]{1,0:T(8,128)(2,1)}) %reduce-scatter.2.cloned.1.call-update) | async-done | bytes 524304 | tf_op jit(solution)/shard_map/reduce_scatter | solution.py:239
  282.2 2.0 fusion.18
  (88 shorter events, 32.4 us)
Async XLA Ops:
  7.2 4.1 %copy-start.7 = (bf16[2,256,256]{2,1,0:T(8,128)(2,1)S(1)}, bf16[2,256,256]{2,1,0:T(8,128)(2,1)}, u32[]{:S(2)}) copy-start(bf16[2,256,256]{2,1,0:T(8,128)(2,1)} %param.17) | copy-start | bytes 786436
  7.2 4.3 %copy-start.8 = (bf16[256,256]{1,0:T(8,128)(2,1)S(1)}, bf16[256,256]{1,0:T(8,128)(2,1)}, u32[]{:S(2)}) copy-start(bf16[256,256]{1,0:T(8,128)(2,1)} %param.25) | copy-start | bytes 393220
  7.2 102.8 %all-gather.4.cloned.1.call-start = ((), (), s32[]{:S(2)}) async-start(), calls=%async_computation.9 | async-start | bytes 8912896 | tf_op jit(solution)/shard_map/all_gather | solution.py:156
  13.4 5.9 %copy-start.13 = (bf16[256]{0:T(256)(128)(2,1)S(1)}, bf16[256]{0:T(256)(128)(2,1)}, u32[]{:S(2)}) copy-start(bf16[256]{0:T(256)(128)(2,1)} %param.22) | copy-start | bytes 1540
  13.4 5.9 %copy-start.9 = (bf16[256,160]{0,1:T(8,128)(2,1)S(1)}, bf16[256,160]{0,1:T(8,128)(2,1)}, u32[]{:S(2)}) copy-start(bf16[256,160]{0,1:T(8,128)(2,1)} %param.20) | copy-start | bytes 245764
  13.4 5.9 %copy-start.10 = (bf16[128,256]{1,0:T(8,128)(2,1)S(1)}, bf16[128,256]{1,0:T(8,128)(2,1)}, u32[]{:S(2)}) copy-start(bf16[128,256]{1,0:T(8,128)(2,1)} %param.21) | copy-start | bytes 196612
  13.4 43.4 %all-to-all-start = ((bf16[8,256,768]{1,2,0:T(8,128)(2,1)}), bf16[8,256,768]{1,2,0:T(8,128)(2,1)S(1)}, u32[]{:S(2)}, u32[]{:S(2)}) async-start(bf16[8,256,768]{1,2,0:T(8,128)(2,1)} %broadcast_in_dim.14), calls=%async_computation | async-start | bytes 6291456 | tf_op jit(solution)/shard_map/all_to_all | solution.py:17
  58.3 8.0 %copy-start.14 = (bf16[256]{0:T(256)(128)(2,1)S(1)}, bf16[256]{0:T(256)(128)(2,1)}, u32[]{:S(2)}) copy-start(bf16[256]{0:T(256)(128)(2,1)} %param.19) | copy-start | bytes 1540
  58.3 57.0 %all-to-all-start.1 = ((bf16[16,289,256]{2,1,0:T(8,128)(2,1)}), bf16[16,289,256]{2,1,0:T(8,128)(2,1)}, u32[]{:S(2)}, u32[]{:S(2)}) async-start(bf16[16,289,256]{2,1,0:T(8,128)(2,1)} %broadcast_in_dim.16), calls=%async_computation.1 | async-start | bytes 4849664 | tf_op jit(solution)/shard_map/all_to_all | solution.py:165
  66.3 166.7 %all-gather.6.cloned.1.call-start = ((), (), s32[]{:S(2)}) async-start(), calls=%async_computation.11 | async-start | bytes 5242880 | tf_op jit(solution)/shard_map/all_gather | solution.py:176
  69.2 40.8 %copy-start.12 = (bf16[4,256]{1,0:T(4,128)(2,1)S(1)}, bf16[4,256]{1,0:T(4,128)(2,1)}, u32[]{:S(2)}) copy-start(bf16[4,256]{1,0:T(4,128)(2,1)} %param.18) | copy-start | bytes 6148
  118.0 5.6 %copy-start = (bf16[8,256,768]{2,1,0:T(8,128)(2,1)S(1)}, bf16[8,256,768]{2,1,0:T(8,128)(2,1)}, u32[]{:S(2)}) copy-start(bf16[8,256,768]{2,1,0:T(8,128)(2,1)} %copy.44) | copy-start | bytes 9437188
  130.8 2.0 copy-start.3
  132.7 6.2 %copy-start.6 = (f32[16,4096]{1,0:T(8,128)S(1)}, f32[16,4096]{1,0:T(8,128)}, u32[]{:S(2)}) copy-start(f32[16,4096]{1,0:T(8,128)} %param.23) | copy-start | bytes 786436
  135.1 5.3 %copy-start.15 = (s32[8]{0:T(128)S(1)}, s32[8]{0:T(128)}, u32[]{:S(2)}) copy-start(s32[8]{0:T(128)} %param.14) | copy-start | bytes 100
  135.1 21.1 %all-to-all-start.2 = ((bf16[16,128,256]{2,1,0:T(8,128)(2,1)}), bf16[16,128,256]{2,1,0:T(8,128)(2,1)S(1)}, u32[]{:S(2)}, u32[]{:S(2)}) async-start(bf16[16,128,256]{2,1,0:T(8,128)(2,1)} %bitcast.14), calls=%async_computation.2 | async-start | bytes 2097152 | tf_op jit(solution)/shard_map/all_to_all | solution.py:188
  138.9 18.0 %copy-start.1 = (bf16[16,20,8,256]{3,2,0,1:T(8,128)(2,1)S(1)}, bf16[16,20,8,256]{3,2,0,1:T(8,128)(2,1)}, u32[]{:S(2)}) copy-start(bf16[16,20,8,256]{3,2,0,1:T(8,128)(2,1)} %copy.61) | copy-start | bytes 3932164
  156.8 2.1 copy-start.5
  178.3 14.5 %all-to-all-start.3 = ((f32[16,17,256]{2,1,0:T(8,128)}), f32[16,17,256]{2,1,0:T(8,128)S(1)}, u32[]{:S(2)}, u32[]{:S(2)}) async-start(f32[16,17,256]{2,1,0:T(8,128)} %maximum_bitcast_fusion), calls=%async_computation.3 | async-start | bytes 786432 | tf_op jit(solution)/shard_map/all_to_all | solution.py:218
  192.7 0.7 copy-start.4
  195.2 11.0 %all-to-all-start.4 = ((f32[16,16,256]{2,1,0:T(8,128)}), f32[16,16,256]{2,1,0:T(8,128)S(1)}, u32[]{:S(2)}, u32[]{:S(2)}) async-start(f32[16,16,256]{2,1,0:T(8,128)} %get-tuple-element.23), calls=%async_computation.4 | async-start | bytes 524288 | tf_op jit(solution)/shard_map/all_to_all | solution.py:223
  206.3 23.1 %all-to-all-start.6 = ((bf16[4,512,256]{2,1,0:T(8,128)(2,1)}), bf16[4,512,256]{2,1,0:T(8,128)(2,1)S(1)}, u32[]{:S(2)}, u32[]{:S(2)}) async-start(bf16[4,512,256]{2,1,0:T(8,128)(2,1)} %bitcast.27), calls=%async_computation.6 | async-start | bytes 2097152 | tf_op jit(solution)/shard_map/all_to_all | solution.py:179
  229.4 15.0 %all-to-all-start.5 = ((bf16[128,4,4,256]{3,0,1,2:T(8,128)(2,1)}), bf16[128,4,4,256]{3,0,1,2:T(8,128)(2,1)S(1)}, u32[]{:S(2)}, u32[]{:S(2)}) async-start(bf16[128,4,4,256]{3,0,1,2:T(8,128)(2,1)} %copy.53), calls=%async_computation.5 | async-start | bytes 2097152 | tf_op jit(solution)/shard_map/all_to_all | solution.py:230
  232.9 49.3 %reduce-scatter.2.cloned.1.call-start = ((), (), s32[]{:S(2)}) async-start(), calls=%async_computation.10 | async-start | bytes 2621440 | tf_op jit(solution)/shard_map/reduce_scatter | solution.py:239
  250.5 0.7 copy-start.11
  250.5 9.2 %copy-start.16 = (s32[8]{0:T(128)S(1)}, s32[8]{0:T(128)}, u32[]{:S(2)}) copy-start(s32[8]{0:T(128)} %param.15) | copy-start | bytes 100
  250.5 31.7 %copy-start.2 = (bf16[1,128,2048]{2,1,0:T(8,128)(2,1)S(1)}, bf16[1,128,2048]{2,1,0:T(8,128)(2,1)}, u32[]{:S(2)}) copy-start(bf16[1,128,2048]{2,1,0:T(8,128)(2,1)} %param.13) | copy-start | bytes 1572868
  251.8 13.1 %all-to-all-start.7 = ((f32[8,1,16,256]{3,2,1,0:T(8,128)}), f32[8,1,16,256]{3,2,1,0:T(8,128)S(1)}, u32[]{:S(2)}, u32[]{:S(2)}) async-start(f32[8,1,16,256]{3,2,1,0:T(8,128)} %broadcast_in_dim.19), calls=%async_computation.8 | async-start | bytes 262144 | tf_op jit(solution)/shard_map/all_to_all | solution.py:17
Sparse Core Ops, SparseCore 0:
  11.4 98.5 all-gather.3
  111.6 63.2 all-gather.5
  250.6 31.4 reduce-scatter.1

commit v10 on v9

--- a/solution.py
+++ b/solution.py
@@ -158,21 +158,15 @@
     pieces_all = gather_a2a(pieces, "req", 0)
     w_flat = pieces_all[:, : 2 * width]
     w_out_t = pieces_all[:, 2 * width :]
-    xproj_w, dt_w, dt_b, _ = lax.optimization_barrier((xproj_weight, dt_weight, dt_bias, normed))
-    proj_cols = xproj_w.shape[1]
-    small = jnp.concatenate((xproj_w.T, dt_w, dt_b[None]), axis=0)
-    copies = jnp.broadcast_to(small[None], (seq_count,) + small.shape)
-    small_all = lax.all_to_all(copies, seq, split_axis=0, concat_axis=0, tiled=True)
-    xproj_full = jnp.swapaxes(small_all[:, :proj_cols], 1, 2).reshape(total_inner, proj_cols)
-    dt_full = jnp.swapaxes(small_all[:, proj_cols : proj_cols + RANK], 0, 1).reshape(
-        RANK, total_inner
-    )
+    proj_cols = xproj_weight.shape[1]
+    small = jnp.concatenate((xproj_weight.T, dt_weight, dt_bias[None]), axis=0)
+    small_late, _ = lax.optimization_barrier((small, normed_all))
+    small_all = lax.all_gather(small_late, seq, axis=0, tiled=False)
+    xproj_g = small_all[:, :proj_cols]
+    dt_g = small_all[:, proj_cols : proj_cols + RANK]
     dt_bias_full = small_all[:, proj_cols + RANK].reshape(total_inner)
-    w_flat, xproj_full, dt_full, dt_bias_full = lax.optimization_barrier(
-        (w_flat, xproj_full, dt_full, dt_bias_full)
-    )
     both = jnp.dot(normed_all, w_flat, preferred_element_type=jnp.float32)
-    w_late, _ = lax.optimization_barrier((w_out_t, normed_all))
+    w_late, _ = lax.optimization_barrier((w_out_t, small_all))
     w_col = lax.all_gather(w_late.T, "sz", axis=0, tiled=False)
     xin = both[:, :width]
     zgate = both[:, width:].astype(jnp.bfloat16)
@@ -186,14 +180,19 @@
         convolved = convolved + taps[tap] * padded[tap : tap + span, :]
     inner = jax.nn.silu(convolved).astype(jnp.bfloat16)
     inner_tok = lax.all_to_all(inner, seq, split_axis=0, concat_axis=1, tiled=True)
-    proj = jnp.dot(inner_tok, xproj_full, preferred_element_type=jnp.float32)
+    proj = jnp.einsum(
+        "tsc,skc->tk", inner_tok.reshape(rows, seq_count, width), xproj_g,
+        preferred_element_type=jnp.float32,
+    )
     length_here = lax.dynamic_index_in_dim(lengths, req_index, 0, keepdims=False)
     positions = seq_index * rows + jnp.arange(rows, dtype=jnp.int32)
     live = (positions < length_here).astype(jnp.float32)
     rate_low = proj[:, :RANK].astype(jnp.bfloat16)
     delta_tok = (
         jax.nn.softplus(
-            jnp.dot(rate_low, dt_full, preferred_element_type=jnp.float32)
+            jnp.einsum("tk,skc->tsc", rate_low, dt_g, preferred_element_type=jnp.float32).reshape(
+                rows, total_inner
+            )
             + dt_bias_full.astype(jnp.float32)
         )
         * live[:, None]

time: 292 us -> 312 us (1.068)
  waiting for transfers between devices: 135 us -> 165 us
  local copies, waits for them, and re-layouts: 43.9 us -> 35.8 us
  starting transfers between devices: 42 us -> 35.1 us
  other arithmetic: 13.8 us -> 17.4 us
    all_gather x1, waiting for transfers between devices: 38.5 us -> 73.4 us  [per_device(): normed_all = lax.all_gather(normed, seq, axis=0, tiled=True)]
    all_to_all x1 -> x0, starting transfers between devices: 7.94 us -> none  [per_device(): lax.all_to_all(copies, seq, split_axis=0, concat_axis=0, tiled=True)]
    unnamed x41 -> x33, local copies, waits for them, and re-layouts: 9.57 us -> 4.19 us
    all_to_all x1 -> x0, waiting for transfers between devices: 5.36 us -> none  [per_device(): lax.all_to_all(copies, seq, split_axis=0, concat_axis=0, tiled=True)]
    slice x3 -> x0, local copies, waits for them, and re-layouts: 3.52 us -> none  [the longest x1 2.46 us: per_device(): small_all[:, proj_cols:proj_cols + RANK]]
  transfers between devices with their start and end apart: 11 -> 11, of which waited for: 9 -> 8; matrix products, arithmetic and copies ran while one was open for 20% -> 18% of each run, Pallas kernels for 9% -> 9%
where the time goes in v10:
time: 312 us; the launch traced here: 311 us
  waiting for transfers between devices  165 us (53%)
  local copies, waits for them, and re-layouts  35.8 us (11%)
  starting transfers between devices  35.1 us (11%)
  Pallas kernels  27.1 us (9%)
  other arithmetic  17.4 us (6%)
  matrix products  16.5 us (5%)
  between operations  14.1 us (5%)
    all_gather x1, waiting for transfers between devices, per_device(): normed_all = lax.all_gather(normed, seq, axis=0, tiled=True)  73.4 us
    all_to_all x2, waiting for transfers between devices, gather_a2a(): lax.all_to_all(copies, axis, split_axis=0, concat_axis=0, tiled=True)  42.7 us
    pallas_call x2, Pallas kernels, run_scan(): pl.pallas_call(functools.partial(scan_body, emit), grid=(chunks,), in_spe...  25.4 us
    reduce_scatter x1, waiting for transfers between devices, per_device(): lax.psum_scatter(partial.reshape(cols_n * rows, model), 'sy', scatter_dim...  16.1 us
    all_to_all x1, waiting for transfers between devices, per_device(): lax.all_to_all(inner, seq, split_axis=0, concat_axis=1, tiled=True)  15.2 us
    all_to_all x2, starting transfers between devices, gather_a2a(): lax.all_to_all(copies, axis, split_axis=0, concat_axis=0, tiled=True)  13.4 us
    all_to_all x1, waiting for transfers between devices, per_device(): lax.all_to_all(jnp.swapaxes(pair, 0, 1), seq, split_axis=0, concat_axis=0...  7.81 us
    dot_general x1, matrix products, per_device(): both = jnp.dot(normed_all, w_flat, preferred_element_type=jnp.float32)  6.86 us
  transfers between devices with their start and end apart: 11, of which 8 were waited for; matrix products, arithmetic and copies ran while one was open for 18% of the time, Pallas kernels for 9%

profile of v10, /device:TPU:1, one launch (start us, length us, event | category | flops | bytes accessed | tf_op | source)
XLA Modules:
  0.0 310.6 jit_solution(5081537497431781461)
XLA Ops:
  9.3 2.0 fusion.19
  12.1 73.4 %all-gather.7.cloned.1.call-done = bf16[2048,2048]{1,0:T(8,128)(2,1)} async-done(((bf16[128,2048]{1,0:T(8,128)(2,1)}), bf16[2048,2048]{1,0:T(8,128)(2,1)}) %all-gather.7.cloned.1.call-update) | async-done | bytes 8388624 | tf_op jit(solution)/shard_map/all_gather | solution.py:156
  85.8 1.8 broadcast_in_dim.12
  87.6 5.2 %all-to-all-start = ((bf16[8,256,768]{1,2,0:T(8,128)(2,1)}), bf16[8,256,768]{1,2,0:T(8,128)(2,1)S(1)}, u32[]{:S(2)}, u32[]{:S(2)}) async-start(bf16[8,256,768]{1,2,0:T(8,128)(2,1)} %broadcast_in_dim.12), calls=%async_computation | async-start | bytes 6291456 | tf_op jit(solution)/shard_map/all_to_all | solution.py:17
  92.9 37.4 %all-to-all-done = bf16[8,256,768]{1,2,0:T(8,128)(2,1)S(1)} async-done(((bf16[8,256,768]{1,2,0:T(8,128)(2,1)}), bf16[8,256,768]{1,2,0:T(8,128)(2,1)S(1)}, u32[]{:S(2)}, u32[]{:S(2)}) %all-to-all-start) | async-done | bytes 3145760 | tf_op jit(solution)/shard_map/all_to_all | solution.py:17
  130.3 2.8 copy.46
  133.1 2.5 slice.92
  135.6 6.9 %fusion.1 = f32[2048,512]{1,0:T(8,128)S(1)} fusion(bf16[2048,2048]{1,0:T(8,128)(2,1)} %all-gather.7.cloned.1.call-done, bf16[2048,768]{1,0:T(8,128)(2,1)S(1)} %bitcast.87), kind=kOutput, calls=%fused_computation.4 | convolution fusion | flops 4294967296 | bytes 14680064 | tf_op jit(solution)/shard_map/dot_general | solution.py:168
  144.4 2.4 multiply_convert_fusion
  146.8 5.1 %all-to-all-start.1 = ((bf16[16,128,256]{2,1,0:T(8,128)(2,1)}), bf16[16,128,256]{2,1,0:T(8,128)(2,1)S(1)}, u32[]{:S(2)}, u32[]{:S(2)}) async-start(bf16[16,128,256]{2,1,0:T(8,128)(2,1)} %bitcast.10), calls=%async_computation.1 | async-start | bytes 2097152 | tf_op jit(solution)/shard_map/all_to_all | solution.py:182
  154.0 15.2 %all-to-all-done.1 = bf16[16,128,256]{2,1,0:T(8,128)(2,1)S(1)} async-done(((bf16[16,128,256]{2,1,0:T(8,128)(2,1)}), bf16[16,128,256]{2,1,0:T(8,128)(2,1)S(1)}, u32[]{:S(2)}, u32[]{:S(2)}) %all-to-all-start.1) | async-done | bytes 1048608 | tf_op jit(solution)/shard_map/all_to_all | solution.py:182
  172.1 1.8 fusion.13
  175.6 2.5 copy.50
  182.2 2.5 fusion.rate_ref
  185.4 10.8 %shard_map.140 = (f32[16,32,128]{2,1,0:T(8,128)}, f32[1,32,128]{2,1,0:T(8,128)}) custom-call(f32[2048]{0:T(1024)} %reshape.101.into_ref, f32[2048]{0:T(1024)} %reshape.102.outof_ref, f32[128,32,128]{2,1,0:T(8,128)} %fusion.rate_ref, f32[128,32,128]{2,1,0:T(8,128)} %reshape.111.value_ref, f32[16,32,128]{2,1,0:T(8,128)} %bitcast.96, ...), custom_call_target="tpu_custom_call" | custom-call | flops 50331648 | bytes 4194304 | tf_op jit(solution)/shard_map/pallas_call | solution.py:84
  198.9 5.8 %all-to-all-start.2 = ((f32[16,17,256]{2,1,0:T(8,128)}), f32[16,17,256]{2,1,0:T(8,128)S(1)}, u32[]{:S(2)}, u32[]{:S(2)}) async-start(f32[16,17,256]{2,1,0:T(8,128)} %maximum_bitcast_fusion), calls=%async_computation.2 | async-start | bytes 786432 | tf_op jit(solution)/shard_map/all_to_all | solution.py:217
  205.3 7.8 %all-to-all-done.2.pair_ref = f32[16,17,256]{2,1,0:T(8,128)S(1)} async-done(((f32[16,17,256]{2,1,0:T(8,128)}), f32[16,17,256]{2,1,0:T(8,128)S(1)}, u32[]{:S(2)}, u32[]{:S(2)}) %all-to-all-start.2) | async-done | bytes 278560 | tf_op jit(solution)/shard_map/all_to_all | solution.py:217
  213.9 1.7 shard_map.141
  215.6 3.5 %all-to-all-start.3 = ((f32[16,16,256]{2,1,0:T(8,128)}), f32[16,16,256]{2,1,0:T(8,128)S(1)}, u32[]{:S(2)}, u32[]{:S(2)}) async-start(f32[16,16,256]{2,1,0:T(8,128)} %get-tuple-element.11), calls=%async_computation.3 | async-start | bytes 524288 | tf_op jit(solution)/shard_map/all_to_all | solution.py:222
  219.2 2.7 slice.116
  221.8 4.9 %all-to-all-done.3 = f32[16,16,256]{2,1,0:T(8,128)S(1)} async-done(((f32[16,16,256]{2,1,0:T(8,128)}), f32[16,16,256]{2,1,0:T(8,128)S(1)}, u32[]{:S(2)}, u32[]{:S(2)}) %all-to-all-start.3) | async-done | bytes 262176 | tf_op jit(solution)/shard_map/all_to_all | solution.py:222
  226.7 3.7 %all-to-all-start.5 = ((bf16[4,512,256]{2,1,0:T(8,128)(2,1)}), bf16[4,512,256]{2,1,0:T(8,128)(2,1)S(1)}, u32[]{:S(2)}, u32[]{:S(2)}) async-start(bf16[4,512,256]{2,1,0:T(8,128)(2,1)} %bitcast.25), calls=%async_computation.5 | async-start | bytes 2097152 | tf_op jit(solution)/shard_map/all_to_all | solution.py:173
  231.3 14.6 %shard_map.142 = f32[128,32,128]{2,1,0:T(8,128)} custom-call(f32[2048]{0:T(1024)} %reshape.101.into_ref, f32[2048]{0:T(1024)} %reshape.102.outof_ref, f32[128,32,128]{2,1,0:T(8,128)} %fusion.rate_ref, f32[128,32,128]{2,1,0:T(8,128)} %reshape.111.value_ref, f32[16,32,128]{2,1,0:T(8,128)} %bitcast.97, f32[16,32,128]{2,1,0:T(8,128)} %reshape_reshape.3.start_ref, ...), custom_call_target="tpu_custom_call" | custom-call | flops 50331648 | bytes 6291456 | tf_op jit(solution)/shard_map/pallas_call | solution.py:84
  245.9 1.8 convert_element_type.103
  249.8 3.5 %all-to-all-start.4 = ((bf16[128,4,4,256]{3,0,1,2:T(8,128)(2,1)}), bf16[128,4,4,256]{3,0,1,2:T(8,128)(2,1)S(1)}, u32[]{:S(2)}, u32[]{:S(2)}) async-start(bf16[128,4,4,256]{3,0,1,2:T(8,128)(2,1)} %copy.54), calls=%async_computation.4 | async-start | bytes 2097152 | tf_op jit(solution)/shard_map/all_to_all | solution.py:229
  253.4 6.5 %copy.56 = bf16[1024,2048]{1,0:T(8,128)(2,1)} copy(bf16[1024,2048]{0,1:T(8,128)(2,1)} %all-gather.9.cloned.1.call-done) | data formatting | bytes 8388608 | tf_op jit(solution)/shard_map/all_gather | solution.py:170
  259.9 4.6 %all-to-all-done.4 = bf16[128,4,4,256]{3,0,1,2:T(8,128)(2,1)S(1)} async-done(((bf16[128,4,4,256]{3,0,1,2:T(8,128)(2,1)}), bf16[128,4,4,256]{3,0,1,2:T(8,128)(2,1)S(1)}, u32[]{:S(2)}, u32[]{:S(2)}) %all-to-all-start.4) | async-done | bytes 1048608 | tf_op jit(solution)/shard_map/all_to_all | solution.py:229
  264.4 6.1 %bitcast_convert_fusion = bf16[4,128,2048]{2,1,0:T(8,128)(2,1)} fusion(bf16[4,256,2048,1]{2,1,3,0:T(8,128)(2,1)} %bitcast.88, bf16[4,4,128,256]{3,2,1,0:T(8,128)(2,1)S(1)} %bitcast.91, bf16[128,4,4,256]{3,0,1,2:T(8,128)(2,1)S(1)} %all-to-all-done.4), kind=kOutput, calls=%fused_computation.1 | convolution fusion | flops 2152726528 | bytes 8388608 | tf_op jit(solution)/shard_map/ktac,acd->ktd/dot_general | solution.py:235
  271.9 8.1 %all-to-all-start.6 = ((f32[8,1,16,256]{3,2,1,0:T(8,128)}), f32[8,1,16,256]{3,2,1,0:T(8,128)S(1)}, u32[]{:S(2)}, u32[]{:S(2)}) async-start(f32[8,1,16,256]{3,2,1,0:T(8,128)} %broadcast_in_dim.16), calls=%async_computation.7 | async-start | bytes 262144 | tf_op jit(solution)/shard_map/all_to_all | solution.py:17
  280.1 5.3 %all-to-all-done.6 = f32[8,1,16,256]{3,2,1,0:T(8,128)S(1)} async-done(((f32[8,1,16,256]{3,2,1,0:T(8,128)}), f32[8,1,16,256]{3,2,1,0:T(8,128)S(1)}, u32[]{:S(2)}, u32[]{:S(2)}) %all-to-all-start.6) | async-done | bytes 131104 | tf_op jit(solution)/shard_map/all_to_all | solution.py:17
  286.1 16.1 %reduce-scatter.2.cloned.1.call-done = bf16[128,2048]{1,0:T(8,128)(2,1)} async-done(((bf16[512,2048]{1,0:T(8,128)(2,1)}), bf16[128,2048]{1,0:T(8,128)(2,1)}) %reduce-scatter.2.cloned.1.call-update) | async-done | bytes 524304 | tf_op jit(solution)/shard_map/reduce_scatter | solution.py:238
  302.1 2.0 fusion.27
  (80 shorter events, 25.5 us)
Async XLA Ops:
  7.2 4.2 %copy-start.11 = (bf16[256]{0:T(256)(128)(2,1)S(1)}, bf16[256]{0:T(256)(128)(2,1)}, u32[]{:S(2)}) copy-start(bf16[256]{0:T(256)(128)(2,1)} %param.22) | copy-start | bytes 1540
  7.2 4.2 %copy-start.8 = (bf16[128,256]{1,0:T(8,128)(2,1)S(1)}, bf16[128,256]{1,0:T(8,128)(2,1)}, u32[]{:S(2)}) copy-start(bf16[128,256]{1,0:T(8,128)(2,1)} %param.21) | copy-start | bytes 196612
  7.2 4.2 %copy-start.7 = (bf16[256,160]{0,1:T(8,128)(2,1)S(1)}, bf16[256,160]{0,1:T(8,128)(2,1)}, u32[]{:S(2)}) copy-start(bf16[256,160]{0,1:T(8,128)(2,1)} %param.20) | copy-start | bytes 245764
  7.2 78.3 %copy-start.5 = (bf16[2,256,256]{2,1,0:T(8,128)(2,1)S(1)}, bf16[2,256,256]{2,1,0:T(8,128)(2,1)}, u32[]{:S(2)}) copy-start(bf16[2,256,256]{2,1,0:T(8,128)(2,1)} %param.17) | copy-start | bytes 786436
  7.2 78.5 %copy-start.6 = (bf16[256,256]{1,0:T(8,128)(2,1)S(1)}, bf16[256,256]{1,0:T(8,128)(2,1)}, u32[]{:S(2)}) copy-start(bf16[256,256]{1,0:T(8,128)(2,1)} %param.25) | copy-start | bytes 393220
  7.2 78.2 %all-gather.7.cloned.1.call-start = ((), (), s32[]{:S(2)}) async-start(), calls=%async_computation.8 | async-start | bytes 8912896 | tf_op jit(solution)/shard_map/all_gather | solution.py:156
  11.3 124.2 %all-gather.11.cloned.1.call-start = ((), (), s32[]{:S(2)}) async-start(), calls=%async_computation.11 | async-start | bytes 2576384 | tf_op jit(solution)/shard_map/all_gather | solution.py:164
  87.6 5.2 %copy-start.12 = (bf16[256]{0:T(256)(128)(2,1)S(1)}, bf16[256]{0:T(256)(128)(2,1)}, u32[]{:S(2)}) copy-start(bf16[256]{0:T(256)(128)(2,1)} %param.19) | copy-start | bytes 1540
  87.6 5.2 %copy-start.10 = (bf16[4,256]{1,0:T(4,128)(2,1)S(1)}, bf16[4,256]{1,0:T(4,128)(2,1)}, u32[]{:S(2)}) copy-start(bf16[4,256]{1,0:T(4,128)(2,1)} %param.18) | copy-start | bytes 6148
  87.6 42.7 %all-to-all-start = ((bf16[8,256,768]{1,2,0:T(8,128)(2,1)}), bf16[8,256,768]{1,2,0:T(8,128)(2,1)S(1)}, u32[]{:S(2)}, u32[]{:S(2)}) async-start(bf16[8,256,768]{1,2,0:T(8,128)(2,1)} %broadcast_in_dim.12), calls=%async_computation | async-start | bytes 6291456 | tf_op jit(solution)/shard_map/all_to_all | solution.py:17
  92.8 160.5 %all-gather.9.cloned.1.call-start = ((), (), s32[]{:S(2)}) async-start(), calls=%async_computation.10 | async-start | bytes 5242880 | tf_op jit(solution)/shard_map/all_gather | solution.py:170
  133.1 2.5 copy-start
  142.4 2.0 copy-start.2
  144.4 7.5 %copy-start.4 = (f32[16,4096]{1,0:T(8,128)S(1)}, f32[16,4096]{1,0:T(8,128)}, u32[]{:S(2)}) copy-start(f32[16,4096]{1,0:T(8,128)} %param.23) | copy-start | bytes 786436
  146.8 6.0 %copy-start.13 = (s32[8]{0:T(128)S(1)}, s32[8]{0:T(128)}, u32[]{:S(2)}) copy-start(s32[8]{0:T(128)} %param.14) | copy-start | bytes 100
  146.8 22.4 %all-to-all-start.1 = ((bf16[16,128,256]{2,1,0:T(8,128)(2,1)}), bf16[16,128,256]{2,1,0:T(8,128)(2,1)S(1)}, u32[]{:S(2)}, u32[]{:S(2)}) async-start(bf16[16,128,256]{2,1,0:T(8,128)(2,1)} %bitcast.10), calls=%async_computation.1 | async-start | bytes 2097152 | tf_op jit(solution)/shard_map/all_to_all | solution.py:182
  198.9 14.2 %all-to-all-start.2 = ((f32[16,17,256]{2,1,0:T(8,128)}), f32[16,17,256]{2,1,0:T(8,128)S(1)}, u32[]{:S(2)}, u32[]{:S(2)}) async-start(f32[16,17,256]{2,1,0:T(8,128)} %maximum_bitcast_fusion), calls=%async_computation.2 | async-start | bytes 786432 | tf_op jit(solution)/shard_map/all_to_all | solution.py:217
  213.1 0.7 copy-start.3
  215.6 11.1 %all-to-all-start.3 = ((f32[16,16,256]{2,1,0:T(8,128)}), f32[16,16,256]{2,1,0:T(8,128)S(1)}, u32[]{:S(2)}, u32[]{:S(2)}) async-start(f32[16,16,256]{2,1,0:T(8,128)} %get-tuple-element.11), calls=%async_computation.3 | async-start | bytes 524288 | tf_op jit(solution)/shard_map/all_to_all | solution.py:222
  226.7 23.1 %all-to-all-start.5 = ((bf16[4,512,256]{2,1,0:T(8,128)(2,1)}), bf16[4,512,256]{2,1,0:T(8,128)(2,1)S(1)}, u32[]{:S(2)}, u32[]{:S(2)}) async-start(bf16[4,512,256]{2,1,0:T(8,128)(2,1)} %bitcast.25), calls=%async_computation.5 | async-start | bytes 2097152 | tf_op jit(solution)/shard_map/all_to_all | solution.py:173
  249.8 14.7 %all-to-all-start.4 = ((bf16[128,4,4,256]{3,0,1,2:T(8,128)(2,1)}), bf16[128,4,4,256]{3,0,1,2:T(8,128)(2,1)S(1)}, u32[]{:S(2)}, u32[]{:S(2)}) async-start(bf16[128,4,4,256]{3,0,1,2:T(8,128)(2,1)} %copy.54), calls=%async_computation.4 | async-start | bytes 2097152 | tf_op jit(solution)/shard_map/all_to_all | solution.py:229
  253.3 48.8 %reduce-scatter.2.cloned.1.call-start = ((), (), s32[]{:S(2)}) async-start(), calls=%async_computation.9 | async-start | bytes 2621440 | tf_op jit(solution)/shard_map/reduce_scatter | solution.py:238
  270.5 0.7 copy-start.9
  270.5 9.5 %copy-start.14 = (s32[8]{0:T(128)S(1)}, s32[8]{0:T(128)}, u32[]{:S(2)}) copy-start(s32[8]{0:T(128)} %param.15) | copy-start | bytes 100
  270.5 31.6 %copy-start.1 = (bf16[1,128,2048]{2,1,0:T(8,128)(2,1)S(1)}, bf16[1,128,2048]{2,1,0:T(8,128)(2,1)}, u32[]{:S(2)}) copy-start(bf16[1,128,2048]{2,1,0:T(8,128)(2,1)} %param.13) | copy-start | bytes 1572868
  271.9 13.5 %all-to-all-start.6 = ((f32[8,1,16,256]{3,2,1,0:T(8,128)}), f32[8,1,16,256]{3,2,1,0:T(8,128)S(1)}, u32[]{:S(2)}, u32[]{:S(2)}) async-start(f32[8,1,16,256]{3,2,1,0:T(8,128)} %broadcast_in_dim.16), calls=%async_computation.7 | async-start | bytes 262144 | tf_op jit(solution)/shard_map/all_to_all | solution.py:17
Sparse Core Ops, SparseCore 0:
  11.4 73.9 all-gather.6
  87.6 44.4 all-gather.10
  135.7 59.8 all-gather.8
  270.7 31.3 reduce-scatter.1

commit v11 on v8

--- a/solution.py
+++ b/solution.py
@@ -56,7 +56,7 @@
 
     held0 = tuple(start_ref[n] for n in range(states))
     acc0 = jnp.zeros((SUB, LANES), jnp.float32)
-    held, acc = lax.fori_loop(0, steps, step, (held0, acc0), unroll=2)
+    held, acc = lax.fori_loop(0, steps, step, (held0, acc0), unroll=4)
     if not emit:
         for n in range(states):
             end_ref[n] = held[n]
@@ -163,10 +163,8 @@
     small = jnp.concatenate((xproj_w.T, dt_w, dt_b[None]), axis=0)
     copies = jnp.broadcast_to(small[None], (seq_count,) + small.shape)
     small_all = lax.all_to_all(copies, seq, split_axis=0, concat_axis=0, tiled=True)
-    xproj_full = jnp.swapaxes(small_all[:, :proj_cols], 1, 2).reshape(total_inner, proj_cols)
-    dt_full = jnp.swapaxes(small_all[:, proj_cols : proj_cols + RANK], 0, 1).reshape(
-        RANK, total_inner
-    )
+    xproj_full = small_all[:, :proj_cols]
+    dt_full = small_all[:, proj_cols : proj_cols + RANK]
     dt_bias_full = small_all[:, proj_cols + RANK].reshape(total_inner)
     w_in, xproj_full, dt_full, dt_bias_full = lax.optimization_barrier(
         (w_in, xproj_full, dt_full, dt_bias_full)
@@ -187,14 +185,19 @@
         convolved = convolved + taps[tap] * padded[tap : tap + span, :]
     inner = jax.nn.silu(convolved).astype(jnp.bfloat16)
     inner_tok = lax.all_to_all(inner, seq, split_axis=0, concat_axis=1, tiled=True)
-    proj = jnp.dot(inner_tok, xproj_full, preferred_element_type=jnp.float32)
+    proj = jnp.einsum(
+        "tsc,skc->tk", inner_tok.reshape(rows, seq_count, width), xproj_full,
+        preferred_element_type=jnp.float32,
+    )
     length_here = lax.dynamic_index_in_dim(lengths, req_index, 0, keepdims=False)
     positions = seq_index * rows + jnp.arange(rows, dtype=jnp.int32)
     live = (positions < length_here).astype(jnp.float32)
     rate_low = proj[:, :RANK].astype(jnp.bfloat16)
     delta_tok = (
         jax.nn.softplus(
-            jnp.dot(rate_low, dt_full, preferred_element_type=jnp.float32)
+            jnp.einsum(
+                "tk,skc->tsc", rate_low, dt_full, preferred_element_type=jnp.float32
+            ).reshape(rows, total_inner)
             + dt_bias_full.astype(jnp.float32)
         )
         * live[:, None]

time: 287 us -> 292 us (1.017)
  waiting for transfers between devices: 125 us -> 131 us
  other arithmetic: 13.8 us -> 17.6 us
    all_to_all x2, waiting for transfers between devices: 34.6 us -> 41.8 us  [gather_a2a(): lax.all_to_all(copies, axis, split_axis=0, concat_axis=0, tiled=True)]
    unnamed x39 -> x30, local copies, waits for them, and re-layouts: 9.56 us -> 4.1 us
    convert_element_type x1 -> x2, local copies, waits for them, and re-layouts: 1.87 us -> 5.29 us  [per_device(): inner_f = inner_tok.astype(jnp.float32)]
  transfers between devices with their start and end apart: 11 -> 11, of which waited for: 8 -> 8; matrix products, arithmetic and copies ran while one was open for 21% -> 21% of each run, Pallas kernels for 10% -> 9%
where the time goes in v11:
time: 292 us; the launch traced here: 291 us
  waiting for transfers between devices  131 us (45%)
  local copies, waits for them, and re-layouts  44 us (15%)
  starting transfers between devices  42.8 us (15%)
  Pallas kernels  27.2 us (9%)
  other arithmetic  17.6 us (6%)
  between operations  14.1 us (5%)
  matrix products  13.9 us (5%)
    all_to_all x1, waiting for transfers between devices, per_device(): lax.all_to_all(copies, seq, split_axis=0, concat_axis=0, tiled=True)  42.4 us
    all_to_all x2, waiting for transfers between devices, gather_a2a(): lax.all_to_all(copies, axis, split_axis=0, concat_axis=0, tiled=True)  41.8 us
    pallas_call x2, Pallas kernels, run_scan(): pl.pallas_call(functools.partial(scan_body, emit), grid=(chunks,), in_spe...  25.4 us
    reduce_scatter x1, waiting for transfers between devices, per_device(): lax.psum_scatter(partial.reshape(cols_n * rows, model), 'sy', scatter_dim...  16 us
    all_to_all x2, starting transfers between devices, gather_a2a(): lax.all_to_all(copies, axis, split_axis=0, concat_axis=0, tiled=True)  13.5 us
    all_to_all x1, waiting for transfers between devices, per_device(): lax.all_to_all(inner, seq, split_axis=0, concat_axis=1, tiled=True)  12.9 us
    all_to_all x1, starting transfers between devices, per_device(): lax.all_to_all(copies, seq, split_axis=0, concat_axis=0, tiled=True)  8.72 us
    all_to_all x1, waiting for transfers between devices, per_device(): lax.all_to_all(jnp.swapaxes(pair, 0, 1), seq, split_axis=0, concat_axis=0...  7.84 us
  transfers between devices with their start and end apart: 11, of which 8 were waited for; matrix products, arithmetic and copies ran while one was open for 21% of the time, Pallas kernels for 9%

profile of v11, /device:TPU:1, one launch (start us, length us, event | category | flops | bytes accessed | tf_op | source)
XLA Modules:
  0.0 290.7 jit_solution(10815349160188118314)
XLA Ops:
  9.2 2.0 fusion.16
  13.0 8.7 %all-to-all-start.1 = ((bf16[16,289,256]{2,1,0:T(8,128)(2,1)}), bf16[16,289,256]{2,1,0:T(8,128)(2,1)S(1)}, u32[]{:S(2)}, u32[]{:S(2)}) async-start(bf16[16,289,256]{2,1,0:T(8,128)(2,1)} %broadcast_in_dim.19), calls=%async_computation.1 | async-start | bytes 4849664 | tf_op jit(solution)/shard_map/all_to_all | solution.py:165
  22.0 42.4 %all-to-all-done.1 = bf16[16,289,256]{2,1,0:T(8,128)(2,1)S(1)} async-done(((bf16[16,289,256]{2,1,0:T(8,128)(2,1)}), bf16[16,289,256]{2,1,0:T(8,128)(2,1)S(1)}, u32[]{:S(2)}, u32[]{:S(2)}) %all-to-all-start.1) | async-done | bytes 2367520 | tf_op jit(solution)/shard_map/all_to_all | solution.py:165
  64.4 2.2 broadcast_in_dim.17
  66.7 6.1 %all-to-all-start = ((bf16[8,3,256,256]{2,3,1,0:T(8,128)(2,1)}), bf16[8,3,256,256]{2,3,1,0:T(8,128)(2,1)S(1)}, u32[]{:S(2)}, u32[]{:S(2)}) async-start(bf16[8,3,256,256]{2,3,1,0:T(8,128)(2,1)} %broadcast_in_dim.17), calls=%async_computation | async-start | bytes 6291456 | tf_op jit(solution)/shard_map/all_to_all | solution.py:17
  73.8 36.5 %all-to-all-done = bf16[8,3,256,256]{2,3,1,0:T(8,128)(2,1)S(1)} async-done(((bf16[8,3,256,256]{2,3,1,0:T(8,128)(2,1)}), bf16[8,3,256,256]{2,3,1,0:T(8,128)(2,1)S(1)}, u32[]{:S(2)}, u32[]{:S(2)}) %all-to-all-start) | async-done | bytes 3145760 | tf_op jit(solution)/shard_map/all_to_all | solution.py:17
  110.3 2.8 copy.48
  113.1 2.3 slice.97
  117.3 6.9 %fusion.1 = f32[2048,512]{1,0:T(8,128)S(1)} fusion(bf16[2048,2048]{1,0:T(8,128)(2,1)} %all-gather.4.cloned.1.call-done, bf16[2048,256]{1,0:T(8,128)(2,1)S(1)} %get-tuple-element.27, bf16[2048,256]{1,0:T(8,128)(2,1)S(1)} %get-tuple-element.26), kind=kOutput, calls=%fused_computation.4 | convolution fusion | flops 4299161600 | bytes 14680064 | tf_op jit(solution)/shard_map/dot_general | solution.py:173
  126.2 2.4 multiply_convert_fusion
  128.5 3.8 %all-to-all-start.2 = ((bf16[16,128,256]{2,1,0:T(8,128)(2,1)}), bf16[16,128,256]{2,1,0:T(8,128)(2,1)S(1)}, u32[]{:S(2)}, u32[]{:S(2)}) async-start(bf16[16,128,256]{2,1,0:T(8,128)(2,1)} %bitcast.13), calls=%async_computation.2 | async-start | bytes 2097152 | tf_op jit(solution)/shard_map/all_to_all | solution.py:187
  136.1 12.9 %all-to-all-done.2 = bf16[16,128,256]{2,1,0:T(8,128)(2,1)S(1)} async-done(((bf16[16,128,256]{2,1,0:T(8,128)(2,1)}), bf16[16,128,256]{2,1,0:T(8,128)(2,1)S(1)}, u32[]{:S(2)}, u32[]{:S(2)}) %all-to-all-start.2) | async-done | bytes 1048608 | tf_op jit(solution)/shard_map/all_to_all | solution.py:187
  151.5 2.6 copy.52
  156.0 2.6 copy.53
  158.6 2.7 reshape.107.value_ref
  161.3 2.6 fusion.rate_ref
  164.6 10.8 %shard_map.140 = (f32[16,32,128]{2,1,0:T(8,128)}, f32[1,32,128]{2,1,0:T(8,128)}) custom-call(f32[2048]{0:T(1024)} %reshape.97.into_ref, f32[2048]{0:T(1024)} %reshape.98.outof_ref, f32[128,32,128]{2,1,0:T(8,128)} %fusion.rate_ref, f32[128,32,128]{2,1,0:T(8,128)} %reshape.107.value_ref, f32[16,32,128]{2,1,0:T(8,128)} %bitcast.105, ...), custom_call_target="tpu_custom_call" | custom-call | flops 50331648 | bytes 4194304 | tf_op jit(solution)/shard_map/pallas_call | solution.py:84
  178.1 6.2 %all-to-all-start.3 = ((f32[16,17,256]{2,1,0:T(8,128)}), f32[16,17,256]{2,1,0:T(8,128)S(1)}, u32[]{:S(2)}, u32[]{:S(2)}) async-start(f32[16,17,256]{2,1,0:T(8,128)} %maximum_bitcast_fusion), calls=%async_computation.3 | async-start | bytes 786432 | tf_op jit(solution)/shard_map/all_to_all | solution.py:222
  185.6 7.8 %all-to-all-done.3.pair_ref = f32[16,17,256]{2,1,0:T(8,128)S(1)} async-done(((f32[16,17,256]{2,1,0:T(8,128)}), f32[16,17,256]{2,1,0:T(8,128)S(1)}, u32[]{:S(2)}, u32[]{:S(2)}) %all-to-all-start.3) | async-done | bytes 278560 | tf_op jit(solution)/shard_map/all_to_all | solution.py:222
  195.9 3.5 %all-to-all-start.4 = ((f32[16,16,256]{2,1,0:T(8,128)}), f32[16,16,256]{2,1,0:T(8,128)S(1)}, u32[]{:S(2)}, u32[]{:S(2)}) async-start(f32[16,16,256]{2,1,0:T(8,128)} %get-tuple-element.23), calls=%async_computation.4 | async-start | bytes 524288 | tf_op jit(solution)/shard_map/all_to_all | solution.py:227
  199.5 2.7 slice.115
  202.2 4.9 %all-to-all-done.4 = f32[16,16,256]{2,1,0:T(8,128)S(1)} async-done(((f32[16,16,256]{2,1,0:T(8,128)}), f32[16,16,256]{2,1,0:T(8,128)S(1)}, u32[]{:S(2)}, u32[]{:S(2)}) %all-to-all-start.4) | async-done | bytes 262176 | tf_op jit(solution)/shard_map/all_to_all | solution.py:227
  207.1 3.5 %all-to-all-start.6 = ((bf16[4,512,256]{2,1,0:T(8,128)(2,1)}), bf16[4,512,256]{2,1,0:T(8,128)(2,1)S(1)}, u32[]{:S(2)}, u32[]{:S(2)}) async-start(bf16[4,512,256]{2,1,0:T(8,128)(2,1)} %bitcast.26), calls=%async_computation.6 | async-start | bytes 2097152 | tf_op jit(solution)/shard_map/all_to_all | solution.py:178
  211.5 14.6 %shard_map.142 = f32[128,32,128]{2,1,0:T(8,128)} custom-call(f32[2048]{0:T(1024)} %reshape.97.into_ref, f32[2048]{0:T(1024)} %reshape.98.outof_ref, f32[128,32,128]{2,1,0:T(8,128)} %fusion.rate_ref, f32[128,32,128]{2,1,0:T(8,128)} %reshape.107.value_ref, f32[16,32,128]{2,1,0:T(8,128)} %bitcast.106, f32[16,32,128]{2,1,0:T(8,128)} %reshape_reshape.3.start_ref, ...), custom_call_target="tpu_custom_call" | custom-call | flops 50331648 | bytes 6291456 | tf_op jit(solution)/shard_map/pallas_call | solution.py:84
  229.9 3.5 %all-to-all-start.5 = ((bf16[128,4,4,256]{3,0,1,2:T(8,128)(2,1)}), bf16[128,4,4,256]{3,0,1,2:T(8,128)(2,1)S(1)}, u32[]{:S(2)}, u32[]{:S(2)}) async-start(bf16[128,4,4,256]{3,0,1,2:T(8,128)(2,1)} %copy.56), calls=%async_computation.5 | async-start | bytes 2097152 | tf_op jit(solution)/shard_map/all_to_all | solution.py:234
  233.5 6.5 %copy.58 = bf16[1024,2048]{1,0:T(8,128)(2,1)} copy(bf16[1024,2048]{0,1:T(8,128)(2,1)} %all-gather.6.cloned.1.call-done) | data formatting | bytes 8388608 | tf_op jit(solution)/shard_map/all_gather | solution.py:175
  240.1 5.3 %all-to-all-done.5 = bf16[128,4,4,256]{3,0,1,2:T(8,128)(2,1)S(1)} async-done(((bf16[128,4,4,256]{3,0,1,2:T(8,128)(2,1)}), bf16[128,4,4,256]{3,0,1,2:T(8,128)(2,1)S(1)}, u32[]{:S(2)}, u32[]{:S(2)}) %all-to-all-start.5) | async-done | bytes 1048608 | tf_op jit(solution)/shard_map/all_to_all | solution.py:234
  245.4 6.1 %bitcast_convert_fusion = bf16[4,128,2048]{2,1,0:T(8,128)(2,1)} fusion(bf16[4,256,2048,1]{2,1,3,0:T(8,128)(2,1)} %bitcast.100, bf16[4,4,128,256]{3,2,1,0:T(8,128)(2,1)S(1)} %bitcast.103, bf16[128,4,4,256]{3,0,1,2:T(8,128)(2,1)S(1)} %all-to-all-done.5), kind=kOutput, calls=%fused_computation.1 | convolution fusion | flops 2152726528 | bytes 8388608 | tf_op jit(solution)/shard_map/ktac,acd->ktd/dot_general | solution.py:240
  252.8 7.4 %all-to-all-start.7 = ((f32[8,1,16,256]{3,2,1,0:T(8,128)}), f32[8,1,16,256]{3,2,1,0:T(8,128)S(1)}, u32[]{:S(2)}, u32[]{:S(2)}) async-start(f32[8,1,16,256]{3,2,1,0:T(8,128)} %broadcast_in_dim.44), calls=%async_computation.8 | async-start | bytes 262144 | tf_op jit(solution)/shard_map/all_to_all | solution.py:17
  260.2 5.3 %all-to-all-done.7 = f32[8,1,16,256]{3,2,1,0:T(8,128)S(1)} async-done(((f32[8,1,16,256]{3,2,1,0:T(8,128)}), f32[8,1,16,256]{3,2,1,0:T(8,128)S(1)}, u32[]{:S(2)}, u32[]{:S(2)}) %all-to-all-start.7) | async-done | bytes 131104 | tf_op jit(solution)/shard_map/all_to_all | solution.py:17
  266.2 16.0 %reduce-scatter.2.cloned.1.call-done = bf16[128,2048]{1,0:T(8,128)(2,1)} async-done(((bf16[512,2048]{1,0:T(8,128)(2,1)}), bf16[128,2048]{1,0:T(8,128)(2,1)}) %reduce-scatter.2.cloned.1.call-update) | async-done | bytes 524304 | tf_op jit(solution)/shard_map/reduce_scatter | solution.py:243
  282.2 2.0 fusion.22
  (85 shorter events, 31.2 us)
Async XLA Ops:
  7.2 4.1 %copy-start.10 = (bf16[256]{0:T(256)(128)(2,1)S(1)}, bf16[256]{0:T(256)(128)(2,1)}, u32[]{:S(2)}) copy-start(bf16[256]{0:T(256)(128)(2,1)} %param.22) | copy-start | bytes 1540
  7.2 4.1 %copy-start.7 = (bf16[128,256]{1,0:T(8,128)(2,1)S(1)}, bf16[128,256]{1,0:T(8,128)(2,1)}, u32[]{:S(2)}) copy-start(bf16[128,256]{1,0:T(8,128)(2,1)} %param.21) | copy-start | bytes 196612
  7.2 4.1 %copy-start.6 = (bf16[256,160]{0,1:T(8,128)(2,1)S(1)}, bf16[256,160]{0,1:T(8,128)(2,1)}, u32[]{:S(2)}) copy-start(bf16[256,160]{0,1:T(8,128)(2,1)} %param.20) | copy-start | bytes 245764
  7.2 110.1 %all-gather.4.cloned.1.call-start = ((), (), s32[]{:S(2)}) async-start(), calls=%async_computation.9 | async-start | bytes 8912896 | tf_op jit(solution)/shard_map/all_gather | solution.py:156
  13.0 8.7 %copy-start.5 = (bf16[256,256]{1,0:T(8,128)(2,1)S(1)}, bf16[256,256]{1,0:T(8,128)(2,1)}, u32[]{:S(2)}) copy-start(bf16[256,256]{1,0:T(8,128)(2,1)} %param.25) | copy-start | bytes 393220
  13.0 8.8 %copy-start.4 = (bf16[2,256,256]{2,1,0:T(8,128)(2,1)S(1)}, bf16[2,256,256]{2,1,0:T(8,128)(2,1)}, u32[]{:S(2)}) copy-start(bf16[2,256,256]{2,1,0:T(8,128)(2,1)} %param.17) | copy-start | bytes 786436
  13.0 51.4 %all-to-all-start.1 = ((bf16[16,289,256]{2,1,0:T(8,128)(2,1)}), bf16[16,289,256]{2,1,0:T(8,128)(2,1)S(1)}, u32[]{:S(2)}, u32[]{:S(2)}) async-start(bf16[16,289,256]{2,1,0:T(8,128)(2,1)} %broadcast_in_dim.19), calls=%async_computation.1 | async-start | bytes 4849664 | tf_op jit(solution)/shard_map/all_to_all | solution.py:165
  64.4 2.3 copy-start
  66.6 6.3 %copy-start.11 = (bf16[256]{0:T(256)(128)(2,1)S(1)}, bf16[256]{0:T(256)(128)(2,1)}, u32[]{:S(2)}) copy-start(bf16[256]{0:T(256)(128)(2,1)} %param.19) | copy-start | bytes 1540
  66.6 6.3 %copy-start.9 = (bf16[4,256]{1,0:T(4,128)(2,1)S(1)}, bf16[4,256]{1,0:T(4,128)(2,1)}, u32[]{:S(2)}) copy-start(bf16[4,256]{1,0:T(4,128)(2,1)} %param.18) | copy-start | bytes 6148
  66.7 43.5 %all-to-all-start = ((bf16[8,3,256,256]{2,3,1,0:T(8,128)(2,1)}), bf16[8,3,256,256]{2,3,1,0:T(8,128)(2,1)S(1)}, u32[]{:S(2)}, u32[]{:S(2)}) async-start(bf16[8,3,256,256]{2,3,1,0:T(8,128)(2,1)} %broadcast_in_dim.17), calls=%async_computation | async-start | bytes 6291456 | tf_op jit(solution)/shard_map/all_to_all | solution.py:17
  72.8 160.7 %all-gather.6.cloned.1.call-start = ((), (), s32[]{:S(2)}) async-start(), calls=%async_computation.11 | async-start | bytes 5242880 | tf_op jit(solution)/shard_map/all_gather | solution.py:175
  124.2 2.0 copy-start.2
  128.5 6.3 %copy-start.12 = (s32[8]{0:T(128)S(1)}, s32[8]{0:T(128)}, u32[]{:S(2)}) copy-start(s32[8]{0:T(128)} %param.14) | copy-start | bytes 100
  128.5 20.5 %slice-start.1 = ((bf16[16,289,256]{2,1,0:T(8,128)(2,1)}), bf16[16,160,256]{2,1,0:T(8,128)(2,1)S(1)}, s32[]{:S(2)}) async-start(bf16[16,289,256]{2,1,0:T(8,128)(2,1)} %copy-done), calls=%async_computation.13 | async-start | bytes 2621440 | tf_op jit(solution)/shard_map/slice | solution.py:166
  128.5 20.5 %all-to-all-start.2 = ((bf16[16,128,256]{2,1,0:T(8,128)(2,1)}), bf16[16,128,256]{2,1,0:T(8,128)(2,1)S(1)}, u32[]{:S(2)}, u32[]{:S(2)}) async-start(bf16[16,128,256]{2,1,0:T(8,128)(2,1)} %bitcast.13), calls=%async_computation.2 | async-start | bytes 2097152 | tf_op jit(solution)/shard_map/all_to_all | solution.py:187
  132.3 18.7 %slice-start = ((bf16[16,289,256]{2,1,0:T(8,128)(2,1)}), bf16[16,128,256]{2,1,0:T(8,128)(2,1)S(1)}, s32[]{:S(2)}) async-start(bf16[16,289,256]{2,1,0:T(8,128)(2,1)} %copy-done), calls=%async_computation.12 | async-start | bytes 2097152 | tf_op jit(solution)/shard_map/slice | solution.py:167
  178.1 15.3 %all-to-all-start.3 = ((f32[16,17,256]{2,1,0:T(8,128)}), f32[16,17,256]{2,1,0:T(8,128)S(1)}, u32[]{:S(2)}, u32[]{:S(2)}) async-start(f32[16,17,256]{2,1,0:T(8,128)} %maximum_bitcast_fusion), calls=%async_computation.3 | async-start | bytes 786432 | tf_op jit(solution)/shard_map/all_to_all | solution.py:222
  193.4 0.7 copy-start.3
  195.9 11.1 %all-to-all-start.4 = ((f32[16,16,256]{2,1,0:T(8,128)}), f32[16,16,256]{2,1,0:T(8,128)S(1)}, u32[]{:S(2)}, u32[]{:S(2)}) async-start(f32[16,16,256]{2,1,0:T(8,128)} %get-tuple-element.23), calls=%async_computation.4 | async-start | bytes 524288 | tf_op jit(solution)/shard_map/all_to_all | solution.py:227
  207.1 22.9 %all-to-all-start.6 = ((bf16[4,512,256]{2,1,0:T(8,128)(2,1)}), bf16[4,512,256]{2,1,0:T(8,128)(2,1)S(1)}, u32[]{:S(2)}, u32[]{:S(2)}) async-start(bf16[4,512,256]{2,1,0:T(8,128)(2,1)} %bitcast.26), calls=%async_computation.6 | async-start | bytes 2097152 | tf_op jit(solution)/shard_map/all_to_all | solution.py:178
  229.9 15.4 %all-to-all-start.5 = ((bf16[128,4,4,256]{3,0,1,2:T(8,128)(2,1)}), bf16[128,4,4,256]{3,0,1,2:T(8,128)(2,1)S(1)}, u32[]{:S(2)}, u32[]{:S(2)}) async-start(bf16[128,4,4,256]{3,0,1,2:T(8,128)(2,1)} %copy.56), calls=%async_computation.5 | async-start | bytes 2097152 | tf_op jit(solution)/shard_map/all_to_all | solution.py:234
  233.5 48.7 %reduce-scatter.2.cloned.1.call-start = ((), (), s32[]{:S(2)}) async-start(), calls=%async_computation.10 | async-start | bytes 2621440 | tf_op jit(solution)/shard_map/reduce_scatter | solution.py:243
  251.5 0.7 copy-start.8
  251.5 8.8 %copy-start.13 = (s32[8]{0:T(128)S(1)}, s32[8]{0:T(128)}, u32[]{:S(2)}) copy-start(s32[8]{0:T(128)} %param.15) | copy-start | bytes 100
  251.5 30.7 %copy-start.1 = (bf16[1,128,2048]{2,1,0:T(8,128)(2,1)S(1)}, bf16[1,128,2048]{2,1,0:T(8,128)(2,1)}, u32[]{:S(2)}) copy-start(bf16[1,128,2048]{2,1,0:T(8,128)(2,1)} %param.13) | copy-start | bytes 1572868
  252.8 12.7 %all-to-all-start.7 = ((f32[8,1,16,256]{3,2,1,0:T(8,128)}), f32[8,1,16,256]{3,2,1,0:T(8,128)S(1)}, u32[]{:S(2)}, u32[]{:S(2)}) async-start(f32[8,1,16,256]{3,2,1,0:T(8,128)} %broadcast_in_dim.44), calls=%async_computation.8 | async-start | bytes 262144 | tf_op jit(solution)/shard_map/all_to_all | solution.py:17
Sparse Core Ops, SparseCore 0:
  11.4 95.6 all-gather.3
  117.4 54.9 all-gather.5
  251.6 30.5 reduce-scatter.1

commit v12 on v8

--- a/solution.py
+++ b/solution.py
@@ -142,7 +142,7 @@
     cols_n = lax.axis_size("sy")
     seq_count = rows_n * cols_n
     seq_index = lax.axis_index(seq)
-    req_index = lax.axis_index("req")
+    req_index = lax.axis_index(("rx", "rc"))
     rows = hidden.shape[1]
     span = rows * seq_count
     width = in_weight.shape[2]
@@ -155,14 +155,23 @@
     normed = (tokens * scale * norm_gain.astype(jnp.float32)).astype(jnp.bfloat16)
     normed_all = lax.all_gather(normed, seq, axis=0, tiled=True)
     pieces = jnp.concatenate((in_weight, out_weight.T[None]), axis=0)
-    pieces_all = gather_a2a(pieces, "req", 1)
+    pieces_row = gather_a2a(pieces[None], "rx", 0)
+    pieces_pair = gather_a2a(pieces_row[None], "rc", 0)
+    pieces_all = jnp.moveaxis(
+        jnp.swapaxes(pieces_pair, 0, 1).reshape((-1,) + pieces.shape), 0, 1
+    ).reshape((pieces.shape[0], -1) + pieces.shape[2:])
     w_in = pieces_all[:2]
     w_out_t = pieces_all[2]
     xproj_w, dt_w, dt_b, _ = lax.optimization_barrier((xproj_weight, dt_weight, dt_bias, normed))
     proj_cols = xproj_w.shape[1]
     small = jnp.concatenate((xproj_w.T, dt_w, dt_b[None]), axis=0)
-    copies = jnp.broadcast_to(small[None], (seq_count,) + small.shape)
-    small_all = lax.all_to_all(copies, seq, split_axis=0, concat_axis=0, tiled=True)
+    lane_half = width // 2
+    core = lax.axis_index("rc")
+    mine = lax.dynamic_slice_in_dim(small, core * lane_half, lane_half, 1)
+    copies = jnp.broadcast_to(mine[None], (seq_count,) + mine.shape)
+    half_all = lax.all_to_all(copies, seq, split_axis=0, concat_axis=0, tiled=True)
+    both_halves = gather_a2a(half_all[None], "rc", 0)
+    small_all = jnp.moveaxis(both_halves, 0, 2).reshape(half_all.shape[:2] + (width,))
     xproj_full = jnp.swapaxes(small_all[:, :proj_cols], 1, 2).reshape(total_inner, proj_cols)
     dt_full = jnp.swapaxes(small_all[:, proj_cols : proj_cols + RANK], 0, 1).reshape(
         RANK, total_inner
@@ -240,7 +249,7 @@
     branch = lax.psum_scatter(
         partial.reshape(cols_n * rows, model), "sy", scatter_dimension=0, tiled=True
     ).astype(jnp.float32)
-    slot_all = gather_a2a(carry[None], "req", 0)
+    slot_all = gather_a2a(carry[None], ("rx", "rc"), 0)
     picked = (slot_request == req_index).astype(jnp.float32)
     final_state = jnp.sum(picked[:, None, None] * slot_all, axis=0, keepdims=True)
     mixed = (tokens + branch).astype(jnp.bfloat16)[None]
@@ -252,14 +261,18 @@
     rows_n = 1
     while rows_n * rows_n < seq_n:
         rows_n *= 2
-    grid = Mesh(mesh.devices.reshape(mesh.shape["req"], rows_n, seq_n // rows_n), ("req", "sz", "sy"))
+    grid = Mesh(
+        mesh.devices.reshape(mesh.shape["req"] // 2, 2, rows_n, seq_n // rows_n),
+        ("rx", "rc", "sz", "sy"),
+    )
+    req = ("rx", "rc")
     seq = ("sz", "sy")
     in_specs = (
-        P("req", seq, None),
-        P(),
-        P(),
-        P(),
-        P(None, "req", seq),
+        P(req, seq, None),
+        P(),
+        P(),
+        P(),
+        P(None, req, seq),
         P(None, seq),
         P(seq),
         P(seq, None),
@@ -267,9 +280,9 @@
         P(seq),
         P(),
         P(),
-        P(seq, "req"),
-    )
-    out_specs = (P("req", seq, None), P("req", None, seq))
+        P(seq, req),
+    )
+    out_specs = (P(req, seq, None), P(req, None, seq))
     return jax.shard_map(
         per_device, mesh=grid, in_specs=in_specs, out_specs=out_specs, check_vma=False
     )

time: 287 us -> 267 us (0.930)
  waiting for transfers between devices: 125 us -> 88.3 us
  blocking collectives: 0 us -> 31.3 us
  local copies, waits for them, and re-layouts: 46.1 us -> 37.8 us
  starting transfers between devices: 42.9 us -> 36.6 us
    all_to_all x0 -> x3, blocking collectives: none -> 31.3 us  [the longest x2 17.1 us: gather_a2a(): lax.all_to_all(copies, axis, split_axis=0, concat_axis=0, tiled=True)]
    all_to_all x1, waiting for transfers between devices: 42.4 us -> 22.4 us  [per_device(): lax.all_to_all(copies, seq, split_axis=0, concat_axis=0, tiled=True)]
    all_to_all x2, waiting for transfers between devices: 34.6 us -> 22 us  [gather_a2a(): lax.all_to_all(copies, axis, split_axis=0, concat_axis=0, tiled=True)]
    all_gather x1 -> x0, local copies, waits for them, and re-layouts: 6.56 us -> none  [per_device(): w_col = lax.all_gather(w_late.T, 'sz', axis=0, tiled=False)]
    all_to_all x1 -> x0, waiting for transfers between devices: 5.47 us -> none  [per_device(): lax.all_to_all(scanned, 'sy', split_axis=2, concat_axis=0, tiled=True)]
    all_to_all x1 -> x0, starting transfers between devices: 3.52 us -> none  [per_device(): lax.all_to_all(scanned, 'sy', split_axis=2, concat_axis=0, tiled=True)]
    slice x2 -> x1, local copies, waits for them, and re-layouts: 3.23 us -> 0.09 us  [per_device(): small_all[:, :proj_cols]]
    broadcast_in_dim x2 -> x5, local copies, waits for them, and re-layouts: 2.85 us -> 5.73 us  [gather_a2a(): copies = jnp.broadcast_to(block[None], (count,) + block.shape)]
  transfers between devices with their start and end apart: 11 -> 10, of which waited for: 8 -> 7; matrix products, arithmetic and copies ran while one was open for 21% -> 18% of each run, Pallas kernels for 10% -> 11%
where the time goes in v12:
time: 267 us; the launch traced here: 266 us
  waiting for transfers between devices  88.3 us (33%)
  local copies, waits for them, and re-layouts  37.8 us (14%)
  starting transfers between devices  36.6 us (14%)
  blocking collectives  31.3 us (12%)
  Pallas kernels  28.9 us (11%)
  matrix products  14.9 us (6%)
  between operations  14.2 us (5%)
  other arithmetic  13.8 us (5%)
    pallas_call x2, Pallas kernels, run_scan(): pl.pallas_call(functools.partial(scan_body, emit), grid=(chunks,), in_spe...  27.2 us
    all_to_all x1, waiting for transfers between devices, per_device(): lax.all_to_all(copies, seq, split_axis=0, concat_axis=0, tiled=True)  22.4 us
    all_to_all x2, waiting for transfers between devices, gather_a2a(): lax.all_to_all(copies, axis, split_axis=0, concat_axis=0, tiled=True)  22 us
    all_to_all x2, blocking collectives, gather_a2a(): lax.all_to_all(copies, axis, split_axis=0, concat_axis=0, tiled=True)  17.1 us
    reduce_scatter x1, waiting for transfers between devices, per_device(): lax.psum_scatter(partial.reshape(cols_n * rows, model), 'sy', scatter_dim...  16.2 us
    all_to_all x1, waiting for transfers between devices, per_device(): lax.all_to_all(inner, seq, split_axis=0, concat_axis=1, tiled=True)  15.3 us
    all_to_all x1, blocking collectives, per_device(): lax.all_to_all(scanned, 'sy', split_axis=2, concat_axis=0, tiled=True)  14.3 us
    all_to_all x2, starting transfers between devices, gather_a2a(): lax.all_to_all(copies, axis, split_axis=0, concat_axis=0, tiled=True)  12 us
  transfers between devices with their start and end apart: 10, of which 7 were waited for; matrix products, arithmetic and copies ran while one was open for 18% of the time, Pallas kernels for 11%

profile of v12, /device:TPU:1, one launch (start us, length us, event | category | flops | bytes accessed | tf_op | source)
XLA Modules:
  0.0 265.7 jit_solution(15880862699218784414)
XLA Ops:
  9.2 2.0 fusion.17
  12.6 8.6 %all-to-all-start.2 = ((bf16[16,289,128]{2,1,0:T(8,128)(2,1)}), bf16[16,289,128]{2,1,0:T(8,128)(2,1)S(1)}, u32[]{:S(2)}, u32[]{:S(2)}) async-start(bf16[16,289,128]{2,1,0:T(8,128)(2,1)} %broadcast_in_dim.54), calls=%async_computation.2 | async-start | bytes 2424832 | tf_op jit(solution)/shard_map/all_to_all | solution.py:172
  21.5 22.4 %all-to-all-done.2 = bf16[16,289,128]{2,1,0:T(8,128)(2,1)S(1)} async-done(((bf16[16,289,128]{2,1,0:T(8,128)(2,1)}), bf16[16,289,128]{2,1,0:T(8,128)(2,1)S(1)}, u32[]{:S(2)}, u32[]{:S(2)}) %all-to-all-start.2) | async-done | bytes 1183776 | tf_op jit(solution)/shard_map/all_to_all | solution.py:172
  44.3 8.9 %all_to_all.68 = bf16[2,1,16,289,128]{4,2,3,1,0:T(8,128)(2,1)S(1)} all-to-all(bf16[2,1,16,289,128]{4,2,3,1,0:T(8,128)(2,1)S(1)} %broadcast_in_dim.55), channel_id=1, replica_groups=mesh['rx'=4,'rc'=2,'sz'=4,'sy'=4] {'rc'}, dimensions={0} | all-to-all | bytes 4734976 | tf_op jit(solution)/shard_map/all_to_all | solution.py:17
  54.6 4.5 %all-to-all-start = ((bf16[4,1,3,256,256]{3,4,2,1,0:T(8,128)(2,1)}), bf16[4,1,3,256,256]{3,4,2,1,0:T(8,128)(2,1)}, u32[]{:S(2)}, u32[]{:S(2)}) async-start(bf16[4,1,3,256,256]{3,4,2,1,0:T(8,128)(2,1)} %broadcast_in_dim.23), calls=%async_computation | async-start | bytes 3145728 | tf_op jit(solution)/shard_map/all_to_all | solution.py:17
  62.9 16.7 %all-to-all-done = bf16[4,1,3,256,256]{3,4,2,1,0:T(8,128)(2,1)} async-done(((bf16[4,1,3,256,256]{3,4,2,1,0:T(8,128)(2,1)}), bf16[4,1,3,256,256]{3,4,2,1,0:T(8,128)(2,1)}, u32[]{:S(2)}, u32[]{:S(2)}) %all-to-all-start) | async-done | bytes 1572896 | tf_op jit(solution)/shard_map/all_to_all | solution.py:17
  79.6 2.7 %copy.61 = bf16[4,3,256,256]{2,0,3,1:T(4,128)(2,1)S(1)} copy(bf16[4,3,256,256]{2,3,1,0:T(8,128)(2,1)} %bitcast.5) | data formatting | bytes 3145728 | tf_op jit(solution)/shard_map/broadcast_in_dim | solution.py:16
  83.1 8.1 %all_to_all.69 = bf16[2,1,4,3,256,256]{4,2,5,3,1,0:T(4,128)(2,1)} all-to-all(bf16[2,1,4,3,256,256]{4,2,5,3,1,0:T(4,128)(2,1)S(1)} %broadcast_in_dim.25), channel_id=1, replica_groups=mesh['rx'=4,'rc'=2,'sz'=4,'sy'=4] {'rc'}, dimensions={0} | all-to-all | bytes 6291456 | tf_op jit(solution)/shard_map/all_to_all | solution.py:17
  91.2 4.4 %copy.62 = bf16[2,1,4,3,256,256]{5,4,3,0,2,1:T(8,128)(2,1)S(1)} copy(bf16[2,1,4,3,256,256]{4,2,5,3,1,0:T(4,128)(2,1)} %all_to_all.69) | data formatting | bytes 6291456 | tf_op jit(solution)/shard_map/all_to_all | solution.py:17
  99.5 6.9 %fusion.2 = f32[2048,512]{1,0:T(8,128)S(1)} fusion(bf16[2048,2048]{1,0:T(8,128)(2,1)} %all-gather.4.cloned.1.call-done, bf16[2048,256]{1,0:T(8,128)(2,1)S(1)} %get-tuple-element.27, bf16[2048,256]{1,0:T(8,128)(2,1)S(1)} %get-tuple-element.26), kind=kOutput, calls=%fused_computation.7 | convolution fusion | flops 4299161600 | bytes 14680064 | tf_op jit(solution)/shard_map/dot_general | solution.py:184
  106.7 1.7 copy-done.3
  108.4 2.4 multiply_convert_fusion
  110.8 4.0 %all-to-all-start.4 = ((bf16[16,128,256]{2,1,0:T(8,128)(2,1)}), bf16[16,128,256]{2,1,0:T(8,128)(2,1)S(1)}, u32[]{:S(2)}, u32[]{:S(2)}) async-start(bf16[16,128,256]{2,1,0:T(8,128)(2,1)} %bitcast.22), calls=%async_computation.4 | async-start | bytes 2097152 | tf_op jit(solution)/shard_map/all_to_all | solution.py:198
  117.6 15.3 %all-to-all-done.4 = bf16[16,128,256]{2,1,0:T(8,128)(2,1)S(1)} async-done(((bf16[16,128,256]{2,1,0:T(8,128)(2,1)}), bf16[16,128,256]{2,1,0:T(8,128)(2,1)S(1)}, u32[]{:S(2)}, u32[]{:S(2)}) %all-to-all-start.4) | async-done | bytes 1048608 | tf_op jit(solution)/shard_map/all_to_all | solution.py:198
  137.1 1.7 copy.81
  138.8 1.9 copy.77.value_ref
  141.4 11.7 %shard_map.140 = (f32[16,32,128]{2,1,0:T(8,128)}, f32[1,32,128]{2,1,0:T(8,128)}) custom-call(f32[2048]{0:T(1024)} %reshape.114.into_ref, f32[2048]{0:T(1024)} %reshape.115.outof_ref, f32[128,32,128]{2,1,0:T(8,128)} %bitcast.129, f32[128,32,128]{2,1,0:T(8,128)} %copy.77.value_ref, f32[16,32,128]{2,1,0:T(8,128)} %bitcast.135, ...), custom_call_target="tpu_custom_call" | custom-call | flops 50331648 | bytes 4194304 | tf_op jit(solution)/shard_map/pallas_call | solution.py:84
  155.8 4.8 %all-to-all-start.5 = ((f32[16,17,256]{2,1,0:T(8,128)}), f32[16,17,256]{2,1,0:T(8,128)S(1)}, u32[]{:S(2)}, u32[]{:S(2)}) async-start(f32[16,17,256]{2,1,0:T(8,128)} %maximum_bitcast_fusion), calls=%async_computation.5 | async-start | bytes 786432 | tf_op jit(solution)/shard_map/all_to_all | solution.py:228
  162.0 7.5 %all-to-all-done.5.pair_ref = f32[16,17,256]{2,1,0:T(8,128)S(1)} async-done(((f32[16,17,256]{2,1,0:T(8,128)}), f32[16,17,256]{2,1,0:T(8,128)S(1)}, u32[]{:S(2)}, u32[]{:S(2)}) %all-to-all-start.5) | async-done | bytes 278560 | tf_op jit(solution)/shard_map/all_to_all | solution.py:228
  170.3 1.7 shard_map.141
  172.0 3.5 %all-to-all-start.6 = ((f32[16,16,256]{2,1,0:T(8,128)}), f32[16,16,256]{2,1,0:T(8,128)S(1)}, u32[]{:S(2)}, u32[]{:S(2)}) async-start(f32[16,16,256]{2,1,0:T(8,128)} %get-tuple-element.23), calls=%async_computation.6 | async-start | bytes 524288 | tf_op jit(solution)/shard_map/all_to_all | solution.py:233
  175.5 2.7 %slice.114 = bf16[2048,256]{1,0:T(8,128)(2,1)} slice(f32[2048,512]{1,0:T(8,128)} %copy-done.3), slice={[0:2048], [256:512]} | slice | bytes 2097152 | tf_op jit(solution)/shard_map/slice | solution.py:188
  178.2 4.8 %all-to-all-done.6 = f32[16,16,256]{2,1,0:T(8,128)S(1)} async-done(((f32[16,16,256]{2,1,0:T(8,128)}), f32[16,16,256]{2,1,0:T(8,128)S(1)}, u32[]{:S(2)}, u32[]{:S(2)}) %all-to-all-start.6) | async-done | bytes 262176 | tf_op jit(solution)/shard_map/all_to_all | solution.py:233
  183.0 3.5 %all-to-all-start.8 = ((bf16[4,512,256]{2,1,0:T(8,128)(2,1)}), bf16[4,512,256]{2,1,0:T(8,128)(2,1)S(1)}, u32[]{:S(2)}, u32[]{:S(2)}) async-start(bf16[4,512,256]{2,1,0:T(8,128)(2,1)} %bitcast.35), calls=%async_computation.8 | async-start | bytes 2097152 | tf_op jit(solution)/shard_map/all_to_all | solution.py:189
  187.5 15.5 %shard_map.142 = f32[128,32,128]{2,1,0:T(8,128)} custom-call(f32[2048]{0:T(1024)} %reshape.114.into_ref, f32[2048]{0:T(1024)} %reshape.115.outof_ref, f32[128,32,128]{2,1,0:T(8,128)} %bitcast.130, f32[128,32,128]{2,1,0:T(8,128)} %copy.77.value_ref, f32[16,32,128]{2,1,0:T(8,128)} %bitcast.136, f32[16,32,128]{2,1,0:T(8,128)} %reshape_reshape.3.start_ref, ...), custom_call_target="tpu_custom_call" | custom-call | flops 50331648 | bytes 6291456 | tf_op jit(solution)/shard_map/pallas_call | solution.py:84
  203.0 1.8 convert_element_type.95
  205.9 14.3 %all_to_all.70 = bf16[128,4,4,256]{3,0,1,2:T(8,128)(2,1)S(1)} all-to-all(bf16[128,4,4,256]{3,0,1,2:T(8,128)(2,1)S(1)} %copy.73), channel_id=1, replica_groups=mesh['rx'=4,'rc'=2,'sz'=4,'sy'=4] {'sy'}, dimensions={2} | all-to-all | bytes 2097152 | tf_op jit(solution)/shard_map/all_to_all | solution.py:240
  220.2 6.1 %bitcast_convert_fusion = bf16[4,128,2048]{2,1,0:T(8,128)(2,1)} fusion(bf16[4,256,2048,1]{2,1,3,0:T(8,128)(2,1)} %bitcast.146, bf16[4,4,128,256]{3,2,1,0:T(8,128)(2,1)S(1)} %bitcast.133, bf16[128,4,4,256]{3,0,1,2:T(8,128)(2,1)S(1)} %all_to_all.70), kind=kOutput, calls=%fused_computation.2 | convolution fusion | flops 2152726528 | bytes 8388608 | tf_op jit(solution)/shard_map/ktac,acd->ktd/dot_general | solution.py:246
  227.6 7.5 %all-to-all-start.9 = ((f32[8,1,16,256]{3,2,1,0:T(8,128)}), f32[8,1,16,256]{3,2,1,0:T(8,128)S(1)}, u32[]{:S(2)}, u32[]{:S(2)}) async-start(f32[8,1,16,256]{3,2,1,0:T(8,128)} %broadcast_in_dim.58), calls=%async_computation.10 | async-start | bytes 262144 | tf_op jit(solution)/shard_map/all_to_all | solution.py:17
  235.1 5.3 %all-to-all-done.9 = f32[8,1,16,256]{3,2,1,0:T(8,128)S(1)} async-done(((f32[8,1,16,256]{3,2,1,0:T(8,128)}), f32[8,1,16,256]{3,2,1,0:T(8,128)S(1)}, u32[]{:S(2)}, u32[]{:S(2)}) %all-to-all-start.9) | async-done | bytes 131104 | tf_op jit(solution)/shard_map/all_to_all | solution.py:17
  241.1 16.2 %reduce-scatter.2.cloned.1.call-done = bf16[128,2048]{1,0:T(8,128)(2,1)} async-done(((bf16[512,2048]{1,0:T(8,128)(2,1)}), bf16[128,2048]{1,0:T(8,128)(2,1)}) %reduce-scatter.2.cloned.1.call-update) | async-done | bytes 524304 | tf_op jit(solution)/shard_map/reduce_scatter | solution.py:249
  257.3 2.0 fusion.22
  (95 shorter events, 30.5 us)
Async XLA Ops:
  7.2 4.1 %copy-start.13 = (bf16[256]{0:T(256)(128)(2,1)S(1)}, bf16[256]{0:T(256)(128)(2,1)}, u32[]{:S(2)}) copy-start(bf16[256]{0:T(256)(128)(2,1)} %param.22) | copy-start | bytes 1540
  7.2 4.1 %copy-start.10 = (bf16[128,256]{1,0:T(8,128)(2,1)S(1)}, bf16[128,256]{1,0:T(8,128)(2,1)}, u32[]{:S(2)}) copy-start(bf16[128,256]{1,0:T(8,128)(2,1)} %param.21) | copy-start | bytes 196612
  7.2 4.1 %copy-start.9 = (bf16[256,160]{0,1:T(8,128)(2,1)S(1)}, bf16[256,160]{0,1:T(8,128)(2,1)}, u32[]{:S(2)}) copy-start(bf16[256,160]{0,1:T(8,128)(2,1)} %param.20) | copy-start | bytes 245764
  7.2 89.7 %all-gather.4.cloned.1.call-start = ((), (), s32[]{:S(2)}) async-start(), calls=%async_computation.11 | async-start | bytes 8912896 | tf_op jit(solution)/shard_map/all_gather | solution.py:156
  11.2 9.9 %copy-start.8 = (bf16[256,256]{1,0:T(8,128)(2,1)S(1)}, bf16[256,256]{1,0:T(8,128)(2,1)}, u32[]{:S(2)}) copy-start(bf16[256,256]{1,0:T(8,128)(2,1)} %param.25) | copy-start | bytes 393220
  11.3 10.0 %copy-start.6 = (bf16[2,256,256]{2,1,0:T(8,128)(2,1)S(1)}, bf16[2,256,256]{2,1,0:T(8,128)(2,1)}, u32[]{:S(2)}) copy-start(bf16[2,256,256]{2,1,0:T(8,128)(2,1)} %param.17) | copy-start | bytes 786436
  12.6 31.3 %all-to-all-start.2 = ((bf16[16,289,128]{2,1,0:T(8,128)(2,1)}), bf16[16,289,128]{2,1,0:T(8,128)(2,1)S(1)}, u32[]{:S(2)}, u32[]{:S(2)}) async-start(bf16[16,289,128]{2,1,0:T(8,128)(2,1)} %broadcast_in_dim.54), calls=%async_computation.2 | async-start | bytes 2424832 | tf_op jit(solution)/shard_map/all_to_all | solution.py:172
  53.3 5.9 %copy-start.14 = (bf16[256]{0:T(256)(128)(2,1)S(1)}, bf16[256]{0:T(256)(128)(2,1)}, u32[]{:S(2)}) copy-start(bf16[256]{0:T(256)(128)(2,1)} %param.19) | copy-start | bytes 1540
  53.3 5.9 %copy-start.12 = (bf16[4,256]{1,0:T(4,128)(2,1)S(1)}, bf16[4,256]{1,0:T(4,128)(2,1)}, u32[]{:S(2)}) copy-start(bf16[4,256]{1,0:T(4,128)(2,1)} %param.18) | copy-start | bytes 6148
  54.6 25.0 %all-to-all-start = ((bf16[4,1,3,256,256]{3,4,2,1,0:T(8,128)(2,1)}), bf16[4,1,3,256,256]{3,4,2,1,0:T(8,128)(2,1)}, u32[]{:S(2)}, u32[]{:S(2)}) async-start(bf16[4,1,3,256,256]{3,4,2,1,0:T(8,128)(2,1)} %broadcast_in_dim.23), calls=%async_computation | async-start | bytes 3145728 | tf_op jit(solution)/shard_map/all_to_all | solution.py:17
  59.1 161.1 %all-gather.6.cloned.1.call-start = ((), (), s32[]{:S(2)}) async-start(), calls=%async_computation.13 | async-start | bytes 5242880 | tf_op jit(solution)/shard_map/all_gather | solution.py:186
  96.7 1.2 copy-start.2
  106.4 2.0 copy-start.3
  108.4 6.4 %copy-start.7 = (f32[16,4096]{1,0:T(8,128)S(1)}, f32[16,4096]{1,0:T(8,128)}, u32[]{:S(2)}) copy-start(f32[16,4096]{1,0:T(8,128)} %param.23) | copy-start | bytes 786436
  110.8 5.5 %copy-start.15 = (s32[8]{0:T(128)S(1)}, s32[8]{0:T(128)}, u32[]{:S(2)}) copy-start(s32[8]{0:T(128)} %param.14) | copy-start | bytes 100
  110.8 22.1 %all-to-all-start.4 = ((bf16[16,128,256]{2,1,0:T(8,128)(2,1)}), bf16[16,128,256]{2,1,0:T(8,128)(2,1)S(1)}, u32[]{:S(2)}, u32[]{:S(2)}) async-start(bf16[16,128,256]{2,1,0:T(8,128)(2,1)} %bitcast.22), calls=%async_computation.4 | async-start | bytes 2097152 | tf_op jit(solution)/shard_map/all_to_all | solution.py:198
  114.8 18.7 %copy-start = (bf16[20,8,16,256]{3,1,2,0:T(8,128)(2,1)S(1)}, bf16[20,8,16,256]{3,1,2,0:T(8,128)(2,1)}, u32[]{:S(2)}) copy-start(bf16[20,8,16,256]{3,1,2,0:T(8,128)(2,1)} %copy.79) | copy-start | bytes 3932164
  133.5 2.1 copy-start.5
  155.8 13.7 %all-to-all-start.5 = ((f32[16,17,256]{2,1,0:T(8,128)}), f32[16,17,256]{2,1,0:T(8,128)S(1)}, u32[]{:S(2)}, u32[]{:S(2)}) async-start(f32[16,17,256]{2,1,0:T(8,128)} %maximum_bitcast_fusion), calls=%async_computation.5 | async-start | bytes 786432 | tf_op jit(solution)/shard_map/all_to_all | solution.py:228
  169.5 0.7 copy-start.4
  172.0 11.0 %all-to-all-start.6 = ((f32[16,16,256]{2,1,0:T(8,128)}), f32[16,16,256]{2,1,0:T(8,128)S(1)}, u32[]{:S(2)}, u32[]{:S(2)}) async-start(f32[16,16,256]{2,1,0:T(8,128)} %get-tuple-element.23), calls=%async_computation.6 | async-start | bytes 524288 | tf_op jit(solution)/shard_map/all_to_all | solution.py:233
  183.0 22.8 %all-to-all-start.8 = ((bf16[4,512,256]{2,1,0:T(8,128)(2,1)}), bf16[4,512,256]{2,1,0:T(8,128)(2,1)S(1)}, u32[]{:S(2)}, u32[]{:S(2)}) async-start(bf16[4,512,256]{2,1,0:T(8,128)(2,1)} %bitcast.35), calls=%async_computation.8 | async-start | bytes 2097152 | tf_op jit(solution)/shard_map/all_to_all | solution.py:189
  186.6 70.7 %reduce-scatter.2.cloned.1.call-start = ((), (), s32[]{:S(2)}) async-start(), calls=%async_computation.12 | async-start | bytes 2621440 | tf_op jit(solution)/shard_map/reduce_scatter | solution.py:249
  226.2 0.7 copy-start.11
  226.2 8.8 %copy-start.16 = (s32[8]{0:T(128)S(1)}, s32[8]{0:T(128)}, u32[]{:S(2)}) copy-start(s32[8]{0:T(128)} %param.15) | copy-start | bytes 100
  226.2 31.0 %copy-start.1 = (bf16[1,128,2048]{2,1,0:T(8,128)(2,1)S(1)}, bf16[1,128,2048]{2,1,0:T(8,128)(2,1)}, u32[]{:S(2)}) copy-start(bf16[1,128,2048]{2,1,0:T(8,128)(2,1)} %param.13) | copy-start | bytes 1572868
  227.6 12.8 %all-to-all-start.9 = ((f32[8,1,16,256]{3,2,1,0:T(8,128)}), f32[8,1,16,256]{3,2,1,0:T(8,128)S(1)}, u32[]{:S(2)}, u32[]{:S(2)}) async-start(f32[8,1,16,256]{3,2,1,0:T(8,128)} %broadcast_in_dim.58), calls=%async_computation.10 | async-start | bytes 262144 | tf_op jit(solution)/shard_map/all_to_all | solution.py:17
Sparse Core Ops, SparseCore 0:
  11.4 82.4 all-gather.3
  99.5 55.7 all-gather.5
  226.4 30.8 reduce-scatter.1

commit v13 on v12

--- a/solution.py
+++ b/solution.py
@@ -56,7 +56,7 @@
 
     held0 = tuple(start_ref[n] for n in range(states))
     acc0 = jnp.zeros((SUB, LANES), jnp.float32)
-    held, acc = lax.fori_loop(0, steps, step, (held0, acc0), unroll=2)
+    held, acc = lax.fori_loop(0, steps, step, (held0, acc0), unroll=4)
     if not emit:
         for n in range(states):
             end_ref[n] = held[n]

time: 267 us -> 265 us (level)
  transfers between devices with their start and end apart: 10 -> 10, of which waited for: 7 -> 7; matrix products, arithmetic and copies ran while one was open for 18% -> 18% of each run, Pallas kernels for 11% -> 10%
where the time goes in v13:
time: 265 us; the launch traced here: 264 us
  waiting for transfers between devices  88.3 us (33%)
  local copies, waits for them, and re-layouts  37.8 us (14%)
  starting transfers between devices  36.6 us (14%)
  blocking collectives  31.3 us (12%)
  Pallas kernels  27.1 us (10%)
  matrix products  14.9 us (6%)
  between operations  14.2 us (5%)
  other arithmetic  13.8 us (5%)
    pallas_call x2, Pallas kernels, run_scan(): pl.pallas_call(functools.partial(scan_body, emit), grid=(chunks,), in_spe...  25.4 us
    all_to_all x1, waiting for transfers between devices, per_device(): lax.all_to_all(copies, seq, split_axis=0, concat_axis=0, tiled=True)  22.4 us
    all_to_all x2, waiting for transfers between devices, gather_a2a(): lax.all_to_all(copies, axis, split_axis=0, concat_axis=0, tiled=True)  22 us
    all_to_all x2, blocking collectives, gather_a2a(): lax.all_to_all(copies, axis, split_axis=0, concat_axis=0, tiled=True)  17.1 us
    reduce_scatter x1, waiting for transfers between devices, per_device(): lax.psum_scatter(partial.reshape(cols_n * rows, model), 'sy', scatter_dim...  16.2 us
    all_to_all x1, waiting for transfers between devices, per_device(): lax.all_to_all(inner, seq, split_axis=0, concat_axis=1, tiled=True)  15.3 us
    all_to_all x1, blocking collectives, per_device(): lax.all_to_all(scanned, 'sy', split_axis=2, concat_axis=0, tiled=True)  14.3 us
    all_to_all x2, starting transfers between devices, gather_a2a(): lax.all_to_all(copies, axis, split_axis=0, concat_axis=0, tiled=True)  12 us
  transfers between devices with their start and end apart: 10, of which 7 were waited for; matrix products, arithmetic and copies ran while one was open for 18% of the time, Pallas kernels for 10%

profile of v13, /device:TPU:1, one launch (start us, length us, event | category | flops | bytes accessed | tf_op | source)
XLA Modules:
  0.0 264.0 jit_solution(3677201734558722463)
XLA Ops:
  9.2 2.0 fusion.17
  12.6 8.6 %all-to-all-start.2 = ((bf16[16,289,128]{2,1,0:T(8,128)(2,1)}), bf16[16,289,128]{2,1,0:T(8,128)(2,1)S(1)}, u32[]{:S(2)}, u32[]{:S(2)}) async-start(bf16[16,289,128]{2,1,0:T(8,128)(2,1)} %broadcast_in_dim.54), calls=%async_computation.2 | async-start | bytes 2424832 | tf_op jit(solution)/shard_map/all_to_all | solution.py:172
  21.5 22.4 %all-to-all-done.2 = bf16[16,289,128]{2,1,0:T(8,128)(2,1)S(1)} async-done(((bf16[16,289,128]{2,1,0:T(8,128)(2,1)}), bf16[16,289,128]{2,1,0:T(8,128)(2,1)S(1)}, u32[]{:S(2)}, u32[]{:S(2)}) %all-to-all-start.2) | async-done | bytes 1183776 | tf_op jit(solution)/shard_map/all_to_all | solution.py:172
  44.3 8.9 %all_to_all.68 = bf16[2,1,16,289,128]{4,2,3,1,0:T(8,128)(2,1)S(1)} all-to-all(bf16[2,1,16,289,128]{4,2,3,1,0:T(8,128)(2,1)S(1)} %broadcast_in_dim.55), channel_id=1, replica_groups=mesh['rx'=4,'rc'=2,'sz'=4,'sy'=4] {'rc'}, dimensions={0} | all-to-all | bytes 4734976 | tf_op jit(solution)/shard_map/all_to_all | solution.py:17
  54.6 4.5 %all-to-all-start = ((bf16[4,1,3,256,256]{3,4,2,1,0:T(8,128)(2,1)}), bf16[4,1,3,256,256]{3,4,2,1,0:T(8,128)(2,1)}, u32[]{:S(2)}, u32[]{:S(2)}) async-start(bf16[4,1,3,256,256]{3,4,2,1,0:T(8,128)(2,1)} %broadcast_in_dim.23), calls=%async_computation | async-start | bytes 3145728 | tf_op jit(solution)/shard_map/all_to_all | solution.py:17
  62.9 16.7 %all-to-all-done = bf16[4,1,3,256,256]{3,4,2,1,0:T(8,128)(2,1)} async-done(((bf16[4,1,3,256,256]{3,4,2,1,0:T(8,128)(2,1)}), bf16[4,1,3,256,256]{3,4,2,1,0:T(8,128)(2,1)}, u32[]{:S(2)}, u32[]{:S(2)}) %all-to-all-start) | async-done | bytes 1572896 | tf_op jit(solution)/shard_map/all_to_all | solution.py:17
  79.6 2.7 %copy.61 = bf16[4,3,256,256]{2,0,3,1:T(4,128)(2,1)S(1)} copy(bf16[4,3,256,256]{2,3,1,0:T(8,128)(2,1)} %bitcast.5) | data formatting | bytes 3145728 | tf_op jit(solution)/shard_map/broadcast_in_dim | solution.py:16
  83.1 8.1 %all_to_all.69 = bf16[2,1,4,3,256,256]{4,2,5,3,1,0:T(4,128)(2,1)} all-to-all(bf16[2,1,4,3,256,256]{4,2,5,3,1,0:T(4,128)(2,1)S(1)} %broadcast_in_dim.25), channel_id=1, replica_groups=mesh['rx'=4,'rc'=2,'sz'=4,'sy'=4] {'rc'}, dimensions={0} | all-to-all | bytes 6291456 | tf_op jit(solution)/shard_map/all_to_all | solution.py:17
  91.2 4.4 %copy.62 = bf16[2,1,4,3,256,256]{5,4,3,0,2,1:T(8,128)(2,1)S(1)} copy(bf16[2,1,4,3,256,256]{4,2,5,3,1,0:T(4,128)(2,1)} %all_to_all.69) | data formatting | bytes 6291456 | tf_op jit(solution)/shard_map/all_to_all | solution.py:17
  99.5 6.9 %fusion.2 = f32[2048,512]{1,0:T(8,128)S(1)} fusion(bf16[2048,2048]{1,0:T(8,128)(2,1)} %all-gather.4.cloned.1.call-done, bf16[2048,256]{1,0:T(8,128)(2,1)S(1)} %get-tuple-element.27, bf16[2048,256]{1,0:T(8,128)(2,1)S(1)} %get-tuple-element.26), kind=kOutput, calls=%fused_computation.7 | convolution fusion | flops 4299161600 | bytes 14680064 | tf_op jit(solution)/shard_map/dot_general | solution.py:184
  106.7 1.7 copy-done.3
  108.4 2.4 multiply_convert_fusion
  110.8 4.0 %all-to-all-start.4 = ((bf16[16,128,256]{2,1,0:T(8,128)(2,1)}), bf16[16,128,256]{2,1,0:T(8,128)(2,1)S(1)}, u32[]{:S(2)}, u32[]{:S(2)}) async-start(bf16[16,128,256]{2,1,0:T(8,128)(2,1)} %bitcast.22), calls=%async_computation.4 | async-start | bytes 2097152 | tf_op jit(solution)/shard_map/all_to_all | solution.py:198
  117.6 15.3 %all-to-all-done.4 = bf16[16,128,256]{2,1,0:T(8,128)(2,1)S(1)} async-done(((bf16[16,128,256]{2,1,0:T(8,128)(2,1)}), bf16[16,128,256]{2,1,0:T(8,128)(2,1)S(1)}, u32[]{:S(2)}, u32[]{:S(2)}) %all-to-all-start.4) | async-done | bytes 1048608 | tf_op jit(solution)/shard_map/all_to_all | solution.py:198
  137.1 1.7 copy.81
  138.8 1.9 copy.77.value_ref
  141.4 10.8 %shard_map.140 = (f32[16,32,128]{2,1,0:T(8,128)}, f32[1,32,128]{2,1,0:T(8,128)}) custom-call(f32[2048]{0:T(1024)} %reshape.114.into_ref, f32[2048]{0:T(1024)} %reshape.115.outof_ref, f32[128,32,128]{2,1,0:T(8,128)} %bitcast.129, f32[128,32,128]{2,1,0:T(8,128)} %copy.77.value_ref, f32[16,32,128]{2,1,0:T(8,128)} %bitcast.135, ...), custom_call_target="tpu_custom_call" | custom-call | flops 50331648 | bytes 4194304 | tf_op jit(solution)/shard_map/pallas_call | solution.py:84
  154.9 4.8 %all-to-all-start.5 = ((f32[16,17,256]{2,1,0:T(8,128)}), f32[16,17,256]{2,1,0:T(8,128)S(1)}, u32[]{:S(2)}, u32[]{:S(2)}) async-start(f32[16,17,256]{2,1,0:T(8,128)} %maximum_bitcast_fusion), calls=%async_computation.5 | async-start | bytes 786432 | tf_op jit(solution)/shard_map/all_to_all | solution.py:228
  161.1 7.5 %all-to-all-done.5.pair_ref = f32[16,17,256]{2,1,0:T(8,128)S(1)} async-done(((f32[16,17,256]{2,1,0:T(8,128)}), f32[16,17,256]{2,1,0:T(8,128)S(1)}, u32[]{:S(2)}, u32[]{:S(2)}) %all-to-all-start.5) | async-done | bytes 278560 | tf_op jit(solution)/shard_map/all_to_all | solution.py:228
  169.4 1.7 shard_map.141
  171.1 3.5 %all-to-all-start.6 = ((f32[16,16,256]{2,1,0:T(8,128)}), f32[16,16,256]{2,1,0:T(8,128)S(1)}, u32[]{:S(2)}, u32[]{:S(2)}) async-start(f32[16,16,256]{2,1,0:T(8,128)} %get-tuple-element.23), calls=%async_computation.6 | async-start | bytes 524288 | tf_op jit(solution)/shard_map/all_to_all | solution.py:233
  174.7 2.7 %slice.114 = bf16[2048,256]{1,0:T(8,128)(2,1)} slice(f32[2048,512]{1,0:T(8,128)} %copy-done.3), slice={[0:2048], [256:512]} | slice | bytes 2097152 | tf_op jit(solution)/shard_map/slice | solution.py:188
  177.3 4.8 %all-to-all-done.6 = f32[16,16,256]{2,1,0:T(8,128)S(1)} async-done(((f32[16,16,256]{2,1,0:T(8,128)}), f32[16,16,256]{2,1,0:T(8,128)S(1)}, u32[]{:S(2)}, u32[]{:S(2)}) %all-to-all-start.6) | async-done | bytes 262176 | tf_op jit(solution)/shard_map/all_to_all | solution.py:233
  182.2 3.5 %all-to-all-start.8 = ((bf16[4,512,256]{2,1,0:T(8,128)(2,1)}), bf16[4,512,256]{2,1,0:T(8,128)(2,1)S(1)}, u32[]{:S(2)}, u32[]{:S(2)}) async-start(bf16[4,512,256]{2,1,0:T(8,128)(2,1)} %bitcast.35), calls=%async_computation.8 | async-start | bytes 2097152 | tf_op jit(solution)/shard_map/all_to_all | solution.py:189
  186.6 14.6 %shard_map.142 = f32[128,32,128]{2,1,0:T(8,128)} custom-call(f32[2048]{0:T(1024)} %reshape.114.into_ref, f32[2048]{0:T(1024)} %reshape.115.outof_ref, f32[128,32,128]{2,1,0:T(8,128)} %bitcast.130, f32[128,32,128]{2,1,0:T(8,128)} %copy.77.value_ref, f32[16,32,128]{2,1,0:T(8,128)} %bitcast.136, f32[16,32,128]{2,1,0:T(8,128)} %reshape_reshape.3.start_ref, ...), custom_call_target="tpu_custom_call" | custom-call | flops 50331648 | bytes 6291456 | tf_op jit(solution)/shard_map/pallas_call | solution.py:84
  201.2 1.8 convert_element_type.95
  204.1 14.3 %all_to_all.70 = bf16[128,4,4,256]{3,0,1,2:T(8,128)(2,1)S(1)} all-to-all(bf16[128,4,4,256]{3,0,1,2:T(8,128)(2,1)S(1)} %copy.73), channel_id=1, replica_groups=mesh['rx'=4,'rc'=2,'sz'=4,'sy'=4] {'sy'}, dimensions={2} | all-to-all | bytes 2097152 | tf_op jit(solution)/shard_map/all_to_all | solution.py:240
  218.4 6.1 %bitcast_convert_fusion = bf16[4,128,2048]{2,1,0:T(8,128)(2,1)} fusion(bf16[4,256,2048,1]{2,1,3,0:T(8,128)(2,1)} %bitcast.146, bf16[4,4,128,256]{3,2,1,0:T(8,128)(2,1)S(1)} %bitcast.133, bf16[128,4,4,256]{3,0,1,2:T(8,128)(2,1)S(1)} %all_to_all.70), kind=kOutput, calls=%fused_computation.2 | convolution fusion | flops 2152726528 | bytes 8388608 | tf_op jit(solution)/shard_map/ktac,acd->ktd/dot_general | solution.py:246
  225.9 7.5 %all-to-all-start.9 = ((f32[8,1,16,256]{3,2,1,0:T(8,128)}), f32[8,1,16,256]{3,2,1,0:T(8,128)S(1)}, u32[]{:S(2)}, u32[]{:S(2)}) async-start(f32[8,1,16,256]{3,2,1,0:T(8,128)} %broadcast_in_dim.58), calls=%async_computation.10 | async-start | bytes 262144 | tf_op jit(solution)/shard_map/all_to_all | solution.py:17
  233.3 5.3 %all-to-all-done.9 = f32[8,1,16,256]{3,2,1,0:T(8,128)S(1)} async-done(((f32[8,1,16,256]{3,2,1,0:T(8,128)}), f32[8,1,16,256]{3,2,1,0:T(8,128)S(1)}, u32[]{:S(2)}, u32[]{:S(2)}) %all-to-all-start.9) | async-done | bytes 131104 | tf_op jit(solution)/shard_map/all_to_all | solution.py:17
  239.3 16.2 %reduce-scatter.2.cloned.1.call-done = bf16[128,2048]{1,0:T(8,128)(2,1)} async-done(((bf16[512,2048]{1,0:T(8,128)(2,1)}), bf16[128,2048]{1,0:T(8,128)(2,1)}) %reduce-scatter.2.cloned.1.call-update) | async-done | bytes 524304 | tf_op jit(solution)/shard_map/reduce_scatter | solution.py:249
  255.5 2.0 fusion.22
  (95 shorter events, 30.5 us)
Async XLA Ops:
  7.2 4.1 %copy-start.13 = (bf16[256]{0:T(256)(128)(2,1)S(1)}, bf16[256]{0:T(256)(128)(2,1)}, u32[]{:S(2)}) copy-start(bf16[256]{0:T(256)(128)(2,1)} %param.22) | copy-start | bytes 1540
  7.2 4.1 %copy-start.10 = (bf16[128,256]{1,0:T(8,128)(2,1)S(1)}, bf16[128,256]{1,0:T(8,128)(2,1)}, u32[]{:S(2)}) copy-start(bf16[128,256]{1,0:T(8,128)(2,1)} %param.21) | copy-start | bytes 196612
  7.2 4.1 %copy-start.9 = (bf16[256,160]{0,1:T(8,128)(2,1)S(1)}, bf16[256,160]{0,1:T(8,128)(2,1)}, u32[]{:S(2)}) copy-start(bf16[256,160]{0,1:T(8,128)(2,1)} %param.20) | copy-start | bytes 245764
  7.2 89.7 %all-gather.4.cloned.1.call-start = ((), (), s32[]{:S(2)}) async-start(), calls=%async_computation.11 | async-start | bytes 8912896 | tf_op jit(solution)/shard_map/all_gather | solution.py:156
  11.2 9.9 %copy-start.8 = (bf16[256,256]{1,0:T(8,128)(2,1)S(1)}, bf16[256,256]{1,0:T(8,128)(2,1)}, u32[]{:S(2)}) copy-start(bf16[256,256]{1,0:T(8,128)(2,1)} %param.25) | copy-start | bytes 393220
  11.3 10.0 %copy-start.6 = (bf16[2,256,256]{2,1,0:T(8,128)(2,1)S(1)}, bf16[2,256,256]{2,1,0:T(8,128)(2,1)}, u32[]{:S(2)}) copy-start(bf16[2,256,256]{2,1,0:T(8,128)(2,1)} %param.17) | copy-start | bytes 786436
  12.6 31.3 %all-to-all-start.2 = ((bf16[16,289,128]{2,1,0:T(8,128)(2,1)}), bf16[16,289,128]{2,1,0:T(8,128)(2,1)S(1)}, u32[]{:S(2)}, u32[]{:S(2)}) async-start(bf16[16,289,128]{2,1,0:T(8,128)(2,1)} %broadcast_in_dim.54), calls=%async_computation.2 | async-start | bytes 2424832 | tf_op jit(solution)/shard_map/all_to_all | solution.py:172
  53.3 5.9 %copy-start.14 = (bf16[256]{0:T(256)(128)(2,1)S(1)}, bf16[256]{0:T(256)(128)(2,1)}, u32[]{:S(2)}) copy-start(bf16[256]{0:T(256)(128)(2,1)} %param.19) | copy-start | bytes 1540
  53.3 5.9 %copy-start.12 = (bf16[4,256]{1,0:T(4,128)(2,1)S(1)}, bf16[4,256]{1,0:T(4,128)(2,1)}, u32[]{:S(2)}) copy-start(bf16[4,256]{1,0:T(4,128)(2,1)} %param.18) | copy-start | bytes 6148
  54.6 25.0 %all-to-all-start = ((bf16[4,1,3,256,256]{3,4,2,1,0:T(8,128)(2,1)}), bf16[4,1,3,256,256]{3,4,2,1,0:T(8,128)(2,1)}, u32[]{:S(2)}, u32[]{:S(2)}) async-start(bf16[4,1,3,256,256]{3,4,2,1,0:T(8,128)(2,1)} %broadcast_in_dim.23), calls=%async_computation | async-start | bytes 3145728 | tf_op jit(solution)/shard_map/all_to_all | solution.py:17
  59.1 159.3 %all-gather.6.cloned.1.call-start = ((), (), s32[]{:S(2)}) async-start(), calls=%async_computation.13 | async-start | bytes 5242880 | tf_op jit(solution)/shard_map/all_gather | solution.py:186
  96.7 1.2 copy-start.2
  106.4 2.0 copy-start.3
  108.4 6.4 %copy-start.7 = (f32[16,4096]{1,0:T(8,128)S(1)}, f32[16,4096]{1,0:T(8,128)}, u32[]{:S(2)}) copy-start(f32[16,4096]{1,0:T(8,128)} %param.23) | copy-start | bytes 786436
  110.8 5.5 %copy-start.15 = (s32[8]{0:T(128)S(1)}, s32[8]{0:T(128)}, u32[]{:S(2)}) copy-start(s32[8]{0:T(128)} %param.14) | copy-start | bytes 100
  110.8 22.1 %all-to-all-start.4 = ((bf16[16,128,256]{2,1,0:T(8,128)(2,1)}), bf16[16,128,256]{2,1,0:T(8,128)(2,1)S(1)}, u32[]{:S(2)}, u32[]{:S(2)}) async-start(bf16[16,128,256]{2,1,0:T(8,128)(2,1)} %bitcast.22), calls=%async_computation.4 | async-start | bytes 2097152 | tf_op jit(solution)/shard_map/all_to_all | solution.py:198
  114.8 18.7 %copy-start = (bf16[20,8,16,256]{3,1,2,0:T(8,128)(2,1)S(1)}, bf16[20,8,16,256]{3,1,2,0:T(8,128)(2,1)}, u32[]{:S(2)}) copy-start(bf16[20,8,16,256]{3,1,2,0:T(8,128)(2,1)} %copy.79) | copy-start | bytes 3932164
  133.5 2.1 copy-start.5
  154.9 13.7 %all-to-all-start.5 = ((f32[16,17,256]{2,1,0:T(8,128)}), f32[16,17,256]{2,1,0:T(8,128)S(1)}, u32[]{:S(2)}, u32[]{:S(2)}) async-start(f32[16,17,256]{2,1,0:T(8,128)} %maximum_bitcast_fusion), calls=%async_computation.5 | async-start | bytes 786432 | tf_op jit(solution)/shard_map/all_to_all | solution.py:228
  168.6 0.7 copy-start.4
  171.1 11.0 %all-to-all-start.6 = ((f32[16,16,256]{2,1,0:T(8,128)}), f32[16,16,256]{2,1,0:T(8,128)S(1)}, u32[]{:S(2)}, u32[]{:S(2)}) async-start(f32[16,16,256]{2,1,0:T(8,128)} %get-tuple-element.23), calls=%async_computation.6 | async-start | bytes 524288 | tf_op jit(solution)/shard_map/all_to_all | solution.py:233
  182.2 21.9 %all-to-all-start.8 = ((bf16[4,512,256]{2,1,0:T(8,128)(2,1)}), bf16[4,512,256]{2,1,0:T(8,128)(2,1)S(1)}, u32[]{:S(2)}, u32[]{:S(2)}) async-start(bf16[4,512,256]{2,1,0:T(8,128)(2,1)} %bitcast.35), calls=%async_computation.8 | async-start | bytes 2097152 | tf_op jit(solution)/shard_map/all_to_all | solution.py:189
  185.7 69.8 %reduce-scatter.2.cloned.1.call-start = ((), (), s32[]{:S(2)}) async-start(), calls=%async_computation.12 | async-start | bytes 2621440 | tf_op jit(solution)/shard_map/reduce_scatter | solution.py:249
  224.5 0.7 copy-start.11
  224.5 8.8 %copy-start.16 = (s32[8]{0:T(128)S(1)}, s32[8]{0:T(128)}, u32[]{:S(2)}) copy-start(s32[8]{0:T(128)} %param.15) | copy-start | bytes 100
  224.5 31.0 %copy-start.1 = (bf16[1,128,2048]{2,1,0:T(8,128)(2,1)S(1)}, bf16[1,128,2048]{2,1,0:T(8,128)(2,1)}, u32[]{:S(2)}) copy-start(bf16[1,128,2048]{2,1,0:T(8,128)(2,1)} %param.13) | copy-start | bytes 1572868
  225.9 12.8 %all-to-all-start.9 = ((f32[8,1,16,256]{3,2,1,0:T(8,128)}), f32[8,1,16,256]{3,2,1,0:T(8,128)S(1)}, u32[]{:S(2)}, u32[]{:S(2)}) async-start(f32[8,1,16,256]{3,2,1,0:T(8,128)} %broadcast_in_dim.58), calls=%async_computation.10 | async-start | bytes 262144 | tf_op jit(solution)/shard_map/all_to_all | solution.py:17
Sparse Core Ops, SparseCore 0:
  11.4 82.4 all-gather.3
  99.5 55.7 all-gather.5
  224.6 30.8 reduce-scatter.1

commit v14 on v13

--- a/solution.py
+++ b/solution.py
@@ -180,12 +180,10 @@
     w_in, xproj_full, dt_full, dt_bias_full = lax.optimization_barrier(
         (w_in, xproj_full, dt_full, dt_bias_full)
     )
-    w_flat = jnp.concatenate((w_in[0], w_in[1]), axis=1)
-    both = jnp.dot(normed_all, w_flat, preferred_element_type=jnp.float32)
+    xin = jnp.dot(normed_all, w_in[0], preferred_element_type=jnp.float32)
     w_late, _ = lax.optimization_barrier((w_out_t, normed_all))
     w_col = lax.all_gather(w_late.T, "sz", axis=0, tiled=False)
-    xin = both[:, :width]
-    zgate = both[:, width:].astype(jnp.bfloat16)
+    zgate = jnp.dot(normed_all, w_in[1], preferred_element_type=jnp.float32).astype(jnp.bfloat16)
     z_grid = lax.all_to_all(
         zgate.reshape(rows_n, span // rows_n, width), "sz", split_axis=0, concat_axis=0, tiled=True
     )

time: 265 us -> 270 us (1.019)
  local copies, waits for them, and re-layouts: 37.8 us -> 42.6 us
  waiting for transfers between devices: 88.3 us -> 84.4 us
    all_to_all x1, waiting for transfers between devices: 4.83 us -> 0.79 us  [per_device(): lax.all_to_all(carry_ch, seq, split_axis=0, concat_axis=0, tiled=True)]
    unnamed x39 -> x43, local copies, waits for them, and re-layouts: 8.39 us -> 12.1 us
    transpose x2, local copies, waits for them, and re-layouts: 1.77 us -> 4.96 us  [per_device(): jnp.swapaxes(small_all[:, proj_cols:proj_cols + RANK], 0, 1)]
    slice x2 -> x0, local copies, waits for them, and re-layouts: 2.91 us -> none  [the longest x1 2.67 us: per_device(): zgate = both[:, width:].astype(jnp.bfloat16)]
    dot_general x1 -> x2, matrix products: 6.87 us -> 9.14 us  [the longest x1 6.71 us: per_device(): jnp.dot(normed_all, w_in[1], preferred_element_type=jnp.float32)]
  transfers between devices with their start and end apart: 10 -> 10, of which waited for: 7 -> 7; matrix products, arithmetic and copies ran while one was open for 18% -> 19% of each run, Pallas kernels for 10% -> 10%
where the time goes in v14:
time: 270 us; the launch traced here: 268 us
  waiting for transfers between devices  84.4 us (31%)
  local copies, waits for them, and re-layouts  42.6 us (16%)
  starting transfers between devices  36.3 us (13%)
  blocking collectives  32.6 us (12%)
  Pallas kernels  27.1 us (10%)
  matrix products  17.2 us (6%)
  between operations  14.2 us (5%)
  other arithmetic  13.7 us (5%)
    pallas_call x2, Pallas kernels, run_scan(): pl.pallas_call(functools.partial(scan_body, emit), grid=(chunks,), in_spe...  25.4 us
    all_to_all x2, waiting for transfers between devices, gather_a2a(): lax.all_to_all(copies, axis, split_axis=0, concat_axis=0, tiled=True)  22.4 us
    all_to_all x1, waiting for transfers between devices, per_device(): lax.all_to_all(copies, seq, split_axis=0, concat_axis=0, tiled=True)  22.4 us
    all_to_all x2, blocking collectives, gather_a2a(): lax.all_to_all(copies, axis, split_axis=0, concat_axis=0, tiled=True)  17.1 us
    reduce_scatter x1, waiting for transfers between devices, per_device(): lax.psum_scatter(partial.reshape(cols_n * rows, model), 'sy', scatter_dim...  16.1 us
    all_to_all x1, blocking collectives, per_device(): lax.all_to_all(scanned, 'sy', split_axis=2, concat_axis=0, tiled=True)  15.6 us
    all_to_all x1, waiting for transfers between devices, per_device(): lax.all_to_all(inner, seq, split_axis=0, concat_axis=1, tiled=True)  15.1 us
    unnamed x43, local copies, waits for them, and re-layouts  12.1 us
  transfers between devices with their start and end apart: 10, of which 7 were waited for; matrix products, arithmetic and copies ran while one was open for 19% of the time, Pallas kernels for 10%

profile of v14, /device:TPU:1, one launch (start us, length us, event | category | flops | bytes accessed | tf_op | source)
XLA Modules:
  0.0 268.3 jit_solution(10254315324500614139)
XLA Ops:
  9.2 2.0 fusion.13
  12.5 8.6 %all-to-all-start.2 = ((bf16[16,289,128]{2,1,0:T(8,128)(2,1)}), bf16[16,289,128]{2,1,0:T(8,128)(2,1)S(1)}, u32[]{:S(2)}, u32[]{:S(2)}) async-start(bf16[16,289,128]{2,1,0:T(8,128)(2,1)} %broadcast_in_dim.54), calls=%async_computation.2 | async-start | bytes 2424832 | tf_op jit(solution)/shard_map/all_to_all | solution.py:172
  21.5 22.4 %all-to-all-done.2 = bf16[16,289,128]{2,1,0:T(8,128)(2,1)S(1)} async-done(((bf16[16,289,128]{2,1,0:T(8,128)(2,1)}), bf16[16,289,128]{2,1,0:T(8,128)(2,1)S(1)}, u32[]{:S(2)}, u32[]{:S(2)}) %all-to-all-start.2) | async-done | bytes 1183776 | tf_op jit(solution)/shard_map/all_to_all | solution.py:172
  44.3 8.9 %all_to_all.68 = bf16[2,1,16,289,128]{4,2,3,1,0:T(8,128)(2,1)S(1)} all-to-all(bf16[2,1,16,289,128]{4,2,3,1,0:T(8,128)(2,1)S(1)} %broadcast_in_dim.55), channel_id=1, replica_groups=mesh['rx'=4,'rc'=2,'sz'=4,'sy'=4] {'rc'}, dimensions={0} | all-to-all | bytes 4734976 | tf_op jit(solution)/shard_map/all_to_all | solution.py:17
  54.5 4.5 %all-to-all-start = ((bf16[4,1,3,256,256]{3,4,2,1,0:T(8,128)(2,1)}), bf16[4,1,3,256,256]{3,4,2,1,0:T(8,128)(2,1)}, u32[]{:S(2)}, u32[]{:S(2)}) async-start(bf16[4,1,3,256,256]{3,4,2,1,0:T(8,128)(2,1)} %broadcast_in_dim.23), calls=%async_computation | async-start | bytes 3145728 | tf_op jit(solution)/shard_map/all_to_all | solution.py:17
  62.5 17.1 %all-to-all-done = bf16[4,1,3,256,256]{3,4,2,1,0:T(8,128)(2,1)} async-done(((bf16[4,1,3,256,256]{3,4,2,1,0:T(8,128)(2,1)}), bf16[4,1,3,256,256]{3,4,2,1,0:T(8,128)(2,1)}, u32[]{:S(2)}, u32[]{:S(2)}) %all-to-all-start) | async-done | bytes 1572896 | tf_op jit(solution)/shard_map/all_to_all | solution.py:17
  79.6 2.7 copy.61
  83.0 8.1 %all_to_all.69 = bf16[2,1,4,3,256,256]{4,2,5,3,1,0:T(4,128)(2,1)} all-to-all(bf16[2,1,4,3,256,256]{4,2,5,3,1,0:T(4,128)(2,1)S(1)} %broadcast_in_dim.25), channel_id=1, replica_groups=mesh['rx'=4,'rc'=2,'sz'=4,'sy'=4] {'rc'}, dimensions={0} | all-to-all | bytes 6291456 | tf_op jit(solution)/shard_map/all_to_all | solution.py:17
  91.1 4.4 %copy.62 = bf16[2,1,4,3,256,256]{5,4,3,0,2,1:T(8,128)(2,1)S(1)} copy(bf16[2,1,4,3,256,256]{4,2,5,3,1,0:T(4,128)(2,1)} %all_to_all.69) | data formatting | bytes 6291456 | tf_op jit(solution)/shard_map/all_to_all | solution.py:17
  96.6 2.3 copy.75
  98.8 2.3 slice_bitcast_fusion
  101.2 2.6 copy.66
  104.8 4.4 %copy-done.14 = bf16[2048,2048]{1,0:T(8,128)(2,1)S(1)} copy-done((bf16[2048,2048]{1,0:T(8,128)(2,1)S(1)}, bf16[2048,2048]{1,0:T(8,128)(2,1)}, u32[]{:S(2)}) %copy-start.14) | copy-done | bytes 8388632
  109.3 2.4 fusion.17
  111.7 2.4 multiply_convert_fusion
  114.1 4.0 %all-to-all-start.4 = ((bf16[16,128,256]{2,1,0:T(8,128)(2,1)}), bf16[16,128,256]{2,1,0:T(8,128)(2,1)S(1)}, u32[]{:S(2)}, u32[]{:S(2)}) async-start(bf16[16,128,256]{2,1,0:T(8,128)(2,1)} %bitcast.21), calls=%async_computation.4 | async-start | bytes 2097152 | tf_op jit(solution)/shard_map/all_to_all | solution.py:196
  120.9 15.1 %all-to-all-done.4 = bf16[16,128,256]{2,1,0:T(8,128)(2,1)S(1)} async-done(((bf16[16,128,256]{2,1,0:T(8,128)(2,1)}), bf16[16,128,256]{2,1,0:T(8,128)(2,1)S(1)}, u32[]{:S(2)}, u32[]{:S(2)}) %all-to-all-start.4) | async-done | bytes 1048608 | tf_op jit(solution)/shard_map/all_to_all | solution.py:196
  141.9 1.9 copy.77.value_ref
  144.5 10.8 %shard_map.140 = (f32[16,32,128]{2,1,0:T(8,128)}, f32[1,32,128]{2,1,0:T(8,128)}) custom-call(f32[2048]{0:T(1024)} %reshape.114.into_ref, f32[2048]{0:T(1024)} %reshape.115.outof_ref, f32[128,32,128]{2,1,0:T(8,128)} %bitcast.133, f32[128,32,128]{2,1,0:T(8,128)} %copy.77.value_ref, f32[16,32,128]{2,1,0:T(8,128)} %bitcast.140, ...), custom_call_target="tpu_custom_call" | custom-call | flops 50331648 | bytes 4194304 | tf_op jit(solution)/shard_map/pallas_call | solution.py:84
  158.2 4.9 %all-to-all-start.5 = ((f32[16,17,256]{2,1,0:T(8,128)}), f32[16,17,256]{2,1,0:T(8,128)S(1)}, u32[]{:S(2)}, u32[]{:S(2)}) async-start(f32[16,17,256]{2,1,0:T(8,128)} %maximum_bitcast_fusion), calls=%async_computation.5 | async-start | bytes 786432 | tf_op jit(solution)/shard_map/all_to_all | solution.py:226
  164.4 7.5 %all-to-all-done.5.pair_ref = f32[16,17,256]{2,1,0:T(8,128)S(1)} async-done(((f32[16,17,256]{2,1,0:T(8,128)}), f32[16,17,256]{2,1,0:T(8,128)S(1)}, u32[]{:S(2)}, u32[]{:S(2)}) %all-to-all-start.5) | async-done | bytes 278560 | tf_op jit(solution)/shard_map/all_to_all | solution.py:226
  174.4 3.5 %all-to-all-start.6 = ((f32[16,16,256]{2,1,0:T(8,128)}), f32[16,16,256]{2,1,0:T(8,128)S(1)}, u32[]{:S(2)}, u32[]{:S(2)}) async-start(f32[16,16,256]{2,1,0:T(8,128)} %get-tuple-element.23), calls=%async_computation.6 | async-start | bytes 524288 | tf_op jit(solution)/shard_map/all_to_all | solution.py:231
  177.9 6.7 %convolution_convert_fusion = bf16[2048,256]{1,0:T(8,128)(2,1)} fusion(bf16[2048,2048]{1,0:T(8,128)(2,1)} %all-gather.4.cloned.1.call-done, bf16[2,2048,256]{2,1,0:T(8,128)(2,1)S(1)} %bitcast.132), kind=kOutput, calls=%fused_computation.3 | convolution fusion | flops 2148007936 | bytes 10485760 | tf_op jit(solution)/shard_map/dot_general | solution.py:186
  185.4 3.5 %all-to-all-start.8 = ((bf16[4,512,256]{2,1,0:T(8,128)(2,1)}), bf16[4,512,256]{2,1,0:T(8,128)(2,1)S(1)}, u32[]{:S(2)}, u32[]{:S(2)}) async-start(bf16[4,512,256]{2,1,0:T(8,128)(2,1)} %bitcast.138), calls=%async_computation.8 | async-start | bytes 2097152 | tf_op jit(solution)/shard_map/all_to_all | solution.py:187
  189.9 14.6 %shard_map.142 = f32[128,32,128]{2,1,0:T(8,128)} custom-call(f32[2048]{0:T(1024)} %reshape.114.into_ref, f32[2048]{0:T(1024)} %reshape.115.outof_ref, f32[128,32,128]{2,1,0:T(8,128)} %bitcast.134, f32[128,32,128]{2,1,0:T(8,128)} %copy.77.value_ref, f32[16,32,128]{2,1,0:T(8,128)} %bitcast.141, f32[16,32,128]{2,1,0:T(8,128)} %reshape_reshape.3.start_ref, ...), custom_call_target="tpu_custom_call" | custom-call | flops 50331648 | bytes 6291456 | tf_op jit(solution)/shard_map/pallas_call | solution.py:84
  204.5 1.8 convert_element_type.97
  207.4 15.6 %all_to_all.70 = bf16[128,4,4,256]{3,0,1,2:T(8,128)(2,1)S(1)} all-to-all(bf16[128,4,4,256]{3,0,1,2:T(8,128)(2,1)S(1)} %copy.73), channel_id=1, replica_groups=mesh['rx'=4,'rc'=2,'sz'=4,'sy'=4] {'sy'}, dimensions={2} | all-to-all | bytes 2097152 | tf_op jit(solution)/shard_map/all_to_all | solution.py:238
  223.0 6.1 %bitcast_convert_fusion = bf16[4,128,2048]{2,1,0:T(8,128)(2,1)} fusion(bf16[4,256,2048,1]{2,1,3,0:T(8,128)(2,1)} %bitcast.151, bf16[4,4,128,256]{3,2,1,0:T(8,128)(2,1)S(1)} %bitcast.137, bf16[128,4,4,256]{3,0,1,2:T(8,128)(2,1)S(1)} %all_to_all.70), kind=kOutput, calls=%fused_computation.2 | convolution fusion | flops 2152726528 | bytes 8388608 | tf_op jit(solution)/shard_map/ktac,acd->ktd/dot_general | solution.py:244
  230.4 7.2 %all-to-all-start.9 = ((f32[8,1,16,256]{3,2,1,0:T(8,128)}), f32[8,1,16,256]{3,2,1,0:T(8,128)S(1)}, u32[]{:S(2)}, u32[]{:S(2)}) async-start(f32[8,1,16,256]{3,2,1,0:T(8,128)} %broadcast_in_dim.58), calls=%async_computation.10 | async-start | bytes 262144 | tf_op jit(solution)/shard_map/all_to_all | solution.py:17
  237.7 5.3 %all-to-all-done.9 = f32[8,1,16,256]{3,2,1,0:T(8,128)S(1)} async-done(((f32[8,1,16,256]{3,2,1,0:T(8,128)}), f32[8,1,16,256]{3,2,1,0:T(8,128)S(1)}, u32[]{:S(2)}, u32[]{:S(2)}) %all-to-all-start.9) | async-done | bytes 131104 | tf_op jit(solution)/shard_map/all_to_all | solution.py:17
  243.7 16.1 %reduce-scatter.2.cloned.1.call-done = bf16[128,2048]{1,0:T(8,128)(2,1)} async-done(((bf16[512,2048]{1,0:T(8,128)(2,1)}), bf16[128,2048]{1,0:T(8,128)(2,1)}) %reduce-scatter.2.cloned.1.call-update) | async-done | bytes 524304 | tf_op jit(solution)/shard_map/reduce_scatter | solution.py:247
  259.8 2.0 fusion.23
  (97 shorter events, 32.3 us)
Async XLA Ops:
  7.2 4.1 %copy-start.10 = (bf16[256,160]{0,1:T(8,128)(2,1)S(1)}, bf16[256,160]{0,1:T(8,128)(2,1)}, u32[]{:S(2)}) copy-start(bf16[256,160]{0,1:T(8,128)(2,1)} %param.20) | copy-start | bytes 245764
  7.2 4.1 %copy-start.11 = (bf16[128,256]{1,0:T(8,128)(2,1)S(1)}, bf16[128,256]{1,0:T(8,128)(2,1)}, u32[]{:S(2)}) copy-start(bf16[128,256]{1,0:T(8,128)(2,1)} %param.21) | copy-start | bytes 196612
  7.2 4.1 %copy-start.15 = (bf16[256]{0:T(256)(128)(2,1)S(1)}, bf16[256]{0:T(256)(128)(2,1)}, u32[]{:S(2)}) copy-start(bf16[256]{0:T(256)(128)(2,1)} %param.22) | copy-start | bytes 1540
  7.2 89.4 %all-gather.4.cloned.1.call-start = ((), (), s32[]{:S(2)}) async-start(), calls=%async_computation.11 | async-start | bytes 8912896 | tf_op jit(solution)/shard_map/all_gather | solution.py:156
  11.2 9.9 %copy-start.9 = (bf16[256,256]{1,0:T(8,128)(2,1)S(1)}, bf16[256,256]{1,0:T(8,128)(2,1)}, u32[]{:S(2)}) copy-start(bf16[256,256]{1,0:T(8,128)(2,1)} %param.25) | copy-start | bytes 393220
  11.3 10.0 %copy-start.7 = (bf16[2,256,256]{2,1,0:T(8,128)(2,1)S(1)}, bf16[2,256,256]{2,1,0:T(8,128)(2,1)}, u32[]{:S(2)}) copy-start(bf16[2,256,256]{2,1,0:T(8,128)(2,1)} %param.17) | copy-start | bytes 786436
  12.5 31.3 %all-to-all-start.2 = ((bf16[16,289,128]{2,1,0:T(8,128)(2,1)}), bf16[16,289,128]{2,1,0:T(8,128)(2,1)S(1)}, u32[]{:S(2)}, u32[]{:S(2)}) async-start(bf16[16,289,128]{2,1,0:T(8,128)(2,1)} %broadcast_in_dim.54), calls=%async_computation.2 | async-start | bytes 2424832 | tf_op jit(solution)/shard_map/all_to_all | solution.py:172
  53.3 5.8 %copy-start.16 = (bf16[256]{0:T(256)(128)(2,1)S(1)}, bf16[256]{0:T(256)(128)(2,1)}, u32[]{:S(2)}) copy-start(bf16[256]{0:T(256)(128)(2,1)} %param.19) | copy-start | bytes 1540
  53.3 5.9 %copy-start.13 = (bf16[4,256]{1,0:T(4,128)(2,1)S(1)}, bf16[4,256]{1,0:T(4,128)(2,1)}, u32[]{:S(2)}) copy-start(bf16[4,256]{1,0:T(4,128)(2,1)} %param.18) | copy-start | bytes 6148
  54.5 25.0 %all-to-all-start = ((bf16[4,1,3,256,256]{3,4,2,1,0:T(8,128)(2,1)}), bf16[4,1,3,256,256]{3,4,2,1,0:T(8,128)(2,1)}, u32[]{:S(2)}, u32[]{:S(2)}) async-start(bf16[4,1,3,256,256]{3,4,2,1,0:T(8,128)(2,1)} %broadcast_in_dim.23), calls=%async_computation | async-start | bytes 3145728 | tf_op jit(solution)/shard_map/all_to_all | solution.py:17
  59.1 163.9 %all-gather.6.cloned.1.call-start = ((), (), s32[]{:S(2)}) async-start(), calls=%async_computation.13 | async-start | bytes 5242880 | tf_op jit(solution)/shard_map/all_gather | solution.py:185
  59.4 1.4 copy-start
  104.5 4.8 %copy-start.14 = (bf16[2048,2048]{1,0:T(8,128)(2,1)S(1)}, bf16[2048,2048]{1,0:T(8,128)(2,1)}, u32[]{:S(2)}) copy-start(bf16[2048,2048]{1,0:T(8,128)(2,1)} %all-gather.4.cloned.1.call-done) | copy-start | bytes 25165828
  104.8 6.9 %copy-start.3 = (bf16[2,8,256,256]{3,2,1,0:T(8,128)(2,1)}, bf16[2,8,256,256]{3,2,1,0:T(8,128)(2,1)S(1)}, u32[]{:S(2)}) copy-start(bf16[2,8,256,256]{3,2,1,0:T(8,128)(2,1)S(1)} %copy.63) | copy-start | bytes 6291460
  111.7 6.4 %copy-start.8 = (f32[16,4096]{1,0:T(8,128)S(1)}, f32[16,4096]{1,0:T(8,128)}, u32[]{:S(2)}) copy-start(f32[16,4096]{1,0:T(8,128)} %param.23) | copy-start | bytes 786436
  114.1 5.5 %copy-start.17 = (s32[8]{0:T(128)S(1)}, s32[8]{0:T(128)}, u32[]{:S(2)}) copy-start(s32[8]{0:T(128)} %param.14) | copy-start | bytes 100
  114.1 21.9 %all-to-all-start.4 = ((bf16[16,128,256]{2,1,0:T(8,128)(2,1)}), bf16[16,128,256]{2,1,0:T(8,128)(2,1)S(1)}, u32[]{:S(2)}, u32[]{:S(2)}) async-start(bf16[16,128,256]{2,1,0:T(8,128)(2,1)} %bitcast.21), calls=%async_computation.4 | async-start | bytes 2097152 | tf_op jit(solution)/shard_map/all_to_all | solution.py:196
  118.1 18.6 %copy-start.1 = (bf16[20,8,16,256]{3,1,2,0:T(8,128)(2,1)S(1)}, bf16[20,8,16,256]{3,1,2,0:T(8,128)(2,1)}, u32[]{:S(2)}) copy-start(bf16[20,8,16,256]{3,1,2,0:T(8,128)(2,1)} %copy.79) | copy-start | bytes 3932164
  136.7 2.1 copy-start.6
  155.3 22.6 %copy-start.4 = (bf16[2,8,256,256]{3,2,1,0:T(8,128)(2,1)S(1)}, bf16[2,8,256,256]{3,2,1,0:T(8,128)(2,1)}, u32[]{:S(2)}) copy-start(bf16[2,8,256,256]{3,2,1,0:T(8,128)(2,1)} %copy-done.3) | copy-start | bytes 6291460
  158.2 13.7 %all-to-all-start.5 = ((f32[16,17,256]{2,1,0:T(8,128)}), f32[16,17,256]{2,1,0:T(8,128)S(1)}, u32[]{:S(2)}, u32[]{:S(2)}) async-start(f32[16,17,256]{2,1,0:T(8,128)} %maximum_bitcast_fusion), calls=%async_computation.5 | async-start | bytes 786432 | tf_op jit(solution)/shard_map/all_to_all | solution.py:226
  171.9 0.7 copy-start.5
  174.4 11.0 %all-to-all-start.6 = ((f32[16,16,256]{2,1,0:T(8,128)}), f32[16,16,256]{2,1,0:T(8,128)S(1)}, u32[]{:S(2)}, u32[]{:S(2)}) async-start(f32[16,16,256]{2,1,0:T(8,128)} %get-tuple-element.23), calls=%async_computation.6 | async-start | bytes 524288 | tf_op jit(solution)/shard_map/all_to_all | solution.py:231
  185.4 21.9 %all-to-all-start.8 = ((bf16[4,512,256]{2,1,0:T(8,128)(2,1)}), bf16[4,512,256]{2,1,0:T(8,128)(2,1)S(1)}, u32[]{:S(2)}, u32[]{:S(2)}) async-start(bf16[4,512,256]{2,1,0:T(8,128)(2,1)} %bitcast.138), calls=%async_computation.8 | async-start | bytes 2097152 | tf_op jit(solution)/shard_map/all_to_all | solution.py:187
  189.0 70.8 %reduce-scatter.2.cloned.1.call-start = ((), (), s32[]{:S(2)}) async-start(), calls=%async_computation.12 | async-start | bytes 2621440 | tf_op jit(solution)/shard_map/reduce_scatter | solution.py:247
  229.0 0.7 copy-start.12
  229.0 8.6 %copy-start.18 = (s32[8]{0:T(128)S(1)}, s32[8]{0:T(128)}, u32[]{:S(2)}) copy-start(s32[8]{0:T(128)} %param.15) | copy-start | bytes 100
  229.0 30.8 %copy-start.2 = (bf16[1,128,2048]{2,1,0:T(8,128)(2,1)S(1)}, bf16[1,128,2048]{2,1,0:T(8,128)(2,1)}, u32[]{:S(2)}) copy-start(bf16[1,128,2048]{2,1,0:T(8,128)(2,1)} %param.13) | copy-start | bytes 1572868
  230.4 12.6 %all-to-all-start.9 = ((f32[8,1,16,256]{3,2,1,0:T(8,128)}), f32[8,1,16,256]{3,2,1,0:T(8,128)S(1)}, u32[]{:S(2)}, u32[]{:S(2)}) async-start(f32[8,1,16,256]{3,2,1,0:T(8,128)} %broadcast_in_dim.58), calls=%async_computation.10 | async-start | bytes 262144 | tf_op jit(solution)/shard_map/all_to_all | solution.py:17
Sparse Core Ops, SparseCore 0:
  11.3 82.4 all-gather.3
  99.0 56.5 all-gather.5
  229.2 30.5 reduce-scatter.1

commit v15 on v13

--- a/solution.py
+++ b/solution.py
@@ -56,7 +56,7 @@
 
     held0 = tuple(start_ref[n] for n in range(states))
     acc0 = jnp.zeros((SUB, LANES), jnp.float32)
-    held, acc = lax.fori_loop(0, steps, step, (held0, acc0), unroll=4)
+    held, acc = lax.fori_loop(0, steps, step, (held0, acc0), unroll=8)
     if not emit:
         for n in range(states):
             end_ref[n] = held[n]

time: 265 us -> 264 us (level)
  transfers between devices with their start and end apart: 10 -> 10, of which waited for: 7 -> 7; matrix products, arithmetic and copies ran while one was open for 18% -> 19% of each run, Pallas kernels for 10% -> 10%
where the time goes in v15:
time: 264 us; the launch traced here: 263 us
  waiting for transfers between devices  88.3 us (33%)
  local copies, waits for them, and re-layouts  37.8 us (14%)
  starting transfers between devices  36.6 us (14%)
  blocking collectives  31.3 us (12%)
  Pallas kernels  25.8 us (10%)
  matrix products  14.9 us (6%)
  between operations  14.2 us (5%)
  other arithmetic  13.8 us (5%)
    pallas_call x2, Pallas kernels, run_scan(): pl.pallas_call(functools.partial(scan_body, emit), grid=(chunks,), in_spe...  24 us
    all_to_all x1, waiting for transfers between devices, per_device(): lax.all_to_all(copies, seq, split_axis=0, concat_axis=0, tiled=True)  22.4 us
    all_to_all x2, waiting for transfers between devices, gather_a2a(): lax.all_to_all(copies, axis, split_axis=0, concat_axis=0, tiled=True)  22 us
    all_to_all x2, blocking collectives, gather_a2a(): lax.all_to_all(copies, axis, split_axis=0, concat_axis=0, tiled=True)  17.1 us
    reduce_scatter x1, waiting for transfers between devices, per_device(): lax.psum_scatter(partial.reshape(cols_n * rows, model), 'sy', scatter_dim...  16.2 us
    all_to_all x1, waiting for transfers between devices, per_device(): lax.all_to_all(inner, seq, split_axis=0, concat_axis=1, tiled=True)  15.3 us
    all_to_all x1, blocking collectives, per_device(): lax.all_to_all(scanned, 'sy', split_axis=2, concat_axis=0, tiled=True)  14.3 us
    all_to_all x2, starting transfers between devices, gather_a2a(): lax.all_to_all(copies, axis, split_axis=0, concat_axis=0, tiled=True)  12 us
  transfers between devices with their start and end apart: 10, of which 7 were waited for; matrix products, arithmetic and copies ran while one was open for 19% of the time, Pallas kernels for 10%

profile of v15, /device:TPU:1, one launch (start us, length us, event | category | flops | bytes accessed | tf_op | source)
XLA Modules:
  0.0 262.6 jit_solution(2000210354831624639)
XLA Ops:
  9.2 2.0 fusion.17
  12.6 8.6 %all-to-all-start.2 = ((bf16[16,289,128]{2,1,0:T(8,128)(2,1)}), bf16[16,289,128]{2,1,0:T(8,128)(2,1)S(1)}, u32[]{:S(2)}, u32[]{:S(2)}) async-start(bf16[16,289,128]{2,1,0:T(8,128)(2,1)} %broadcast_in_dim.54), calls=%async_computation.2 | async-start | bytes 2424832 | tf_op jit(solution)/shard_map/all_to_all | solution.py:172
  21.5 22.4 %all-to-all-done.2 = bf16[16,289,128]{2,1,0:T(8,128)(2,1)S(1)} async-done(((bf16[16,289,128]{2,1,0:T(8,128)(2,1)}), bf16[16,289,128]{2,1,0:T(8,128)(2,1)S(1)}, u32[]{:S(2)}, u32[]{:S(2)}) %all-to-all-start.2) | async-done | bytes 1183776 | tf_op jit(solution)/shard_map/all_to_all | solution.py:172
  44.3 8.9 %all_to_all.68 = bf16[2,1,16,289,128]{4,2,3,1,0:T(8,128)(2,1)S(1)} all-to-all(bf16[2,1,16,289,128]{4,2,3,1,0:T(8,128)(2,1)S(1)} %broadcast_in_dim.55), channel_id=1, replica_groups=mesh['rx'=4,'rc'=2,'sz'=4,'sy'=4] {'rc'}, dimensions={0} | all-to-all | bytes 4734976 | tf_op jit(solution)/shard_map/all_to_all | solution.py:17
  54.6 4.5 %all-to-all-start = ((bf16[4,1,3,256,256]{3,4,2,1,0:T(8,128)(2,1)}), bf16[4,1,3,256,256]{3,4,2,1,0:T(8,128)(2,1)}, u32[]{:S(2)}, u32[]{:S(2)}) async-start(bf16[4,1,3,256,256]{3,4,2,1,0:T(8,128)(2,1)} %broadcast_in_dim.23), calls=%async_computation | async-start | bytes 3145728 | tf_op jit(solution)/shard_map/all_to_all | solution.py:17
  62.9 16.7 %all-to-all-done = bf16[4,1,3,256,256]{3,4,2,1,0:T(8,128)(2,1)} async-done(((bf16[4,1,3,256,256]{3,4,2,1,0:T(8,128)(2,1)}), bf16[4,1,3,256,256]{3,4,2,1,0:T(8,128)(2,1)}, u32[]{:S(2)}, u32[]{:S(2)}) %all-to-all-start) | async-done | bytes 1572896 | tf_op jit(solution)/shard_map/all_to_all | solution.py:17
  79.6 2.7 %copy.61 = bf16[4,3,256,256]{2,0,3,1:T(4,128)(2,1)S(1)} copy(bf16[4,3,256,256]{2,3,1,0:T(8,128)(2,1)} %bitcast.5) | data formatting | bytes 3145728 | tf_op jit(solution)/shard_map/broadcast_in_dim | solution.py:16
  83.1 8.1 %all_to_all.69 = bf16[2,1,4,3,256,256]{4,2,5,3,1,0:T(4,128)(2,1)} all-to-all(bf16[2,1,4,3,256,256]{4,2,5,3,1,0:T(4,128)(2,1)S(1)} %broadcast_in_dim.25), channel_id=1, replica_groups=mesh['rx'=4,'rc'=2,'sz'=4,'sy'=4] {'rc'}, dimensions={0} | all-to-all | bytes 6291456 | tf_op jit(solution)/shard_map/all_to_all | solution.py:17
  91.2 4.4 %copy.62 = bf16[2,1,4,3,256,256]{5,4,3,0,2,1:T(8,128)(2,1)S(1)} copy(bf16[2,1,4,3,256,256]{4,2,5,3,1,0:T(4,128)(2,1)} %all_to_all.69) | data formatting | bytes 6291456 | tf_op jit(solution)/shard_map/all_to_all | solution.py:17
  99.5 6.9 %fusion.2 = f32[2048,512]{1,0:T(8,128)S(1)} fusion(bf16[2048,2048]{1,0:T(8,128)(2,1)} %all-gather.4.cloned.1.call-done, bf16[2048,256]{1,0:T(8,128)(2,1)S(1)} %get-tuple-element.27, bf16[2048,256]{1,0:T(8,128)(2,1)S(1)} %get-tuple-element.26), kind=kOutput, calls=%fused_computation.7 | convolution fusion | flops 4299161600 | bytes 14680064 | tf_op jit(solution)/shard_map/dot_general | solution.py:184
  106.7 1.7 copy-done.3
  108.4 2.4 multiply_convert_fusion
  110.8 4.0 %all-to-all-start.4 = ((bf16[16,128,256]{2,1,0:T(8,128)(2,1)}), bf16[16,128,256]{2,1,0:T(8,128)(2,1)S(1)}, u32[]{:S(2)}, u32[]{:S(2)}) async-start(bf16[16,128,256]{2,1,0:T(8,128)(2,1)} %bitcast.22), calls=%async_computation.4 | async-start | bytes 2097152 | tf_op jit(solution)/shard_map/all_to_all | solution.py:198
  117.6 15.3 %all-to-all-done.4 = bf16[16,128,256]{2,1,0:T(8,128)(2,1)S(1)} async-done(((bf16[16,128,256]{2,1,0:T(8,128)(2,1)}), bf16[16,128,256]{2,1,0:T(8,128)(2,1)S(1)}, u32[]{:S(2)}, u32[]{:S(2)}) %all-to-all-start.4) | async-done | bytes 1048608 | tf_op jit(solution)/shard_map/all_to_all | solution.py:198
  137.1 1.7 copy.81
  138.8 1.9 copy.77.value_ref
  141.4 10.2 %shard_map.140 = (f32[16,32,128]{2,1,0:T(8,128)}, f32[1,32,128]{2,1,0:T(8,128)}) custom-call(f32[2048]{0:T(1024)} %reshape.114.into_ref, f32[2048]{0:T(1024)} %reshape.115.outof_ref, f32[128,32,128]{2,1,0:T(8,128)} %bitcast.129, f32[128,32,128]{2,1,0:T(8,128)} %copy.77.value_ref, f32[16,32,128]{2,1,0:T(8,128)} %bitcast.135, ...), custom_call_target="tpu_custom_call" | custom-call | flops 50331648 | bytes 4194304 | tf_op jit(solution)/shard_map/pallas_call | solution.py:84
  154.4 4.8 %all-to-all-start.5 = ((f32[16,17,256]{2,1,0:T(8,128)}), f32[16,17,256]{2,1,0:T(8,128)S(1)}, u32[]{:S(2)}, u32[]{:S(2)}) async-start(f32[16,17,256]{2,1,0:T(8,128)} %maximum_bitcast_fusion), calls=%async_computation.5 | async-start | bytes 786432 | tf_op jit(solution)/shard_map/all_to_all | solution.py:228
  160.5 7.5 %all-to-all-done.5.pair_ref = f32[16,17,256]{2,1,0:T(8,128)S(1)} async-done(((f32[16,17,256]{2,1,0:T(8,128)}), f32[16,17,256]{2,1,0:T(8,128)S(1)}, u32[]{:S(2)}, u32[]{:S(2)}) %all-to-all-start.5) | async-done | bytes 278560 | tf_op jit(solution)/shard_map/all_to_all | solution.py:228
  168.8 1.7 shard_map.141
  170.6 3.5 %all-to-all-start.6 = ((f32[16,16,256]{2,1,0:T(8,128)}), f32[16,16,256]{2,1,0:T(8,128)S(1)}, u32[]{:S(2)}, u32[]{:S(2)}) async-start(f32[16,16,256]{2,1,0:T(8,128)} %get-tuple-element.23), calls=%async_computation.6 | async-start | bytes 524288 | tf_op jit(solution)/shard_map/all_to_all | solution.py:233
  174.1 2.7 %slice.114 = bf16[2048,256]{1,0:T(8,128)(2,1)} slice(f32[2048,512]{1,0:T(8,128)} %copy-done.3), slice={[0:2048], [256:512]} | slice | bytes 2097152 | tf_op jit(solution)/shard_map/slice | solution.py:188
  176.8 4.8 %all-to-all-done.6 = f32[16,16,256]{2,1,0:T(8,128)S(1)} async-done(((f32[16,16,256]{2,1,0:T(8,128)}), f32[16,16,256]{2,1,0:T(8,128)S(1)}, u32[]{:S(2)}, u32[]{:S(2)}) %all-to-all-start.6) | async-done | bytes 262176 | tf_op jit(solution)/shard_map/all_to_all | solution.py:233
  181.6 3.5 %all-to-all-start.8 = ((bf16[4,512,256]{2,1,0:T(8,128)(2,1)}), bf16[4,512,256]{2,1,0:T(8,128)(2,1)S(1)}, u32[]{:S(2)}, u32[]{:S(2)}) async-start(bf16[4,512,256]{2,1,0:T(8,128)(2,1)} %bitcast.35), calls=%async_computation.8 | async-start | bytes 2097152 | tf_op jit(solution)/shard_map/all_to_all | solution.py:189
  186.1 13.8 %shard_map.142 = f32[128,32,128]{2,1,0:T(8,128)} custom-call(f32[2048]{0:T(1024)} %reshape.114.into_ref, f32[2048]{0:T(1024)} %reshape.115.outof_ref, f32[128,32,128]{2,1,0:T(8,128)} %bitcast.130, f32[128,32,128]{2,1,0:T(8,128)} %copy.77.value_ref, f32[16,32,128]{2,1,0:T(8,128)} %bitcast.136, f32[16,32,128]{2,1,0:T(8,128)} %reshape_reshape.3.start_ref, ...), custom_call_target="tpu_custom_call" | custom-call | flops 50331648 | bytes 6291456 | tf_op jit(solution)/shard_map/pallas_call | solution.py:84
  199.9 1.8 convert_element_type.95
  202.7 14.3 %all_to_all.70 = bf16[128,4,4,256]{3,0,1,2:T(8,128)(2,1)S(1)} all-to-all(bf16[128,4,4,256]{3,0,1,2:T(8,128)(2,1)S(1)} %copy.73), channel_id=1, replica_groups=mesh['rx'=4,'rc'=2,'sz'=4,'sy'=4] {'sy'}, dimensions={2} | all-to-all | bytes 2097152 | tf_op jit(solution)/shard_map/all_to_all | solution.py:240
  217.0 6.1 %bitcast_convert_fusion = bf16[4,128,2048]{2,1,0:T(8,128)(2,1)} fusion(bf16[4,256,2048,1]{2,1,3,0:T(8,128)(2,1)} %bitcast.146, bf16[4,4,128,256]{3,2,1,0:T(8,128)(2,1)S(1)} %bitcast.133, bf16[128,4,4,256]{3,0,1,2:T(8,128)(2,1)S(1)} %all_to_all.70), kind=kOutput, calls=%fused_computation.2 | convolution fusion | flops 2152726528 | bytes 8388608 | tf_op jit(solution)/shard_map/ktac,acd->ktd/dot_general | solution.py:246
  224.5 7.5 %all-to-all-start.9 = ((f32[8,1,16,256]{3,2,1,0:T(8,128)}), f32[8,1,16,256]{3,2,1,0:T(8,128)S(1)}, u32[]{:S(2)}, u32[]{:S(2)}) async-start(f32[8,1,16,256]{3,2,1,0:T(8,128)} %broadcast_in_dim.58), calls=%async_computation.10 | async-start | bytes 262144 | tf_op jit(solution)/shard_map/all_to_all | solution.py:17
  231.9 5.3 %all-to-all-done.9 = f32[8,1,16,256]{3,2,1,0:T(8,128)S(1)} async-done(((f32[8,1,16,256]{3,2,1,0:T(8,128)}), f32[8,1,16,256]{3,2,1,0:T(8,128)S(1)}, u32[]{:S(2)}, u32[]{:S(2)}) %all-to-all-start.9) | async-done | bytes 131104 | tf_op jit(solution)/shard_map/all_to_all | solution.py:17
  237.9 16.2 %reduce-scatter.2.cloned.1.call-done = bf16[128,2048]{1,0:T(8,128)(2,1)} async-done(((bf16[512,2048]{1,0:T(8,128)(2,1)}), bf16[128,2048]{1,0:T(8,128)(2,1)}) %reduce-scatter.2.cloned.1.call-update) | async-done | bytes 524304 | tf_op jit(solution)/shard_map/reduce_scatter | solution.py:249
  254.1 2.0 fusion.22
  (95 shorter events, 30.5 us)
Async XLA Ops:
  7.2 4.1 %copy-start.13 = (bf16[256]{0:T(256)(128)(2,1)S(1)}, bf16[256]{0:T(256)(128)(2,1)}, u32[]{:S(2)}) copy-start(bf16[256]{0:T(256)(128)(2,1)} %param.22) | copy-start | bytes 1540
  7.2 4.1 %copy-start.10 = (bf16[128,256]{1,0:T(8,128)(2,1)S(1)}, bf16[128,256]{1,0:T(8,128)(2,1)}, u32[]{:S(2)}) copy-start(bf16[128,256]{1,0:T(8,128)(2,1)} %param.21) | copy-start | bytes 196612
  7.2 4.1 %copy-start.9 = (bf16[256,160]{0,1:T(8,128)(2,1)S(1)}, bf16[256,160]{0,1:T(8,128)(2,1)}, u32[]{:S(2)}) copy-start(bf16[256,160]{0,1:T(8,128)(2,1)} %param.20) | copy-start | bytes 245764
  7.2 89.7 %all-gather.4.cloned.1.call-start = ((), (), s32[]{:S(2)}) async-start(), calls=%async_computation.11 | async-start | bytes 8912896 | tf_op jit(solution)/shard_map/all_gather | solution.py:156
  11.2 9.9 %copy-start.8 = (bf16[256,256]{1,0:T(8,128)(2,1)S(1)}, bf16[256,256]{1,0:T(8,128)(2,1)}, u32[]{:S(2)}) copy-start(bf16[256,256]{1,0:T(8,128)(2,1)} %param.25) | copy-start | bytes 393220
  11.3 10.0 %copy-start.6 = (bf16[2,256,256]{2,1,0:T(8,128)(2,1)S(1)}, bf16[2,256,256]{2,1,0:T(8,128)(2,1)}, u32[]{:S(2)}) copy-start(bf16[2,256,256]{2,1,0:T(8,128)(2,1)} %param.17) | copy-start | bytes 786436
  12.6 31.3 %all-to-all-start.2 = ((bf16[16,289,128]{2,1,0:T(8,128)(2,1)}), bf16[16,289,128]{2,1,0:T(8,128)(2,1)S(1)}, u32[]{:S(2)}, u32[]{:S(2)}) async-start(bf16[16,289,128]{2,1,0:T(8,128)(2,1)} %broadcast_in_dim.54), calls=%async_computation.2 | async-start | bytes 2424832 | tf_op jit(solution)/shard_map/all_to_all | solution.py:172
  53.3 5.9 %copy-start.14 = (bf16[256]{0:T(256)(128)(2,1)S(1)}, bf16[256]{0:T(256)(128)(2,1)}, u32[]{:S(2)}) copy-start(bf16[256]{0:T(256)(128)(2,1)} %param.19) | copy-start | bytes 1540
  53.3 5.9 %copy-start.12 = (bf16[4,256]{1,0:T(4,128)(2,1)S(1)}, bf16[4,256]{1,0:T(4,128)(2,1)}, u32[]{:S(2)}) copy-start(bf16[4,256]{1,0:T(4,128)(2,1)} %param.18) | copy-start | bytes 6148
  54.6 25.0 %all-to-all-start = ((bf16[4,1,3,256,256]{3,4,2,1,0:T(8,128)(2,1)}), bf16[4,1,3,256,256]{3,4,2,1,0:T(8,128)(2,1)}, u32[]{:S(2)}, u32[]{:S(2)}) async-start(bf16[4,1,3,256,256]{3,4,2,1,0:T(8,128)(2,1)} %broadcast_in_dim.23), calls=%async_computation | async-start | bytes 3145728 | tf_op jit(solution)/shard_map/all_to_all | solution.py:17
  59.1 158.0 %all-gather.6.cloned.1.call-start = ((), (), s32[]{:S(2)}) async-start(), calls=%async_computation.13 | async-start | bytes 5242880 | tf_op jit(solution)/shard_map/all_gather | solution.py:186
  96.7 1.2 copy-start.2
  106.4 2.0 copy-start.3
  108.4 6.4 %copy-start.7 = (f32[16,4096]{1,0:T(8,128)S(1)}, f32[16,4096]{1,0:T(8,128)}, u32[]{:S(2)}) copy-start(f32[16,4096]{1,0:T(8,128)} %param.23) | copy-start | bytes 786436
  110.8 5.5 %copy-start.15 = (s32[8]{0:T(128)S(1)}, s32[8]{0:T(128)}, u32[]{:S(2)}) copy-start(s32[8]{0:T(128)} %param.14) | copy-start | bytes 100
  110.8 22.1 %all-to-all-start.4 = ((bf16[16,128,256]{2,1,0:T(8,128)(2,1)}), bf16[16,128,256]{2,1,0:T(8,128)(2,1)S(1)}, u32[]{:S(2)}, u32[]{:S(2)}) async-start(bf16[16,128,256]{2,1,0:T(8,128)(2,1)} %bitcast.22), calls=%async_computation.4 | async-start | bytes 2097152 | tf_op jit(solution)/shard_map/all_to_all | solution.py:198
  114.8 18.7 %copy-start = (bf16[20,8,16,256]{3,1,2,0:T(8,128)(2,1)S(1)}, bf16[20,8,16,256]{3,1,2,0:T(8,128)(2,1)}, u32[]{:S(2)}) copy-start(bf16[20,8,16,256]{3,1,2,0:T(8,128)(2,1)} %copy.79) | copy-start | bytes 3932164
  133.5 2.1 copy-start.5
  154.4 13.7 %all-to-all-start.5 = ((f32[16,17,256]{2,1,0:T(8,128)}), f32[16,17,256]{2,1,0:T(8,128)S(1)}, u32[]{:S(2)}, u32[]{:S(2)}) async-start(f32[16,17,256]{2,1,0:T(8,128)} %maximum_bitcast_fusion), calls=%async_computation.5 | async-start | bytes 786432 | tf_op jit(solution)/shard_map/all_to_all | solution.py:228
  168.1 0.7 copy-start.4
  170.6 11.0 %all-to-all-start.6 = ((f32[16,16,256]{2,1,0:T(8,128)}), f32[16,16,256]{2,1,0:T(8,128)S(1)}, u32[]{:S(2)}, u32[]{:S(2)}) async-start(f32[16,16,256]{2,1,0:T(8,128)} %get-tuple-element.23), calls=%async_computation.6 | async-start | bytes 524288 | tf_op jit(solution)/shard_map/all_to_all | solution.py:233
  181.6 21.1 %all-to-all-start.8 = ((bf16[4,512,256]{2,1,0:T(8,128)(2,1)}), bf16[4,512,256]{2,1,0:T(8,128)(2,1)S(1)}, u32[]{:S(2)}, u32[]{:S(2)}) async-start(bf16[4,512,256]{2,1,0:T(8,128)(2,1)} %bitcast.35), calls=%async_computation.8 | async-start | bytes 2097152 | tf_op jit(solution)/shard_map/all_to_all | solution.py:189
  185.1 69.0 %reduce-scatter.2.cloned.1.call-start = ((), (), s32[]{:S(2)}) async-start(), calls=%async_computation.12 | async-start | bytes 2621440 | tf_op jit(solution)/shard_map/reduce_scatter | solution.py:249
  223.1 0.7 copy-start.11
  223.1 8.8 %copy-start.16 = (s32[8]{0:T(128)S(1)}, s32[8]{0:T(128)}, u32[]{:S(2)}) copy-start(s32[8]{0:T(128)} %param.15) | copy-start | bytes 100
  223.1 31.0 %copy-start.1 = (bf16[1,128,2048]{2,1,0:T(8,128)(2,1)S(1)}, bf16[1,128,2048]{2,1,0:T(8,128)(2,1)}, u32[]{:S(2)}) copy-start(bf16[1,128,2048]{2,1,0:T(8,128)(2,1)} %param.13) | copy-start | bytes 1572868
  224.5 12.8 %all-to-all-start.9 = ((f32[8,1,16,256]{3,2,1,0:T(8,128)}), f32[8,1,16,256]{3,2,1,0:T(8,128)S(1)}, u32[]{:S(2)}, u32[]{:S(2)}) async-start(f32[8,1,16,256]{3,2,1,0:T(8,128)} %broadcast_in_dim.58), calls=%async_computation.10 | async-start | bytes 262144 | tf_op jit(solution)/shard_map/all_to_all | solution.py:17
Sparse Core Ops, SparseCore 0:
  11.4 82.4 all-gather.3
  99.5 55.7 all-gather.5
  223.2 30.8 reduce-scatter.1

commit v16 on v15

--- a/solution.py
+++ b/solution.py
@@ -56,7 +56,7 @@
 
     held0 = tuple(start_ref[n] for n in range(states))
     acc0 = jnp.zeros((SUB, LANES), jnp.float32)
-    held, acc = lax.fori_loop(0, steps, step, (held0, acc0), unroll=8)
+    held, acc = lax.fori_loop(0, steps, step, (held0, acc0), unroll=16)
     if not emit:
         for n in range(states):
             end_ref[n] = held[n]

time: 264 us -> 264 us (level)
  no operation moved by 1% of the time
where the time goes in v16:
time: 264 us; the launch traced here: 262 us
  waiting for transfers between devices  88.2 us (33%)
  local copies, waits for them, and re-layouts  37.8 us (14%)
  starting transfers between devices  36.6 us (14%)
  blocking collectives  31.3 us (12%)
  Pallas kernels  25.3 us (10%)
  matrix products  14.9 us (6%)
  between operations  14.2 us (5%)
  other arithmetic  13.8 us (5%)
    pallas_call x2, Pallas kernels, run_scan(): pl.pallas_call(functools.partial(scan_body, emit), grid=(chunks,), in_spe...  23.5 us
    all_to_all x1, waiting for transfers between devices, per_device(): lax.all_to_all(copies, seq, split_axis=0, concat_axis=0, tiled=True)  22.4 us
    all_to_all x2, waiting for transfers between devices, gather_a2a(): lax.all_to_all(copies, axis, split_axis=0, concat_axis=0, tiled=True)  22 us
    all_to_all x2, blocking collectives, gather_a2a(): lax.all_to_all(copies, axis, split_axis=0, concat_axis=0, tiled=True)  17.1 us
    reduce_scatter x1, waiting for transfers between devices, per_device(): lax.psum_scatter(partial.reshape(cols_n * rows, model), 'sy', scatter_dim...  16.2 us
    all_to_all x1, waiting for transfers between devices, per_device(): lax.all_to_all(inner, seq, split_axis=0, concat_axis=1, tiled=True)  15.3 us
    all_to_all x1, blocking collectives, per_device(): lax.all_to_all(scanned, 'sy', split_axis=2, concat_axis=0, tiled=True)  14.3 us
    all_to_all x2, starting transfers between devices, gather_a2a(): lax.all_to_all(copies, axis, split_axis=0, concat_axis=0, tiled=True)  12 us
  transfers between devices with their start and end apart: 10, of which 7 were waited for; matrix products, arithmetic and copies ran while one was open for 19% of the time, Pallas kernels for 10%

profile of v16, /device:TPU:1, one launch (start us, length us, event | category | flops | bytes accessed | tf_op | source)
XLA Modules:
  0.0 262.1 jit_solution(3910160389307196338)
XLA Ops:
  9.2 2.0 fusion.17
  12.6 8.6 %all-to-all-start.2 = ((bf16[16,289,128]{2,1,0:T(8,128)(2,1)}), bf16[16,289,128]{2,1,0:T(8,128)(2,1)S(1)}, u32[]{:S(2)}, u32[]{:S(2)}) async-start(bf16[16,289,128]{2,1,0:T(8,128)(2,1)} %broadcast_in_dim.54), calls=%async_computation.2 | async-start | bytes 2424832 | tf_op jit(solution)/shard_map/all_to_all | solution.py:172
  21.5 22.4 %all-to-all-done.2 = bf16[16,289,128]{2,1,0:T(8,128)(2,1)S(1)} async-done(((bf16[16,289,128]{2,1,0:T(8,128)(2,1)}), bf16[16,289,128]{2,1,0:T(8,128)(2,1)S(1)}, u32[]{:S(2)}, u32[]{:S(2)}) %all-to-all-start.2) | async-done | bytes 1183776 | tf_op jit(solution)/shard_map/all_to_all | solution.py:172
  44.3 8.9 %all_to_all.68 = bf16[2,1,16,289,128]{4,2,3,1,0:T(8,128)(2,1)S(1)} all-to-all(bf16[2,1,16,289,128]{4,2,3,1,0:T(8,128)(2,1)S(1)} %broadcast_in_dim.55), channel_id=1, replica_groups=mesh['rx'=4,'rc'=2,'sz'=4,'sy'=4] {'rc'}, dimensions={0} | all-to-all | bytes 4734976 | tf_op jit(solution)/shard_map/all_to_all | solution.py:17
  54.6 4.5 %all-to-all-start = ((bf16[4,1,3,256,256]{3,4,2,1,0:T(8,128)(2,1)}), bf16[4,1,3,256,256]{3,4,2,1,0:T(8,128)(2,1)}, u32[]{:S(2)}, u32[]{:S(2)}) async-start(bf16[4,1,3,256,256]{3,4,2,1,0:T(8,128)(2,1)} %broadcast_in_dim.23), calls=%async_computation | async-start | bytes 3145728 | tf_op jit(solution)/shard_map/all_to_all | solution.py:17
  62.9 16.7 %all-to-all-done = bf16[4,1,3,256,256]{3,4,2,1,0:T(8,128)(2,1)} async-done(((bf16[4,1,3,256,256]{3,4,2,1,0:T(8,128)(2,1)}), bf16[4,1,3,256,256]{3,4,2,1,0:T(8,128)(2,1)}, u32[]{:S(2)}, u32[]{:S(2)}) %all-to-all-start) | async-done | bytes 1572896 | tf_op jit(solution)/shard_map/all_to_all | solution.py:17
  79.6 2.7 %copy.61 = bf16[4,3,256,256]{2,0,3,1:T(4,128)(2,1)S(1)} copy(bf16[4,3,256,256]{2,3,1,0:T(8,128)(2,1)} %bitcast.5) | data formatting | bytes 3145728 | tf_op jit(solution)/shard_map/broadcast_in_dim | solution.py:16
  83.1 8.1 %all_to_all.69 = bf16[2,1,4,3,256,256]{4,2,5,3,1,0:T(4,128)(2,1)} all-to-all(bf16[2,1,4,3,256,256]{4,2,5,3,1,0:T(4,128)(2,1)S(1)} %broadcast_in_dim.25), channel_id=1, replica_groups=mesh['rx'=4,'rc'=2,'sz'=4,'sy'=4] {'rc'}, dimensions={0} | all-to-all | bytes 6291456 | tf_op jit(solution)/shard_map/all_to_all | solution.py:17
  91.2 4.4 %copy.62 = bf16[2,1,4,3,256,256]{5,4,3,0,2,1:T(8,128)(2,1)S(1)} copy(bf16[2,1,4,3,256,256]{4,2,5,3,1,0:T(4,128)(2,1)} %all_to_all.69) | data formatting | bytes 6291456 | tf_op jit(solution)/shard_map/all_to_all | solution.py:17
  99.5 6.9 %fusion.2 = f32[2048,512]{1,0:T(8,128)S(1)} fusion(bf16[2048,2048]{1,0:T(8,128)(2,1)} %all-gather.4.cloned.1.call-done, bf16[2048,256]{1,0:T(8,128)(2,1)S(1)} %get-tuple-element.27, bf16[2048,256]{1,0:T(8,128)(2,1)S(1)} %get-tuple-element.26), kind=kOutput, calls=%fused_computation.7 | convolution fusion | flops 4299161600 | bytes 14680064 | tf_op jit(solution)/shard_map/dot_general | solution.py:184
  106.7 1.7 copy-done.3
  108.4 2.4 multiply_convert_fusion
  110.8 4.0 %all-to-all-start.4 = ((bf16[16,128,256]{2,1,0:T(8,128)(2,1)}), bf16[16,128,256]{2,1,0:T(8,128)(2,1)S(1)}, u32[]{:S(2)}, u32[]{:S(2)}) async-start(bf16[16,128,256]{2,1,0:T(8,128)(2,1)} %bitcast.22), calls=%async_computation.4 | async-start | bytes 2097152 | tf_op jit(solution)/shard_map/all_to_all | solution.py:198
  117.6 15.3 %all-to-all-done.4 = bf16[16,128,256]{2,1,0:T(8,128)(2,1)S(1)} async-done(((bf16[16,128,256]{2,1,0:T(8,128)(2,1)}), bf16[16,128,256]{2,1,0:T(8,128)(2,1)S(1)}, u32[]{:S(2)}, u32[]{:S(2)}) %all-to-all-start.4) | async-done | bytes 1048608 | tf_op jit(solution)/shard_map/all_to_all | solution.py:198
  137.1 1.7 copy.81
  138.8 1.9 copy.77.value_ref
  141.4 10.0 %shard_map.140 = (f32[16,32,128]{2,1,0:T(8,128)}, f32[1,32,128]{2,1,0:T(8,128)}) custom-call(f32[2048]{0:T(1024)} %reshape.114.into_ref, f32[2048]{0:T(1024)} %reshape.115.outof_ref, f32[128,32,128]{2,1,0:T(8,128)} %bitcast.129, f32[128,32,128]{2,1,0:T(8,128)} %copy.77.value_ref, f32[16,32,128]{2,1,0:T(8,128)} %bitcast.135, ...), custom_call_target="tpu_custom_call" | custom-call | flops 50331648 | bytes 4194304 | tf_op jit(solution)/shard_map/pallas_call | solution.py:84
  154.2 4.8 %all-to-all-start.5 = ((f32[16,17,256]{2,1,0:T(8,128)}), f32[16,17,256]{2,1,0:T(8,128)S(1)}, u32[]{:S(2)}, u32[]{:S(2)}) async-start(f32[16,17,256]{2,1,0:T(8,128)} %maximum_bitcast_fusion), calls=%async_computation.5 | async-start | bytes 786432 | tf_op jit(solution)/shard_map/all_to_all | solution.py:228
  160.3 7.5 %all-to-all-done.5.pair_ref = f32[16,17,256]{2,1,0:T(8,128)S(1)} async-done(((f32[16,17,256]{2,1,0:T(8,128)}), f32[16,17,256]{2,1,0:T(8,128)S(1)}, u32[]{:S(2)}, u32[]{:S(2)}) %all-to-all-start.5) | async-done | bytes 278560 | tf_op jit(solution)/shard_map/all_to_all | solution.py:228
  168.6 1.7 shard_map.141
  170.3 3.5 %all-to-all-start.6 = ((f32[16,16,256]{2,1,0:T(8,128)}), f32[16,16,256]{2,1,0:T(8,128)S(1)}, u32[]{:S(2)}, u32[]{:S(2)}) async-start(f32[16,16,256]{2,1,0:T(8,128)} %get-tuple-element.23), calls=%async_computation.6 | async-start | bytes 524288 | tf_op jit(solution)/shard_map/all_to_all | solution.py:233
  173.9 2.7 %slice.114 = bf16[2048,256]{1,0:T(8,128)(2,1)} slice(f32[2048,512]{1,0:T(8,128)} %copy-done.3), slice={[0:2048], [256:512]} | slice | bytes 2097152 | tf_op jit(solution)/shard_map/slice | solution.py:188
  176.6 4.8 %all-to-all-done.6 = f32[16,16,256]{2,1,0:T(8,128)S(1)} async-done(((f32[16,16,256]{2,1,0:T(8,128)}), f32[16,16,256]{2,1,0:T(8,128)S(1)}, u32[]{:S(2)}, u32[]{:S(2)}) %all-to-all-start.6) | async-done | bytes 262176 | tf_op jit(solution)/shard_map/all_to_all | solution.py:233
  181.4 3.5 %all-to-all-start.8 = ((bf16[4,512,256]{2,1,0:T(8,128)(2,1)}), bf16[4,512,256]{2,1,0:T(8,128)(2,1)S(1)}, u32[]{:S(2)}, u32[]{:S(2)}) async-start(bf16[4,512,256]{2,1,0:T(8,128)(2,1)} %bitcast.35), calls=%async_computation.8 | async-start | bytes 2097152 | tf_op jit(solution)/shard_map/all_to_all | solution.py:189
  185.9 13.5 %shard_map.142 = f32[128,32,128]{2,1,0:T(8,128)} custom-call(f32[2048]{0:T(1024)} %reshape.114.into_ref, f32[2048]{0:T(1024)} %reshape.115.outof_ref, f32[128,32,128]{2,1,0:T(8,128)} %bitcast.130, f32[128,32,128]{2,1,0:T(8,128)} %copy.77.value_ref, f32[16,32,128]{2,1,0:T(8,128)} %bitcast.136, f32[16,32,128]{2,1,0:T(8,128)} %reshape_reshape.3.start_ref, ...), custom_call_target="tpu_custom_call" | custom-call | flops 50331648 | bytes 6291456 | tf_op jit(solution)/shard_map/pallas_call | solution.py:84
  199.3 1.8 convert_element_type.95
  202.2 14.3 %all_to_all.70 = bf16[128,4,4,256]{3,0,1,2:T(8,128)(2,1)S(1)} all-to-all(bf16[128,4,4,256]{3,0,1,2:T(8,128)(2,1)S(1)} %copy.73), channel_id=1, replica_groups=mesh['rx'=4,'rc'=2,'sz'=4,'sy'=4] {'sy'}, dimensions={2} | all-to-all | bytes 2097152 | tf_op jit(solution)/shard_map/all_to_all | solution.py:240
  216.5 6.1 %bitcast_convert_fusion = bf16[4,128,2048]{2,1,0:T(8,128)(2,1)} fusion(bf16[4,256,2048,1]{2,1,3,0:T(8,128)(2,1)} %bitcast.146, bf16[4,4,128,256]{3,2,1,0:T(8,128)(2,1)S(1)} %bitcast.133, bf16[128,4,4,256]{3,0,1,2:T(8,128)(2,1)S(1)} %all_to_all.70), kind=kOutput, calls=%fused_computation.2 | convolution fusion | flops 2152726528 | bytes 8388608 | tf_op jit(solution)/shard_map/ktac,acd->ktd/dot_general | solution.py:246
  224.0 7.5 %all-to-all-start.9 = ((f32[8,1,16,256]{3,2,1,0:T(8,128)}), f32[8,1,16,256]{3,2,1,0:T(8,128)S(1)}, u32[]{:S(2)}, u32[]{:S(2)}) async-start(f32[8,1,16,256]{3,2,1,0:T(8,128)} %broadcast_in_dim.58), calls=%async_computation.10 | async-start | bytes 262144 | tf_op jit(solution)/shard_map/all_to_all | solution.py:17
  231.4 5.3 %all-to-all-done.9 = f32[8,1,16,256]{3,2,1,0:T(8,128)S(1)} async-done(((f32[8,1,16,256]{3,2,1,0:T(8,128)}), f32[8,1,16,256]{3,2,1,0:T(8,128)S(1)}, u32[]{:S(2)}, u32[]{:S(2)}) %all-to-all-start.9) | async-done | bytes 131104 | tf_op jit(solution)/shard_map/all_to_all | solution.py:17
  237.4 16.2 %reduce-scatter.2.cloned.1.call-done = bf16[128,2048]{1,0:T(8,128)(2,1)} async-done(((bf16[512,2048]{1,0:T(8,128)(2,1)}), bf16[128,2048]{1,0:T(8,128)(2,1)}) %reduce-scatter.2.cloned.1.call-update) | async-done | bytes 524304 | tf_op jit(solution)/shard_map/reduce_scatter | solution.py:249
  253.6 2.0 fusion.22
  (95 shorter events, 30.5 us)
Async XLA Ops:
  7.2 4.1 %copy-start.13 = (bf16[256]{0:T(256)(128)(2,1)S(1)}, bf16[256]{0:T(256)(128)(2,1)}, u32[]{:S(2)}) copy-start(bf16[256]{0:T(256)(128)(2,1)} %param.22) | copy-start | bytes 1540
  7.2 4.1 %copy-start.10 = (bf16[128,256]{1,0:T(8,128)(2,1)S(1)}, bf16[128,256]{1,0:T(8,128)(2,1)}, u32[]{:S(2)}) copy-start(bf16[128,256]{1,0:T(8,128)(2,1)} %param.21) | copy-start | bytes 196612
  7.2 4.1 %copy-start.9 = (bf16[256,160]{0,1:T(8,128)(2,1)S(1)}, bf16[256,160]{0,1:T(8,128)(2,1)}, u32[]{:S(2)}) copy-start(bf16[256,160]{0,1:T(8,128)(2,1)} %param.20) | copy-start | bytes 245764
  7.2 89.7 %all-gather.4.cloned.1.call-start = ((), (), s32[]{:S(2)}) async-start(), calls=%async_computation.11 | async-start | bytes 8912896 | tf_op jit(solution)/shard_map/all_gather | solution.py:156
  11.2 9.9 %copy-start.8 = (bf16[256,256]{1,0:T(8,128)(2,1)S(1)}, bf16[256,256]{1,0:T(8,128)(2,1)}, u32[]{:S(2)}) copy-start(bf16[256,256]{1,0:T(8,128)(2,1)} %param.25) | copy-start | bytes 393220
  11.3 10.0 %copy-start.6 = (bf16[2,256,256]{2,1,0:T(8,128)(2,1)S(1)}, bf16[2,256,256]{2,1,0:T(8,128)(2,1)}, u32[]{:S(2)}) copy-start(bf16[2,256,256]{2,1,0:T(8,128)(2,1)} %param.17) | copy-start | bytes 786436
  12.6 31.3 %all-to-all-start.2 = ((bf16[16,289,128]{2,1,0:T(8,128)(2,1)}), bf16[16,289,128]{2,1,0:T(8,128)(2,1)S(1)}, u32[]{:S(2)}, u32[]{:S(2)}) async-start(bf16[16,289,128]{2,1,0:T(8,128)(2,1)} %broadcast_in_dim.54), calls=%async_computation.2 | async-start | bytes 2424832 | tf_op jit(solution)/shard_map/all_to_all | solution.py:172
  53.3 5.9 %copy-start.14 = (bf16[256]{0:T(256)(128)(2,1)S(1)}, bf16[256]{0:T(256)(128)(2,1)}, u32[]{:S(2)}) copy-start(bf16[256]{0:T(256)(128)(2,1)} %param.19) | copy-start | bytes 1540
  53.3 5.9 %copy-start.12 = (bf16[4,256]{1,0:T(4,128)(2,1)S(1)}, bf16[4,256]{1,0:T(4,128)(2,1)}, u32[]{:S(2)}) copy-start(bf16[4,256]{1,0:T(4,128)(2,1)} %param.18) | copy-start | bytes 6148
  54.6 25.0 %all-to-all-start = ((bf16[4,1,3,256,256]{3,4,2,1,0:T(8,128)(2,1)}), bf16[4,1,3,256,256]{3,4,2,1,0:T(8,128)(2,1)}, u32[]{:S(2)}, u32[]{:S(2)}) async-start(bf16[4,1,3,256,256]{3,4,2,1,0:T(8,128)(2,1)} %broadcast_in_dim.23), calls=%async_computation | async-start | bytes 3145728 | tf_op jit(solution)/shard_map/all_to_all | solution.py:17
  59.1 157.4 %all-gather.6.cloned.1.call-start = ((), (), s32[]{:S(2)}) async-start(), calls=%async_computation.13 | async-start | bytes 5242880 | tf_op jit(solution)/shard_map/all_gather | solution.py:186
  96.7 1.2 copy-start.2
  106.4 2.0 copy-start.3
  108.4 6.4 %copy-start.7 = (f32[16,4096]{1,0:T(8,128)S(1)}, f32[16,4096]{1,0:T(8,128)}, u32[]{:S(2)}) copy-start(f32[16,4096]{1,0:T(8,128)} %param.23) | copy-start | bytes 786436
  110.8 5.5 %copy-start.15 = (s32[8]{0:T(128)S(1)}, s32[8]{0:T(128)}, u32[]{:S(2)}) copy-start(s32[8]{0:T(128)} %param.14) | copy-start | bytes 100
  110.8 22.1 %all-to-all-start.4 = ((bf16[16,128,256]{2,1,0:T(8,128)(2,1)}), bf16[16,128,256]{2,1,0:T(8,128)(2,1)S(1)}, u32[]{:S(2)}, u32[]{:S(2)}) async-start(bf16[16,128,256]{2,1,0:T(8,128)(2,1)} %bitcast.22), calls=%async_computation.4 | async-start | bytes 2097152 | tf_op jit(solution)/shard_map/all_to_all | solution.py:198
  114.8 18.7 %copy-start = (bf16[20,8,16,256]{3,1,2,0:T(8,128)(2,1)S(1)}, bf16[20,8,16,256]{3,1,2,0:T(8,128)(2,1)}, u32[]{:S(2)}) copy-start(bf16[20,8,16,256]{3,1,2,0:T(8,128)(2,1)} %copy.79) | copy-start | bytes 3932164
  133.5 2.1 copy-start.5
  154.2 13.7 %all-to-all-start.5 = ((f32[16,17,256]{2,1,0:T(8,128)}), f32[16,17,256]{2,1,0:T(8,128)S(1)}, u32[]{:S(2)}, u32[]{:S(2)}) async-start(f32[16,17,256]{2,1,0:T(8,128)} %maximum_bitcast_fusion), calls=%async_computation.5 | async-start | bytes 786432 | tf_op jit(solution)/shard_map/all_to_all | solution.py:228
  167.9 0.7 copy-start.4
  170.3 11.0 %all-to-all-start.6 = ((f32[16,16,256]{2,1,0:T(8,128)}), f32[16,16,256]{2,1,0:T(8,128)S(1)}, u32[]{:S(2)}, u32[]{:S(2)}) async-start(f32[16,16,256]{2,1,0:T(8,128)} %get-tuple-element.23), calls=%async_computation.6 | async-start | bytes 524288 | tf_op jit(solution)/shard_map/all_to_all | solution.py:233
  181.4 20.8 %all-to-all-start.8 = ((bf16[4,512,256]{2,1,0:T(8,128)(2,1)}), bf16[4,512,256]{2,1,0:T(8,128)(2,1)S(1)}, u32[]{:S(2)}, u32[]{:S(2)}) async-start(bf16[4,512,256]{2,1,0:T(8,128)(2,1)} %bitcast.35), calls=%async_computation.8 | async-start | bytes 2097152 | tf_op jit(solution)/shard_map/all_to_all | solution.py:189
  184.9 68.7 %reduce-scatter.2.cloned.1.call-start = ((), (), s32[]{:S(2)}) async-start(), calls=%async_computation.12 | async-start | bytes 2621440 | tf_op jit(solution)/shard_map/reduce_scatter | solution.py:249
  222.6 0.7 copy-start.11
  222.6 8.8 %copy-start.16 = (s32[8]{0:T(128)S(1)}, s32[8]{0:T(128)}, u32[]{:S(2)}) copy-start(s32[8]{0:T(128)} %param.15) | copy-start | bytes 100
  222.6 31.0 %copy-start.1 = (bf16[1,128,2048]{2,1,0:T(8,128)(2,1)S(1)}, bf16[1,128,2048]{2,1,0:T(8,128)(2,1)}, u32[]{:S(2)}) copy-start(bf16[1,128,2048]{2,1,0:T(8,128)(2,1)} %param.13) | copy-start | bytes 1572868
  224.0 12.8 %all-to-all-start.9 = ((f32[8,1,16,256]{3,2,1,0:T(8,128)}), f32[8,1,16,256]{3,2,1,0:T(8,128)S(1)}, u32[]{:S(2)}, u32[]{:S(2)}) async-start(f32[8,1,16,256]{3,2,1,0:T(8,128)} %broadcast_in_dim.58), calls=%async_computation.10 | async-start | bytes 262144 | tf_op jit(solution)/shard_map/all_to_all | solution.py:17
Sparse Core Ops, SparseCore 0:
  11.4 82.4 all-gather.3
  99.5 55.7 all-gather.5
  222.7 30.8 reduce-scatter.1
